TPU v7x, 32 devices: a whole 2x2x4 slice. The times are simulated.
32 devices in a mesh: uv: 8 (over z, y), tm: 4 (over x, core).
Axes of the slice: x: 2, y: 2, z: 4, core: 2. Of those that a mesh axis runs over, the one named last changes fastest.
Arguments:
- visibility: bfloat16 [4, 1024, 2048], P('tm', 'uv'), may hold values from -1536 to 1536
- anchor: int32 [4, 1024], P('tm', 'uv'), may hold values from 0 to 80
- offset: int32 [4, 1024], P('tm', 'uv'), may hold values from 0 to 63
- slot_rows: int32 [4, 8, 8, 32], P('tm', 'uv'), may hold values from 0 to 127, as said below
- counts: int32 [4, 8, 8], P('tm', 'uv'), may hold values from 0 to 32, as said below
Outputs:
- delay: float32 [2048, 2048], P(('uv', 'tm'))
Inputs may be any that keep to these rules, and one draw needn't show every extreme that they name: For every g and s the first counts[g, s, d] entries of slot_rows[g, s, d] over all d name each of the 128 rows of device s exactly once; entries at slots k >= counts[g, s, d] are arbitrary rows and are not used. counts[g, s, :] sums to 128; in each time group one tile receives 32 rows from every device and another tile none; the other tiles come in pairs whose counts from one device sum to 32.
All inputs are finite; a program needn't handle non-finite values.
Results may differ from a plain program's by a relative error of at most 0.0047.
Values may be sent and summed in bfloat16 or wider, within the bound.
No kernel may reach another device: no remote copies, remote signals or barrier semaphores. Data moves between devices by JAX's collectives and lax.ppermute only.
A program may use at most 64 MiB of HBM per device.

v0:
```python
import math

import jax
import jax.numpy as jnp
from jax import lax
from jax.sharding import PartitionSpec as P

NCH = 1024
ROWS_DEV = 128
TS = 16
KTAPS = 8
OSAMP = 8


def kernel_taps(offsets):
    tap_index = jnp.arange(KTAPS, dtype=jnp.float32)
    sub_shift = (offsets.astype(jnp.float32) + 0.5) / OSAMP
    distance = tap_index[None, :] - (KTAPS / 2 - 1.0) - sub_shift[:, None]
    return jnp.exp(-distance * distance / (2.0 * 1.2 * 1.2))


def tap_matrix(cell_ids, anchors, offsets):
    span = TS - KTAPS + 1
    anchor_y = anchors // span
    anchor_x = anchors % span
    taps_y = kernel_taps(offsets // OSAMP)
    taps_x = kernel_taps(offsets % OSAMP)
    cell_y = cell_ids // TS
    cell_x = cell_ids % TS
    along_y = jnp.zeros((cell_ids.shape[0], anchors.shape[0]), jnp.float32)
    along_x = jnp.zeros((cell_ids.shape[0], anchors.shape[0]), jnp.float32)
    for step in range(KTAPS):
        along_y = along_y + jnp.where(
            cell_y[:, None] == anchor_y[None, :] + step, taps_y[None, :, step], 0.0
        )
        along_x = along_x + jnp.where(
            cell_x[:, None] == anchor_x[None, :] + step, taps_x[None, :, step], 0.0
        )
    return (along_y * along_x).astype(jnp.bfloat16)


def delay_table():
    freq = jnp.arange(NCH, dtype=jnp.int32)
    phase = freq[:, None] * freq[None, :] % NCH
    angle = 2.0 * math.pi / NCH * phase.astype(jnp.float32)
    cosine = jnp.cos(angle)
    sine = jnp.sin(angle)
    window_arg = 2.0 * math.pi * freq.astype(jnp.float32) / (NCH - 1)
    taper = (
        0.35875
        - 0.48829 * jnp.cos(window_arg)
        + 0.14128 * jnp.cos(2.0 * window_arg)
        - 0.01168 * jnp.cos(3.0 * window_arg)
    )
    tap_cos = taper[:, None] * cosine
    tap_sin = taper[:, None] * sine
    upper = jnp.concatenate([tap_cos, -tap_sin], axis=1)
    lower = jnp.concatenate([tap_sin, tap_cos], axis=1)
    return jnp.concatenate([upper, lower], axis=0).astype(jnp.bfloat16)


def per_device(visibility, anchor, offset, slot_rows, counts):
    time_groups = lax.axis_size("tm")
    cell_share = TS * TS // time_groups
    vis_rows = visibility[0]
    row_width = vis_rows.shape[1]
    slot_table = slot_rows[0, 0]
    tile_count, slot_depth = slot_table.shape
    is_live = (jnp.arange(slot_depth, dtype=jnp.int32)[None, :] < counts[0, 0][:, None]).reshape(-1)
    flat_index = slot_table.reshape(-1)
    outgoing = jnp.where(
        is_live[:, None], jnp.take(vis_rows, flat_index, axis=0), jnp.zeros((), vis_rows.dtype)
    )
    outgoing = outgoing.reshape(tile_count, slot_depth, row_width)
    out_anchor = jnp.take(anchor[0], flat_index).reshape(tile_count, slot_depth)
    out_offset = jnp.take(offset[0], flat_index).reshape(tile_count, slot_depth)
    arrived, arr_anchor, arr_offset = (
        lax.all_to_all(outgoing, "uv", split_axis=0, concat_axis=0, tiled=True),
        lax.all_to_all(out_anchor, "uv", split_axis=0, concat_axis=0, tiled=True),
        lax.all_to_all(out_offset, "uv", split_axis=0, concat_axis=0, tiled=True),
    )
    my_start = lax.axis_index("tm") * cell_share
    all_cells = jnp.arange(TS * TS, dtype=jnp.int32)
    weights = tap_matrix(all_cells, arr_anchor.reshape(-1), arr_offset.reshape(-1))
    flat_vis = arrived.reshape(-1, row_width)
    full_sum = lax.psum(jnp.dot(weights, flat_vis, preferred_element_type=jnp.float32), "tm")
    summed = lax.dynamic_slice_in_dim(full_sum, my_start, cell_share, 0)
    grid = summed.astype(jnp.bfloat16)
    transform = delay_table()
    out_scale = 4.0 / math.sqrt(NCH * time_groups * ROWS_DEV)
    return jnp.dot(grid, transform, preferred_element_type=jnp.float32) * out_scale


def solution(mesh):
    in_specs = (
        P("tm", "uv", None),
        P("tm", "uv"),
        P("tm", "uv"),
        P("tm", "uv", None, None),
        P("tm", "uv", None),
    )
    out_specs = P(("uv", "tm"), None)
    return jax.shard_map(
        per_device, mesh=mesh, in_specs=in_specs, out_specs=out_specs, check_vma=False
    )
```

profile of v0, /device:TPU:0, one launch (start us, length us, event | category | flops | bytes accessed | tf_op | source)
XLA Modules:
  0.0 105.8 jit_solution(13739666395043265725)
XLA Ops:
  0.0 0.0 copy-start
  0.0 0.0 copy-start.2
  0.0 0.0 copy-start.3
  0.0 0.8 reshape_squeeze.7
  0.9 1.9 %gather_fusion.2 = s32[256]{0:T(256)S(1)} fusion(s32[128]{0:T(128)} %bitcast.33, s32[1024]{0:T(1024)S(1)} %pad_clamp_fusion.1), kind=kCustom, calls=%fused_computation.1.clone | custom fusion | bytes 3072 | tf_op jit(solution)/shard_map/jit(_take)/gather | solution.py:76
  2.7 1.9 %gather_fusion.1 = s32[256]{0:T(256)S(1)} fusion(s32[128]{0:T(128)} %bitcast.34, s32[1024]{0:T(1024)S(1)} %pad_clamp_fusion.1), kind=kCustom, calls=%fused_computation.clone | custom fusion | bytes 3072 | tf_op jit(solution)/shard_map/jit(_take)/gather | solution.py:75
  4.7 0.7 all_to_all.17
  5.3 7.3 %all-to-all-start.1 = ((s32[8,1,32]{2,1,0:T(1,128)}), s32[8,1,32]{2,1,0:T(1,128)S(1)}, u32[]{:S(2)}, u32[]{:S(2)}) async-start(s32[8,1,32]{2,1,0:T(1,128)} %all_to_all.17), calls=%async_computation.1 | async-start | bytes 8192 | tf_op jit(solution)/shard_map/all_to_all | solution.py:80
  12.6 0.0 copy-done.2
  12.6 0.1 reshape_squeeze.9
  12.7 0.1 multiply_subtract_fusion
  12.8 0.0 copy-done.3
  12.8 0.1 iota_compare_fusion
  12.9 0.0 copy-done
  12.9 1.4 %gather_fusion = bf16[256,2048]{1,0:T(8,128)(2,1)S(1)} fusion(bf16[128,2048]{1,0:T(8,128)(2,1)S(1)} %bitcast.32, s32[1024]{0:T(1024)S(1)} %pad_clamp_fusion), kind=kCustom, calls=%fused_computation.2 | custom fusion | bytes 2098176 | tf_op jit(solution)/shard_map/jit(_take)/gather | solution.py:72
  14.2 1.2 %select_select_fusion = bf16[8,32,2048]{2,1,0:T(8,128)(2,1)} fusion(bf16[8,32,2048]{2,1,0:T(8,128)(2,1)S(1)} %bitcast.35, pred[8,32]{1,0:T(8,128)(4,1)S(1)} %get-tuple-element.60, pred[8,32]{1,0:T(8,128)(4,1)S(1)} %get-tuple-element.59), kind=kLoop, calls=%fused_computation.25 | loop fusion | flops 1048576 | bytes 2097664 | tf_op jit(solution)/shard_map/jit(_where)/select_n | solution.py:71
  15.4 0.7 all_to_all.15
  16.1 2.9 %all-to-all-done.1 = s32[8,1,32]{2,1,0:T(1,128)S(1)} async-done(((s32[8,1,32]{2,1,0:T(1,128)}), s32[8,1,32]{2,1,0:T(1,128)S(1)}, u32[]{:S(2)}, u32[]{:S(2)}) %all-to-all-start.1) | async-done | bytes 1056 | tf_op jit(solution)/shard_map/all_to_all | solution.py:80
  19.0 3.2 %all-to-all-start = ((s32[8,1,32]{2,1,0:T(1,128)}), s32[8,1,32]{2,1,0:T(1,128)S(1)}, u32[]{:S(2)}, u32[]{:S(2)}) async-start(s32[8,1,32]{2,1,0:T(1,128)} %all_to_all.15), calls=%async_computation | async-start | bytes 8192 | tf_op jit(solution)/shard_map/all_to_all | solution.py:79
  22.3 6.4 %all-to-all-done = s32[8,1,32]{2,1,0:T(1,128)S(1)} async-done(((s32[8,1,32]{2,1,0:T(1,128)}), s32[8,1,32]{2,1,0:T(1,128)S(1)}, u32[]{:S(2)}, u32[]{:S(2)}) %all-to-all-start) | async-done | bytes 1056 | tf_op jit(solution)/shard_map/all_to_all | solution.py:79
  28.7 3.6 %all-to-all-start.2 = ((bf16[8,32,2048]{2,1,0:T(8,128)(2,1)}), bf16[8,32,2048]{2,1,0:T(8,128)(2,1)S(1)}, u32[]{:S(2)}, u32[]{:S(2)}) async-start(bf16[8,32,2048]{2,1,0:T(8,128)(2,1)} %select_select_fusion), calls=%async_computation.2 | async-start | bytes 2097152 | tf_op jit(solution)/shard_map/all_to_all | solution.py:78
  32.2 19.1 %negate_convert_fusion = (bf16[1024,1024]{1,0:T(8,128)(2,1)}, bf16[1024,1024]{1,0:T(8,128)(2,1)}, bf16[1024,1024]{1,0:T(8,128)(2,1)}) fusion(f32[1024]{0:T(1024)S(1)} %multiply_subtract_fusion), kind=kLoop, calls=%fused_computation.17 | loop fusion | flops 20971520 | bytes 6295552 | tf_op jit(solution)/shard_map/convert.5
  51.3 0.5 broadcast.585
  51.8 0.7 reduce.13
  52.5 0.1 reshape.340
  52.6 0.1 ne.248
  52.7 0.1 div.91
  52.8 0.1 rem.188
  52.9 0.1 fusion.55
  53.0 3.3 %all-to-all-done.2 = bf16[8,32,2048]{2,1,0:T(8,128)(2,1)S(1)} async-done(((bf16[8,32,2048]{2,1,0:T(8,128)(2,1)}), bf16[8,32,2048]{2,1,0:T(8,128)(2,1)S(1)}, u32[]{:S(2)}, u32[]{:S(2)}) %all-to-all-start.2) | async-done | bytes 1048608 | tf_op jit(solution)/shard_map/all_to_all | solution.py:78
  56.3 0.0 copy-start.1
  56.3 1.0 copy-done.1
  57.3 2.1 %fusion.18 = f32[256,2048]{1,0:T(8,128)S(1)} fusion(bf16[256,2048]{1,0:T(8,128)(2,1)} %bitcast.36, f32[256]{0:T(256)S(1)} %bitcast.52, s32[256]{0:T(256)S(1)} %get-tuple-element.46, f32[256]{0:T(256)S(1)} %bitcast.51, s32[256]{0:T(256)S(1)} %get-tuple-element.42, f32[256]{0:T(256)S(1)} %bitcast.50, s32[256]{0:T(256)S(1)} %get-tuple-element.43, ...), kind=kOutput, calls=%fused_computation.28 | convolution fusion | flops 271581184 | bytes 3180544 | tf_op jit(solution)/shard_map/dot_general | solution.py:86
  59.4 40.5 %all-reduce.1 = bf16[256,2048]{1,0:T(8,128)(2,1)} all-reduce(f32[256,2048]{1,0:T(8,128)S(1)} %fusion.18), channel_id=1, replica_groups=mesh['uv'=8,'tm'=4] {'tm'}, use_global_device_ids=true, to_apply=%region_0.0 | all-reduce | flops 524288 | bytes 3145728 | tf_op jit(solution)/shard_map/psum | solution.py:86
  99.9 5.9 %fusion.15 = f32[64,2048]{1,0:T(8,128)} fusion(bf16[1024,1024]{1,0:T(8,128)(2,1)} %get-tuple-element.30, bf16[1024,1024]{1,0:T(8,128)(2,1)} %get-tuple-element.29, bf16[1024,1024]{1,0:T(8,128)(2,1)} %get-tuple-element.28, bf16[256,2048]{1,0:T(8,128)(2,1)} %all-reduce.1, s32[]{:T(128)S(6)} %select_n.242), kind=kOutput, calls=%fused_computation.24 | convolution fusion | flops 570556416 | bytes 7077892 | tf_op jit(solution)/shard_map/dot_general | solution.py:91
  (13 shorter events, 0.2 us)
Async XLA Ops:
  0.0 12.9 %copy-start = (bf16[1,128,2048]{2,1,0:T(8,128)(2,1)S(1)}, bf16[1,128,2048]{2,1,0:T(8,128)(2,1)}, u32[]{:S(2)}) copy-start(bf16[1,128,2048]{2,1,0:T(8,128)(2,1)} %param.7) | copy-start | bytes 1572868
  0.0 12.6 %copy-start.2 = (s32[1,1,8,32]{3,2,1,0:T(8,128)S(1)}, s32[1,1,8,32]{3,2,1,0:T(8,128)}, u32[]{:S(2)}) copy-start(s32[1,1,8,32]{3,2,1,0:T(8,128)} %param.10) | copy-start | bytes 3076
  0.0 12.8 %copy-start.3 = (s32[1,1,8]{2,1,0:T(1,128)S(1)}, s32[1,1,8]{2,1,0:T(1,128)}, u32[]{:S(2)}) copy-start(s32[1,1,8]{2,1,0:T(1,128)} %param.11) | copy-start | bytes 100
  5.3 13.7 %all-to-all-start.1 = ((s32[8,1,32]{2,1,0:T(1,128)}), s32[8,1,32]{2,1,0:T(1,128)S(1)}, u32[]{:S(2)}, u32[]{:S(2)}) async-start(s32[8,1,32]{2,1,0:T(1,128)} %all_to_all.17), calls=%async_computation.1 | async-start | bytes 8192 | tf_op jit(solution)/shard_map/all_to_all | solution.py:80
  19.0 9.7 %all-to-all-start = ((s32[8,1,32]{2,1,0:T(1,128)}), s32[8,1,32]{2,1,0:T(1,128)S(1)}, u32[]{:S(2)}, u32[]{:S(2)}) async-start(s32[8,1,32]{2,1,0:T(1,128)} %all_to_all.15), calls=%async_computation | async-start | bytes 8192 | tf_op jit(solution)/shard_map/all_to_all | solution.py:79
  28.7 27.6 %all-to-all-start.2 = ((bf16[8,32,2048]{2,1,0:T(8,128)(2,1)}), bf16[8,32,2048]{2,1,0:T(8,128)(2,1)S(1)}, u32[]{:S(2)}, u32[]{:S(2)}) async-start(bf16[8,32,2048]{2,1,0:T(8,128)(2,1)} %select_select_fusion), calls=%async_computation.2 | async-start | bytes 2097152 | tf_op jit(solution)/shard_map/all_to_all | solution.py:78
  56.3 1.0 copy-start.1
where the time goes:
time: 106 us
  blocking collectives  40.5 us (38%)
  other arithmetic  21.3 us (20%)
  starting transfers between devices  14.1 us (13%)
  waiting for transfers between devices  12.6 us (12%)
  local copies, waits for them, and re-layouts  9.27 us (9%)
  matrix products  7.99 us (8%)
    psum x1, blocking collectives, per_device(): lax.psum(jnp.dot(weights, flat_vis, preferred_element_type=jnp.float32),...  40.5 us
    another operation x1, other arithmetic  19.1 us
    all_to_all x1, starting transfers between devices, per_device(): lax.all_to_all(out_offset, 'uv', split_axis=0, concat_axis=0, tiled=True)  7.28 us
    all_to_all x1, waiting for transfers between devices, per_device(): lax.all_to_all(out_anchor, 'uv', split_axis=0, concat_axis=0, tiled=True)  6.38 us
    dot_general x1, matrix products, per_device(): jnp.dot(grid, transform, preferred_element_type=jnp.float32) * out_scale  5.92 us
    all_to_all x1, starting transfers between devices, per_device(): lax.all_to_all(outgoing, 'uv', split_axis=0, concat_axis=0, tiled=True)  3.56 us
    all_to_all x1, waiting for transfers between devices, per_device(): lax.all_to_all(outgoing, 'uv', split_axis=0, concat_axis=0, tiled=True)  3.3 us
    all_to_all x1, starting transfers between devices, per_device(): lax.all_to_all(out_anchor, 'uv', split_axis=0, concat_axis=0, tiled=True)  3.25 us
  transfers between devices with their start and end apart: 3, of which 3 were waited for; matrix products, arithmetic and copies ran while one was open for 22% of the time, Pallas kernels for 0%

commit v1 on v0

v1 whole, which is shorter than its diff:
```python
import math

import jax
import jax.numpy as jnp
from jax import lax
from jax.sharding import PartitionSpec as P

NCH = 1024
ROWS_DEV = 128
TS = 16
KTAPS = 8
OSAMP = 8
META = 128
SPLIT = 32


def kernel_taps(offsets):
    tap_index = jnp.arange(KTAPS, dtype=jnp.float32)
    sub_shift = (offsets.astype(jnp.float32) + 0.5) / OSAMP
    distance = tap_index[None, :] - (KTAPS / 2 - 1.0) - sub_shift[:, None]
    return jnp.exp(-distance * distance / (2.0 * 1.2 * 1.2))


def tap_matrix(cell_ids, anchors, offsets):
    span = TS - KTAPS + 1
    anchor_y = anchors // span
    anchor_x = anchors % span
    taps_y = kernel_taps(offsets // OSAMP)
    taps_x = kernel_taps(offsets % OSAMP)
    cell_y = cell_ids // TS
    cell_x = cell_ids % TS
    along_y = jnp.zeros((cell_ids.shape[0], anchors.shape[0]), jnp.float32)
    along_x = jnp.zeros((cell_ids.shape[0], anchors.shape[0]), jnp.float32)
    for step in range(KTAPS):
        along_y = along_y + jnp.where(
            cell_y[:, None] == anchor_y[None, :] + step, taps_y[None, :, step], 0.0
        )
        along_x = along_x + jnp.where(
            cell_x[:, None] == anchor_x[None, :] + step, taps_x[None, :, step], 0.0
        )
    return (along_y * along_x).astype(jnp.bfloat16)


def delay_halves():
    freq = jnp.arange(NCH, dtype=jnp.int32)
    hi = jnp.arange(NCH // SPLIT, dtype=jnp.int32)
    lo = jnp.arange(SPLIT, dtype=jnp.int32)
    scale = 2.0 * math.pi / NCH
    ang_hi = scale * ((freq[:, None] * (SPLIT * hi)[None, :]) % NCH).astype(jnp.float32)
    ang_lo = scale * ((freq[:, None] * lo[None, :]) % NCH).astype(jnp.float32)
    c_hi, s_hi = jnp.cos(ang_hi), jnp.sin(ang_hi)
    c_lo, s_lo = jnp.cos(ang_lo), jnp.sin(ang_lo)
    cosine = c_hi[:, :, None] * c_lo[:, None, :] - s_hi[:, :, None] * s_lo[:, None, :]
    sine = s_hi[:, :, None] * c_lo[:, None, :] + c_hi[:, :, None] * s_lo[:, None, :]
    window_arg = 2.0 * math.pi * freq.astype(jnp.float32) / (NCH - 1)
    taper = (
        0.35875
        - 0.48829 * jnp.cos(window_arg)
        + 0.14128 * jnp.cos(2.0 * window_arg)
        - 0.01168 * jnp.cos(3.0 * window_arg)
    )
    tap_cos = (taper[:, None, None] * cosine).reshape(NCH, NCH)
    tap_sin = (taper[:, None, None] * sine).reshape(NCH, NCH)
    return jnp.concatenate([tap_cos, tap_sin], axis=0).astype(jnp.bfloat16)


def per_device(visibility, anchor, offset, slot_rows, counts):
    time_groups = lax.axis_size("tm")
    vis_rows = visibility[0]
    row_width = vis_rows.shape[1]
    slot_table = slot_rows[0, 0]
    tile_count, slot_depth = slot_table.shape
    is_live = (jnp.arange(slot_depth, dtype=jnp.int32)[None, :] < counts[0, 0][:, None]).reshape(-1)
    flat_index = slot_table.reshape(-1)
    picked = jnp.where(
        is_live[:, None], jnp.take(vis_rows, flat_index, axis=0), jnp.zeros((), vis_rows.dtype)
    )
    out_anchor = jnp.take(anchor[0], flat_index).astype(jnp.bfloat16)
    out_offset = jnp.take(offset[0], flat_index).astype(jnp.bfloat16)
    meta = jnp.zeros((flat_index.shape[0], META), jnp.bfloat16)
    meta = meta.at[:, 0].set(out_anchor).at[:, 1].set(out_offset)
    outgoing = jnp.concatenate([picked, meta], axis=1).reshape(tile_count, slot_depth, row_width + META)
    arrived = lax.all_to_all(outgoing, "uv", split_axis=0, concat_axis=0, tiled=True)
    arrived = arrived.reshape(-1, row_width + META)
    arr_anchor = arrived[:, row_width].astype(jnp.int32)
    arr_offset = arrived[:, row_width + 1].astype(jnp.int32)
    all_cells = jnp.arange(TS * TS, dtype=jnp.int32)
    weights = tap_matrix(all_cells, arr_anchor, arr_offset)
    partial = jnp.dot(weights, arrived[:, :row_width], preferred_element_type=jnp.float32)
    summed = lax.psum_scatter(partial, "tm", scatter_dimension=0, tiled=True)
    grid = summed.astype(jnp.bfloat16)
    grid_re, grid_im = grid[:, :NCH], grid[:, NCH:]
    lhs = jnp.concatenate(
        [grid, jnp.concatenate([grid_im, -grid_re], axis=1)], axis=0
    )
    out_scale = 4.0 / math.sqrt(NCH * time_groups * ROWS_DEV)
    both = jnp.dot(lhs, delay_halves(), preferred_element_type=jnp.float32) * out_scale
    cells = grid.shape[0]
    return jnp.concatenate([both[:cells], both[cells:]], axis=1)


def solution(mesh):
    in_specs = (
        P("tm", "uv", None),
        P("tm", "uv"),
        P("tm", "uv"),
        P("tm", "uv", None, None),
        P("tm", "uv", None),
    )
    out_specs = P(("uv", "tm"), None)
    return jax.shard_map(
        per_device, mesh=mesh, in_specs=in_specs, out_specs=out_specs, check_vma=False
    )
```

time: 106 us -> 98.6 us (0.930)
  the two profiles are of different devices: /device:TPU:0 before, /device:TPU:12 now
where the time goes in v1:
time: 98.6 us; the launch traced here: 96.7 us
  waiting for transfers between devices  52.2 us (53%)
  between operations  13.6 us (14%)
  other arithmetic  11.8 us (12%)
  local copies, waits for them, and re-layouts  7.55 us (8%)
  starting transfers between devices  6.22 us (6%)
  matrix products  5.3 us (5%)
    reduce_scatter x1, waiting for transfers between devices, per_device(): summed = lax.psum_scatter(partial, 'tm', scatter_dimension=0, tiled=True)  28.3 us
    all_to_all x1, waiting for transfers between devices, per_device(): lax.all_to_all(outgoing, 'uv', split_axis=0, concat_axis=0, tiled=True)  23.9 us
    all_to_all x1, starting transfers between devices, per_device(): lax.all_to_all(outgoing, 'uv', split_axis=0, concat_axis=0, tiled=True)  6.22 us
    another operation x5, other arithmetic  5.25 us
    dot_general x1, matrix products, per_device(): jnp.dot(lhs, delay_halves(), preferred_element_type=jnp.float32) * out_scale  3.1 us
    dot_general x1, matrix products, per_device(): jnp.dot(weights, arrived[:, :row_width], preferred_element_type=jnp.float32)  2.2 us
  transfers between devices with their start and end apart: 2, of which 2 were waited for; matrix products, arithmetic and copies ran while one was open for 5% of the time, Pallas kernels for 0%

profile of v1, /device:TPU:12, one launch (start us, length us, event | category | flops | bytes accessed | tf_op | source)
XLA Modules:
  0.0 96.7 jit_solution(15615122636479654901)
XLA Ops:
  6.5 0.0 copy-start
  6.5 0.6 compare_reduce_fusion.2
  7.2 0.7 compare_reduce_fusion.1
  7.9 0.8 reshape_squeeze.5
  8.6 0.8 reshape_squeeze.6
  9.4 1.9 %gather_fusion.2 = s32[256]{0:T(256)S(1)} fusion(s32[128]{0:T(128)} %bitcast.40, s32[1024]{0:T(1024)S(1)} %pad_clamp_fusion), kind=kCustom, calls=%fused_computation.1.clone | custom fusion | bytes 3072 | tf_op jit(solution)/shard_map/jit(_take)/gather | solution.py:79
  11.3 1.9 %gather_fusion.1 = s32[256]{0:T(256)S(1)} fusion(s32[128]{0:T(128)} %bitcast.41, s32[1024]{0:T(1024)S(1)} %pad_clamp_fusion), kind=kCustom, calls=%fused_computation.clone | custom fusion | bytes 3072 | tf_op jit(solution)/shard_map/jit(_take)/gather | solution.py:78
  13.2 0.6 broadcast_select_fusion
  13.9 0.7 broadcast_select_fusion.1
  14.5 0.1 reshape.409
  14.6 0.1 reshape.410
  14.7 0.7 iota_compare_fusion
  15.5 0.1 lt.91
  15.6 0.0 copy-done
  15.6 1.4 %gather_fusion = bf16[256,2048]{1,0:T(8,128)(2,1)S(1)} fusion(bf16[128,2048]{1,0:T(8,128)(2,1)S(1)} %bitcast.39, s32[1024]{0:T(1024)S(1)} %pad_clamp_fusion.1), kind=kCustom, calls=%fused_computation.2 | custom fusion | bytes 2098176 | tf_op jit(solution)/shard_map/jit(_take)/gather | solution.py:76
  17.0 0.2 select_select_fusion
  17.2 0.3 scatter.9
  17.4 1.1 %pad_maximum_fusion = bf16[256,2176]{1,0:T(8,128)(2,1)} fusion(bf16[256,128]{1,0:T(8,128)(2,1)S(1)} %scatter.9, bf16[256,2048]{1,0:T(8,128)(2,1)S(1)} %select_select_fusion), kind=kLoop, calls=%fused_computation.14 | loop fusion | flops 2228224 | bytes 2228224 | tf_op jit(solution)/shard_map/concatenate | solution.py:82
  18.5 6.2 %all-to-all-start = ((bf16[8,32,2176]{2,1,0:T(8,128)(2,1)}), bf16[8,32,2176]{2,1,0:T(8,128)(2,1)S(1)}, u32[]{:S(2)}, u32[]{:S(2)}) async-start(bf16[8,32,2176]{2,1,0:T(8,128)(2,1)} %bitcast.5), calls=%async_computation | async-start | bytes 2228224 | tf_op jit(solution)/shard_map/all_to_all | solution.py:83
  24.7 0.0 reduce-scatter.2.cloned.1.call-start
  24.8 23.9 %all-to-all-done = bf16[8,32,2176]{2,1,0:T(8,128)(2,1)S(1)} async-done(((bf16[8,32,2176]{2,1,0:T(8,128)(2,1)}), bf16[8,32,2176]{2,1,0:T(8,128)(2,1)S(1)}, u32[]{:S(2)}, u32[]{:S(2)}) %all-to-all-start) | async-done | bytes 1114144 | tf_op jit(solution)/shard_map/all_to_all | solution.py:83
  48.6 0.1 fusion.78
  48.7 0.1 copy.12
  48.9 0.1 copy.13
  49.0 0.1 fusion.68
  49.2 2.2 %fusion.9 = f32[256,2048]{1,0:T(8,128)} fusion(bf16[256,2176]{1,0:T(8,128)(2,1)S(1)} %bitcast.43, f32[256]{0:T(256)S(1)} %bitcast.63, s32[256]{0:T(256)S(1)} %get-tuple-element.79, f32[256]{0:T(256)S(1)} %bitcast.62, s32[256]{0:T(256)S(1)} %get-tuple-element.75, f32[256]{0:T(256)S(1)} %bitcast.61, s32[256]{0:T(256)S(1)} %get-tuple-element.76, ...), kind=kOutput, calls=%fused_computation.15 | convolution fusion | flops 271581184 | bytes 3180544 | tf_op jit(solution)/shard_map/dot_general | solution.py:89
  51.4 0.0 reduce-scatter.2.cloned.1.call-update
  51.4 0.1 multiply_subtract_fusion.1
  51.5 0.5 fusion.63
  52.0 0.6 fusion.66
  52.6 1.2 %multiply_subtract_fusion = (f32[1024,32,32]{0,2,1:T(8,128)S(1)}, f32[1024,32,32]{0,2,1:T(8,128)S(1)}) fusion(f32[1024,32]{0,1:T(8,128)S(1)} %get-tuple-element.92, f32[1024,32]{0,1:T(8,128)S(1)} %get-tuple-element.83, f32[1024,32]{0,1:T(8,128)S(1)} %get-tuple-element.93, f32[1024,32]{0,1:T(8,128)S(1)} %get-tuple-element.82), kind=kLoop, calls=%fused_computation.12 | loop fusion | flops 6291456 | bytes 8912896 | tf_op jit(solution)/shard_map/sub | solution.py:53
  53.8 2.6 %fusion.5 = (bf16[1024,1024]{0,1:T(8,128)(2,1)S(1)}, bf16[1024,1024]{0,1:T(8,128)(2,1)}) fusion(f32[1024,32,32]{0,2,1:T(8,128)S(1)} %get-tuple-element.42, f32[1024]{0:T(1024)S(1)} %multiply_subtract_fusion.1, f32[1024,32,32]{0,2,1:T(8,128)S(1)} %get-tuple-element.43), kind=kLoop, calls=%fused_computation.10 | loop fusion | flops 4194304 | bytes 12587008 | tf_op jit(solution)/shard_map/convert
  56.4 28.3 %reduce-scatter.2.cloned.1.call-done = f32[64,2048]{1,0:T(8,128)} async-done(((f32[256,2048]{1,0:T(8,128)}), f32[64,2048]{1,0:T(8,128)}) %reduce-scatter.2.cloned.1.call-update) | async-done | bytes 524304 | tf_op jit(solution)/shard_map/reduce_scatter | solution.py:90
  84.7 1.1 %convert_element_type.119 = bf16[64,2048]{1,0:T(8,128)(2,1)S(1)} convert(f32[64,2048]{1,0:T(8,128)} %reduce-scatter.2.cloned.1.call-done) | non-fusion elementwise | flops 131072 | bytes 786432 | tf_op jit(solution)/shard_map/convert_element_type | solution.py:91
  85.8 3.1 %fusion.6 = f32[128,1024]{1,0:T(8,128)S(1)} fusion(bf16[1024,1024]{0,1:T(8,128)(2,1)} %get-tuple-element.63, bf16[1024,1024]{0,1:T(8,128)(2,1)S(1)} %get-tuple-element.62, bf16[64,1024]{1,0:T(8,128)(2,1)S(1)} %get-tuple-element.45, bf16[64,1024]{1,0:T(8,128)(2,1)S(1)} %get-tuple-element.44, bf16[64,2048]{1,0:T(8,128)(2,1)S(1)} %convert_element_type.119), kind=kOutput, calls=%fused_computation.13 | convolution fusion | flops 546963456 | bytes 5242880 | tf_op jit(solution)/shard_map/dot_general | solution.py:97
  89.0 0.8 pad_maximum_fusion.1
  (17 shorter events, 0.2 us)
Async XLA Ops:
  6.5 9.1 %copy-start = (bf16[1,128,2048]{2,1,0:T(8,128)(2,1)S(1)}, bf16[1,128,2048]{2,1,0:T(8,128)(2,1)}, u32[]{:S(2)}) copy-start(bf16[1,128,2048]{2,1,0:T(8,128)(2,1)} %param.11) | copy-start | bytes 1572868
  18.5 30.1 %all-to-all-start = ((bf16[8,32,2176]{2,1,0:T(8,128)(2,1)}), bf16[8,32,2176]{2,1,0:T(8,128)(2,1)S(1)}, u32[]{:S(2)}, u32[]{:S(2)}) async-start(bf16[8,32,2176]{2,1,0:T(8,128)(2,1)} %bitcast.5), calls=%async_computation | async-start | bytes 2228224 | tf_op jit(solution)/shard_map/all_to_all | solution.py:83
  24.7 60.0 %reduce-scatter.2.cloned.1.call-start = ((), (), s32[]{:S(2)}) async-start(), calls=%async_computation.2 | async-start | bytes 2621440 | tf_op jit(solution)/shard_map/reduce_scatter | solution.py:90
Sparse Core Ops, SparseCore 0:
  51.5 33.2 reduce-scatter.1

commit v2 on v1

--- a/solution.py
+++ b/solution.py
@@ -64,30 +64,68 @@
     return jnp.concatenate([tap_cos, tap_sin], axis=0).astype(jnp.bfloat16)
 
 
+def halving_order(tm_index, time_groups, cell_share):
+    level_bits = int(math.log2(time_groups))
+    quarter = jnp.zeros((time_groups,), jnp.int32)
+    for j in range(time_groups):
+        value = tm_index
+        pos = j
+        for level in range(level_bits):
+            half = time_groups >> (level + 1)
+            sent = pos < half
+            bit = 1 << level
+            value = jnp.where(sent, value ^ bit, value)
+            pos = pos % half if half > 0 else pos
+        quarter = quarter.at[j].set(value)
+    cells = quarter[:, None] * cell_share + jnp.arange(cell_share, dtype=jnp.int32)[None, :]
+    return cells.reshape(-1)
+
+
+def halving_reduce(partial, time_groups):
+    level_bits = int(math.log2(time_groups))
+    for level in range(level_bits):
+        half = partial.shape[0] // 2
+        bit = 1 << level
+        perm = [(i, i ^ bit) for i in range(time_groups)]
+        received = lax.ppermute(partial[:half], "tm", perm)
+        partial = partial[half:] + received
+    return partial
+
+
 def per_device(visibility, anchor, offset, slot_rows, counts):
     time_groups = lax.axis_size("tm")
+    cell_share = TS * TS // time_groups
     vis_rows = visibility[0]
-    row_width = vis_rows.shape[1]
+    row_count, row_width = vis_rows.shape
     slot_table = slot_rows[0, 0]
     tile_count, slot_depth = slot_table.shape
     is_live = (jnp.arange(slot_depth, dtype=jnp.int32)[None, :] < counts[0, 0][:, None]).reshape(-1)
     flat_index = slot_table.reshape(-1)
-    picked = jnp.where(
-        is_live[:, None], jnp.take(vis_rows, flat_index, axis=0), jnp.zeros((), vis_rows.dtype)
-    )
-    out_anchor = jnp.take(anchor[0], flat_index).astype(jnp.bfloat16)
-    out_offset = jnp.take(offset[0], flat_index).astype(jnp.bfloat16)
-    meta = jnp.zeros((flat_index.shape[0], META), jnp.bfloat16)
-    meta = meta.at[:, 0].set(out_anchor).at[:, 1].set(out_offset)
+    pick = (
+        (flat_index[:, None] == jnp.arange(row_count, dtype=jnp.int32)[None, :]) & is_live[:, None]
+    ).astype(jnp.bfloat16)
+    picked = jnp.dot(pick, vis_rows, preferred_element_type=jnp.float32).astype(jnp.bfloat16)
+    meta_src = jnp.zeros((row_count, META), jnp.float32)
+    meta_src = meta_src.at[:, 0].set(anchor[0].astype(jnp.float32))
+    meta_src = meta_src.at[:, 1].set(offset[0].astype(jnp.float32))
+    meta = jnp.dot(pick, meta_src.astype(jnp.bfloat16), preferred_element_type=jnp.float32)
+    meta = meta.astype(jnp.bfloat16)
     outgoing = jnp.concatenate([picked, meta], axis=1).reshape(tile_count, slot_depth, row_width + META)
     arrived = lax.all_to_all(outgoing, "uv", split_axis=0, concat_axis=0, tiled=True)
     arrived = arrived.reshape(-1, row_width + META)
     arr_anchor = arrived[:, row_width].astype(jnp.int32)
     arr_offset = arrived[:, row_width + 1].astype(jnp.int32)
-    all_cells = jnp.arange(TS * TS, dtype=jnp.int32)
-    weights = tap_matrix(all_cells, arr_anchor, arr_offset)
+    tm_index = lax.axis_index("tm")
+    if time_groups & (time_groups - 1) == 0:
+        cells = halving_order(tm_index, time_groups, cell_share)
+    else:
+        cells = jnp.arange(TS * TS, dtype=jnp.int32)
+    weights = tap_matrix(cells, arr_anchor, arr_offset)
     partial = jnp.dot(weights, arrived[:, :row_width], preferred_element_type=jnp.float32)
-    summed = lax.psum_scatter(partial, "tm", scatter_dimension=0, tiled=True)
+    if time_groups & (time_groups - 1) == 0:
+        summed = halving_reduce(partial, time_groups)
+    else:
+        summed = lax.psum_scatter(partial, "tm", scatter_dimension=0, tiled=True)
     grid = summed.astype(jnp.bfloat16)
     grid_re, grid_im = grid[:, :NCH], grid[:, NCH:]
     lhs = jnp.concatenate(
@@ -95,8 +133,8 @@
     )
     out_scale = 4.0 / math.sqrt(NCH * time_groups * ROWS_DEV)
     both = jnp.dot(lhs, delay_halves(), preferred_element_type=jnp.float32) * out_scale
-    cells = grid.shape[0]
-    return jnp.concatenate([both[:cells], both[cells:]], axis=1)
+    cells_out = grid.shape[0]
+    return jnp.concatenate([both[:cells_out], both[cells_out:]], axis=1)
 
 
 def solution(mesh):

time: 98.6 us -> 63.4 us (0.64)
  the two profiles are of different devices: /device:TPU:12 before, /device:TPU:0 now
where the time goes in v2:
time: 63.4 us; the launch traced here: 63.2 us
  waiting for transfers between devices  38.2 us (60%)
  other arithmetic  11.3 us (18%)
  starting transfers between devices  8.91 us (14%)
  matrix products  3.1 us (5%)
  local copies, waits for them, and re-layouts  1.47 us (2%)
    all_to_all x1, waiting for transfers between devices, per_device(): lax.all_to_all(outgoing, 'uv', split_axis=0, concat_axis=0, tiled=True)  26.6 us
    ppermute x2, waiting for transfers between devices, halving_reduce(): received = lax.ppermute(partial[:half], 'tm', perm)  11.6 us
    all_to_all x1, starting transfers between devices, per_device(): lax.all_to_all(outgoing, 'uv', split_axis=0, concat_axis=0, tiled=True)  7.28 us
    another operation x5, other arithmetic  5.29 us
    ppermute x2, starting transfers between devices, halving_reduce(): received = lax.ppermute(partial[:half], 'tm', perm)  1.63 us
    dot_general x1, matrix products, per_device(): jnp.dot(lhs, delay_halves(), preferred_element_type=jnp.float32) * out_scale  1.51 us
  transfers between devices with their start and end apart: 3, of which 3 were waited for; matrix products, arithmetic and copies ran while one was open for 7% of the time, Pallas kernels for 0%

profile of v2, /device:TPU:0, one launch (start us, length us, event | category | flops | bytes accessed | tf_op | source)
XLA Modules:
  0.0 63.2 jit_solution(14465553597396516047)
XLA Ops:
  0.0 0.0 copy-start
  0.0 0.6 %compare_reduce_fusion.1 = pred[]{:T(512)} fusion(), kind=kLoop, calls=%fused_computation.133 | loop fusion | flops 5 | bytes 1 | tf_op jit(solution)/shard_map/reduce.10
  0.6 0.7 %compare_reduce_fusion = pred[]{:T(512)} fusion(), kind=kLoop, calls=%fused_computation.132 | loop fusion | flops 5 | bytes 1 | tf_op jit(solution)/shard_map/reduce.11
  1.4 0.8 %eq.83 = s32[256]{0:T(256)S(1)} reshape(s32[1,1,8,32]{3,2,1,0:T(8,128)} %param.20) | data formatting | bytes 2048 | tf_op jit(solution)/shard_map/eq | solution.py:105
  2.1 0.7 %iota_compare_fusion.1 = pred[8,32]{1,0:T(8,128)(4,1)S(1)} fusion(s32[8]{0:T(128)} %bitcast.65), kind=kLoop, calls=%fused_computation.127 | loop fusion | flops 256 | bytes 288 | tf_op jit(solution)/shard_map/lt | solution.py:102
  2.9 0.1 lt.54
  2.9 1.3 %fusion.98 = bf16[128,1]{0,1:T(2,128)(2,1)S(1)} fusion(pred[]{:T(512)} %compare_reduce_fusion.1, s32[1,128]{1,0:T(1,128)} %param.18), kind=kLoop, calls=%fused_computation.140 | loop fusion | flops 256 | bytes 769 | tf_op jit(solution)/shard_map/reshape.462
  4.3 1.3 %fusion.99 = bf16[128,1]{0,1:T(2,128)(2,1)S(1)} fusion(pred[]{:T(512)} %compare_reduce_fusion, s32[1,128]{1,0:T(1,128)} %param.19), kind=kLoop, calls=%fused_computation.141 | loop fusion | flops 256 | bytes 769 | tf_op jit(solution)/shard_map/reshape.465
  5.6 0.2 convolution_convert_fusion.1
  5.9 0.0 copy-done
  5.9 0.5 convolution_convert_fusion
  6.4 1.1 %pad_maximum_fusion = bf16[256,2176]{1,0:T(8,128)(2,1)} fusion(bf16[256,128]{1,0:T(8,128)(2,1)S(1)} %convolution_convert_fusion.1, bf16[256,2048]{1,0:T(8,128)(2,1)S(1)} %convolution_convert_fusion), kind=kLoop, calls=%fused_computation.13 | loop fusion | flops 2228224 | bytes 2228224 | tf_op jit(solution)/shard_map/concatenate | solution.py:113
  7.5 7.3 %all-to-all-start = ((bf16[8,32,2176]{2,1,0:T(8,128)(2,1)}), bf16[8,32,2176]{2,1,0:T(8,128)(2,1)S(1)}, u32[]{:S(2)}, u32[]{:S(2)}) async-start(bf16[8,32,2176]{2,1,0:T(8,128)(2,1)} %bitcast.10), calls=%async_computation | async-start | bytes 2228224 | tf_op jit(solution)/shard_map/all_to_all | solution.py:114
  14.7 0.1 scatter.21
  14.9 0.1 scatter.24
  15.0 0.1 scatter.25
  15.1 0.1 iota_add_fusion
  15.1 0.1 add.341
  15.3 26.6 %all-to-all-done = bf16[8,32,2176]{2,1,0:T(8,128)(2,1)S(1)} async-done(((bf16[8,32,2176]{2,1,0:T(8,128)(2,1)}), bf16[8,32,2176]{2,1,0:T(8,128)(2,1)S(1)}, u32[]{:S(2)}, u32[]{:S(2)}) %all-to-all-start) | async-done | bytes 1114144 | tf_op jit(solution)/shard_map/all_to_all | solution.py:114
  41.9 0.3 fusion.74
  42.2 0.2 fusion.73
  42.4 0.1 fusion.81
  42.5 0.1 fusion.95
  42.7 0.8 %fusion.9 = f32[256,2048]{1,0:T(8,128)S(1)} fusion(bf16[256,2176]{1,0:T(8,128)(2,1)S(1)} %bitcast.48, f32[256]{0:T(256)S(1)} %bitcast.63, s32[256]{0:T(256)S(1)} %get-tuple-element.124, f32[256]{0:T(256)S(1)} %bitcast.62, s32[256]{0:T(256)S(1)} %get-tuple-element.120, f32[256]{0:T(256)S(1)} %bitcast.61, s32[256]{0:T(256)S(1)} %get-tuple-element.121, ...), kind=kOutput, calls=%fused_computation.15 | convolution fusion | flops 271581184 | bytes 3180544 | tf_op jit(solution)/shard_map/dot_general | solution.py:124
  43.5 0.1 slice.196
  43.6 0.1 collective-permute-start
  43.7 0.1 multiply_subtract_fusion.1
  43.8 0.5 fusion.85
  44.3 0.6 fusion.88
  44.9 1.2 %multiply_subtract_fusion = (f32[1024,32,32]{0,2,1:T(8,128)S(1)}, f32[1024,32,32]{0,2,1:T(8,128)S(1)}) fusion(f32[1024,32]{0,1:T(8,128)S(1)} %get-tuple-element.137, f32[1024,32]{0,1:T(8,128)S(1)} %get-tuple-element.128, f32[1024,32]{0,1:T(8,128)S(1)} %get-tuple-element.138, f32[1024,32]{0,1:T(8,128)S(1)} %get-tuple-element.127), kind=kLoop, calls=%fused_computation.9 | loop fusion | flops 6291456 | bytes 8912896 | tf_op jit(solution)/shard_map/sub | solution.py:53
  46.1 0.2 collective-permute-done
  46.4 0.1 slice_add_fusion
  46.5 1.6 %collective-permute-start.1 = (f32[64,2048]{1,0:T(8,128)S(1)}, f32[64,2048]{1,0:T(8,128)S(1)}, u32[]{:S(2)}, u32[]{:S(2)}) collective-permute-start(f32[64,2048]{1,0:T(8,128)S(1)} %slice.198), channel_id=1, source_target_pairs={{0,2},{1,3},{2,0},{3,1},{4,6},{5,7},{6,4},{7,5},{8,10},{9,11},{10,... | collective-permute-start | bytes 1572872 | tf_op jit(solution)/shard_map/ppermute | solution.py:90
  48.1 1.3 %fusion.5 = (bf16[1024,1024]{0,1:T(8,128)(2,1)S(1)}, bf16[1024,1024]{0,1:T(8,128)(2,1)S(1)}) fusion(f32[1024,32,32]{0,2,1:T(8,128)S(1)} %get-tuple-element.87, f32[1024]{0:T(1024)S(1)} %multiply_subtract_fusion.1, f32[1024,32,32]{0,2,1:T(8,128)S(1)} %get-tuple-element.88), kind=kLoop, calls=%fused_computation.7 | loop fusion | flops 4194304 | bytes 12587008 | tf_op jit(solution)/shard_map/convert
  49.4 11.3 %collective-permute-done.1 = f32[64,2048]{1,0:T(8,128)S(1)} collective-permute-done((f32[64,2048]{1,0:T(8,128)S(1)}, f32[64,2048]{1,0:T(8,128)S(1)}, u32[]{:S(2)}, u32[]{:S(2)}) %collective-permute-start.1) | collective-permute-done | bytes 524320 | tf_op jit(solution)/shard_map/ppermute | solution.py:90
  60.7 0.1 fusion.11
  60.8 1.5 %fusion.6 = f32[128,1024]{1,0:T(8,128)S(1)} fusion(bf16[1024,1024]{0,1:T(8,128)(2,1)S(1)} %get-tuple-element.108, bf16[1024,1024]{0,1:T(8,128)(2,1)S(1)} %get-tuple-element.107, bf16[64,1024]{1,0:T(8,128)(2,1)S(1)} %get-tuple-element.90, bf16[64,1024]{1,0:T(8,128)(2,1)S(1)} %get-tuple-element.89, bf16[64,2048]{1,0:T(8,128)(2,1)S(1)} %fusion.11), kind=kOutput, calls=%fused_computation.11 | convolution fusion | flops 546963456 | bytes 5242880 | tf_op jit(solution)/shard_map/dot_general | solution.py:135
  62.3 0.8 %pad_maximum_fusion.1 = f32[64,2048]{1,0:T(8,128)} fusion(f32[64,1024]{1,0:T(8,128)S(1)} %get-tuple-element.86, f32[64,1024]{1,0:T(8,128)S(1)} %get-tuple-element.85), kind=kLoop, calls=%fused_computation.24 | loop fusion | flops 131072 | bytes 1048576 | tf_op jit(solution)/shard_map/concatenate | solution.py:137
  (13 shorter events, 0.2 us)
Async XLA Ops:
  0.0 5.9 %copy-start = (bf16[1,128,2048]{2,1,0:T(8,128)(2,1)S(1)}, bf16[1,128,2048]{2,1,0:T(8,128)(2,1)}, u32[]{:S(2)}) copy-start(bf16[1,128,2048]{2,1,0:T(8,128)(2,1)} %param.17) | copy-start | bytes 1572868
  7.5 34.5 %all-to-all-start = ((bf16[8,32,2176]{2,1,0:T(8,128)(2,1)}), bf16[8,32,2176]{2,1,0:T(8,128)(2,1)S(1)}, u32[]{:S(2)}, u32[]{:S(2)}) async-start(bf16[8,32,2176]{2,1,0:T(8,128)(2,1)} %bitcast.10), calls=%async_computation | async-start | bytes 2228224 | tf_op jit(solution)/shard_map/all_to_all | solution.py:114
  43.6 2.7 %collective-permute-start = (f32[128,2048]{1,0:T(8,128)S(1)}, f32[128,2048]{1,0:T(8,128)S(1)}, u32[]{:S(2)}, u32[]{:S(2)}) collective-permute-start(f32[128,2048]{1,0:T(8,128)S(1)} %slice.196), channel_id=1, source_target_pairs={{0,1},{1,0},{2,3},{3,2},{4,5},{5,4},{6,7},{7,6},{8,9},{9,8},{10,11... | collective-permute-start | bytes 3145736 | tf_op jit(solution)/shard_map/ppermute | solution.py:90
  46.5 14.2 %collective-permute-start.1 = (f32[64,2048]{1,0:T(8,128)S(1)}, f32[64,2048]{1,0:T(8,128)S(1)}, u32[]{:S(2)}, u32[]{:S(2)}) collective-permute-start(f32[64,2048]{1,0:T(8,128)S(1)} %slice.198), channel_id=1, source_target_pairs={{0,2},{1,3},{2,0},{3,1},{4,6},{5,7},{6,4},{7,5},{8,10},{9,11},{10,... | collective-permute-start | bytes 1572872 | tf_op jit(solution)/shard_map/ppermute | solution.py:90

commit v3 on v2

--- a/solution.py
+++ b/solution.py
@@ -12,6 +12,7 @@
 OSAMP = 8
 META = 128
 SPLIT = 32
+CHUNKS = 2
 
 
 def kernel_taps(offsets):
@@ -41,7 +42,7 @@
     return (along_y * along_x).astype(jnp.bfloat16)
 
 
-def delay_halves():
+def delay_table():
     freq = jnp.arange(NCH, dtype=jnp.int32)
     hi = jnp.arange(NCH // SPLIT, dtype=jnp.int32)
     lo = jnp.arange(SPLIT, dtype=jnp.int32)
@@ -61,7 +62,9 @@
     )
     tap_cos = (taper[:, None, None] * cosine).reshape(NCH, NCH)
     tap_sin = (taper[:, None, None] * sine).reshape(NCH, NCH)
-    return jnp.concatenate([tap_cos, tap_sin], axis=0).astype(jnp.bfloat16)
+    upper = jnp.concatenate([tap_cos, -tap_sin], axis=1)
+    lower = jnp.concatenate([tap_sin, tap_cos], axis=1)
+    return jnp.concatenate([upper, lower], axis=0).astype(jnp.bfloat16)
 
 
 def halving_order(tm_index, time_groups, cell_share):
@@ -104,37 +107,50 @@
     pick = (
         (flat_index[:, None] == jnp.arange(row_count, dtype=jnp.int32)[None, :]) & is_live[:, None]
     ).astype(jnp.bfloat16)
-    picked = jnp.dot(pick, vis_rows, preferred_element_type=jnp.float32).astype(jnp.bfloat16)
-    meta_src = jnp.zeros((row_count, META), jnp.float32)
-    meta_src = meta_src.at[:, 0].set(anchor[0].astype(jnp.float32))
-    meta_src = meta_src.at[:, 1].set(offset[0].astype(jnp.float32))
-    meta = jnp.dot(pick, meta_src.astype(jnp.bfloat16), preferred_element_type=jnp.float32)
-    meta = meta.astype(jnp.bfloat16)
-    outgoing = jnp.concatenate([picked, meta], axis=1).reshape(tile_count, slot_depth, row_width + META)
-    arrived = lax.all_to_all(outgoing, "uv", split_axis=0, concat_axis=0, tiled=True)
-    arrived = arrived.reshape(-1, row_width + META)
-    arr_anchor = arrived[:, row_width].astype(jnp.int32)
-    arr_offset = arrived[:, row_width + 1].astype(jnp.int32)
+    meta_rows = jnp.concatenate(
+        [
+            anchor.astype(jnp.bfloat16),
+            offset.astype(jnp.bfloat16),
+            jnp.zeros((META - 2, row_count), jnp.bfloat16),
+        ],
+        axis=0,
+    )
+    meta = lax.dot_general(
+        pick, meta_rows, (((1,), (1,)), ((), ())), preferred_element_type=jnp.float32
+    ).astype(jnp.bfloat16)
+    pow2 = time_groups & (time_groups - 1) == 0
     tm_index = lax.axis_index("tm")
-    if time_groups & (time_groups - 1) == 0:
+    if pow2:
         cells = halving_order(tm_index, time_groups, cell_share)
     else:
         cells = jnp.arange(TS * TS, dtype=jnp.int32)
-    weights = tap_matrix(cells, arr_anchor, arr_offset)
-    partial = jnp.dot(weights, arrived[:, :row_width], preferred_element_type=jnp.float32)
-    if time_groups & (time_groups - 1) == 0:
-        summed = halving_reduce(partial, time_groups)
-    else:
-        summed = lax.psum_scatter(partial, "tm", scatter_dimension=0, tiled=True)
-    grid = summed.astype(jnp.bfloat16)
-    grid_re, grid_im = grid[:, :NCH], grid[:, NCH:]
-    lhs = jnp.concatenate(
-        [grid, jnp.concatenate([grid_im, -grid_re], axis=1)], axis=0
-    )
+    transform = delay_table()
+    width = row_width // CHUNKS
+    weights = None
+    total = None
+    for chunk in range(CHUNKS):
+        cols = slice(chunk * width, (chunk + 1) * width)
+        picked = jnp.dot(pick, vis_rows[:, cols], preferred_element_type=jnp.float32)
+        picked = picked.astype(jnp.bfloat16)
+        if chunk == 0:
+            picked = jnp.concatenate([picked, meta], axis=1)
+        outgoing = picked.reshape(tile_count, slot_depth, picked.shape[1])
+        arrived = lax.all_to_all(outgoing, "uv", split_axis=0, concat_axis=0, tiled=True)
+        arrived = arrived.reshape(-1, picked.shape[1])
+        if chunk == 0:
+            arr_anchor = arrived[:, width].astype(jnp.int32)
+            arr_offset = arrived[:, width + 1].astype(jnp.int32)
+            weights = tap_matrix(cells, arr_anchor, arr_offset)
+        partial = jnp.dot(weights, arrived[:, :width], preferred_element_type=jnp.float32)
+        if pow2:
+            summed = halving_reduce(partial, time_groups)
+        else:
+            summed = lax.psum_scatter(partial, "tm", scatter_dimension=0, tiled=True)
+        grid = summed.astype(jnp.bfloat16)
+        part = jnp.dot(grid, transform[cols], preferred_element_type=jnp.float32)
+        total = part if total is None else total + part
     out_scale = 4.0 / math.sqrt(NCH * time_groups * ROWS_DEV)
-    both = jnp.dot(lhs, delay_halves(), preferred_element_type=jnp.float32) * out_scale
-    cells_out = grid.shape[0]
-    return jnp.concatenate([both[:cells_out], both[cells_out:]], axis=1)
+    return total * out_scale
 
 
 def solution(mesh):

time: 63.4 us -> 69.1 us (1.090)
  waiting for transfers between devices: 38.2 us -> 30.3 us
  matrix products: 3.1 us -> 8.63 us
  starting transfers between devices: 8.91 us -> 13.7 us
  other arithmetic: 11.3 us -> 13.5 us
  local copies, waits for them, and re-layouts: 1.47 us -> 2.23 us
    all_to_all x1 -> x2, waiting for transfers between devices: 26.6 us -> 20.8 us  [per_device(): lax.all_to_all(outgoing, 'uv', split_axis=0, concat_axis=0, tiled=True)]
    dot_general x4 -> x7, matrix products: 3.1 us -> 8.63 us  [the longest x2 3.59 us: per_device(): part = jnp.dot(grid, transform[cols], preferred_element_type=jnp.float32)]
    add x0 -> x1, other arithmetic: none -> 4.45 us  [delay_table(): s_hi[:, :, None] * c_lo[:, None, :] + c_hi[:, :, None] * s_lo[:, None, :]]
    all_to_all x1 -> x2, starting transfers between devices: 7.28 us -> 10.9 us  [per_device(): lax.all_to_all(outgoing, 'uv', split_axis=0, concat_axis=0, tiled=True)]
    ppermute x2 -> x4, waiting for transfers between devices: 11.6 us -> 9.51 us  [halving_reduce(): received = lax.ppermute(partial[:half], 'tm', perm)]
    another operation x5 -> x1, other arithmetic: 5.29 us -> 3.99 us
    convert_element_type x1 -> x2, other arithmetic: 0.05 us -> 1.32 us  [the longest x1 0.66 us: per_device(): offset.astype(jnp.bfloat16)]
    sub x2 -> x1, other arithmetic: 1.28 us -> 0.06 us  [delay_table(): 0.35875 - 0.48829 * jnp.cos(window_arg)]
  transfers between devices with their start and end apart: 3 -> 6, of which waited for: 3 -> 4; matrix products, arithmetic and copies ran while one was open for 7% -> 22% of each run, Pallas kernels for 0% -> 0%
where the time goes in v3:
time: 69.1 us; the launch traced here: 68.6 us
  waiting for transfers between devices  30.3 us (44%)
  starting transfers between devices  13.7 us (20%)
  other arithmetic  13.5 us (20%)
  matrix products  8.63 us (12%)
  local copies, waits for them, and re-layouts  2.23 us (3%)
    all_to_all x2, waiting for transfers between devices, per_device(): lax.all_to_all(outgoing, 'uv', split_axis=0, concat_axis=0, tiled=True)  20.8 us
    all_to_all x2, starting transfers between devices, per_device(): lax.all_to_all(outgoing, 'uv', split_axis=0, concat_axis=0, tiled=True)  10.9 us
    ppermute x4, waiting for transfers between devices, halving_reduce(): received = lax.ppermute(partial[:half], 'tm', perm)  9.51 us
    add x1, other arithmetic, delay_table(): s_hi[:, :, None] * c_lo[:, None, :] + c_hi[:, :, None] * s_lo[:, None, :]  4.45 us
    another operation x1, other arithmetic  3.99 us
    dot_general x2, matrix products, per_device(): part = jnp.dot(grid, transform[cols], preferred_element_type=jnp.float32)  3.59 us
    dot_general x2, matrix products, per_device(): jnp.dot(pick, vis_rows[:, cols], preferred_element_type=jnp.float32)  3.39 us
    ppermute x4, starting transfers between devices, halving_reduce(): received = lax.ppermute(partial[:half], 'tm', perm)  2.79 us
  transfers between devices with their start and end apart: 6, of which 4 were waited for; matrix products, arithmetic and copies ran while one was open for 22% of the time, Pallas kernels for 0%

profile of v3, /device:TPU:0, one launch (start us, length us, event | category | flops | bytes accessed | tf_op | source)
XLA Modules:
  0.0 68.6 jit_solution(15283698421332834715)
XLA Ops:
  0.0 0.8 %eq.84 = s32[256]{0:T(256)S(1)} reshape(s32[1,1,8,32]{3,2,1,0:T(8,128)} %param.16) | data formatting | bytes 2048 | tf_op jit(solution)/shard_map/eq | solution.py:108
  0.8 0.7 %iota_compare_fusion.1 = pred[8,32]{1,0:T(8,128)(4,1)S(1)} fusion(s32[8]{0:T(128)} %bitcast.82), kind=kLoop, calls=%fused_computation.102 | loop fusion | flops 256 | bytes 288 | tf_op jit(solution)/shard_map/lt | solution.py:105
  1.5 0.1 lt.62
  1.6 0.7 convert_element_type.139
  2.2 0.7 convert_element_type.138
  2.9 0.1 pad.17.clone
  3.0 1.3 %convolution_convert_fusion.1 = bf16[256,1024]{1,0:T(8,128)(2,1)S(1)} fusion(bf16[128,2048]{1,0:T(8,128)(2,1)} %bitcast.47, s32[256]{0:T(256)S(1)} %eq.84, pred[256]{0:T(512)(128)(4,1)S(1)} %lt.62), kind=kOutput, calls=%fused_computation.18 | convolution fusion | flops 67436544 | bytes 787712 | tf_op jit(solution)/shard_map/dot_general | solution.py:133
  4.3 0.3 convolution_convert_fusion.2
  4.6 0.9 %pad_maximum_fusion = bf16[256,1152]{1,0:T(8,128)(2,1)} fusion(bf16[256,128]{1,0:T(8,128)(2,1)S(1)} %convolution_convert_fusion.2, bf16[256,1024]{1,0:T(8,128)(2,1)S(1)} %convolution_convert_fusion.1), kind=kLoop, calls=%fused_computation.20 | loop fusion | flops 1179648 | bytes 1179648 | tf_op jit(solution)/shard_map/concatenate | solution.py:136
  5.5 7.3 %all-to-all-start = ((bf16[8,32,1152]{2,1,0:T(8,128)(2,1)}), bf16[8,32,1152]{2,1,0:T(8,128)(2,1)S(1)}, u32[]{:S(2)}, u32[]{:S(2)}) async-start(bf16[8,32,1152]{2,1,0:T(8,128)(2,1)} %bitcast.8), calls=%async_computation | async-start | bytes 1179648 | tf_op jit(solution)/shard_map/all_to_all | solution.py:138
  12.8 0.5 fusion.57
  13.3 0.1 multiply_subtract_fusion.1
  13.4 0.1 scatter.15
  13.5 0.1 scatter.16
  13.6 0.1 scatter.19
  13.7 0.1 iota_add_fusion
  13.8 0.1 add.360
  13.9 0.6 fusion.60
  14.5 2.1 %convolution_convert_fusion = bf16[256,1024]{1,0:T(8,128)(2,1)} fusion(bf16[128,2048]{1,0:T(8,128)(2,1)} %bitcast.48, s32[256]{0:T(256)S(1)} %eq.84, pred[256]{0:T(512)(128)(4,1)S(1)} %lt.62), kind=kOutput, calls=%fused_computation.17 | convolution fusion | flops 67436544 | bytes 787712 | tf_op jit(solution)/shard_map/dot_general | solution.py:133
  16.6 4.5 %multiply_add_fusion = (f32[1024,32,32]{0,2,1:T(8,128)}, f32[1024,32,32]{0,2,1:T(8,128)}) fusion(f32[1024,32]{0,1:T(8,128)S(1)} %get-tuple-element.110, f32[1024,32]{0,1:T(8,128)S(1)} %get-tuple-element.101, f32[1024,32]{0,1:T(8,128)S(1)} %get-tuple-element.111, f32[1024,32]{0,1:T(8,128)S(1)} %get-tuple-element.100), kind=kLoop, calls=%fused_computation.12 | loop fusion | flops 6291456 | bytes 8912896 | tf_op jit(solution)/shard_map/add | solution.py:55
  21.0 7.6 %all-to-all-done = bf16[8,32,1152]{2,1,0:T(8,128)(2,1)S(1)} async-done(((bf16[8,32,1152]{2,1,0:T(8,128)(2,1)}), bf16[8,32,1152]{2,1,0:T(8,128)(2,1)S(1)}, u32[]{:S(2)}, u32[]{:S(2)}) %all-to-all-start) | async-done | bytes 589856 | tf_op jit(solution)/shard_map/all_to_all | solution.py:138
  28.6 3.6 %all-to-all-start.1 = ((bf16[8,32,1024]{2,1,0:T(8,128)(2,1)}), bf16[8,32,1024]{2,1,0:T(8,128)(2,1)S(1)}, u32[]{:S(2)}, u32[]{:S(2)}) async-start(bf16[8,32,1024]{2,1,0:T(8,128)(2,1)} %bitcast.28), calls=%async_computation.1 | async-start | bytes 1048576 | tf_op jit(solution)/shard_map/all_to_all | solution.py:138
  32.3 0.3 fusion.47
  32.6 0.2 fusion.46
  32.8 0.1 fusion.55
  32.9 0.1 fusion.73
  33.0 0.7 %fusion.16 = f32[256,1024]{1,0:T(8,128)S(1)} fusion(bf16[256,1152]{1,0:T(8,128)(2,1)S(1)} %bitcast.46, f32[256]{0:T(256)S(1)} %bitcast.78, s32[256]{0:T(256)S(1)} %get-tuple-element.93, f32[256]{0:T(256)S(1)} %bitcast.76, s32[256]{0:T(256)S(1)} %get-tuple-element.94, f32[256]{0:T(256)S(1)} %bitcast.74, s32[256]{0:T(256)S(1)} %get-tuple-element.95, ...), kind=kOutput, calls=%fused_computation.23 | convolution fusion | flops 137363456 | bytes 1607680 | tf_op jit(solution)/shard_map/dot_general | solution.py:144
  33.7 13.2 %all-to-all-done.1 = bf16[8,32,1024]{2,1,0:T(8,128)(2,1)S(1)} async-done(((bf16[8,32,1024]{2,1,0:T(8,128)(2,1)}), bf16[8,32,1024]{2,1,0:T(8,128)(2,1)S(1)}, u32[]{:S(2)}, u32[]{:S(2)}) %all-to-all-start.1) | async-done | bytes 524320 | tf_op jit(solution)/shard_map/all_to_all | solution.py:138
  47.0 0.0 copy-start
  47.0 0.7 fusion.79
  47.7 0.1 collective-permute-start.2
  47.8 0.6 collective-permute-start
  48.4 0.8 %copy-done = f32[1024,32,32]{0,2,1:T(8,128)S(1)} copy-done((f32[1024,32,32]{0,2,1:T(8,128)S(1)}, f32[1024,32,32]{0,2,1:T(8,128)}, u32[]{:S(2)}) %copy-start) | copy-done | bytes 4194328
  49.1 4.0 %negate_convert_fusion = (bf16[1024,1024]{0,1:T(8,128)(2,1)S(1)}, bf16[1024,1024]{0,1:T(8,128)(2,1)S(1)}, bf16[1024,1024]{0,1:T(8,128)(2,1)S(1)}) fusion(f32[1024,32,32]{0,2,1:T(8,128)S(1)} %copy-done, f32[1024]{0:T(1024)S(1)} %multiply_subtract_fusion.1, f32[1024,32,32]{0,2,1:T(8,128)} %get-tuple-element.64), kind=kLoop, calls=%fused_computation.11 | loop fusion | flops 6291456 | bytes 14684160 | tf_op jit(solution)/shard_map/convert.5
  53.1 0.0 collective-permute-done.2
  53.2 0.1 slice_add_fusion
  53.2 1.6 %collective-permute-start.3 = (f32[64,1024]{1,0:T(8,128)S(1)}, f32[64,1024]{1,0:T(8,128)S(1)}, u32[]{:S(2)}, u32[]{:S(2)}) collective-permute-start(f32[64,1024]{1,0:T(8,128)S(1)} %slice.185), channel_id=1, source_target_pairs={{0,2},{1,3},{2,0},{3,1},{4,6},{5,7},{6,4},{7,5},{8,10},{9,11},{10,... | collective-permute-start | bytes 786440 | tf_op jit(solution)/shard_map/ppermute | solution.py:93
  54.8 0.0 collective-permute-done
  54.8 0.1 slice_add_fusion.1
  54.9 0.6 collective-permute-start.1
  55.5 7.0 %collective-permute-done.3 = f32[64,1024]{1,0:T(8,128)S(1)} collective-permute-done((f32[64,1024]{1,0:T(8,128)S(1)}, f32[64,1024]{1,0:T(8,128)S(1)}, u32[]{:S(2)}, u32[]{:S(2)}) %collective-permute-start.3) | collective-permute-done | bytes 262176 | tf_op jit(solution)/shard_map/ppermute | solution.py:93
  62.6 1.4 %fusion.4 = f32[64,2048]{1,0:T(8,128)S(1)} fusion(bf16[1024,1024]{0,1:T(8,128)(2,1)S(1)} %get-tuple-element.81, bf16[1024,1024]{0,1:T(8,128)(2,1)S(1)} %get-tuple-element.62, f32[64,1024]{1,0:T(8,128)S(1)} %collective-permute-done.3, f32[128,1024]{1,0:T(8,128)S(1)} %slice_add_fusion), kind=kOutput, calls=%fused_computation.4 | convolution fusion | flops 276955136 | bytes 5242880 | tf_op jit(solution)/shard_map/dot_general | solution.py:150
  64.0 2.5 %collective-permute-done.1 = f32[64,1024]{1,0:T(8,128)S(1)} collective-permute-done((f32[64,1024]{1,0:T(8,128)S(1)}, f32[64,1024]{1,0:T(8,128)S(1)}, u32[]{:S(2)}, u32[]{:S(2)}) %collective-permute-start.1) | collective-permute-done | bytes 262176 | tf_op jit(solution)/shard_map/ppermute | solution.py:93
  66.4 2.2 %fusion.13 = f32[64,2048]{1,0:T(8,128)} fusion(f32[64,2048]{1,0:T(8,128)S(1)} %fusion.4, bf16[1024,1024]{0,1:T(8,128)(2,1)S(1)} %get-tuple-element.61, bf16[1024,1024]{0,1:T(8,128)(2,1)S(1)} %get-tuple-element.81, f32[64,1024]{1,0:T(8,128)S(1)} %collective-permute-done.1, f32[128,1024]{1,0:T(8,128)S(1)} %slice_add_fusion.1), kind=kOutput, calls=%fused_computation.16 | convolution fusion | flops 277217280 | bytes 5767168 | tf_op jit(solution)/shard_map/dot_general | solution.py:150
  (13 shorter events, 0.2 us)
Async XLA Ops:
  5.5 23.2 %all-to-all-start = ((bf16[8,32,1152]{2,1,0:T(8,128)(2,1)}), bf16[8,32,1152]{2,1,0:T(8,128)(2,1)S(1)}, u32[]{:S(2)}, u32[]{:S(2)}) async-start(bf16[8,32,1152]{2,1,0:T(8,128)(2,1)} %bitcast.8), calls=%async_computation | async-start | bytes 1179648 | tf_op jit(solution)/shard_map/all_to_all | solution.py:138
  28.6 18.3 %all-to-all-start.1 = ((bf16[8,32,1024]{2,1,0:T(8,128)(2,1)}), bf16[8,32,1024]{2,1,0:T(8,128)(2,1)S(1)}, u32[]{:S(2)}, u32[]{:S(2)}) async-start(bf16[8,32,1024]{2,1,0:T(8,128)(2,1)} %bitcast.28), calls=%async_computation.1 | async-start | bytes 1048576 | tf_op jit(solution)/shard_map/all_to_all | solution.py:138
  47.0 2.2 %copy-start = (f32[1024,32,32]{0,2,1:T(8,128)S(1)}, f32[1024,32,32]{0,2,1:T(8,128)}, u32[]{:S(2)}) copy-start(f32[1024,32,32]{0,2,1:T(8,128)} %get-tuple-element.63) | copy-start | bytes 12582916
  47.7 5.4 %collective-permute-start.2 = (f32[128,1024]{1,0:T(8,128)S(1)}, f32[128,1024]{1,0:T(8,128)S(1)}, u32[]{:S(2)}, u32[]{:S(2)}) collective-permute-start(f32[128,1024]{1,0:T(8,128)S(1)} %slice.183), channel_id=1, source_target_pairs={{0,1},{1,0},{2,3},{3,2},{4,5},{5,4},{6,7},{7,6},{8,9},{9,8},{10,11... | collective-permute-start | bytes 1572872 | tf_op jit(solution)/shard_map/ppermute | solution.py:93
  47.8 7.0 %collective-permute-start = (f32[128,1024]{1,0:T(8,128)S(1)}, f32[128,1024]{1,0:T(8,128)S(1)}, u32[]{:S(2)}, u32[]{:S(2)}) collective-permute-start(f32[128,1024]{1,0:T(8,128)S(1)} %slice.178), channel_id=1, source_target_pairs={{0,1},{1,0},{2,3},{3,2},{4,5},{5,4},{6,7},{7,6},{8,9},{9,8},{10,11... | collective-permute-start | bytes 1572872 | tf_op jit(solution)/shard_map/ppermute | solution.py:93
  53.2 9.3 %collective-permute-start.3 = (f32[64,1024]{1,0:T(8,128)S(1)}, f32[64,1024]{1,0:T(8,128)S(1)}, u32[]{:S(2)}, u32[]{:S(2)}) collective-permute-start(f32[64,1024]{1,0:T(8,128)S(1)} %slice.185), channel_id=1, source_target_pairs={{0,2},{1,3},{2,0},{3,1},{4,6},{5,7},{6,4},{7,5},{8,10},{9,11},{10,... | collective-permute-start | bytes 786440 | tf_op jit(solution)/shard_map/ppermute | solution.py:93
  54.9 11.5 %collective-permute-start.1 = (f32[64,1024]{1,0:T(8,128)S(1)}, f32[64,1024]{1,0:T(8,128)S(1)}, u32[]{:S(2)}, u32[]{:S(2)}) collective-permute-start(f32[64,1024]{1,0:T(8,128)S(1)} %slice.180), channel_id=1, source_target_pairs={{0,2},{1,3},{2,0},{3,1},{4,6},{5,7},{6,4},{7,5},{8,10},{9,11},{10,... | collective-permute-start | bytes 786440 | tf_op jit(solution)/shard_map/ppermute | solution.py:93

commit v4 on v2

--- a/solution.py
+++ b/solution.py
@@ -92,37 +92,60 @@
     return partial
 
 
+def uv_exchange(outgoing, uv_size):
+    if uv_size > 16:
+        return lax.all_to_all(outgoing, "uv", split_axis=0, concat_axis=0, tiled=True)
+    pieces = [outgoing[0]]
+    for shift in range(1, uv_size):
+        perm = [(i, (i + shift) % uv_size) for i in range(uv_size)]
+        pieces.append(lax.ppermute(outgoing[shift], "uv", perm))
+    return jnp.stack(pieces)
+
+
 def per_device(visibility, anchor, offset, slot_rows, counts):
     time_groups = lax.axis_size("tm")
+    uv_size = lax.axis_size("uv")
     cell_share = TS * TS // time_groups
     vis_rows = visibility[0]
     row_count, row_width = vis_rows.shape
     slot_table = slot_rows[0, 0]
+    live_count = counts[0, 0]
     tile_count, slot_depth = slot_table.shape
-    is_live = (jnp.arange(slot_depth, dtype=jnp.int32)[None, :] < counts[0, 0][:, None]).reshape(-1)
+    if uv_size <= 16:
+        rotate = (lax.axis_index("uv") + jnp.arange(tile_count, dtype=jnp.int32)) % tile_count
+        slot_table = jnp.take(slot_table, rotate, axis=0)
+        live_count = jnp.take(live_count, rotate)
+    is_live = (jnp.arange(slot_depth, dtype=jnp.int32)[None, :] < live_count[:, None]).reshape(-1)
     flat_index = slot_table.reshape(-1)
     pick = (
         (flat_index[:, None] == jnp.arange(row_count, dtype=jnp.int32)[None, :]) & is_live[:, None]
     ).astype(jnp.bfloat16)
     picked = jnp.dot(pick, vis_rows, preferred_element_type=jnp.float32).astype(jnp.bfloat16)
-    meta_src = jnp.zeros((row_count, META), jnp.float32)
-    meta_src = meta_src.at[:, 0].set(anchor[0].astype(jnp.float32))
-    meta_src = meta_src.at[:, 1].set(offset[0].astype(jnp.float32))
-    meta = jnp.dot(pick, meta_src.astype(jnp.bfloat16), preferred_element_type=jnp.float32)
-    meta = meta.astype(jnp.bfloat16)
+    meta_rows = jnp.concatenate(
+        [
+            anchor.astype(jnp.bfloat16),
+            offset.astype(jnp.bfloat16),
+            jnp.zeros((META - 2, row_count), jnp.bfloat16),
+        ],
+        axis=0,
+    )
+    meta = lax.dot_general(
+        pick, meta_rows, (((1,), (1,)), ((), ())), preferred_element_type=jnp.float32
+    ).astype(jnp.bfloat16)
     outgoing = jnp.concatenate([picked, meta], axis=1).reshape(tile_count, slot_depth, row_width + META)
-    arrived = lax.all_to_all(outgoing, "uv", split_axis=0, concat_axis=0, tiled=True)
+    arrived = uv_exchange(outgoing, uv_size)
     arrived = arrived.reshape(-1, row_width + META)
     arr_anchor = arrived[:, row_width].astype(jnp.int32)
     arr_offset = arrived[:, row_width + 1].astype(jnp.int32)
     tm_index = lax.axis_index("tm")
-    if time_groups & (time_groups - 1) == 0:
+    pow2 = time_groups & (time_groups - 1) == 0
+    if pow2:
         cells = halving_order(tm_index, time_groups, cell_share)
     else:
         cells = jnp.arange(TS * TS, dtype=jnp.int32)
     weights = tap_matrix(cells, arr_anchor, arr_offset)
     partial = jnp.dot(weights, arrived[:, :row_width], preferred_element_type=jnp.float32)
-    if time_groups & (time_groups - 1) == 0:
+    if pow2:
         summed = halving_reduce(partial, time_groups)
     else:
         summed = lax.psum_scatter(partial, "tm", scatter_dimension=0, tiled=True)

time: 63.4 us -> 54.9 us (0.87)
  the two profiles are of different devices: /device:TPU:0 before, /device:TPU:12 now
where the time goes in v4:
time: 54.9 us; the launch traced here: 54.7 us
  waiting for transfers between devices  30.7 us (56%)
  starting transfers between devices  10.3 us (19%)
  other arithmetic  6.61 us (12%)
  local copies, waits for them, and re-layouts  3.8 us (7%)
  matrix products  3.12 us (6%)
    ppermute x7, waiting for transfers between devices, uv_exchange(): pieces.append(lax.ppermute(outgoing[shift], 'uv', perm))  19.1 us
    ppermute x2, waiting for transfers between devices, halving_reduce(): received = lax.ppermute(partial[:half], 'tm', perm)  11.6 us
    ppermute x7, starting transfers between devices, uv_exchange(): pieces.append(lax.ppermute(outgoing[shift], 'uv', perm))  8.61 us
    ppermute x2, starting transfers between devices, halving_reduce(): received = lax.ppermute(partial[:half], 'tm', perm)  1.64 us
    dot_general x1, matrix products, per_device(): jnp.dot(lhs, delay_halves(), preferred_element_type=jnp.float32) * out_scale  1.51 us
    gather x1, local copies, waits for them, and re-layouts, per_device(): live_count = jnp.take(live_count, rotate)  1.3 us
    gather x1, local copies, waits for them, and re-layouts, per_device(): slot_table = jnp.take(slot_table, rotate, axis=0)  1.29 us
    another operation x1, other arithmetic  1.28 us
  transfers between devices with their start and end apart: 9, of which 7 were waited for; matrix products, arithmetic and copies ran while one was open for 8% of the time, Pallas kernels for 0%

profile of v4, /device:TPU:12, one launch (start us, length us, event | category | flops | bytes accessed | tf_op | source)
XLA Modules:
  0.0 54.7 jit_solution(15159805128359751437)
XLA Ops:
  0.0 0.0 copy-start
  0.0 1.3 %gather_fusion = s32[8,32]{1,0:T(8,128)S(1)} fusion(s32[8,32]{1,0:T(8,128)} %bitcast.61, s32[1024]{0:T(1024)S(1)} %pad_clamp_fusion), kind=kCustom, calls=%fused_computation | custom fusion | bytes 2080 | tf_op jit(solution)/shard_map/jit(_take)/gather | solution.py:116
  1.3 0.1 broadcast_select_fusion
  1.4 0.1 select_n.238
  1.5 1.3 %gather_fusion.1 = s32[8]{0:T(128)S(1)} fusion(s32[8]{0:T(128)} %bitcast.60, s32[1024]{0:T(1024)S(1)} %pad_clamp_fusion), kind=kCustom, calls=%fused_computation.1 | custom fusion | bytes 96 | tf_op jit(solution)/shard_map/jit(_take)/gather | solution.py:117
  2.8 0.1 iota_compare_fusion.1
  2.9 0.1 lt.83
  3.0 0.7 %convert_element_type.121 = bf16[1,128]{1,0:T(2,128)(2,1)S(1)} convert(s32[1,128]{1,0:T(1,128)} %param.15) | non-fusion elementwise | flops 128 | bytes 768 | tf_op jit(solution)/shard_map/convert_element_type | solution.py:127
  3.6 0.7 %convert_element_type.120 = bf16[1,128]{1,0:T(2,128)(2,1)S(1)} convert(s32[1,128]{1,0:T(1,128)} %param.14) | non-fusion elementwise | flops 128 | bytes 768 | tf_op jit(solution)/shard_map/convert_element_type | solution.py:126
  4.3 0.1 pad.20.clone
  4.4 0.0 copy-done
  4.4 0.5 convolution_convert_fusion
  4.9 0.3 convolution_convert_fusion.1
  5.1 0.1 pad_maximum_fusion.1
  5.2 1.6 %collective-permute-start = (bf16[32,2176]{1,0:T(8,128)(2,1)S(1)}, bf16[32,2176]{1,0:T(8,128)(2,1)S(1)}, u32[]{:S(2)}, u32[]{:S(2)}) collective-permute-start(bf16[32,2176]{1,0:T(8,128)(2,1)S(1)} %get-tuple-element.62), channel_id=1, source_target_pairs={{0,4},{4,8},{8,12},{12,16},{16,20},{20,24},{24,28},{28,0},{1,5},{5... | collective-permute-start | bytes 417800 | tf_op jit(solution)/shard_map/ppermute | solution.py:101
  6.8 1.6 %collective-permute-start.1 = (bf16[32,2176]{1,0:T(8,128)(2,1)S(1)}, bf16[32,2176]{1,0:T(8,128)(2,1)S(1)}, u32[]{:S(2)}, u32[]{:S(2)}) collective-permute-start(bf16[32,2176]{1,0:T(8,128)(2,1)S(1)} %get-tuple-element.63), channel_id=1, source_target_pairs={{0,8},{4,12},{8,16},{12,20},{16,24},{20,28},{24,0},{28,4},{1,9},{5... | collective-permute-start | bytes 417800 | tf_op jit(solution)/shard_map/ppermute | solution.py:101
  8.4 1.2 %collective-permute-start.2 = (bf16[32,2176]{1,0:T(8,128)(2,1)S(1)}, bf16[32,2176]{1,0:T(8,128)(2,1)S(1)}, u32[]{:S(2)}, u32[]{:S(2)}) collective-permute-start(bf16[32,2176]{1,0:T(8,128)(2,1)S(1)} %get-tuple-element.64), channel_id=1, source_target_pairs={{0,12},{4,16},{8,20},{12,24},{16,28},{20,0},{24,4},{28,8},{1,13},{... | collective-permute-start | bytes 417800 | tf_op jit(solution)/shard_map/ppermute | solution.py:101
  9.6 1.7 %collective-permute-start.3 = (bf16[32,2176]{1,0:T(8,128)(2,1)S(1)}, bf16[32,2176]{1,0:T(8,128)(2,1)S(1)}, u32[]{:S(2)}, u32[]{:S(2)}) collective-permute-start(bf16[32,2176]{1,0:T(8,128)(2,1)S(1)} %get-tuple-element.65), channel_id=1, source_target_pairs={{0,16},{4,20},{8,24},{12,28},{16,0},{20,4},{24,8},{28,12},{1,17},{... | collective-permute-start | bytes 417800 | tf_op jit(solution)/shard_map/ppermute | solution.py:101
  11.3 1.3 %collective-permute-start.4 = (bf16[32,2176]{1,0:T(8,128)(2,1)S(1)}, bf16[32,2176]{1,0:T(8,128)(2,1)S(1)}, u32[]{:S(2)}, u32[]{:S(2)}) collective-permute-start(bf16[32,2176]{1,0:T(8,128)(2,1)S(1)} %get-tuple-element.66), channel_id=1, source_target_pairs={{0,20},{4,24},{8,28},{12,0},{16,4},{20,8},{24,12},{28,16},{1,21},{... | collective-permute-start | bytes 417800 | tf_op jit(solution)/shard_map/ppermute | solution.py:101
  12.6 0.1 scatter.15
  12.7 0.1 scatter.16
  12.8 0.1 scatter.19
  12.9 0.1 iota_add_fusion
  13.0 0.1 add.397
  13.1 0.0 collective-permute-done
  13.1 1.3 %collective-permute-start.5 = (bf16[32,2176]{1,0:T(8,128)(2,1)S(1)}, bf16[32,2176]{1,0:T(8,128)(2,1)S(1)}, u32[]{:S(2)}, u32[]{:S(2)}) collective-permute-start(bf16[32,2176]{1,0:T(8,128)(2,1)S(1)} %get-tuple-element.67), channel_id=1, source_target_pairs={{0,24},{4,28},{8,0},{12,4},{16,8},{20,12},{24,16},{28,20},{1,25},{... | collective-permute-start | bytes 417800 | tf_op jit(solution)/shard_map/ppermute | solution.py:101
  14.4 11.4 %collective-permute-done.1 = bf16[32,2176]{1,0:T(8,128)(2,1)S(1)} collective-permute-done((bf16[32,2176]{1,0:T(8,128)(2,1)S(1)}, bf16[32,2176]{1,0:T(8,128)(2,1)S(1)}, u32[]{:S(2)}, u32[]{:S(2)}) %collective-permute-start.1) | collective-permute-done | bytes 139296 | tf_op jit(solution)/shard_map/ppermute | solution.py:101
  25.8 0.0 collective-permute-start.6
  25.8 3.0 %collective-permute-done.2 = bf16[32,2176]{1,0:T(8,128)(2,1)S(1)} collective-permute-done((bf16[32,2176]{1,0:T(8,128)(2,1)S(1)}, bf16[32,2176]{1,0:T(8,128)(2,1)S(1)}, u32[]{:S(2)}, u32[]{:S(2)}) %collective-permute-start.2) | collective-permute-done | bytes 139296 | tf_op jit(solution)/shard_map/ppermute | solution.py:101
  28.8 1.8 %collective-permute-done.3 = bf16[32,2176]{1,0:T(8,128)(2,1)S(1)} collective-permute-done((bf16[32,2176]{1,0:T(8,128)(2,1)S(1)}, bf16[32,2176]{1,0:T(8,128)(2,1)S(1)}, u32[]{:S(2)}, u32[]{:S(2)}) %collective-permute-start.3) | collective-permute-done | bytes 139296 | tf_op jit(solution)/shard_map/ppermute | solution.py:101
  30.6 0.0 collective-permute-done.4
  30.7 1.8 %collective-permute-done.5 = bf16[32,2176]{1,0:T(8,128)(2,1)S(1)} collective-permute-done((bf16[32,2176]{1,0:T(8,128)(2,1)S(1)}, bf16[32,2176]{1,0:T(8,128)(2,1)S(1)}, u32[]{:S(2)}, u32[]{:S(2)}) %collective-permute-start.5) | collective-permute-done | bytes 139296 | tf_op jit(solution)/shard_map/ppermute | solution.py:101
  32.5 1.2 %collective-permute-done.6 = bf16[32,2176]{1,0:T(8,128)(2,1)S(1)} collective-permute-done((bf16[32,2176]{1,0:T(8,128)(2,1)S(1)}, bf16[32,2176]{1,0:T(8,128)(2,1)S(1)}, u32[]{:S(2)}, u32[]{:S(2)}) %collective-permute-start.6) | collective-permute-done | bytes 139296 | tf_op jit(solution)/shard_map/ppermute | solution.py:101
  33.7 0.1 fusion.101
  33.8 0.1 copy.11
  33.9 0.1 copy.12
  34.1 0.1 fusion.89
  34.2 0.9 %fusion.9 = f32[256,2048]{1,0:T(8,128)S(1)} fusion(bf16[256,2176]{1,0:T(8,128)(2,1)S(1)} %bitcast.63, f32[256]{0:T(256)S(1)} %bitcast.82, s32[256]{0:T(256)S(1)} %get-tuple-element.109, f32[256]{0:T(256)S(1)} %bitcast.81, s32[256]{0:T(256)S(1)} %get-tuple-element.105, f32[256]{0:T(256)S(1)} %bitcast.80, s32[256]{0:T(256)S(1)} %get-tuple-element.106, ...), kind=kOutput, calls=%fused_computation.23 | convolution fusion | flops 271581184 | bytes 3180544 | tf_op jit(solution)/shard_map/dot_general | solution.py:147
  35.0 0.1 slice.228
  35.1 0.1 collective-permute-start.7
  35.2 0.1 multiply_subtract_fusion.1
  35.3 0.5 fusion.75
  35.8 0.6 %fusion.78 = (f32[1024,32]{0,1:T(8,128)S(1)}, f32[1024,32]{0,1:T(8,128)S(1)}) fusion(s32[32]{0:T(128)S(1)} %iota_multiply_fusion), kind=kLoop, calls=%fused_computation.117 | loop fusion | flops 458752 | bytes 262272 | tf_op jit(solution)/shard_map/cos | solution.py:51
  36.4 1.2 %multiply_subtract_fusion = (f32[1024,32,32]{0,2,1:T(8,128)S(1)}, f32[1024,32,32]{0,2,1:T(8,128)S(1)}) fusion(f32[1024,32]{0,1:T(8,128)S(1)} %get-tuple-element.122, f32[1024,32]{0,1:T(8,128)S(1)} %get-tuple-element.113, f32[1024,32]{0,1:T(8,128)S(1)} %get-tuple-element.123, f32[1024,32]{0,1:T(8,128)S(1)} %get-tuple-element.112), kind=kLoop, calls=%fused_computation.11 | loop fusion | flops 6291456 | bytes 8912896 | tf_op jit(solution)/shard_map/sub | solution.py:53
  37.7 0.2 collective-permute-done.7
  37.9 0.1 slice_add_fusion
  38.0 1.6 %collective-permute-start.8 = (f32[64,2048]{1,0:T(8,128)S(1)}, f32[64,2048]{1,0:T(8,128)S(1)}, u32[]{:S(2)}, u32[]{:S(2)}) collective-permute-start(f32[64,2048]{1,0:T(8,128)S(1)} %slice.230), channel_id=1, source_target_pairs={{0,2},{1,3},{2,0},{3,1},{4,6},{5,7},{6,4},{7,5},{8,10},{9,11},{10,... | collective-permute-start | bytes 1572872 | tf_op jit(solution)/shard_map/ppermute | solution.py:90
  39.6 1.3 %fusion.5 = (bf16[1024,1024]{0,1:T(8,128)(2,1)S(1)}, bf16[1024,1024]{0,1:T(8,128)(2,1)S(1)}) fusion(f32[1024,32,32]{0,2,1:T(8,128)S(1)} %get-tuple-element.70, f32[1024]{0:T(1024)S(1)} %multiply_subtract_fusion.1, f32[1024,32,32]{0,2,1:T(8,128)S(1)} %get-tuple-element.71), kind=kLoop, calls=%fused_computation.9 | loop fusion | flops 4194304 | bytes 12587008 | tf_op jit(solution)/shard_map/convert
  40.9 11.3 %collective-permute-done.8 = f32[64,2048]{1,0:T(8,128)S(1)} collective-permute-done((f32[64,2048]{1,0:T(8,128)S(1)}, f32[64,2048]{1,0:T(8,128)S(1)}, u32[]{:S(2)}, u32[]{:S(2)}) %collective-permute-start.8) | collective-permute-done | bytes 524320 | tf_op jit(solution)/shard_map/ppermute | solution.py:90
  52.2 0.1 fusion.11
  52.3 1.5 %fusion.6 = f32[128,1024]{1,0:T(8,128)S(1)} fusion(bf16[1024,1024]{0,1:T(8,128)(2,1)S(1)} %get-tuple-element.91, bf16[1024,1024]{0,1:T(8,128)(2,1)S(1)} %get-tuple-element.90, bf16[64,1024]{1,0:T(8,128)(2,1)S(1)} %get-tuple-element.73, bf16[64,1024]{1,0:T(8,128)(2,1)S(1)} %get-tuple-element.72, bf16[64,2048]{1,0:T(8,128)(2,1)S(1)} %fusion.11), kind=kOutput, calls=%fused_computation.20 | convolution fusion | flops 546963456 | bytes 5242880 | tf_op jit(solution)/shard_map/dot_general | solution.py:158
  53.9 0.8 %pad_maximum_fusion = f32[64,2048]{1,0:T(8,128)} fusion(f32[64,1024]{1,0:T(8,128)S(1)} %get-tuple-element.69, f32[64,1024]{1,0:T(8,128)S(1)} %get-tuple-element.68), kind=kLoop, calls=%fused_computation.32 | loop fusion | flops 131072 | bytes 1048576 | tf_op jit(solution)/shard_map/concatenate | solution.py:160
  (28 shorter events, 0.4 us)
Async XLA Ops:
  0.0 4.4 %copy-start = (bf16[1,128,2048]{2,1,0:T(8,128)(2,1)S(1)}, bf16[1,128,2048]{2,1,0:T(8,128)(2,1)}, u32[]{:S(2)}) copy-start(bf16[1,128,2048]{2,1,0:T(8,128)(2,1)} %param.13) | copy-start | bytes 1572868
  5.2 7.9 %collective-permute-start = (bf16[32,2176]{1,0:T(8,128)(2,1)S(1)}, bf16[32,2176]{1,0:T(8,128)(2,1)S(1)}, u32[]{:S(2)}, u32[]{:S(2)}) collective-permute-start(bf16[32,2176]{1,0:T(8,128)(2,1)S(1)} %get-tuple-element.62), channel_id=1, source_target_pairs={{0,4},{4,8},{8,12},{12,16},{16,20},{20,24},{24,28},{28,0},{1,5},{5... | collective-permute-start | bytes 417800 | tf_op jit(solution)/shard_map/ppermute | solution.py:101
  6.8 19.0 %collective-permute-start.1 = (bf16[32,2176]{1,0:T(8,128)(2,1)S(1)}, bf16[32,2176]{1,0:T(8,128)(2,1)S(1)}, u32[]{:S(2)}, u32[]{:S(2)}) collective-permute-start(bf16[32,2176]{1,0:T(8,128)(2,1)S(1)} %get-tuple-element.63), channel_id=1, source_target_pairs={{0,8},{4,12},{8,16},{12,20},{16,24},{20,28},{24,0},{28,4},{1,9},{5... | collective-permute-start | bytes 417800 | tf_op jit(solution)/shard_map/ppermute | solution.py:101
  8.4 20.4 %collective-permute-start.2 = (bf16[32,2176]{1,0:T(8,128)(2,1)S(1)}, bf16[32,2176]{1,0:T(8,128)(2,1)S(1)}, u32[]{:S(2)}, u32[]{:S(2)}) collective-permute-start(bf16[32,2176]{1,0:T(8,128)(2,1)S(1)} %get-tuple-element.64), channel_id=1, source_target_pairs={{0,12},{4,16},{8,20},{12,24},{16,28},{20,0},{24,4},{28,8},{1,13},{... | collective-permute-start | bytes 417800 | tf_op jit(solution)/shard_map/ppermute | solution.py:101
  9.6 21.1 %collective-permute-start.3 = (bf16[32,2176]{1,0:T(8,128)(2,1)S(1)}, bf16[32,2176]{1,0:T(8,128)(2,1)S(1)}, u32[]{:S(2)}, u32[]{:S(2)}) collective-permute-start(bf16[32,2176]{1,0:T(8,128)(2,1)S(1)} %get-tuple-element.65), channel_id=1, source_target_pairs={{0,16},{4,20},{8,24},{12,28},{16,0},{20,4},{24,8},{28,12},{1,17},{... | collective-permute-start | bytes 417800 | tf_op jit(solution)/shard_map/ppermute | solution.py:101
  11.3 19.4 %collective-permute-start.4 = (bf16[32,2176]{1,0:T(8,128)(2,1)S(1)}, bf16[32,2176]{1,0:T(8,128)(2,1)S(1)}, u32[]{:S(2)}, u32[]{:S(2)}) collective-permute-start(bf16[32,2176]{1,0:T(8,128)(2,1)S(1)} %get-tuple-element.66), channel_id=1, source_target_pairs={{0,20},{4,24},{8,28},{12,0},{16,4},{20,8},{24,12},{28,16},{1,21},{... | collective-permute-start | bytes 417800 | tf_op jit(solution)/shard_map/ppermute | solution.py:101
  13.1 19.3 %collective-permute-start.5 = (bf16[32,2176]{1,0:T(8,128)(2,1)S(1)}, bf16[32,2176]{1,0:T(8,128)(2,1)S(1)}, u32[]{:S(2)}, u32[]{:S(2)}) collective-permute-start(bf16[32,2176]{1,0:T(8,128)(2,1)S(1)} %get-tuple-element.67), channel_id=1, source_target_pairs={{0,24},{4,28},{8,0},{12,4},{16,8},{20,12},{24,16},{28,20},{1,25},{... | collective-permute-start | bytes 417800 | tf_op jit(solution)/shard_map/ppermute | solution.py:101
  25.8 7.9 %collective-permute-start.6 = (bf16[32,2176]{1,0:T(8,128)(2,1)S(1)}, bf16[32,2176]{1,0:T(8,128)(2,1)S(1)}, u32[]{:S(2)}, u32[]{:S(2)}) collective-permute-start(bf16[32,2176]{1,0:T(8,128)(2,1)S(1)} %get-tuple-element.61), channel_id=1, source_target_pairs={{0,28},{4,0},{8,4},{12,8},{16,12},{20,16},{24,20},{28,24},{1,29},{... | collective-permute-start | bytes 417800 | tf_op jit(solution)/shard_map/ppermute | solution.py:101
  35.1 2.7 %collective-permute-start.7 = (f32[128,2048]{1,0:T(8,128)S(1)}, f32[128,2048]{1,0:T(8,128)S(1)}, u32[]{:S(2)}, u32[]{:S(2)}) collective-permute-start(f32[128,2048]{1,0:T(8,128)S(1)} %slice.228), channel_id=1, source_target_pairs={{0,1},{1,0},{2,3},{3,2},{4,5},{5,4},{6,7},{7,6},{8,9},{9,8},{10,11... | collective-permute-start | bytes 3145736 | tf_op jit(solution)/shard_map/ppermute | solution.py:90
  38.0 14.2 %collective-permute-start.8 = (f32[64,2048]{1,0:T(8,128)S(1)}, f32[64,2048]{1,0:T(8,128)S(1)}, u32[]{:S(2)}, u32[]{:S(2)}) collective-permute-start(f32[64,2048]{1,0:T(8,128)S(1)} %slice.230), channel_id=1, source_target_pairs={{0,2},{1,3},{2,0},{3,1},{4,6},{5,7},{6,4},{7,5},{8,10},{9,11},{10,... | collective-permute-start | bytes 1572872 | tf_op jit(solution)/shard_map/ppermute | solution.py:90

commit v5 on v4

--- a/solution.py
+++ b/solution.py
@@ -87,8 +87,11 @@
         half = partial.shape[0] // 2
         bit = 1 << level
         perm = [(i, i ^ bit) for i in range(time_groups)]
-        received = lax.ppermute(partial[:half], "tm", perm)
-        partial = partial[half:] + received
+        outgoing = partial[:half]
+        if level > 0:
+            outgoing = outgoing.astype(jnp.bfloat16)
+        received = lax.ppermute(outgoing, "tm", perm)
+        partial = partial[half:] + received.astype(jnp.float32)
     return partial
 
 
@@ -112,9 +115,13 @@
     live_count = counts[0, 0]
     tile_count, slot_depth = slot_table.shape
     if uv_size <= 16:
-        rotate = (lax.axis_index("uv") + jnp.arange(tile_count, dtype=jnp.int32)) % tile_count
-        slot_table = jnp.take(slot_table, rotate, axis=0)
-        live_count = jnp.take(live_count, rotate)
+        uv_index = lax.axis_index("uv")
+        slot_table = lax.dynamic_slice_in_dim(
+            jnp.concatenate([slot_table, slot_table], axis=0), uv_index, tile_count, 0
+        )
+        live_count = lax.dynamic_slice_in_dim(
+            jnp.concatenate([live_count, live_count], axis=0), uv_index, tile_count, 0
+        )
     is_live = (jnp.arange(slot_depth, dtype=jnp.int32)[None, :] < live_count[:, None]).reshape(-1)
     flat_index = slot_table.reshape(-1)
     pick = (
@@ -122,13 +129,8 @@
     ).astype(jnp.bfloat16)
     picked = jnp.dot(pick, vis_rows, preferred_element_type=jnp.float32).astype(jnp.bfloat16)
     meta_rows = jnp.concatenate(
-        [
-            anchor.astype(jnp.bfloat16),
-            offset.astype(jnp.bfloat16),
-            jnp.zeros((META - 2, row_count), jnp.bfloat16),
-        ],
-        axis=0,
-    )
+        [anchor, offset, jnp.zeros((META - 2, row_count), jnp.int32)], axis=0
+    ).astype(jnp.bfloat16)
     meta = lax.dot_general(
         pick, meta_rows, (((1,), (1,)), ((), ())), preferred_element_type=jnp.float32
     ).astype(jnp.bfloat16)

time: 54.9 us -> 48.2 us (0.88)
  waiting for transfers between devices: 30.7 us -> 25.1 us
  local copies, waits for them, and re-layouts: 3.8 us -> 1.28 us
  other arithmetic: 6.61 us -> 8.05 us
    ppermute x2, waiting for transfers between devices: 11.6 us -> 5.94 us  [halving_reduce(): received = lax.ppermute(outgoing, 'tm', perm)]
    gather x2 -> x0, local copies, waits for them, and re-layouts: 2.59 us -> none  [the longest x1 1.3 us: per_device(): live_count = jnp.take(live_count, rotate)]
    concatenate x0 -> x2, other arithmetic: none -> 1.58 us  [the longest x1 0.8 us: per_device(): jnp.concatenate([live_count, live_count], axis=0)]
    convert_element_type x2 -> x0, other arithmetic: 1.32 us -> none  [the longest x1 0.67 us: per_device(): offset.astype(jnp.bfloat16)]
    another operation x1 -> x3, other arithmetic: 1.28 us -> 2.59 us
  transfers between devices with their start and end apart: 9 -> 9, of which waited for: 7 -> 7; matrix products, arithmetic and copies ran while one was open for 8% -> 9% of each run, Pallas kernels for 0% -> 0%
where the time goes in v5:
time: 48.2 us; the launch traced here: 48 us
  waiting for transfers between devices  25.1 us (52%)
  starting transfers between devices  10.2 us (21%)
  other arithmetic  8.05 us (17%)
  matrix products  3.12 us (6%)
  local copies, waits for them, and re-layouts  1.28 us (3%)
    ppermute x7, waiting for transfers between devices, uv_exchange(): pieces.append(lax.ppermute(outgoing[shift], 'uv', perm))  19.1 us
    ppermute x7, starting transfers between devices, uv_exchange(): pieces.append(lax.ppermute(outgoing[shift], 'uv', perm))  8.61 us
    ppermute x2, waiting for transfers between devices, halving_reduce(): received = lax.ppermute(outgoing, 'tm', perm)  5.94 us
    another operation x3, other arithmetic  2.59 us
    ppermute x2, starting transfers between devices, halving_reduce(): received = lax.ppermute(outgoing, 'tm', perm)  1.64 us
    dot_general x1, matrix products, per_device(): jnp.dot(lhs, delay_halves(), preferred_element_type=jnp.float32) * out_scale  1.51 us
    sub x1, other arithmetic, delay_halves(): c_hi[:, :, None] * c_lo[:, None, :] - s_hi[:, :, None] * s_lo[:, None, :]  1.22 us
  transfers between devices with their start and end apart: 9, of which 7 were waited for; matrix products, arithmetic and copies ran while one was open for 9% of the time, Pallas kernels for 0%

profile of v5, /device:TPU:12, one launch (start us, length us, event | category | flops | bytes accessed | tf_op | source)
XLA Modules:
  0.0 48.0 jit_solution(14308453900850600209)
XLA Ops:
  0.0 0.0 copy-start
  0.0 0.8 %fusion.92 = s32[8,32]{1,0:T(8,128)S(1)} fusion(s32[]{:T(128)S(6)} %select_n.177, s32[8,32]{1,0:T(8,128)} %bitcast.62), kind=kLoop, calls=%fused_computation.134 | loop fusion | flops 256 | bytes 2052 | tf_op jit(solution)/shard_map/concatenate | solution.py:120
  0.8 0.1 eq.83
  0.9 0.8 %pad_add_fusion = s32[16]{0:T(128)S(1)} fusion(s32[8]{0:T(128)} %bitcast.81), kind=kLoop, calls=%fused_computation.157 | loop fusion | flops 16 | bytes 96 | tf_op jit(solution)/shard_map/concatenate | solution.py:123
  1.7 0.1 dynamic_slice.7
  1.7 0.1 iota_compare_fusion.1
  1.8 0.1 lt.56
  1.9 0.7 %convert.18 = bf16[1,128]{1,0:T(2,128)(2,1)S(1)} convert(s32[1,128]{1,0:T(1,128)} %param.15) | non-fusion elementwise | flops 128 | bytes 768 | tf_op jit(solution)/shard_map/convert.4
  2.6 0.7 %convert.17 = bf16[1,128]{1,0:T(2,128)(2,1)S(1)} convert(s32[1,128]{1,0:T(1,128)} %param.14) | non-fusion elementwise | flops 128 | bytes 768 | tf_op jit(solution)/shard_map/convert.3
  3.2 0.1 pad.20.clone
  3.3 0.0 copy-done
  3.3 0.5 %convolution_convert_fusion = bf16[256,2048]{1,0:T(8,128)(2,1)S(1)} fusion(bf16[1,128,2048]{2,1,0:T(8,128)(2,1)S(1)} %copy-done, s32[256]{0:T(256)S(1)} %eq.83, pred[256]{0:T(512)(128)(4,1)S(1)} %lt.56), kind=kOutput, calls=%fused_computation.17 | convolution fusion | flops 134807552 | bytes 1574144 | tf_op jit(solution)/shard_map/dot_general | solution.py:130
  3.8 0.3 convolution_convert_fusion.1
  4.1 0.1 pad_maximum_fusion.1
  4.2 1.6 %collective-permute-start = (bf16[32,2176]{1,0:T(8,128)(2,1)S(1)}, bf16[32,2176]{1,0:T(8,128)(2,1)S(1)}, u32[]{:S(2)}, u32[]{:S(2)}) collective-permute-start(bf16[32,2176]{1,0:T(8,128)(2,1)S(1)} %get-tuple-element.62), channel_id=1, source_target_pairs={{0,4},{4,8},{8,12},{12,16},{16,20},{20,24},{24,28},{28,0},{1,5},{5... | collective-permute-start | bytes 417800 | tf_op jit(solution)/shard_map/ppermute | solution.py:104
  5.7 1.6 %collective-permute-start.1 = (bf16[32,2176]{1,0:T(8,128)(2,1)S(1)}, bf16[32,2176]{1,0:T(8,128)(2,1)S(1)}, u32[]{:S(2)}, u32[]{:S(2)}) collective-permute-start(bf16[32,2176]{1,0:T(8,128)(2,1)S(1)} %get-tuple-element.63), channel_id=1, source_target_pairs={{0,8},{4,12},{8,16},{12,20},{16,24},{20,28},{24,0},{28,4},{1,9},{5... | collective-permute-start | bytes 417800 | tf_op jit(solution)/shard_map/ppermute | solution.py:104
  7.3 1.2 %collective-permute-start.2 = (bf16[32,2176]{1,0:T(8,128)(2,1)S(1)}, bf16[32,2176]{1,0:T(8,128)(2,1)S(1)}, u32[]{:S(2)}, u32[]{:S(2)}) collective-permute-start(bf16[32,2176]{1,0:T(8,128)(2,1)S(1)} %get-tuple-element.64), channel_id=1, source_target_pairs={{0,12},{4,16},{8,20},{12,24},{16,28},{20,0},{24,4},{28,8},{1,13},{... | collective-permute-start | bytes 417800 | tf_op jit(solution)/shard_map/ppermute | solution.py:104
  8.5 1.7 %collective-permute-start.3 = (bf16[32,2176]{1,0:T(8,128)(2,1)S(1)}, bf16[32,2176]{1,0:T(8,128)(2,1)S(1)}, u32[]{:S(2)}, u32[]{:S(2)}) collective-permute-start(bf16[32,2176]{1,0:T(8,128)(2,1)S(1)} %get-tuple-element.65), channel_id=1, source_target_pairs={{0,16},{4,20},{8,24},{12,28},{16,0},{20,4},{24,8},{28,12},{1,17},{... | collective-permute-start | bytes 417800 | tf_op jit(solution)/shard_map/ppermute | solution.py:104
  10.2 1.3 %collective-permute-start.4 = (bf16[32,2176]{1,0:T(8,128)(2,1)S(1)}, bf16[32,2176]{1,0:T(8,128)(2,1)S(1)}, u32[]{:S(2)}, u32[]{:S(2)}) collective-permute-start(bf16[32,2176]{1,0:T(8,128)(2,1)S(1)} %get-tuple-element.66), channel_id=1, source_target_pairs={{0,20},{4,24},{8,28},{12,0},{16,4},{20,8},{24,12},{28,16},{1,21},{... | collective-permute-start | bytes 417800 | tf_op jit(solution)/shard_map/ppermute | solution.py:104
  11.5 0.1 scatter.15
  11.6 0.1 scatter.16
  11.7 0.1 scatter.19
  11.8 0.1 iota_add_fusion
  11.9 0.1 add.339
  12.0 0.0 collective-permute-done
  12.0 1.3 %collective-permute-start.5 = (bf16[32,2176]{1,0:T(8,128)(2,1)S(1)}, bf16[32,2176]{1,0:T(8,128)(2,1)S(1)}, u32[]{:S(2)}, u32[]{:S(2)}) collective-permute-start(bf16[32,2176]{1,0:T(8,128)(2,1)S(1)} %get-tuple-element.67), channel_id=1, source_target_pairs={{0,24},{4,28},{8,0},{12,4},{16,8},{20,12},{24,16},{28,20},{1,25},{... | collective-permute-start | bytes 417800 | tf_op jit(solution)/shard_map/ppermute | solution.py:104
  13.3 11.4 %collective-permute-done.1 = bf16[32,2176]{1,0:T(8,128)(2,1)S(1)} collective-permute-done((bf16[32,2176]{1,0:T(8,128)(2,1)S(1)}, bf16[32,2176]{1,0:T(8,128)(2,1)S(1)}, u32[]{:S(2)}, u32[]{:S(2)}) %collective-permute-start.1) | collective-permute-done | bytes 139296 | tf_op jit(solution)/shard_map/ppermute | solution.py:104
  24.7 0.0 collective-permute-start.6
  24.7 3.0 %collective-permute-done.2 = bf16[32,2176]{1,0:T(8,128)(2,1)S(1)} collective-permute-done((bf16[32,2176]{1,0:T(8,128)(2,1)S(1)}, bf16[32,2176]{1,0:T(8,128)(2,1)S(1)}, u32[]{:S(2)}, u32[]{:S(2)}) %collective-permute-start.2) | collective-permute-done | bytes 139296 | tf_op jit(solution)/shard_map/ppermute | solution.py:104
  27.7 1.8 %collective-permute-done.3 = bf16[32,2176]{1,0:T(8,128)(2,1)S(1)} collective-permute-done((bf16[32,2176]{1,0:T(8,128)(2,1)S(1)}, bf16[32,2176]{1,0:T(8,128)(2,1)S(1)}, u32[]{:S(2)}, u32[]{:S(2)}) %collective-permute-start.3) | collective-permute-done | bytes 139296 | tf_op jit(solution)/shard_map/ppermute | solution.py:104
  29.6 0.0 collective-permute-done.4
  29.6 1.8 %collective-permute-done.5 = bf16[32,2176]{1,0:T(8,128)(2,1)S(1)} collective-permute-done((bf16[32,2176]{1,0:T(8,128)(2,1)S(1)}, bf16[32,2176]{1,0:T(8,128)(2,1)S(1)}, u32[]{:S(2)}, u32[]{:S(2)}) %collective-permute-start.5) | collective-permute-done | bytes 139296 | tf_op jit(solution)/shard_map/ppermute | solution.py:104
  31.4 1.2 %collective-permute-done.6 = bf16[32,2176]{1,0:T(8,128)(2,1)S(1)} collective-permute-done((bf16[32,2176]{1,0:T(8,128)(2,1)S(1)}, bf16[32,2176]{1,0:T(8,128)(2,1)S(1)}, u32[]{:S(2)}, u32[]{:S(2)}) %collective-permute-start.6) | collective-permute-done | bytes 139296 | tf_op jit(solution)/shard_map/ppermute | solution.py:104
  32.6 0.1 fusion.99
  32.7 0.1 copy.11
  32.8 0.1 copy.12
  33.0 0.1 fusion.89
  33.1 0.9 %fusion.9 = f32[256,2048]{1,0:T(8,128)S(1)} fusion(bf16[256,2176]{1,0:T(8,128)(2,1)S(1)} %bitcast.59, f32[256]{0:T(256)S(1)} %bitcast.79, s32[256]{0:T(256)S(1)} %get-tuple-element.109, f32[256]{0:T(256)S(1)} %bitcast.78, s32[256]{0:T(256)S(1)} %get-tuple-element.105, f32[256]{0:T(256)S(1)} %bitcast.77, s32[256]{0:T(256)S(1)} %get-tuple-element.106, ...), kind=kOutput, calls=%fused_computation.21 | convolution fusion | flops 271581184 | bytes 3180544 | tf_op jit(solution)/shard_map/dot_general | solution.py:149
  34.0 0.1 slice.225
  34.1 0.1 collective-permute-start.7
  34.2 0.1 multiply_subtract_fusion.1
  34.2 0.5 %fusion.75 = (f32[1024,32]{0,1:T(8,128)S(1)}, f32[1024,32]{0,1:T(8,128)S(1)}) fusion(), kind=kLoop, calls=%fused_computation.113 | loop fusion | flops 458752 | bytes 262144 | tf_op jit(solution)/shard_map/sin | solution.py:52
  34.8 0.6 %fusion.78 = (f32[1024,32]{0,1:T(8,128)S(1)}, f32[1024,32]{0,1:T(8,128)S(1)}) fusion(s32[32]{0:T(128)S(1)} %iota_multiply_fusion), kind=kLoop, calls=%fused_computation.116 | loop fusion | flops 458752 | bytes 262272 | tf_op jit(solution)/shard_map/cos | solution.py:51
  35.3 1.2 %multiply_subtract_fusion = (f32[1024,32,32]{0,2,1:T(8,128)S(1)}, f32[1024,32,32]{0,2,1:T(8,128)S(1)}) fusion(f32[1024,32]{0,1:T(8,128)S(1)} %get-tuple-element.122, f32[1024,32]{0,1:T(8,128)S(1)} %get-tuple-element.113, f32[1024,32]{0,1:T(8,128)S(1)} %get-tuple-element.123, f32[1024,32]{0,1:T(8,128)S(1)} %get-tuple-element.112), kind=kLoop, calls=%fused_computation.9 | loop fusion | flops 6291456 | bytes 8912896 | tf_op jit(solution)/shard_map/sub | solution.py:53
  36.6 0.2 collective-permute-done.7
  36.8 0.1 slice_add_fusion
  36.9 1.6 %collective-permute-start.8 = (bf16[64,2048]{1,0:T(8,128)(2,1)S(1)}, bf16[64,2048]{1,0:T(8,128)(2,1)S(1)}, u32[]{:S(2)}, u32[]{:S(2)}) collective-permute-start(bf16[64,2048]{1,0:T(8,128)(2,1)S(1)} %slice.286), channel_id=1, source_target_pairs={{0,2},{1,3},{2,0},{3,1},{4,6},{5,7},{6,4},{7,5},{8,10},{9,11},{10,... | collective-permute-start | bytes 786440 | tf_op jit(solution)/shard_map/ppermute | solution.py:93
  38.5 1.3 %fusion.5 = (bf16[1024,1024]{0,1:T(8,128)(2,1)S(1)}, bf16[1024,1024]{0,1:T(8,128)(2,1)S(1)}) fusion(f32[1024,32,32]{0,2,1:T(8,128)S(1)} %get-tuple-element.70, f32[1024]{0:T(1024)S(1)} %multiply_subtract_fusion.1, f32[1024,32,32]{0,2,1:T(8,128)S(1)} %get-tuple-element.71), kind=kLoop, calls=%fused_computation.7 | loop fusion | flops 4194304 | bytes 12587008 | tf_op jit(solution)/shard_map/convert
  39.8 5.7 %collective-permute-done.8 = bf16[64,2048]{1,0:T(8,128)(2,1)S(1)} collective-permute-done((bf16[64,2048]{1,0:T(8,128)(2,1)S(1)}, bf16[64,2048]{1,0:T(8,128)(2,1)S(1)}, u32[]{:S(2)}, u32[]{:S(2)}) %collective-permute-start.8) | collective-permute-done | bytes 262176 | tf_op jit(solution)/shard_map/ppermute | solution.py:93
  45.6 1.5 %fusion.6 = f32[128,1024]{1,0:T(8,128)S(1)} fusion(bf16[1024,1024]{0,1:T(8,128)(2,1)S(1)} %get-tuple-element.91, bf16[1024,1024]{0,1:T(8,128)(2,1)S(1)} %get-tuple-element.90, bf16[64,1024]{1,0:T(8,128)(2,1)S(1)} %get-tuple-element.73, bf16[64,1024]{1,0:T(8,128)(2,1)S(1)} %get-tuple-element.72, bf16[64,2048]{1,0:T(8,128)(2,1)S(1)} %fusion.11), kind=kOutput, calls=%fused_computation.18 | convolution fusion | flops 546963456 | bytes 5242880 | tf_op jit(solution)/shard_map/dot_general | solution.py:160
  47.2 0.8 %pad_maximum_fusion = f32[64,2048]{1,0:T(8,128)} fusion(f32[64,1024]{1,0:T(8,128)S(1)} %get-tuple-element.69, f32[64,1024]{1,0:T(8,128)S(1)} %get-tuple-element.68), kind=kLoop, calls=%fused_computation.31 | loop fusion | flops 131072 | bytes 1048576 | tf_op jit(solution)/shard_map/concatenate | solution.py:162
  (25 shorter events, 0.4 us)
Async XLA Ops:
  0.0 3.3 %copy-start = (bf16[1,128,2048]{2,1,0:T(8,128)(2,1)S(1)}, bf16[1,128,2048]{2,1,0:T(8,128)(2,1)}, u32[]{:S(2)}) copy-start(bf16[1,128,2048]{2,1,0:T(8,128)(2,1)} %param.13) | copy-start | bytes 1572868
  4.2 7.9 %collective-permute-start = (bf16[32,2176]{1,0:T(8,128)(2,1)S(1)}, bf16[32,2176]{1,0:T(8,128)(2,1)S(1)}, u32[]{:S(2)}, u32[]{:S(2)}) collective-permute-start(bf16[32,2176]{1,0:T(8,128)(2,1)S(1)} %get-tuple-element.62), channel_id=1, source_target_pairs={{0,4},{4,8},{8,12},{12,16},{16,20},{20,24},{24,28},{28,0},{1,5},{5... | collective-permute-start | bytes 417800 | tf_op jit(solution)/shard_map/ppermute | solution.py:104
  5.7 19.0 %collective-permute-start.1 = (bf16[32,2176]{1,0:T(8,128)(2,1)S(1)}, bf16[32,2176]{1,0:T(8,128)(2,1)S(1)}, u32[]{:S(2)}, u32[]{:S(2)}) collective-permute-start(bf16[32,2176]{1,0:T(8,128)(2,1)S(1)} %get-tuple-element.63), channel_id=1, source_target_pairs={{0,8},{4,12},{8,16},{12,20},{16,24},{20,28},{24,0},{28,4},{1,9},{5... | collective-permute-start | bytes 417800 | tf_op jit(solution)/shard_map/ppermute | solution.py:104
  7.3 20.4 %collective-permute-start.2 = (bf16[32,2176]{1,0:T(8,128)(2,1)S(1)}, bf16[32,2176]{1,0:T(8,128)(2,1)S(1)}, u32[]{:S(2)}, u32[]{:S(2)}) collective-permute-start(bf16[32,2176]{1,0:T(8,128)(2,1)S(1)} %get-tuple-element.64), channel_id=1, source_target_pairs={{0,12},{4,16},{8,20},{12,24},{16,28},{20,0},{24,4},{28,8},{1,13},{... | collective-permute-start | bytes 417800 | tf_op jit(solution)/shard_map/ppermute | solution.py:104
  8.5 21.1 %collective-permute-start.3 = (bf16[32,2176]{1,0:T(8,128)(2,1)S(1)}, bf16[32,2176]{1,0:T(8,128)(2,1)S(1)}, u32[]{:S(2)}, u32[]{:S(2)}) collective-permute-start(bf16[32,2176]{1,0:T(8,128)(2,1)S(1)} %get-tuple-element.65), channel_id=1, source_target_pairs={{0,16},{4,20},{8,24},{12,28},{16,0},{20,4},{24,8},{28,12},{1,17},{... | collective-permute-start | bytes 417800 | tf_op jit(solution)/shard_map/ppermute | solution.py:104
  10.2 19.4 %collective-permute-start.4 = (bf16[32,2176]{1,0:T(8,128)(2,1)S(1)}, bf16[32,2176]{1,0:T(8,128)(2,1)S(1)}, u32[]{:S(2)}, u32[]{:S(2)}) collective-permute-start(bf16[32,2176]{1,0:T(8,128)(2,1)S(1)} %get-tuple-element.66), channel_id=1, source_target_pairs={{0,20},{4,24},{8,28},{12,0},{16,4},{20,8},{24,12},{28,16},{1,21},{... | collective-permute-start | bytes 417800 | tf_op jit(solution)/shard_map/ppermute | solution.py:104
  12.0 19.3 %collective-permute-start.5 = (bf16[32,2176]{1,0:T(8,128)(2,1)S(1)}, bf16[32,2176]{1,0:T(8,128)(2,1)S(1)}, u32[]{:S(2)}, u32[]{:S(2)}) collective-permute-start(bf16[32,2176]{1,0:T(8,128)(2,1)S(1)} %get-tuple-element.67), channel_id=1, source_target_pairs={{0,24},{4,28},{8,0},{12,4},{16,8},{20,12},{24,16},{28,20},{1,25},{... | collective-permute-start | bytes 417800 | tf_op jit(solution)/shard_map/ppermute | solution.py:104
  24.7 7.8 %collective-permute-start.6 = (bf16[32,2176]{1,0:T(8,128)(2,1)S(1)}, bf16[32,2176]{1,0:T(8,128)(2,1)S(1)}, u32[]{:S(2)}, u32[]{:S(2)}) collective-permute-start(bf16[32,2176]{1,0:T(8,128)(2,1)S(1)} %get-tuple-element.61), channel_id=1, source_target_pairs={{0,28},{4,0},{8,4},{12,8},{16,12},{20,16},{24,20},{28,24},{1,29},{... | collective-permute-start | bytes 417800 | tf_op jit(solution)/shard_map/ppermute | solution.py:104
  34.1 2.7 %collective-permute-start.7 = (f32[128,2048]{1,0:T(8,128)S(1)}, f32[128,2048]{1,0:T(8,128)S(1)}, u32[]{:S(2)}, u32[]{:S(2)}) collective-permute-start(f32[128,2048]{1,0:T(8,128)S(1)} %slice.225), channel_id=1, source_target_pairs={{0,1},{1,0},{2,3},{3,2},{4,5},{5,4},{6,7},{7,6},{8,9},{9,8},{10,11... | collective-permute-start | bytes 3145736 | tf_op jit(solution)/shard_map/ppermute | solution.py:93
  36.9 8.6 %collective-permute-start.8 = (bf16[64,2048]{1,0:T(8,128)(2,1)S(1)}, bf16[64,2048]{1,0:T(8,128)(2,1)S(1)}, u32[]{:S(2)}, u32[]{:S(2)}) collective-permute-start(bf16[64,2048]{1,0:T(8,128)(2,1)S(1)} %slice.286), channel_id=1, source_target_pairs={{0,2},{1,3},{2,0},{3,1},{4,6},{5,7},{6,4},{7,5},{8,10},{9,11},{10,... | collective-permute-start | bytes 786440 | tf_op jit(solution)/shard_map/ppermute | solution.py:93

commit v6 on v5

--- a/solution.py
+++ b/solution.py
@@ -12,6 +12,7 @@
 OSAMP = 8
 META = 128
 SPLIT = 32
+CHUNKS = 2
 
 
 def kernel_taps(offsets):
@@ -64,6 +65,14 @@
     return jnp.concatenate([tap_cos, tap_sin], axis=0).astype(jnp.bfloat16)
 
 
+def full_table():
+    halves = delay_halves()
+    tap_cos, tap_sin = halves[:NCH], halves[NCH:]
+    upper = jnp.concatenate([tap_cos, -tap_sin], axis=1)
+    lower = jnp.concatenate([tap_sin, tap_cos], axis=1)
+    return jnp.concatenate([upper, lower], axis=0)
+
+
 def halving_order(tm_index, time_groups, cell_share):
     level_bits = int(math.log2(time_groups))
     quarter = jnp.zeros((time_groups,), jnp.int32)
@@ -81,6 +90,16 @@
     return cells.reshape(-1)
 
 
+def halving_send(partial, level, time_groups):
+    half = partial.shape[0] // 2
+    bit = 1 << level
+    perm = [(i, i ^ bit) for i in range(time_groups)]
+    outgoing = partial[:half]
+    if level > 0:
+        outgoing = outgoing.astype(jnp.bfloat16)
+    return partial[half:], lax.ppermute(outgoing, "tm", perm)
+
+
 def halving_reduce(partial, time_groups):
     level_bits = int(math.log2(time_groups))
     for level in range(level_bits):
@@ -134,32 +153,55 @@
     meta = lax.dot_general(
         pick, meta_rows, (((1,), (1,)), ((), ())), preferred_element_type=jnp.float32
     ).astype(jnp.bfloat16)
-    outgoing = jnp.concatenate([picked, meta], axis=1).reshape(tile_count, slot_depth, row_width + META)
-    arrived = uv_exchange(outgoing, uv_size)
-    arrived = arrived.reshape(-1, row_width + META)
-    arr_anchor = arrived[:, row_width].astype(jnp.int32)
-    arr_offset = arrived[:, row_width + 1].astype(jnp.int32)
     tm_index = lax.axis_index("tm")
     pow2 = time_groups & (time_groups - 1) == 0
     if pow2:
         cells = halving_order(tm_index, time_groups, cell_share)
     else:
         cells = jnp.arange(TS * TS, dtype=jnp.int32)
-    weights = tap_matrix(cells, arr_anchor, arr_offset)
-    partial = jnp.dot(weights, arrived[:, :row_width], preferred_element_type=jnp.float32)
+    transform = full_table()
+    width = row_width // CHUNKS
+    total = None
+    weights = None
+    partial = None
+    for chunk in range(CHUNKS):
+        cols = slice(chunk * width, (chunk + 1) * width)
+        piece = picked[:, cols]
+        if chunk == 0:
+            piece = jnp.concatenate([piece, meta], axis=1)
+        elif pow2:
+            levels = int(math.log2(time_groups))
+            for level in range(levels - 1):
+                kept, received = halving_send(partial, level, time_groups)
+                partial = kept + received.astype(jnp.float32)
+            partial, piece = lax.optimization_barrier((partial, piece))
+            kept, received = halving_send(partial, levels - 1, time_groups)
+        outgoing = piece.reshape(tile_count, slot_depth, piece.shape[1])
+        arrived = uv_exchange(outgoing, uv_size).reshape(-1, piece.shape[1])
+        if chunk > 0:
+            if pow2:
+                received, arrived = lax.optimization_barrier((received, arrived))
+                summed = kept + received.astype(jnp.float32)
+            else:
+                summed = lax.psum_scatter(partial, "tm", scatter_dimension=0, tiled=True)
+            grid = summed.astype(jnp.bfloat16)
+            prev = slice((chunk - 1) * width, chunk * width)
+            part = jnp.dot(grid, transform[prev], preferred_element_type=jnp.float32)
+            total = part if total is None else total + part
+        if chunk == 0:
+            arr_anchor = arrived[:, width].astype(jnp.int32)
+            arr_offset = arrived[:, width + 1].astype(jnp.int32)
+            weights = tap_matrix(cells, arr_anchor, arr_offset)
+        partial = jnp.dot(weights, arrived[:, :width], preferred_element_type=jnp.float32)
     if pow2:
         summed = halving_reduce(partial, time_groups)
     else:
         summed = lax.psum_scatter(partial, "tm", scatter_dimension=0, tiled=True)
     grid = summed.astype(jnp.bfloat16)
-    grid_re, grid_im = grid[:, :NCH], grid[:, NCH:]
-    lhs = jnp.concatenate(
-        [grid, jnp.concatenate([grid_im, -grid_re], axis=1)], axis=0
-    )
+    part = jnp.dot(grid, transform[cols], preferred_element_type=jnp.float32)
+    total = part if total is None else total + part
     out_scale = 4.0 / math.sqrt(NCH * time_groups * ROWS_DEV)
-    both = jnp.dot(lhs, delay_halves(), preferred_element_type=jnp.float32) * out_scale
-    cells_out = grid.shape[0]
-    return jnp.concatenate([both[:cells_out], both[cells_out:]], axis=1)
+    return total * out_scale
 
 
 def solution(mesh):

time: 48.2 us -> 66.1 us (1.37)
  the two profiles are of different devices: /device:TPU:12 before, /device:TPU:0 now
where the time goes in v6:
time: 66.1 us; the launch traced here: 65.9 us
  waiting for transfers between devices  26.3 us (40%)
  starting transfers between devices  24.7 us (37%)
  other arithmetic  7.39 us (11%)
  matrix products  5.74 us (9%)
  local copies, waits for them, and re-layouts  1.37 us (2%)
    ppermute x14, starting transfers between devices, uv_exchange(): pieces.append(lax.ppermute(outgoing[shift], 'uv', perm))  22.5 us
    ppermute x14, waiting for transfers between devices, uv_exchange(): pieces.append(lax.ppermute(outgoing[shift], 'uv', perm))  21.6 us
    ppermute x2, waiting for transfers between devices, halving_reduce(): received = lax.ppermute(outgoing, 'tm', perm)  4.06 us
    dot_general x1, matrix products, per_device(): part = jnp.dot(grid, transform[cols], preferred_element_type=jnp.float32)  2.19 us
    ppermute x2, starting transfers between devices, halving_send(): return (partial[half:], lax.ppermute(outgoing, 'tm', perm))  1.63 us
    dot_general x2, matrix products, per_device(): jnp.dot(weights, arrived[:, :width], preferred_element_type=jnp.float32)  1.41 us
    dot_general x1, matrix products, per_device(): part = jnp.dot(grid, transform[prev], preferred_element_type=jnp.float32)  1.39 us
    another operation x2, other arithmetic  1.37 us
  transfers between devices with their start and end apart: 18, of which 9 were waited for; matrix products, arithmetic and copies ran while one was open for 9% of the time, Pallas kernels for 0%

profile of v6, /device:TPU:0, one launch (start us, length us, event | category | flops | bytes accessed | tf_op | source)
XLA Modules:
  0.0 65.9 jit_solution(4009653800934152967)
XLA Ops:
  0.0 0.7 %convert.16 = bf16[1,128]{1,0:T(2,128)(2,1)S(1)} convert(s32[1,128]{1,0:T(1,128)} %param.14) | non-fusion elementwise | flops 128 | bytes 768 | tf_op jit(solution)/shard_map/convert.4
  0.7 0.7 convert.17
  1.4 0.8 %pad_add_fusion = s32[16]{0:T(128)S(1)} fusion(s32[8]{0:T(128)} %bitcast.117), kind=kLoop, calls=%fused_computation.131 | loop fusion | flops 16 | bytes 96 | tf_op jit(solution)/shard_map/concatenate | solution.py:142
  2.2 0.1 dynamic_slice.7
  2.3 0.1 iota_compare_fusion.1
  2.3 0.1 lt.64
  2.4 0.8 %fusion.60 = s32[8,32]{1,0:T(8,128)S(1)} fusion(s32[]{:T(128)S(6)} %select_n.185, s32[8,32]{1,0:T(8,128)} %bitcast.82), kind=kLoop, calls=%fused_computation.108 | loop fusion | flops 256 | bytes 2052 | tf_op jit(solution)/shard_map/concatenate | solution.py:139
  3.2 0.1 eq.84
  3.3 0.5 convolution_convert_fusion
  3.8 0.1 fusion.70
  3.9 0.1 pad.17.clone
  3.9 0.3 convolution_convert_fusion.1
  4.3 6.1 %collective-permute-start.6 = (bf16[32,1152]{1,0:T(8,128)(2,1)S(1)}, bf16[32,1152]{1,0:T(8,128)(2,1)S(1)}, u32[]{:S(2)}, u32[]{:S(2)}) collective-permute-start(bf16[32,1152]{1,0:T(8,128)(2,1)S(1)} %get-tuple-element.73), channel_id=1, source_target_pairs={{0,28},{4,0},{8,4},{12,8},{16,12},{20,16},{24,20},{28,24},{1,29},{... | collective-permute-start | bytes 221192 | tf_op jit(solution)/shard_map/ppermute | solution.py:123
  10.3 0.0 collective-permute-start
  10.3 0.0 collective-permute-start.1
  10.3 2.5 %collective-permute-start.2 = (bf16[32,1152]{1,0:T(8,128)(2,1)S(1)}, bf16[32,1152]{1,0:T(8,128)(2,1)S(1)}, u32[]{:S(2)}, u32[]{:S(2)}) collective-permute-start(bf16[32,1152]{1,0:T(8,128)(2,1)S(1)} %get-tuple-element.76), channel_id=1, source_target_pairs={{0,12},{4,16},{8,20},{12,24},{16,28},{20,0},{24,4},{28,8},{1,13},{... | collective-permute-start | bytes 221192 | tf_op jit(solution)/shard_map/ppermute | solution.py:123
  12.8 2.8 %collective-permute-start.3 = (bf16[32,1152]{1,0:T(8,128)(2,1)S(1)}, bf16[32,1152]{1,0:T(8,128)(2,1)S(1)}, u32[]{:S(2)}, u32[]{:S(2)}) collective-permute-start(bf16[32,1152]{1,0:T(8,128)(2,1)S(1)} %get-tuple-element.77), channel_id=1, source_target_pairs={{0,16},{4,20},{8,24},{12,28},{16,0},{20,4},{24,8},{28,12},{1,17},{... | collective-permute-start | bytes 221192 | tf_op jit(solution)/shard_map/ppermute | solution.py:123
  15.6 0.5 fusion.43
  16.2 0.1 scatter.15
  16.3 0.1 scatter.16
  16.4 0.1 scatter.19
  16.5 0.1 iota_add_fusion
  16.6 0.1 add.364
  16.7 0.6 fusion.46
  17.3 1.0 %collective-permute-done = bf16[32,1152]{1,0:T(8,128)(2,1)S(1)} collective-permute-done((bf16[32,1152]{1,0:T(8,128)(2,1)S(1)}, bf16[32,1152]{1,0:T(8,128)(2,1)S(1)}, u32[]{:S(2)}, u32[]{:S(2)}) %collective-permute-start) | collective-permute-done | bytes 73760 | tf_op jit(solution)/shard_map/ppermute | solution.py:123
  18.3 0.0 collective-permute-start.4
  18.3 0.0 collective-permute-done.1
  18.3 2.0 %collective-permute-start.5 = (bf16[32,1152]{1,0:T(8,128)(2,1)S(1)}, bf16[32,1152]{1,0:T(8,128)(2,1)S(1)}, u32[]{:S(2)}, u32[]{:S(2)}) collective-permute-start(bf16[32,1152]{1,0:T(8,128)(2,1)S(1)} %get-tuple-element.79), channel_id=1, source_target_pairs={{0,24},{4,28},{8,0},{12,4},{16,8},{20,12},{24,16},{28,20},{1,25},{... | collective-permute-start | bytes 221192 | tf_op jit(solution)/shard_map/ppermute | solution.py:123
  20.4 2.9 %collective-permute-done.2 = bf16[32,1152]{1,0:T(8,128)(2,1)S(1)} collective-permute-done((bf16[32,1152]{1,0:T(8,128)(2,1)S(1)}, bf16[32,1152]{1,0:T(8,128)(2,1)S(1)}, u32[]{:S(2)}, u32[]{:S(2)}) %collective-permute-start.2) | collective-permute-done | bytes 73760 | tf_op jit(solution)/shard_map/ppermute | solution.py:123
  23.3 0.0 collective-permute-done.3
  23.3 2.4 %collective-permute-done.4 = bf16[32,1152]{1,0:T(8,128)(2,1)S(1)} collective-permute-done((bf16[32,1152]{1,0:T(8,128)(2,1)S(1)}, bf16[32,1152]{1,0:T(8,128)(2,1)S(1)}, u32[]{:S(2)}, u32[]{:S(2)}) %collective-permute-start.4) | collective-permute-done | bytes 73760 | tf_op jit(solution)/shard_map/ppermute | solution.py:123
  25.7 0.0 collective-permute-done.5
  25.8 0.0 collective-permute-done.6
  25.8 0.1 fusion.71
  25.9 0.1 copy.11
  26.0 0.1 copy.12
  26.2 0.1 fusion.57
  26.3 0.7 %fusion.16 = f32[256,1024]{1,0:T(8,128)S(1)} fusion(bf16[256,1152]{1,0:T(8,128)(2,1)S(1)} %bitcast.78, f32[256]{0:T(256)S(1)} %bitcast.113, s32[256]{0:T(256)S(1)} %get-tuple-element.118, f32[256]{0:T(256)S(1)} %bitcast.111, s32[256]{0:T(256)S(1)} %get-tuple-element.119, f32[256]{0:T(256)S(1)} %bitcast.109, s32[256]{0:T(256)S(1)} %get-tuple-element.120, ...), kind=kOutput, calls=%fused_computation.27 | convolution fusion | flops 137363456 | bytes 1607680 | tf_op jit(solution)/shard_map/dot_general | solution.py:195
  27.1 0.1 collective-permute-start.7
  27.2 0.1 multiply_subtract_fusion.1
  27.2 1.2 %multiply_subtract_fusion = (f32[1024,32,32]{0,2,1:T(8,128)S(1)}, f32[1024,32,32]{0,2,1:T(8,128)S(1)}) fusion(f32[1024,32]{0,1:T(8,128)S(1)} %get-tuple-element.141, f32[1024,32]{0,1:T(8,128)S(1)} %get-tuple-element.126, f32[1024,32]{0,1:T(8,128)S(1)} %get-tuple-element.142, f32[1024,32]{0,1:T(8,128)S(1)} %get-tuple-element.125), kind=kLoop, calls=%fused_computation.13 | loop fusion | flops 6291456 | bytes 8912896 | tf_op jit(solution)/shard_map/sub | solution.py:54
  28.4 0.6 collective-permute-done.7
  29.0 0.1 slice_add_fusion.1
  29.2 1.4 %collective-permute-start.9 = (bf16[32,1024]{1,0:T(8,128)(2,1)S(1)}, bf16[32,1024]{1,0:T(8,128)(2,1)S(1)}, u32[]{:S(2)}, u32[]{:S(2)}) collective-permute-start(bf16[32,1024]{1,0:T(8,128)(2,1)S(1)} %get-tuple-element.86), channel_id=1, source_target_pairs={{0,4},{4,8},{8,12},{12,16},{16,20},{20,24},{24,28},{28,0},{1,5},{5... | collective-permute-start | bytes 196616 | tf_op jit(solution)/shard_map/ppermute | solution.py:123
  30.6 1.6 %collective-permute-start.8 = (bf16[64,1024]{1,0:T(8,128)(2,1)S(1)}, bf16[64,1024]{1,0:T(8,128)(2,1)S(1)}, u32[]{:S(2)}, u32[]{:S(2)}) collective-permute-start(bf16[64,1024]{1,0:T(8,128)(2,1)S(1)} %slice.359), channel_id=1, source_target_pairs={{0,2},{1,3},{2,0},{3,1},{4,6},{5,7},{6,4},{7,5},{8,10},{9,11},{10,... | collective-permute-start | bytes 393224 | tf_op jit(solution)/shard_map/ppermute | solution.py:100
  32.1 3.4 %collective-permute-start.15 = (bf16[32,1024]{1,0:T(8,128)(2,1)S(1)}, bf16[32,1024]{1,0:T(8,128)(2,1)S(1)}, u32[]{:S(2)}, u32[]{:S(2)}) collective-permute-start(bf16[32,1024]{1,0:T(8,128)(2,1)S(1)} %get-tuple-element.80), channel_id=1, source_target_pairs={{0,28},{4,0},{8,4},{12,8},{16,12},{20,16},{24,20},{28,24},{1,29},{... | collective-permute-start | bytes 196616 | tf_op jit(solution)/shard_map/ppermute | solution.py:123
  35.5 1.4 %collective-permute-start.13 = (bf16[32,1024]{1,0:T(8,128)(2,1)S(1)}, bf16[32,1024]{1,0:T(8,128)(2,1)S(1)}, u32[]{:S(2)}, u32[]{:S(2)}) collective-permute-start(bf16[32,1024]{1,0:T(8,128)(2,1)S(1)} %get-tuple-element.82), channel_id=1, source_target_pairs={{0,20},{4,24},{8,28},{12,0},{16,4},{20,8},{24,12},{28,16},{1,21},{... | collective-permute-start | bytes 196616 | tf_op jit(solution)/shard_map/ppermute | solution.py:123
  36.9 0.6 collective-permute-start.10
  37.6 5.5 %collective-permute-done.10 = bf16[32,1024]{1,0:T(8,128)(2,1)S(1)} collective-permute-done((bf16[32,1024]{1,0:T(8,128)(2,1)S(1)}, bf16[32,1024]{1,0:T(8,128)(2,1)S(1)}, u32[]{:S(2)}, u32[]{:S(2)}) %collective-permute-start.10) | collective-permute-done | bytes 65568 | tf_op jit(solution)/shard_map/ppermute | solution.py:123
  43.0 6.8 %collective-permute-done.11 = bf16[32,1024]{1,0:T(8,128)(2,1)S(1)} collective-permute-done((bf16[32,1024]{1,0:T(8,128)(2,1)S(1)}, bf16[32,1024]{1,0:T(8,128)(2,1)S(1)}, u32[]{:S(2)}, u32[]{:S(2)}) %collective-permute-start.11) | collective-permute-done | bytes 65568 | tf_op jit(solution)/shard_map/ppermute | solution.py:123
  49.8 2.3 %collective-permute-start.12 = (bf16[32,1024]{1,0:T(8,128)(2,1)S(1)}, bf16[32,1024]{1,0:T(8,128)(2,1)S(1)}, u32[]{:S(2)}, u32[]{:S(2)}) collective-permute-start(bf16[32,1024]{1,0:T(8,128)(2,1)S(1)} %get-tuple-element.83), channel_id=1, source_target_pairs={{0,16},{4,20},{8,24},{12,28},{16,0},{20,4},{24,8},{28,12},{1,17},{... | collective-permute-start | bytes 196616 | tf_op jit(solution)/shard_map/ppermute | solution.py:123
  52.1 3.1 %collective-permute-done.12 = bf16[32,1024]{1,0:T(8,128)(2,1)S(1)} collective-permute-done((bf16[32,1024]{1,0:T(8,128)(2,1)S(1)}, bf16[32,1024]{1,0:T(8,128)(2,1)S(1)}, u32[]{:S(2)}, u32[]{:S(2)}) %collective-permute-start.12) | collective-permute-done | bytes 65568 | tf_op jit(solution)/shard_map/ppermute | solution.py:123
  55.2 0.0 collective-permute-done.14
  55.2 0.0 collective-permute-done.15
  55.2 0.7 %fusion.67 = f32[256,1024]{1,0:T(8,128)S(1)} fusion(bf16[256,1024]{1,0:T(8,128)(2,1)S(1)} %bitcast.79, f32[256]{0:T(256)S(1)} %bitcast.114, s32[256]{0:T(256)S(1)} %get-tuple-element.118, f32[256]{0:T(256)S(1)} %bitcast.112, s32[256]{0:T(256)S(1)} %get-tuple-element.119, f32[256]{0:T(256)S(1)} %bitcast.110, s32[256]{0:T(256)S(1)} %get-tuple-element.120, ...), kind=kOutput, calls=%fused_computation.156 | convolution fusion | flops 137363456 | bytes 1607680 | tf_op jit(solution)/shard_map/dot_general | solution.py:195
  56.0 0.1 collective-permute-start.16
  56.1 0.6 fusion.9
  56.7 0.9 %fusion.68 = (bf16[1024,1024]{0,1:T(8,128)(2,1)S(1)}, bf16[1024,1024]{0,1:T(8,128)(2,1)S(1)}) fusion(f32[1024,32,32]{0,2,1:T(8,128)S(1)} %get-tuple-element.88, f32[1024]{0:T(1024)S(1)} %multiply_subtract_fusion.1), kind=kLoop, calls=%fused_computation.157 | loop fusion | flops 3145728 | bytes 8392704 | tf_op jit(solution)/shard_map/neg | solution.py:71
  57.6 0.4 collective-permute-done.16
  58.0 0.1 slice_add_fusion
  58.1 0.5 collective-permute-start.17
  58.6 1.4 %fusion = f32[64,2048]{1,0:T(8,128)S(1)} fusion(bf16[1024,1024]{0,1:T(8,128)(2,1)S(1)} %get-tuple-element.67, bf16[1024,1024]{0,1:T(8,128)(2,1)S(1)} %fusion.9, bf16[64,1024]{1,0:T(8,128)(2,1)S(1)} %collective-permute-done.8, f32[128,1024]{1,0:T(8,128)S(1)} %slice_add_fusion.1), kind=kOutput, calls=%fused_computation | convolution fusion | flops 277020672 | bytes 5111808 | tf_op jit(solution)/shard_map/dot_general | solution.py:189
  60.0 3.7 %collective-permute-done.17 = bf16[64,1024]{1,0:T(8,128)(2,1)S(1)} collective-permute-done((bf16[64,1024]{1,0:T(8,128)(2,1)S(1)}, bf16[64,1024]{1,0:T(8,128)(2,1)S(1)}, u32[]{:S(2)}, u32[]{:S(2)}) %collective-permute-start.17) | collective-permute-done | bytes 131104 | tf_op jit(solution)/shard_map/ppermute | solution.py:112
  63.7 2.2 %fusion.13 = f32[64,2048]{1,0:T(8,128)} fusion(f32[64,2048]{1,0:T(8,128)S(1)} %fusion, bf16[1024,1024]{0,1:T(8,128)(2,1)S(1)} %fusion.9, bf16[1024,1024]{0,1:T(8,128)(2,1)S(1)} %get-tuple-element.68, f32[128,1024]{1,0:T(8,128)S(1)} %slice_add_fusion, bf16[64,1024]{1,0:T(8,128)(2,1)S(1)} %collective-permute-done.17), kind=kOutput, calls=%fused_computation.16 | convolution fusion | flops 277282816 | bytes 5636096 | tf_op jit(solution)/shard_map/dot_general | solution.py:201
  (42 shorter events, 0.5 us)
Async XLA Ops:
  0.0 3.3 %copy-start = (bf16[1,128,2048]{2,1,0:T(8,128)(2,1)S(1)}, bf16[1,128,2048]{2,1,0:T(8,128)(2,1)}, u32[]{:S(2)}) copy-start(bf16[1,128,2048]{2,1,0:T(8,128)(2,1)} %param.13) | copy-start | bytes 1572868
  4.3 21.5 %collective-permute-start.6 = (bf16[32,1152]{1,0:T(8,128)(2,1)S(1)}, bf16[32,1152]{1,0:T(8,128)(2,1)S(1)}, u32[]{:S(2)}, u32[]{:S(2)}) collective-permute-start(bf16[32,1152]{1,0:T(8,128)(2,1)S(1)} %get-tuple-element.73), channel_id=1, source_target_pairs={{0,28},{4,0},{8,4},{12,8},{16,12},{20,16},{24,20},{28,24},{1,29},{... | collective-permute-start | bytes 221192 | tf_op jit(solution)/shard_map/ppermute | solution.py:123
  10.3 8.0 %collective-permute-start = (bf16[32,1152]{1,0:T(8,128)(2,1)S(1)}, bf16[32,1152]{1,0:T(8,128)(2,1)S(1)}, u32[]{:S(2)}, u32[]{:S(2)}) collective-permute-start(bf16[32,1152]{1,0:T(8,128)(2,1)S(1)} %get-tuple-element.74), channel_id=1, source_target_pairs={{0,4},{4,8},{8,12},{12,16},{16,20},{20,24},{24,28},{28,0},{1,5},{5... | collective-permute-start | bytes 221192 | tf_op jit(solution)/shard_map/ppermute | solution.py:123
  10.3 8.0 %collective-permute-start.1 = (bf16[32,1152]{1,0:T(8,128)(2,1)S(1)}, bf16[32,1152]{1,0:T(8,128)(2,1)S(1)}, u32[]{:S(2)}, u32[]{:S(2)}) collective-permute-start(bf16[32,1152]{1,0:T(8,128)(2,1)S(1)} %get-tuple-element.75), channel_id=1, source_target_pairs={{0,8},{4,12},{8,16},{12,20},{16,24},{20,28},{24,0},{28,4},{1,9},{5... | collective-permute-start | bytes 221192 | tf_op jit(solution)/shard_map/ppermute | solution.py:123
  10.3 12.9 %collective-permute-start.2 = (bf16[32,1152]{1,0:T(8,128)(2,1)S(1)}, bf16[32,1152]{1,0:T(8,128)(2,1)S(1)}, u32[]{:S(2)}, u32[]{:S(2)}) collective-permute-start(bf16[32,1152]{1,0:T(8,128)(2,1)S(1)} %get-tuple-element.76), channel_id=1, source_target_pairs={{0,12},{4,16},{8,20},{12,24},{16,28},{20,0},{24,4},{28,8},{1,13},{... | collective-permute-start | bytes 221192 | tf_op jit(solution)/shard_map/ppermute | solution.py:123
  12.8 10.5 %collective-permute-start.3 = (bf16[32,1152]{1,0:T(8,128)(2,1)S(1)}, bf16[32,1152]{1,0:T(8,128)(2,1)S(1)}, u32[]{:S(2)}, u32[]{:S(2)}) collective-permute-start(bf16[32,1152]{1,0:T(8,128)(2,1)S(1)} %get-tuple-element.77), channel_id=1, source_target_pairs={{0,16},{4,20},{8,24},{12,28},{16,0},{20,4},{24,8},{28,12},{1,17},{... | collective-permute-start | bytes 221192 | tf_op jit(solution)/shard_map/ppermute | solution.py:123
  18.3 7.4 %collective-permute-start.4 = (bf16[32,1152]{1,0:T(8,128)(2,1)S(1)}, bf16[32,1152]{1,0:T(8,128)(2,1)S(1)}, u32[]{:S(2)}, u32[]{:S(2)}) collective-permute-start(bf16[32,1152]{1,0:T(8,128)(2,1)S(1)} %get-tuple-element.78), channel_id=1, source_target_pairs={{0,20},{4,24},{8,28},{12,0},{16,4},{20,8},{24,12},{28,16},{1,21},{... | collective-permute-start | bytes 221192 | tf_op jit(solution)/shard_map/ppermute | solution.py:123
  18.3 7.4 %collective-permute-start.5 = (bf16[32,1152]{1,0:T(8,128)(2,1)S(1)}, bf16[32,1152]{1,0:T(8,128)(2,1)S(1)}, u32[]{:S(2)}, u32[]{:S(2)}) collective-permute-start(bf16[32,1152]{1,0:T(8,128)(2,1)S(1)} %get-tuple-element.79), channel_id=1, source_target_pairs={{0,24},{4,28},{8,0},{12,4},{16,8},{20,12},{24,16},{28,20},{1,25},{... | collective-permute-start | bytes 221192 | tf_op jit(solution)/shard_map/ppermute | solution.py:123
  27.1 2.0 %collective-permute-start.7 = (f32[128,1024]{1,0:T(8,128)S(1)}, f32[128,1024]{1,0:T(8,128)S(1)}, u32[]{:S(2)}, u32[]{:S(2)}) collective-permute-start(f32[128,1024]{1,0:T(8,128)S(1)} %slice.290), channel_id=1, source_target_pairs={{0,1},{1,0},{2,3},{3,2},{4,5},{5,4},{6,7},{7,6},{8,9},{9,8},{10,11... | collective-permute-start | bytes 1572872 | tf_op jit(solution)/shard_map/ppermute | solution.py:100
  29.2 7.8 %collective-permute-start.9 = (bf16[32,1024]{1,0:T(8,128)(2,1)S(1)}, bf16[32,1024]{1,0:T(8,128)(2,1)S(1)}, u32[]{:S(2)}, u32[]{:S(2)}) collective-permute-start(bf16[32,1024]{1,0:T(8,128)(2,1)S(1)} %get-tuple-element.86), channel_id=1, source_target_pairs={{0,4},{4,8},{8,12},{12,16},{16,20},{20,24},{24,28},{28,0},{1,5},{5... | collective-permute-start | bytes 196616 | tf_op jit(solution)/shard_map/ppermute | solution.py:123
  30.6 24.7 %collective-permute-start.8 = (bf16[64,1024]{1,0:T(8,128)(2,1)S(1)}, bf16[64,1024]{1,0:T(8,128)(2,1)S(1)}, u32[]{:S(2)}, u32[]{:S(2)}) collective-permute-start(bf16[64,1024]{1,0:T(8,128)(2,1)S(1)} %slice.359), channel_id=1, source_target_pairs={{0,2},{1,3},{2,0},{3,1},{4,6},{5,7},{6,4},{7,5},{8,10},{9,11},{10,... | collective-permute-start | bytes 393224 | tf_op jit(solution)/shard_map/ppermute | solution.py:100
  32.1 23.1 %collective-permute-start.15 = (bf16[32,1024]{1,0:T(8,128)(2,1)S(1)}, bf16[32,1024]{1,0:T(8,128)(2,1)S(1)}, u32[]{:S(2)}, u32[]{:S(2)}) collective-permute-start(bf16[32,1024]{1,0:T(8,128)(2,1)S(1)} %get-tuple-element.80), channel_id=1, source_target_pairs={{0,28},{4,0},{8,4},{12,8},{16,12},{20,16},{24,20},{28,24},{1,29},{... | collective-permute-start | bytes 196616 | tf_op jit(solution)/shard_map/ppermute | solution.py:123
  35.5 19.7 %collective-permute-start.14 = (bf16[32,1024]{1,0:T(8,128)(2,1)S(1)}, bf16[32,1024]{1,0:T(8,128)(2,1)S(1)}, u32[]{:S(2)}, u32[]{:S(2)}) collective-permute-start(bf16[32,1024]{1,0:T(8,128)(2,1)S(1)} %get-tuple-element.81), channel_id=1, source_target_pairs={{0,24},{4,28},{8,0},{12,4},{16,8},{20,12},{24,16},{28,20},{1,25},{... | collective-permute-start | bytes 196616 | tf_op jit(solution)/shard_map/ppermute | solution.py:123
  35.5 19.6 %collective-permute-start.13 = (bf16[32,1024]{1,0:T(8,128)(2,1)S(1)}, bf16[32,1024]{1,0:T(8,128)(2,1)S(1)}, u32[]{:S(2)}, u32[]{:S(2)}) collective-permute-start(bf16[32,1024]{1,0:T(8,128)(2,1)S(1)} %get-tuple-element.82), channel_id=1, source_target_pairs={{0,20},{4,24},{8,28},{12,0},{16,4},{20,8},{24,12},{28,16},{1,21},{... | collective-permute-start | bytes 196616 | tf_op jit(solution)/shard_map/ppermute | solution.py:123
  36.9 6.1 %collective-permute-start.10 = (bf16[32,1024]{1,0:T(8,128)(2,1)S(1)}, bf16[32,1024]{1,0:T(8,128)(2,1)S(1)}, u32[]{:S(2)}, u32[]{:S(2)}) collective-permute-start(bf16[32,1024]{1,0:T(8,128)(2,1)S(1)} %get-tuple-element.85), channel_id=1, source_target_pairs={{0,8},{4,12},{8,16},{12,20},{16,24},{20,28},{24,0},{28,4},{1,9},{5... | collective-permute-start | bytes 196616 | tf_op jit(solution)/shard_map/ppermute | solution.py:123
  43.0 6.8 %collective-permute-start.11 = (bf16[32,1024]{1,0:T(8,128)(2,1)S(1)}, bf16[32,1024]{1,0:T(8,128)(2,1)S(1)}, u32[]{:S(2)}, u32[]{:S(2)}) collective-permute-start(bf16[32,1024]{1,0:T(8,128)(2,1)S(1)} %get-tuple-element.84), channel_id=1, source_target_pairs={{0,12},{4,16},{8,20},{12,24},{16,28},{20,0},{24,4},{28,8},{1,13},{... | collective-permute-start | bytes 196616 | tf_op jit(solution)/shard_map/ppermute | solution.py:123
  49.8 5.4 %collective-permute-start.12 = (bf16[32,1024]{1,0:T(8,128)(2,1)S(1)}, bf16[32,1024]{1,0:T(8,128)(2,1)S(1)}, u32[]{:S(2)}, u32[]{:S(2)}) collective-permute-start(bf16[32,1024]{1,0:T(8,128)(2,1)S(1)} %get-tuple-element.83), channel_id=1, source_target_pairs={{0,16},{4,20},{8,24},{12,28},{16,0},{20,4},{24,8},{28,12},{1,17},{... | collective-permute-start | bytes 196616 | tf_op jit(solution)/shard_map/ppermute | solution.py:123
  56.0 2.0 %collective-permute-start.16 = (f32[128,1024]{1,0:T(8,128)S(1)}, f32[128,1024]{1,0:T(8,128)S(1)}, u32[]{:S(2)}, u32[]{:S(2)}) collective-permute-start(f32[128,1024]{1,0:T(8,128)S(1)} %slice.294), channel_id=1, source_target_pairs={{0,1},{1,0},{2,3},{3,2},{4,5},{5,4},{6,7},{7,6},{8,9},{9,8},{10,11... | collective-permute-start | bytes 1572872 | tf_op jit(solution)/shard_map/ppermute | solution.py:112
  58.1 5.6 %collective-permute-start.17 = (bf16[64,1024]{1,0:T(8,128)(2,1)S(1)}, bf16[64,1024]{1,0:T(8,128)(2,1)S(1)}, u32[]{:S(2)}, u32[]{:S(2)}) collective-permute-start(bf16[64,1024]{1,0:T(8,128)(2,1)S(1)} %slice.358), channel_id=1, source_target_pairs={{0,2},{1,3},{2,0},{3,1},{4,6},{5,7},{6,4},{7,5},{8,10},{9,11},{10,... | collective-permute-start | bytes 393224 | tf_op jit(solution)/shard_map/ppermute | solution.py:112

commit v7 on v5

--- a/solution.py
+++ b/solution.py
@@ -62,6 +62,14 @@
     tap_cos = (taper[:, None, None] * cosine).reshape(NCH, NCH)
     tap_sin = (taper[:, None, None] * sine).reshape(NCH, NCH)
     return jnp.concatenate([tap_cos, tap_sin], axis=0).astype(jnp.bfloat16)
+
+
+def full_table():
+    halves = delay_halves()
+    tap_cos, tap_sin = halves[:NCH], halves[NCH:]
+    upper = jnp.concatenate([tap_cos, -tap_sin], axis=1)
+    lower = jnp.concatenate([tap_sin, tap_cos], axis=1)
+    return jnp.concatenate([upper, lower], axis=0)
 
 
 def halving_order(tm_index, time_groups, cell_share):
@@ -135,7 +143,9 @@
         pick, meta_rows, (((1,), (1,)), ((), ())), preferred_element_type=jnp.float32
     ).astype(jnp.bfloat16)
     outgoing = jnp.concatenate([picked, meta], axis=1).reshape(tile_count, slot_depth, row_width + META)
+    transform = full_table()
     arrived = uv_exchange(outgoing, uv_size)
+    transform, arrived = lax.optimization_barrier((transform, arrived))
     arrived = arrived.reshape(-1, row_width + META)
     arr_anchor = arrived[:, row_width].astype(jnp.int32)
     arr_offset = arrived[:, row_width + 1].astype(jnp.int32)
@@ -152,14 +162,8 @@
     else:
         summed = lax.psum_scatter(partial, "tm", scatter_dimension=0, tiled=True)
     grid = summed.astype(jnp.bfloat16)
-    grid_re, grid_im = grid[:, :NCH], grid[:, NCH:]
-    lhs = jnp.concatenate(
-        [grid, jnp.concatenate([grid_im, -grid_re], axis=1)], axis=0
-    )
     out_scale = 4.0 / math.sqrt(NCH * time_groups * ROWS_DEV)
-    both = jnp.dot(lhs, delay_halves(), preferred_element_type=jnp.float32) * out_scale
-    cells_out = grid.shape[0]
-    return jnp.concatenate([both[:cells_out], both[cells_out:]], axis=1)
+    return jnp.dot(grid, transform, preferred_element_type=jnp.float32) * out_scale
 
 
 def solution(mesh):

time: 48.2 us -> 73.2 us (1.52)
  the two profiles are of different devices: /device:TPU:12 before, /device:TPU:0 now
where the time goes in v7:
time: 73.2 us; the launch traced here: 73 us
  other arithmetic  34.3 us (47%)
  starting transfers between devices  15.6 us (21%)
  waiting for transfers between devices  9.51 us (13%)
  local copies, waits for them, and re-layouts  6.83 us (9%)
  matrix products  6.48 us (9%)
    concatenate x1, other arithmetic, full_table(): return jnp.concatenate([upper, lower], axis=0)  23.6 us
    ppermute x7, starting transfers between devices, uv_exchange(): pieces.append(lax.ppermute(outgoing[shift], 'uv', perm))  14 us
    ppermute x2, waiting for transfers between devices, halving_reduce(): received = lax.ppermute(outgoing, 'tm', perm)  9.49 us
    unnamed x16, local copies, waits for them, and re-layouts  5.89 us
    dot_general x1, matrix products, per_device(): jnp.dot(grid, transform, preferred_element_type=jnp.float32) * out_scale  3.45 us
    neg x1, other arithmetic, full_table(): upper = jnp.concatenate([tap_cos, -tap_sin], axis=1)  2.91 us
    dot_general x1, matrix products, per_device(): jnp.dot(weights, arrived[:, :row_width], preferred_element_type=jnp.float32)  2.27 us
    ppermute x2, starting transfers between devices, halving_reduce(): received = lax.ppermute(outgoing, 'tm', perm)  1.64 us
  transfers between devices with their start and end apart: 9, of which 2 were waited for; matrix products, arithmetic and copies ran while one was open for 48% of the time, Pallas kernels for 0%

profile of v7, /device:TPU:0, one launch (start us, length us, event | category | flops | bytes accessed | tf_op | source)
XLA Modules:
  0.0 73.0 jit_solution(5504035538281785628)
XLA Ops:
  0.0 0.0 copy-start
  0.0 0.8 %fusion.81 = s32[8,32]{1,0:T(8,128)S(1)} fusion(s32[]{:T(128)S(6)} %select_n.187, s32[8,32]{1,0:T(8,128)} %bitcast.64), kind=kLoop, calls=%fused_computation.124 | loop fusion | flops 256 | bytes 2052 | tf_op jit(solution)/shard_map/concatenate | solution.py:128
  0.8 0.1 eq.84
  0.9 0.8 %pad_add_fusion = s32[16]{0:T(128)S(1)} fusion(s32[8]{0:T(128)} %bitcast.83), kind=kLoop, calls=%fused_computation.147 | loop fusion | flops 16 | bytes 96 | tf_op jit(solution)/shard_map/concatenate | solution.py:131
  1.7 0.1 dynamic_slice.7
  1.7 0.1 iota_compare_fusion.1
  1.8 0.1 lt.66
  1.9 0.7 convert.14
  2.6 0.7 convert.13
  3.2 0.1 pad.13.clone
  3.3 0.0 copy-done
  3.3 0.5 convolution_convert_fusion
  3.8 0.3 convolution_convert_fusion.1
  4.1 0.7 %pad_maximum_fusion = (bf16[32,2176]{1,0:T(8,128)(2,1)S(1)}, bf16[32,2176]{1,0:T(8,128)(2,1)}, bf16[32,2176]{1,0:T(8,128)(2,1)S(1)}, bf16[32,2176]{1,0:T(8,128)(...) fusion(bf16[256,128]{1,0:T(8,128)(2,1)S(1)} %convolution_convert_fusion.1, ...), kind=kLoop, calls=%fused_computation.45 | loop fusion | flops 1949696 | bytes 2088960 | tf_op jit(solution)/shard_map/concatenate | solution.py:145
  4.8 3.0 %collective-permute-start = (bf16[32,2176]{1,0:T(8,128)(2,1)}, bf16[32,2176]{1,0:T(8,128)(2,1)}, u32[]{:S(2)}, u32[]{:S(2)}) collective-permute-start(bf16[32,2176]{1,0:T(8,128)(2,1)} %get-tuple-element.68), channel_id=1, source_target_pairs={{0,4},{4,8},{8,12},{12,16},{16,20},{20,24},{24,28},{28,0},{1,5},{5... | collective-permute-start | bytes 417800 | tf_op jit(solution)/shard_map/ppermute | solution.py:112
  7.8 1.6 %collective-permute-start.1 = (bf16[32,2176]{1,0:T(8,128)(2,1)S(1)}, bf16[32,2176]{1,0:T(8,128)(2,1)}, u32[]{:S(2)}, u32[]{:S(2)}) collective-permute-start(bf16[32,2176]{1,0:T(8,128)(2,1)S(1)} %get-tuple-element.69), channel_id=1, source_target_pairs={{0,8},{4,12},{8,16},{12,20},{16,24},{20,28},{24,0},{28,4},{1,9},{5... | collective-permute-start | bytes 417800 | tf_op jit(solution)/shard_map/ppermute | solution.py:112
  9.4 2.5 %collective-permute-start.2 = (bf16[32,2176]{1,0:T(8,128)(2,1)S(1)}, bf16[32,2176]{1,0:T(8,128)(2,1)}, u32[]{:S(2)}, u32[]{:S(2)}) collective-permute-start(bf16[32,2176]{1,0:T(8,128)(2,1)S(1)} %get-tuple-element.70), channel_id=1, source_target_pairs={{0,12},{4,16},{8,20},{12,24},{16,28},{20,0},{24,4},{28,8},{1,13},{... | collective-permute-start | bytes 417800 | tf_op jit(solution)/shard_map/ppermute | solution.py:112
  11.9 1.2 %collective-permute-start.3 = (bf16[32,2176]{1,0:T(8,128)(2,1)S(1)}, bf16[32,2176]{1,0:T(8,128)(2,1)}, u32[]{:S(2)}, u32[]{:S(2)}) collective-permute-start(bf16[32,2176]{1,0:T(8,128)(2,1)S(1)} %get-tuple-element.71), channel_id=1, source_target_pairs={{0,16},{4,20},{8,24},{12,28},{16,0},{20,4},{24,8},{28,12},{1,17},{... | collective-permute-start | bytes 417800 | tf_op jit(solution)/shard_map/ppermute | solution.py:112
  13.1 2.6 %collective-permute-start.4 = (bf16[32,2176]{1,0:T(8,128)(2,1)S(1)}, bf16[32,2176]{1,0:T(8,128)(2,1)}, u32[]{:S(2)}, u32[]{:S(2)}) collective-permute-start(bf16[32,2176]{1,0:T(8,128)(2,1)S(1)} %get-tuple-element.72), channel_id=1, source_target_pairs={{0,20},{4,24},{8,28},{12,0},{16,4},{20,8},{24,12},{28,16},{1,21},{... | collective-permute-start | bytes 417800 | tf_op jit(solution)/shard_map/ppermute | solution.py:112
  15.8 0.5 fusion.66
  16.3 0.1 multiply_subtract_fusion.1
  16.4 0.7 bitcast_dynamic-update-slice_fusion.7
  17.0 0.6 fusion.69
  17.6 1.2 %multiply_add_fusion = (f32[1024,32,32]{0,2,1:T(8,128)S(1)}, f32[1024,32,32]{0,2,1:T(8,128)S(1)}) fusion(f32[1024,32]{0,1:T(8,128)S(1)} %get-tuple-element.114, f32[1024,32]{0,1:T(8,128)S(1)} %get-tuple-element.113, f32[1024,32]{0,1:T(8,128)S(1)} %get-tuple-element.115, f32[1024,32]{0,1:T(8,128)S(1)} %get-tuple-element.112), kind=kLoop, calls=%fused_computation.5 | loop fusion | flops 6291456 | bytes 8912896 | tf_op jit(solution)/shard_map/add | solution.py:54
  18.9 0.6 fusion.1
  19.5 2.9 %fusion.87 = (bf16[1024,1024]{0,1:T(8,128)(2,1)}, bf16[1024,1024]{0,1:T(8,128)(2,1)}) fusion(f32[1024,32,32]{0,2,1:T(8,128)S(1)} %get-tuple-element.74, f32[1024]{0:T(1024)S(1)} %multiply_subtract_fusion.1), kind=kLoop, calls=%fused_computation.171 | loop fusion | flops 3145728 | bytes 8392704 | tf_op jit(solution)/shard_map/neg | solution.py:70
  22.4 0.1 scatter.15
  22.5 0.1 scatter.16
  22.6 0.1 scatter.19
  22.7 0.1 iota_add_fusion
  22.8 0.1 add.355
  22.9 0.0 copy-start.2
  22.9 23.6 %maximum_maximum_fusion = bf16[2048,2048]{0,1:T(8,128)(2,1)} fusion(bf16[1024,1024]{0,1:T(8,128)(2,1)S(1)} %fusion.1, bf16[1024,1024]{0,1:T(8,128)(2,1)} %get-tuple-element.64, bf16[1024,1024]{0,1:T(8,128)(2,1)} %get-tuple-element.63), kind=kLoop, calls=%fused_computation | loop fusion | flops 33554432 | bytes 14680064 | tf_op jit(solution)/shard_map/concatenate | solution.py:72
  46.5 0.0 collective-permute-done
  46.5 1.4 %collective-permute-start.5 = (bf16[32,2176]{1,0:T(8,128)(2,1)S(1)}, bf16[32,2176]{1,0:T(8,128)(2,1)S(1)}, u32[]{:S(2)}, u32[]{:S(2)}) collective-permute-start(bf16[32,2176]{1,0:T(8,128)(2,1)S(1)} %get-tuple-element.73), channel_id=1, source_target_pairs={{0,24},{4,28},{8,0},{12,4},{16,8},{20,12},{24,16},{28,20},{1,25},{... | collective-permute-start | bytes 417800 | tf_op jit(solution)/shard_map/ppermute | solution.py:112
  47.9 0.0 copy-done.2
  47.9 0.9 %bitcast_dynamic-update-slice_fusion.6 = bf16[8,32,2176]{2,1,0:T(8,128)(2,1)S(1)} fusion(bf16[8,32,2176]{2,1,0:T(8,128)(2,1)S(1)} %copy-done.2, bf16[32,2176]{1,0:T(8,128)(2,1)} %collective-permute-done), kind=kLoop, calls=%fused_computation.52 | loop fusion | bytes 278528
  48.8 0.0 collective-permute-done.1
  48.8 1.6 %collective-permute-start.6 = (bf16[32,2176]{1,0:T(8,128)(2,1)S(1)}, bf16[32,2176]{1,0:T(8,128)(2,1)S(1)}, u32[]{:S(2)}, u32[]{:S(2)}) collective-permute-start(bf16[32,2176]{1,0:T(8,128)(2,1)S(1)} %get-tuple-element.67), channel_id=1, source_target_pairs={{0,28},{4,0},{8,4},{12,8},{16,12},{20,16},{24,20},{28,24},{1,29},{... | collective-permute-start | bytes 417800 | tf_op jit(solution)/shard_map/ppermute | solution.py:112
  50.4 0.9 %bitcast_dynamic-update-slice_fusion.5 = bf16[8,32,2176]{2,1,0:T(8,128)(2,1)S(1)} fusion(bf16[8,32,2176]{2,1,0:T(8,128)(2,1)S(1)} %bitcast_dynamic-update-slice_fusion.6, bf16[32,2176]{1,0:T(8,128)(2,1)} %collective-permute-done.1), kind=kLoop, calls=%fused_computation.51 | loop fusion | bytes 278528
  51.4 0.0 collective-permute-done.2
  51.4 0.9 %bitcast_dynamic-update-slice_fusion.4 = bf16[8,32,2176]{2,1,0:T(8,128)(2,1)S(1)} fusion(bf16[8,32,2176]{2,1,0:T(8,128)(2,1)S(1)} %bitcast_dynamic-update-slice_fusion.5, bf16[32,2176]{1,0:T(8,128)(2,1)} %collective-permute-done.2), kind=kLoop, calls=%fused_computation.50 | loop fusion | bytes 278528
  52.3 0.0 collective-permute-done.3
  52.3 0.9 %bitcast_dynamic-update-slice_fusion.3 = bf16[8,32,2176]{2,1,0:T(8,128)(2,1)S(1)} fusion(bf16[8,32,2176]{2,1,0:T(8,128)(2,1)S(1)} %bitcast_dynamic-update-slice_fusion.4, bf16[32,2176]{1,0:T(8,128)(2,1)} %collective-permute-done.3), kind=kLoop, calls=%fused_computation.49 | loop fusion | bytes 278528
  53.2 0.0 collective-permute-done.4
  53.2 0.9 %bitcast_dynamic-update-slice_fusion.2 = bf16[8,32,2176]{2,1,0:T(8,128)(2,1)S(1)} fusion(bf16[8,32,2176]{2,1,0:T(8,128)(2,1)S(1)} %bitcast_dynamic-update-slice_fusion.3, bf16[32,2176]{1,0:T(8,128)(2,1)} %collective-permute-done.4), kind=kLoop, calls=%fused_computation.48 | loop fusion | bytes 278528
  54.2 0.0 collective-permute-done.5
  54.2 0.0 collective-permute-done.6
  54.2 0.0 copy-start.3
  54.2 1.1 %copy-done.3 = bf16[8,32,2176]{2,1,0:T(8,128)(2,1)} copy-done((bf16[8,32,2176]{2,1,0:T(8,128)(2,1)}, bf16[8,32,2176]{2,1,0:T(8,128)(2,1)S(1)}, u32[]{:S(2)}) %copy-start.3) | copy-done | bytes 1114136
  55.3 0.1 fusion.89
  55.4 0.1 copy.11
  55.5 0.1 copy.12
  55.7 0.1 fusion.78
  55.8 0.0 copy-start.1
  55.9 2.3 %fusion.2 = f32[256,2048]{1,0:T(8,128)S(1)} fusion(bf16[256,2176]{1,0:T(8,128)(2,1)} %bitcast.61, f32[256]{0:T(256)S(1)} %bitcast.68, s32[256]{0:T(256)S(1)} %get-tuple-element.109, f32[256]{0:T(256)S(1)} %bitcast.69, s32[256]{0:T(256)S(1)} %get-tuple-element.105, f32[256]{0:T(256)S(1)} %bitcast.70, s32[256]{0:T(256)S(1)} %get-tuple-element.106, ...), kind=kOutput, calls=%fused_computation.18 | convolution fusion | flops 271581184 | bytes 3180544 | tf_op jit(solution)/shard_map/dot_general | solution.py:159
  58.1 0.1 slice.221
  58.2 0.1 collective-permute-start.7
  58.3 2.6 %collective-permute-done.7 = f32[128,2048]{1,0:T(8,128)S(1)} collective-permute-done((f32[128,2048]{1,0:T(8,128)S(1)}, f32[128,2048]{1,0:T(8,128)S(1)}, u32[]{:S(2)}, u32[]{:S(2)}) %collective-permute-start.7) | collective-permute-done | bytes 1048608 | tf_op jit(solution)/shard_map/ppermute | solution.py:101
  60.9 0.1 slice_add_fusion
  61.1 1.6 %collective-permute-start.8 = (bf16[64,2048]{1,0:T(8,128)(2,1)S(1)}, bf16[64,2048]{1,0:T(8,128)(2,1)S(1)}, u32[]{:S(2)}, u32[]{:S(2)}) collective-permute-start(bf16[64,2048]{1,0:T(8,128)(2,1)S(1)} %slice.280), channel_id=1, source_target_pairs={{0,2},{1,3},{2,0},{3,1},{4,6},{5,7},{6,4},{7,5},{8,10},{9,11},{10,... | collective-permute-start | bytes 786440 | tf_op jit(solution)/shard_map/ppermute | solution.py:101
  62.7 6.8 %collective-permute-done.8 = bf16[64,2048]{1,0:T(8,128)(2,1)S(1)} collective-permute-done((bf16[64,2048]{1,0:T(8,128)(2,1)S(1)}, bf16[64,2048]{1,0:T(8,128)(2,1)S(1)}, u32[]{:S(2)}, u32[]{:S(2)}) %collective-permute-start.8) | collective-permute-done | bytes 262176 | tf_op jit(solution)/shard_map/ppermute | solution.py:101
  69.5 0.0 copy-done.1
  69.5 3.5 %convolution_multiply_fusion = f32[64,2048]{1,0:T(8,128)} fusion(bf16[2048,2048]{0,1:T(8,128)(2,1)S(1)} %copy-done.1, f32[128,2048]{1,0:T(8,128)S(1)} %slice_add_fusion, bf16[64,2048]{1,0:T(8,128)(2,1)S(1)} %collective-permute-done.8), kind=kOutput, calls=%fused_computation.15 | convolution fusion | flops 537395200 | bytes 9699328 | tf_op jit(solution)/shard_map/dot_general | solution.py:166
  (18 shorter events, 0.2 us)
Async XLA Ops:
  0.0 3.3 %copy-start = (bf16[1,128,2048]{2,1,0:T(8,128)(2,1)S(1)}, bf16[1,128,2048]{2,1,0:T(8,128)(2,1)}, u32[]{:S(2)}) copy-start(bf16[1,128,2048]{2,1,0:T(8,128)(2,1)} %param.13) | copy-start | bytes 1572868
  4.8 41.6 %collective-permute-start = (bf16[32,2176]{1,0:T(8,128)(2,1)}, bf16[32,2176]{1,0:T(8,128)(2,1)}, u32[]{:S(2)}, u32[]{:S(2)}) collective-permute-start(bf16[32,2176]{1,0:T(8,128)(2,1)} %get-tuple-element.68), channel_id=1, source_target_pairs={{0,4},{4,8},{8,12},{12,16},{16,20},{20,24},{24,28},{28,0},{1,5},{5... | collective-permute-start | bytes 417800 | tf_op jit(solution)/shard_map/ppermute | solution.py:112
  7.8 41.0 %collective-permute-start.1 = (bf16[32,2176]{1,0:T(8,128)(2,1)S(1)}, bf16[32,2176]{1,0:T(8,128)(2,1)}, u32[]{:S(2)}, u32[]{:S(2)}) collective-permute-start(bf16[32,2176]{1,0:T(8,128)(2,1)S(1)} %get-tuple-element.69), channel_id=1, source_target_pairs={{0,8},{4,12},{8,16},{12,20},{16,24},{20,28},{24,0},{28,4},{1,9},{5... | collective-permute-start | bytes 417800 | tf_op jit(solution)/shard_map/ppermute | solution.py:112
  9.4 42.0 %collective-permute-start.2 = (bf16[32,2176]{1,0:T(8,128)(2,1)S(1)}, bf16[32,2176]{1,0:T(8,128)(2,1)}, u32[]{:S(2)}, u32[]{:S(2)}) collective-permute-start(bf16[32,2176]{1,0:T(8,128)(2,1)S(1)} %get-tuple-element.70), channel_id=1, source_target_pairs={{0,12},{4,16},{8,20},{12,24},{16,28},{20,0},{24,4},{28,8},{1,13},{... | collective-permute-start | bytes 417800 | tf_op jit(solution)/shard_map/ppermute | solution.py:112
  11.9 40.4 %collective-permute-start.3 = (bf16[32,2176]{1,0:T(8,128)(2,1)S(1)}, bf16[32,2176]{1,0:T(8,128)(2,1)}, u32[]{:S(2)}, u32[]{:S(2)}) collective-permute-start(bf16[32,2176]{1,0:T(8,128)(2,1)S(1)} %get-tuple-element.71), channel_id=1, source_target_pairs={{0,16},{4,20},{8,24},{12,28},{16,0},{20,4},{24,8},{28,12},{1,17},{... | collective-permute-start | bytes 417800 | tf_op jit(solution)/shard_map/ppermute | solution.py:112
  13.1 40.1 %collective-permute-start.4 = (bf16[32,2176]{1,0:T(8,128)(2,1)S(1)}, bf16[32,2176]{1,0:T(8,128)(2,1)}, u32[]{:S(2)}, u32[]{:S(2)}) collective-permute-start(bf16[32,2176]{1,0:T(8,128)(2,1)S(1)} %get-tuple-element.72), channel_id=1, source_target_pairs={{0,20},{4,24},{8,28},{12,0},{16,4},{20,8},{24,12},{28,16},{1,21},{... | collective-permute-start | bytes 417800 | tf_op jit(solution)/shard_map/ppermute | solution.py:112
  22.9 25.0 %copy-start.2 = (bf16[8,32,2176]{2,1,0:T(8,128)(2,1)S(1)}, bf16[8,32,2176]{2,1,0:T(8,128)(2,1)}, u32[]{:S(2)}) copy-start(bf16[8,32,2176]{2,1,0:T(8,128)(2,1)} %bitcast_dynamic-update-slice_fusion.7) | copy-start | bytes 3342340
  46.5 7.7 %collective-permute-start.5 = (bf16[32,2176]{1,0:T(8,128)(2,1)S(1)}, bf16[32,2176]{1,0:T(8,128)(2,1)S(1)}, u32[]{:S(2)}, u32[]{:S(2)}) collective-permute-start(bf16[32,2176]{1,0:T(8,128)(2,1)S(1)} %get-tuple-element.73), channel_id=1, source_target_pairs={{0,24},{4,28},{8,0},{12,4},{16,8},{20,12},{24,16},{28,20},{1,25},{... | collective-permute-start | bytes 417800 | tf_op jit(solution)/shard_map/ppermute | solution.py:112
  48.8 5.4 %collective-permute-start.6 = (bf16[32,2176]{1,0:T(8,128)(2,1)S(1)}, bf16[32,2176]{1,0:T(8,128)(2,1)S(1)}, u32[]{:S(2)}, u32[]{:S(2)}) collective-permute-start(bf16[32,2176]{1,0:T(8,128)(2,1)S(1)} %get-tuple-element.67), channel_id=1, source_target_pairs={{0,28},{4,0},{8,4},{12,8},{16,12},{20,16},{24,20},{28,24},{1,29},{... | collective-permute-start | bytes 417800 | tf_op jit(solution)/shard_map/ppermute | solution.py:112
  54.2 1.1 %copy-start.3 = (bf16[8,32,2176]{2,1,0:T(8,128)(2,1)}, bf16[8,32,2176]{2,1,0:T(8,128)(2,1)S(1)}, u32[]{:S(2)}) copy-start(bf16[8,32,2176]{2,1,0:T(8,128)(2,1)S(1)} %bitcast_dynamic-update-slice_fusion) | copy-start | bytes 3342340
  55.8 13.7 %copy-start.1 = (bf16[2048,2048]{0,1:T(8,128)(2,1)S(1)}, bf16[2048,2048]{0,1:T(8,128)(2,1)}, u32[]{:S(2)}) copy-start(bf16[2048,2048]{0,1:T(8,128)(2,1)} %maximum_maximum_fusion) | copy-start | bytes 25165828
  58.2 2.7 %collective-permute-start.7 = (f32[128,2048]{1,0:T(8,128)S(1)}, f32[128,2048]{1,0:T(8,128)S(1)}, u32[]{:S(2)}, u32[]{:S(2)}) collective-permute-start(f32[128,2048]{1,0:T(8,128)S(1)} %slice.221), channel_id=1, source_target_pairs={{0,1},{1,0},{2,3},{3,2},{4,5},{5,4},{6,7},{7,6},{8,9},{9,8},{10,11... | collective-permute-start | bytes 3145736 | tf_op jit(solution)/shard_map/ppermute | solution.py:101
  61.1 8.4 %collective-permute-start.8 = (bf16[64,2048]{1,0:T(8,128)(2,1)S(1)}, bf16[64,2048]{1,0:T(8,128)(2,1)S(1)}, u32[]{:S(2)}, u32[]{:S(2)}) collective-permute-start(bf16[64,2048]{1,0:T(8,128)(2,1)S(1)} %slice.280), channel_id=1, source_target_pairs={{0,2},{1,3},{2,0},{3,1},{4,6},{5,7},{6,4},{7,5},{8,10},{9,11},{10,... | collective-permute-start | bytes 786440 | tf_op jit(solution)/shard_map/ppermute | solution.py:101

commit v8 on v5

--- a/solution.py
+++ b/solution.py
@@ -61,7 +61,7 @@
     )
     tap_cos = (taper[:, None, None] * cosine).reshape(NCH, NCH)
     tap_sin = (taper[:, None, None] * sine).reshape(NCH, NCH)
-    return jnp.concatenate([tap_cos, tap_sin], axis=0).astype(jnp.bfloat16)
+    return tap_cos.astype(jnp.bfloat16), tap_sin.astype(jnp.bfloat16)
 
 
 def halving_order(tm_index, time_groups, cell_share):
@@ -136,6 +136,7 @@
     ).astype(jnp.bfloat16)
     outgoing = jnp.concatenate([picked, meta], axis=1).reshape(tile_count, slot_depth, row_width + META)
     arrived = uv_exchange(outgoing, uv_size)
+    (tap_cos, tap_sin), arrived = lax.optimization_barrier((delay_halves(), arrived))
     arrived = arrived.reshape(-1, row_width + META)
     arr_anchor = arrived[:, row_width].astype(jnp.int32)
     arr_offset = arrived[:, row_width + 1].astype(jnp.int32)
@@ -157,7 +158,10 @@
         [grid, jnp.concatenate([grid_im, -grid_re], axis=1)], axis=0
     )
     out_scale = 4.0 / math.sqrt(NCH * time_groups * ROWS_DEV)
-    both = jnp.dot(lhs, delay_halves(), preferred_element_type=jnp.float32) * out_scale
+    both = jnp.dot(lhs[:, :NCH], tap_cos, preferred_element_type=jnp.float32) + jnp.dot(
+        lhs[:, NCH:], tap_sin, preferred_element_type=jnp.float32
+    )
+    both = both * out_scale
     cells_out = grid.shape[0]
     return jnp.concatenate([both[:cells_out], both[cells_out:]], axis=1)
 

time: 48.2 us -> 52.3 us (1.085)
  waiting for transfers between devices: 25.1 us -> 18.5 us
  local copies, waits for them, and re-layouts: 1.28 us -> 7.57 us
  other arithmetic: 8.05 us -> 10.8 us
  matrix products: 3.12 us -> 4.55 us
    ppermute x7, waiting for transfers between devices: 19.1 us -> 8.96 us  [uv_exchange(): pieces.append(lax.ppermute(outgoing[shift], 'uv', perm))]
    unnamed x10 -> x16, local copies, waits for them, and re-layouts: 0.28 us -> 6.56 us
    ppermute x2, waiting for transfers between devices: 5.94 us -> 9.52 us  [halving_reduce(): received = lax.ppermute(outgoing, 'tm', perm)]
    convert_element_type x0 -> x1, other arithmetic: none -> 2.63 us  [delay_halves(): return (tap_cos.astype(jnp.bfloat16), tap_sin.astype(jnp.bfloat16))]
    dot_general x1, matrix products: 0.85 us -> 2.13 us  [per_device(): jnp.dot(weights, arrived[:, :row_width], preferred_element_type=jnp.float32)]
    another operation x3 -> x2, other arithmetic: 2.59 us -> 1.32 us
    add x0 -> x1, other arithmetic: none -> 1.24 us  [delay_halves(): s_hi[:, :, None] * c_lo[:, None, :] + c_hi[:, :, None] * s_lo[:, None, :]]
    sub x1 -> x0, other arithmetic: 1.22 us -> none  [delay_halves(): c_hi[:, :, None] * c_lo[:, None, :] - s_hi[:, :, None] * s_lo[:, None, :]]
  transfers between devices with their start and end apart: 9 -> 9, of which waited for: 7 -> 6; matrix products, arithmetic and copies ran while one was open for 9% -> 21% of each run, Pallas kernels for 0% -> 0%
where the time goes in v8:
time: 52.3 us; the launch traced here: 51.7 us
  waiting for transfers between devices  18.5 us (35%)
  other arithmetic  10.8 us (21%)
  starting transfers between devices  10.1 us (19%)
  local copies, waits for them, and re-layouts  7.57 us (14%)
  matrix products  4.55 us (9%)
    ppermute x2, waiting for transfers between devices, halving_reduce(): received = lax.ppermute(outgoing, 'tm', perm)  9.52 us
    ppermute x7, waiting for transfers between devices, uv_exchange(): pieces.append(lax.ppermute(outgoing[shift], 'uv', perm))  8.96 us
    ppermute x7, starting transfers between devices, uv_exchange(): pieces.append(lax.ppermute(outgoing[shift], 'uv', perm))  8.5 us
    unnamed x16, local copies, waits for them, and re-layouts  6.56 us
    convert_element_type x1, other arithmetic, delay_halves(): return (tap_cos.astype(jnp.bfloat16), tap_sin.astype(jnp.bfloat16))  2.63 us
    dot_general x1, matrix products, per_device(): jnp.dot(weights, arrived[:, :row_width], preferred_element_type=jnp.float32)  2.13 us
    ppermute x2, starting transfers between devices, halving_reduce(): received = lax.ppermute(outgoing, 'tm', perm)  1.61 us
    another operation x2, other arithmetic  1.32 us
  transfers between devices with their start and end apart: 9, of which 6 were waited for; matrix products, arithmetic and copies ran while one was open for 21% of the time, Pallas kernels for 0%

profile of v8, /device:TPU:12, one launch (start us, length us, event | category | flops | bytes accessed | tf_op | source)
XLA Modules:
  0.0 51.7 jit_solution(9797281553762150063)
XLA Ops:
  0.0 0.0 copy-start
  0.0 0.8 %fusion.84 = s32[8,32]{1,0:T(8,128)S(1)} fusion(s32[]{:T(128)S(6)} %select_n.179, s32[8,32]{1,0:T(8,128)} %bitcast.64), kind=kLoop, calls=%fused_computation.130 | loop fusion | flops 256 | bytes 2052 | tf_op jit(solution)/shard_map/concatenate | solution.py:120
  0.8 0.1 eq.84
  0.9 0.8 %pad_add_fusion = s32[16]{0:T(128)S(1)} fusion(s32[8]{0:T(128)} %bitcast.83), kind=kLoop, calls=%fused_computation.153 | loop fusion | flops 16 | bytes 96 | tf_op jit(solution)/shard_map/concatenate | solution.py:123
  1.7 0.1 dynamic_slice.7
  1.7 0.1 iota_compare_fusion.1
  1.8 0.1 lt.58
  1.9 0.7 %convert.12 = bf16[1,128]{1,0:T(2,128)(2,1)S(1)} convert(s32[1,128]{1,0:T(1,128)} %param.15) | non-fusion elementwise | flops 128 | bytes 768 | tf_op jit(solution)/shard_map/convert.2
  2.6 0.7 %convert.11 = bf16[1,128]{1,0:T(2,128)(2,1)S(1)} convert(s32[1,128]{1,0:T(1,128)} %param.14) | non-fusion elementwise | flops 128 | bytes 768 | tf_op jit(solution)/shard_map/convert.1
  3.2 0.1 pad.18.clone
  3.3 0.0 copy-done
  3.3 0.5 convolution_convert_fusion
  3.8 0.3 convolution_convert_fusion.1
  4.1 0.7 %pad_maximum_fusion.1 = (bf16[32,2176]{1,0:T(8,128)(2,1)S(1)}, bf16[32,2176]{1,0:T(8,128)(2,1)}, bf16[32,2176]{1,0:T(8,128)(2,1)S(1)}, bf16[32,2176]{1,0:T(8,128...) fusion(bf16[256,128]{1,0:T(8,128)(2,1)S(1)} %convolution_convert_fusion.1, ...), kind=kLoop, calls=%fused_computation.50 | loop fusion | flops 1949696 | bytes 2088960 | tf_op jit(solution)/shard_map/concatenate | solution.py:137
  4.8 1.5 %collective-permute-start = (bf16[32,2176]{1,0:T(8,128)(2,1)}, bf16[32,2176]{1,0:T(8,128)(2,1)}, u32[]{:S(2)}, u32[]{:S(2)}) collective-permute-start(bf16[32,2176]{1,0:T(8,128)(2,1)} %get-tuple-element.68), channel_id=1, source_target_pairs={{0,4},{4,8},{8,12},{12,16},{16,20},{20,24},{24,28},{28,0},{1,5},{5... | collective-permute-start | bytes 417800 | tf_op jit(solution)/shard_map/ppermute | solution.py:104
  6.3 1.6 %collective-permute-start.1 = (bf16[32,2176]{1,0:T(8,128)(2,1)S(1)}, bf16[32,2176]{1,0:T(8,128)(2,1)}, u32[]{:S(2)}, u32[]{:S(2)}) collective-permute-start(bf16[32,2176]{1,0:T(8,128)(2,1)S(1)} %get-tuple-element.69), channel_id=1, source_target_pairs={{0,8},{4,12},{8,16},{12,20},{16,24},{20,28},{24,0},{28,4},{1,9},{5... | collective-permute-start | bytes 417800 | tf_op jit(solution)/shard_map/ppermute | solution.py:104
  7.9 1.2 %collective-permute-start.2 = (bf16[32,2176]{1,0:T(8,128)(2,1)S(1)}, bf16[32,2176]{1,0:T(8,128)(2,1)}, u32[]{:S(2)}, u32[]{:S(2)}) collective-permute-start(bf16[32,2176]{1,0:T(8,128)(2,1)S(1)} %get-tuple-element.70), channel_id=1, source_target_pairs={{0,12},{4,16},{8,20},{12,24},{16,28},{20,0},{24,4},{28,8},{1,13},{... | collective-permute-start | bytes 417800 | tf_op jit(solution)/shard_map/ppermute | solution.py:104
  9.1 1.7 %collective-permute-start.3 = (bf16[32,2176]{1,0:T(8,128)(2,1)S(1)}, bf16[32,2176]{1,0:T(8,128)(2,1)}, u32[]{:S(2)}, u32[]{:S(2)}) collective-permute-start(bf16[32,2176]{1,0:T(8,128)(2,1)S(1)} %get-tuple-element.71), channel_id=1, source_target_pairs={{0,16},{4,20},{8,24},{12,28},{16,0},{20,4},{24,8},{28,12},{1,17},{... | collective-permute-start | bytes 417800 | tf_op jit(solution)/shard_map/ppermute | solution.py:104
  10.8 1.3 %collective-permute-start.4 = (bf16[32,2176]{1,0:T(8,128)(2,1)S(1)}, bf16[32,2176]{1,0:T(8,128)(2,1)}, u32[]{:S(2)}, u32[]{:S(2)}) collective-permute-start(bf16[32,2176]{1,0:T(8,128)(2,1)S(1)} %get-tuple-element.72), channel_id=1, source_target_pairs={{0,20},{4,24},{8,28},{12,0},{16,4},{20,8},{24,12},{28,16},{1,21},{... | collective-permute-start | bytes 417800 | tf_op jit(solution)/shard_map/ppermute | solution.py:104
  12.1 0.5 %fusion.69 = (f32[1024,32]{0,1:T(8,128)S(1)}, f32[1024,32]{0,1:T(8,128)S(1)}) fusion(), kind=kLoop, calls=%fused_computation.111 | loop fusion | flops 458752 | bytes 262144 | tf_op jit(solution)/shard_map/sin | solution.py:52
  12.6 0.1 multiply_subtract_fusion.1
  12.7 0.7 %bitcast_dynamic-update-slice_fusion.7 = bf16[8,32,2176]{2,1,0:T(8,128)(2,1)} fusion(bf16[256,128]{1,0:T(8,128)(2,1)S(1)} %convolution_convert_fusion.1, bf16[256,2048]{1,0:T(8,128)(2,1)S(1)} %convolution_convert_fusion), kind=kLoop, calls=%fused_computation.58 | loop fusion | flops 278527 | bytes 1253376
  13.3 0.6 %fusion.72 = (f32[1024,32]{0,1:T(8,128)S(1)}, f32[1024,32]{0,1:T(8,128)S(1)}) fusion(s32[32]{0:T(128)S(1)} %iota_multiply_fusion), kind=kLoop, calls=%fused_computation.114 | loop fusion | flops 458752 | bytes 262272 | tf_op jit(solution)/shard_map/cos | solution.py:51
  13.9 0.1 scatter.15
  14.0 0.1 scatter.16
  14.1 0.1 scatter.19
  14.3 0.1 iota_add_fusion
  14.3 0.1 add.342
  14.4 1.2 %multiply_add_fusion = (f32[1024,32,32]{0,2,1:T(8,128)S(1)}, f32[1024,32,32]{0,2,1:T(8,128)S(1)}) fusion(f32[1024,32]{0,1:T(8,128)S(1)} %get-tuple-element.120, f32[1024,32]{0,1:T(8,128)S(1)} %get-tuple-element.119, f32[1024,32]{0,1:T(8,128)S(1)} %get-tuple-element.121, f32[1024,32]{0,1:T(8,128)S(1)} %get-tuple-element.118), kind=kLoop, calls=%fused_computation.4 | loop fusion | flops 6291456 | bytes 8912896 | tf_op jit(solution)/shard_map/add | solution.py:54
  15.7 0.0 copy-start.2
  15.7 2.6 %fusion = (bf16[1024,1024]{0,1:T(8,128)(2,1)}, bf16[1024,1024]{0,1:T(8,128)(2,1)S(1)}) fusion(f32[1024,32,32]{0,2,1:T(8,128)S(1)} %get-tuple-element.76, f32[1024]{0:T(1024)S(1)} %multiply_subtract_fusion.1, f32[1024,32,32]{0,2,1:T(8,128)S(1)} %get-tuple-element.77), kind=kLoop, calls=%fused_computation.1 | loop fusion | flops 4194304 | bytes 12587008 | tf_op jit(solution)/shard_map/convert_element_type | solution.py:64
  18.3 0.0 collective-permute-done
  18.3 1.2 %collective-permute-start.5 = (bf16[32,2176]{1,0:T(8,128)(2,1)S(1)}, bf16[32,2176]{1,0:T(8,128)(2,1)S(1)}, u32[]{:S(2)}, u32[]{:S(2)}) collective-permute-start(bf16[32,2176]{1,0:T(8,128)(2,1)S(1)} %get-tuple-element.73), channel_id=1, source_target_pairs={{0,24},{4,28},{8,0},{12,4},{16,8},{20,12},{24,16},{28,20},{1,25},{... | collective-permute-start | bytes 417800 | tf_op jit(solution)/shard_map/ppermute | solution.py:104
  19.6 0.0 copy-done.2
  19.6 0.9 %bitcast_dynamic-update-slice_fusion.6 = bf16[8,32,2176]{2,1,0:T(8,128)(2,1)S(1)} fusion(bf16[8,32,2176]{2,1,0:T(8,128)(2,1)S(1)} %copy-done.2, bf16[32,2176]{1,0:T(8,128)(2,1)} %collective-permute-done), kind=kLoop, calls=%fused_computation.57 | loop fusion | bytes 278528
  20.5 5.0 %collective-permute-done.1 = bf16[32,2176]{1,0:T(8,128)(2,1)} collective-permute-done((bf16[32,2176]{1,0:T(8,128)(2,1)S(1)}, bf16[32,2176]{1,0:T(8,128)(2,1)}, u32[]{:S(2)}, u32[]{:S(2)}) %collective-permute-start.1) | collective-permute-done | bytes 139296 | tf_op jit(solution)/shard_map/ppermute | solution.py:104
  25.5 0.0 collective-permute-start.6
  25.5 0.9 %bitcast_dynamic-update-slice_fusion.5 = bf16[8,32,2176]{2,1,0:T(8,128)(2,1)S(1)} fusion(bf16[8,32,2176]{2,1,0:T(8,128)(2,1)S(1)} %bitcast_dynamic-update-slice_fusion.6, bf16[32,2176]{1,0:T(8,128)(2,1)} %collective-permute-done.1), kind=kLoop, calls=%fused_computation.56 | loop fusion | bytes 278528
  26.5 2.1 %collective-permute-done.2 = bf16[32,2176]{1,0:T(8,128)(2,1)} collective-permute-done((bf16[32,2176]{1,0:T(8,128)(2,1)S(1)}, bf16[32,2176]{1,0:T(8,128)(2,1)}, u32[]{:S(2)}, u32[]{:S(2)}) %collective-permute-start.2) | collective-permute-done | bytes 139296 | tf_op jit(solution)/shard_map/ppermute | solution.py:104
  28.5 0.9 %bitcast_dynamic-update-slice_fusion.4 = bf16[8,32,2176]{2,1,0:T(8,128)(2,1)S(1)} fusion(bf16[8,32,2176]{2,1,0:T(8,128)(2,1)S(1)} %bitcast_dynamic-update-slice_fusion.5, bf16[32,2176]{1,0:T(8,128)(2,1)} %collective-permute-done.2), kind=kLoop, calls=%fused_computation.55 | loop fusion | bytes 278528
  29.5 0.9 %collective-permute-done.3 = bf16[32,2176]{1,0:T(8,128)(2,1)} collective-permute-done((bf16[32,2176]{1,0:T(8,128)(2,1)S(1)}, bf16[32,2176]{1,0:T(8,128)(2,1)}, u32[]{:S(2)}, u32[]{:S(2)}) %collective-permute-start.3) | collective-permute-done | bytes 139296 | tf_op jit(solution)/shard_map/ppermute | solution.py:104
  30.4 0.9 %bitcast_dynamic-update-slice_fusion.3 = bf16[8,32,2176]{2,1,0:T(8,128)(2,1)S(1)} fusion(bf16[8,32,2176]{2,1,0:T(8,128)(2,1)S(1)} %bitcast_dynamic-update-slice_fusion.4, bf16[32,2176]{1,0:T(8,128)(2,1)} %collective-permute-done.3), kind=kLoop, calls=%fused_computation.54 | loop fusion | bytes 278528
  31.3 0.0 collective-permute-done.4
  31.3 0.9 %bitcast_dynamic-update-slice_fusion.2 = bf16[8,32,2176]{2,1,0:T(8,128)(2,1)S(1)} fusion(bf16[8,32,2176]{2,1,0:T(8,128)(2,1)S(1)} %bitcast_dynamic-update-slice_fusion.3, bf16[32,2176]{1,0:T(8,128)(2,1)} %collective-permute-done.4), kind=kLoop, calls=%fused_computation.53 | loop fusion | bytes 278528
  32.2 0.0 collective-permute-done.5
  32.3 0.9 %collective-permute-done.6 = bf16[32,2176]{1,0:T(8,128)(2,1)S(1)} collective-permute-done((bf16[32,2176]{1,0:T(8,128)(2,1)S(1)}, bf16[32,2176]{1,0:T(8,128)(2,1)S(1)}, u32[]{:S(2)}, u32[]{:S(2)}) %collective-permute-start.6) | collective-permute-done | bytes 139296 | tf_op jit(solution)/shard_map/ppermute | solution.py:104
  33.2 1.0 %copy-done.3 = bf16[8,32,2176]{2,1,0:T(8,128)(2,1)} copy-done((bf16[8,32,2176]{2,1,0:T(8,128)(2,1)}, bf16[8,32,2176]{2,1,0:T(8,128)(2,1)S(1)}, u32[]{:S(2)}) %copy-start.3) | copy-done | bytes 1114136
  34.2 0.1 fusion.90
  34.3 0.1 copy.11
  34.5 0.1 copy.12
  34.6 0.1 fusion.81
  34.8 2.1 %fusion.3 = f32[256,2048]{1,0:T(8,128)S(1)} fusion(bf16[256,2176]{1,0:T(8,128)(2,1)} %bitcast.61, f32[256]{0:T(256)S(1)} %bitcast.68, s32[256]{0:T(256)S(1)} %get-tuple-element.115, f32[256]{0:T(256)S(1)} %bitcast.69, s32[256]{0:T(256)S(1)} %get-tuple-element.111, f32[256]{0:T(256)S(1)} %bitcast.70, s32[256]{0:T(256)S(1)} %get-tuple-element.112, ...), kind=kOutput, calls=%fused_computation.18 | convolution fusion | flops 271581184 | bytes 3180544 | tf_op jit(solution)/shard_map/dot_general | solution.py:150
  36.9 0.1 slice.233
  37.0 0.1 collective-permute-start.7
  37.1 2.6 %collective-permute-done.7 = f32[128,2048]{1,0:T(8,128)S(1)} collective-permute-done((f32[128,2048]{1,0:T(8,128)S(1)}, f32[128,2048]{1,0:T(8,128)S(1)}, u32[]{:S(2)}, u32[]{:S(2)}) %collective-permute-start.7) | collective-permute-done | bytes 1048608 | tf_op jit(solution)/shard_map/ppermute | solution.py:93
  39.7 0.1 slice_add_fusion
  39.9 1.5 %collective-permute-start.8 = (bf16[64,2048]{1,0:T(8,128)(2,1)S(1)}, bf16[64,2048]{1,0:T(8,128)(2,1)S(1)}, u32[]{:S(2)}, u32[]{:S(2)}) collective-permute-start(bf16[64,2048]{1,0:T(8,128)(2,1)S(1)} %slice.300), channel_id=1, source_target_pairs={{0,2},{1,3},{2,0},{3,1},{4,6},{5,7},{6,4},{7,5},{8,10},{9,11},{10,... | collective-permute-start | bytes 786440 | tf_op jit(solution)/shard_map/ppermute | solution.py:93
  41.4 6.9 %collective-permute-done.8 = bf16[64,2048]{1,0:T(8,128)(2,1)S(1)} collective-permute-done((bf16[64,2048]{1,0:T(8,128)(2,1)S(1)}, bf16[64,2048]{1,0:T(8,128)(2,1)S(1)}, u32[]{:S(2)}, u32[]{:S(2)}) %collective-permute-start.8) | collective-permute-done | bytes 262176 | tf_op jit(solution)/shard_map/ppermute | solution.py:93
  48.3 0.1 fusion.5
  48.4 0.0 copy-start.1
  48.4 0.8 %fusion.8 = f32[128,1024]{1,0:T(8,128)S(1)} fusion(bf16[1024,1024]{0,1:T(8,128)(2,1)S(1)} %get-tuple-element.57, bf16[128,2048]{1,0:T(8,128)(2,1)S(1)} %maximum_maximum_fusion), kind=kOutput, calls=%fused_computation.34 | convolution fusion | flops 268435456 | bytes 2883584 | tf_op jit(solution)/shard_map/dot_general | solution.py:161
  49.3 0.7 %copy-done.1 = bf16[1024,1024]{0,1:T(8,128)(2,1)S(1)} copy-done((bf16[1024,1024]{0,1:T(8,128)(2,1)S(1)}, bf16[1024,1024]{0,1:T(8,128)(2,1)}, u32[]{:S(2)}) %copy-start.1) | copy-done | bytes 2097176
  50.0 0.8 %fusion.2 = f32[128,1024]{1,0:T(8,128)S(1)} fusion(f32[128,1024]{1,0:T(8,128)S(1)} %fusion.8, bf16[1024,1024]{0,1:T(8,128)(2,1)S(1)} %copy-done.1, bf16[128,2048]{1,0:T(8,128)(2,1)S(1)} %maximum_maximum_fusion), kind=kOutput, calls=%fused_computation.15 | convolution fusion | flops 268697600 | bytes 3407872 | tf_op jit(solution)/shard_map/dot_general | solution.py:161
  50.9 0.8 %pad_maximum_fusion = f32[64,2048]{1,0:T(8,128)} fusion(f32[64,1024]{1,0:T(8,128)S(1)} %get-tuple-element.75, f32[64,1024]{1,0:T(8,128)S(1)} %get-tuple-element.74), kind=kLoop, calls=%fused_computation.24 | loop fusion | flops 131072 | bytes 1048576 | tf_op jit(solution)/shard_map/concatenate | solution.py:166
  (22 shorter events, 0.3 us)
Async XLA Ops:
  0.0 3.3 %copy-start = (bf16[1,128,2048]{2,1,0:T(8,128)(2,1)S(1)}, bf16[1,128,2048]{2,1,0:T(8,128)(2,1)}, u32[]{:S(2)}) copy-start(bf16[1,128,2048]{2,1,0:T(8,128)(2,1)} %param.13) | copy-start | bytes 1572868
  4.8 13.5 %collective-permute-start = (bf16[32,2176]{1,0:T(8,128)(2,1)}, bf16[32,2176]{1,0:T(8,128)(2,1)}, u32[]{:S(2)}, u32[]{:S(2)}) collective-permute-start(bf16[32,2176]{1,0:T(8,128)(2,1)} %get-tuple-element.68), channel_id=1, source_target_pairs={{0,4},{4,8},{8,12},{12,16},{16,20},{20,24},{24,28},{28,0},{1,5},{5... | collective-permute-start | bytes 417800 | tf_op jit(solution)/shard_map/ppermute | solution.py:104
  6.3 19.2 %collective-permute-start.1 = (bf16[32,2176]{1,0:T(8,128)(2,1)S(1)}, bf16[32,2176]{1,0:T(8,128)(2,1)}, u32[]{:S(2)}, u32[]{:S(2)}) collective-permute-start(bf16[32,2176]{1,0:T(8,128)(2,1)S(1)} %get-tuple-element.69), channel_id=1, source_target_pairs={{0,8},{4,12},{8,16},{12,20},{16,24},{20,28},{24,0},{28,4},{1,9},{5... | collective-permute-start | bytes 417800 | tf_op jit(solution)/shard_map/ppermute | solution.py:104
  7.9 20.6 %collective-permute-start.2 = (bf16[32,2176]{1,0:T(8,128)(2,1)S(1)}, bf16[32,2176]{1,0:T(8,128)(2,1)}, u32[]{:S(2)}, u32[]{:S(2)}) collective-permute-start(bf16[32,2176]{1,0:T(8,128)(2,1)S(1)} %get-tuple-element.70), channel_id=1, source_target_pairs={{0,12},{4,16},{8,20},{12,24},{16,28},{20,0},{24,4},{28,8},{1,13},{... | collective-permute-start | bytes 417800 | tf_op jit(solution)/shard_map/ppermute | solution.py:104
  9.1 21.3 %collective-permute-start.3 = (bf16[32,2176]{1,0:T(8,128)(2,1)S(1)}, bf16[32,2176]{1,0:T(8,128)(2,1)}, u32[]{:S(2)}, u32[]{:S(2)}) collective-permute-start(bf16[32,2176]{1,0:T(8,128)(2,1)S(1)} %get-tuple-element.71), channel_id=1, source_target_pairs={{0,16},{4,20},{8,24},{12,28},{16,0},{20,4},{24,8},{28,12},{1,17},{... | collective-permute-start | bytes 417800 | tf_op jit(solution)/shard_map/ppermute | solution.py:104
  10.8 20.5 %collective-permute-start.4 = (bf16[32,2176]{1,0:T(8,128)(2,1)S(1)}, bf16[32,2176]{1,0:T(8,128)(2,1)}, u32[]{:S(2)}, u32[]{:S(2)}) collective-permute-start(bf16[32,2176]{1,0:T(8,128)(2,1)S(1)} %get-tuple-element.72), channel_id=1, source_target_pairs={{0,20},{4,24},{8,28},{12,0},{16,4},{20,8},{24,12},{28,16},{1,21},{... | collective-permute-start | bytes 417800 | tf_op jit(solution)/shard_map/ppermute | solution.py:104
  15.7 3.9 %copy-start.2 = (bf16[8,32,2176]{2,1,0:T(8,128)(2,1)S(1)}, bf16[8,32,2176]{2,1,0:T(8,128)(2,1)}, u32[]{:S(2)}) copy-start(bf16[8,32,2176]{2,1,0:T(8,128)(2,1)} %bitcast_dynamic-update-slice_fusion.7) | copy-start | bytes 3342340
  18.3 13.9 %collective-permute-start.5 = (bf16[32,2176]{1,0:T(8,128)(2,1)S(1)}, bf16[32,2176]{1,0:T(8,128)(2,1)S(1)}, u32[]{:S(2)}, u32[]{:S(2)}) collective-permute-start(bf16[32,2176]{1,0:T(8,128)(2,1)S(1)} %get-tuple-element.73), channel_id=1, source_target_pairs={{0,24},{4,28},{8,0},{12,4},{16,8},{20,12},{24,16},{28,20},{1,25},{... | collective-permute-start | bytes 417800 | tf_op jit(solution)/shard_map/ppermute | solution.py:104
  25.5 7.6 %collective-permute-start.6 = (bf16[32,2176]{1,0:T(8,128)(2,1)S(1)}, bf16[32,2176]{1,0:T(8,128)(2,1)S(1)}, u32[]{:S(2)}, u32[]{:S(2)}) collective-permute-start(bf16[32,2176]{1,0:T(8,128)(2,1)S(1)} %get-tuple-element.67), channel_id=1, source_target_pairs={{0,28},{4,0},{8,4},{12,8},{16,12},{20,16},{24,20},{28,24},{1,29},{... | collective-permute-start | bytes 417800 | tf_op jit(solution)/shard_map/ppermute | solution.py:104
  33.2 1.0 %copy-start.3 = (bf16[8,32,2176]{2,1,0:T(8,128)(2,1)}, bf16[8,32,2176]{2,1,0:T(8,128)(2,1)S(1)}, u32[]{:S(2)}) copy-start(bf16[8,32,2176]{2,1,0:T(8,128)(2,1)S(1)} %bitcast_dynamic-update-slice_fusion) | copy-start | bytes 3342340
  37.0 2.7 %collective-permute-start.7 = (f32[128,2048]{1,0:T(8,128)S(1)}, f32[128,2048]{1,0:T(8,128)S(1)}, u32[]{:S(2)}, u32[]{:S(2)}) collective-permute-start(f32[128,2048]{1,0:T(8,128)S(1)} %slice.233), channel_id=1, source_target_pairs={{0,1},{1,0},{2,3},{3,2},{4,5},{5,4},{6,7},{7,6},{8,9},{9,8},{10,11... | collective-permute-start | bytes 3145736 | tf_op jit(solution)/shard_map/ppermute | solution.py:93
  39.9 8.4 %collective-permute-start.8 = (bf16[64,2048]{1,0:T(8,128)(2,1)S(1)}, bf16[64,2048]{1,0:T(8,128)(2,1)S(1)}, u32[]{:S(2)}, u32[]{:S(2)}) collective-permute-start(bf16[64,2048]{1,0:T(8,128)(2,1)S(1)} %slice.300), channel_id=1, source_target_pairs={{0,2},{1,3},{2,0},{3,1},{4,6},{5,7},{6,4},{7,5},{8,10},{9,11},{10,... | collective-permute-start | bytes 786440 | tf_op jit(solution)/shard_map/ppermute | solution.py:93
  48.4 1.6 %copy-start.1 = (bf16[1024,1024]{0,1:T(8,128)(2,1)S(1)}, bf16[1024,1024]{0,1:T(8,128)(2,1)}, u32[]{:S(2)}) copy-start(bf16[1024,1024]{0,1:T(8,128)(2,1)} %get-tuple-element.58) | copy-start | bytes 6291460

commit v9 on v5

--- a/solution.py
+++ b/solution.py
@@ -98,10 +98,12 @@
 def uv_exchange(outgoing, uv_size):
     if uv_size > 16:
         return lax.all_to_all(outgoing, "uv", split_axis=0, concat_axis=0, tiled=True)
-    pieces = [outgoing[0]]
+    uv_index = lax.axis_index("uv")
+    pieces = [lax.dynamic_index_in_dim(outgoing, uv_index, 0, keepdims=False)]
     for shift in range(1, uv_size):
         perm = [(i, (i + shift) % uv_size) for i in range(uv_size)]
-        pieces.append(lax.ppermute(outgoing[shift], "uv", perm))
+        piece = lax.dynamic_index_in_dim(outgoing, (uv_index + shift) % uv_size, 0, keepdims=False)
+        pieces.append(lax.ppermute(piece, "uv", perm))
     return jnp.stack(pieces)
 
 
@@ -111,25 +113,23 @@
     cell_share = TS * TS // time_groups
     vis_rows = visibility[0]
     row_count, row_width = vis_rows.shape
-    slot_table = slot_rows[0, 0]
-    live_count = counts[0, 0]
-    tile_count, slot_depth = slot_table.shape
-    if uv_size <= 16:
-        uv_index = lax.axis_index("uv")
-        slot_table = lax.dynamic_slice_in_dim(
-            jnp.concatenate([slot_table, slot_table], axis=0), uv_index, tile_count, 0
-        )
-        live_count = lax.dynamic_slice_in_dim(
-            jnp.concatenate([live_count, live_count], axis=0), uv_index, tile_count, 0
-        )
+    tile_count, slot_depth = slot_rows.shape[2:]
+    slot_size = tile_count * slot_depth
+    ints = jnp.concatenate(
+        [slot_rows.reshape(-1), counts.reshape(-1), anchor.reshape(-1), offset.reshape(-1)]
+    )
+    flat_index = ints[:slot_size]
+    live_count = ints[slot_size:slot_size + tile_count]
+    anchor_row = ints[slot_size + tile_count:slot_size + tile_count + row_count]
+    offset_row = ints[slot_size + tile_count + row_count:]
     is_live = (jnp.arange(slot_depth, dtype=jnp.int32)[None, :] < live_count[:, None]).reshape(-1)
-    flat_index = slot_table.reshape(-1)
     pick = (
         (flat_index[:, None] == jnp.arange(row_count, dtype=jnp.int32)[None, :]) & is_live[:, None]
     ).astype(jnp.bfloat16)
     picked = jnp.dot(pick, vis_rows, preferred_element_type=jnp.float32).astype(jnp.bfloat16)
     meta_rows = jnp.concatenate(
-        [anchor, offset, jnp.zeros((META - 2, row_count), jnp.int32)], axis=0
+        [anchor_row[None, :], offset_row[None, :], jnp.zeros((META - 2, row_count), jnp.int32)],
+        axis=0,
     ).astype(jnp.bfloat16)
     meta = lax.dot_general(
         pick, meta_rows, (((1,), (1,)), ((), ())), preferred_element_type=jnp.float32

time: 48.2 us -> 53.8 us (1.12)
  local copies, waits for them, and re-layouts: 1.28 us -> 6.96 us
  waiting for transfers between devices: 25.1 us -> 21.3 us
  other arithmetic: 8.05 us -> 10.2 us
  matrix products: 3.12 us -> 4.39 us
    ppermute x7, waiting for transfers between devices: 19.1 us -> 15.4 us  [uv_exchange(): pieces.append(lax.ppermute(piece, 'uv', perm))]
    unnamed x10 -> x8, local copies, waits for them, and re-layouts: 0.28 us -> 4 us
    concatenate x2 -> x0, other arithmetic: 1.58 us -> none  [the longest x1 0.8 us: per_device(): jnp.concatenate([live_count, live_count], axis=0)]
    dot_general x1, matrix products: 0.85 us -> 2.12 us  [per_device(): jnp.dot(weights, arrived[:, :row_width], preferred_element_type=jnp.float32)]
    div x2 -> x1, other arithmetic: 0.04 us -> 1.16 us  [kernel_taps(): sub_shift = (offsets.astype(jnp.float32) + 0.5) / OSAMP]
    div x1, other arithmetic: 0.02 us -> 1.01 us  [tap_matrix(): anchor_y = anchors // span]
    ne x1, other arithmetic: 0.03 us -> 0.97 us  [tap_matrix(): anchor_y = anchors // span]
    squeeze x0 -> x1, local copies, waits for them, and re-layouts: none -> 0.74 us  [uv_exchange(): lax.dynamic_index_in_dim(outgoing, (uv_index + shift) % uv_size, 0, keepd...]
  transfers between devices with their start and end apart: 9 -> 9, of which waited for: 7 -> 7; matrix products, arithmetic and copies ran while one was open for 9% -> 15% of each run, Pallas kernels for 0% -> 0%
where the time goes in v9:
time: 53.8 us; the launch traced here: 53.1 us
  waiting for transfers between devices  21.3 us (40%)
  other arithmetic  10.2 us (19%)
  starting transfers between devices  10.1 us (19%)
  local copies, waits for them, and re-layouts  6.96 us (13%)
  matrix products  4.39 us (8%)
    ppermute x7, waiting for transfers between devices, uv_exchange(): pieces.append(lax.ppermute(piece, 'uv', perm))  15.4 us
    ppermute x7, starting transfers between devices, uv_exchange(): pieces.append(lax.ppermute(piece, 'uv', perm))  8.5 us
    ppermute x2, waiting for transfers between devices, halving_reduce(): received = lax.ppermute(outgoing, 'tm', perm)  5.93 us
    unnamed x8, local copies, waits for them, and re-layouts  4 us
    another operation x3, other arithmetic  2.59 us
    dot_general x1, matrix products, per_device(): jnp.dot(weights, arrived[:, :row_width], preferred_element_type=jnp.float32)  2.12 us
    ppermute x2, starting transfers between devices, halving_reduce(): received = lax.ppermute(outgoing, 'tm', perm)  1.64 us
    dot_general x1, matrix products, per_device(): jnp.dot(lhs, delay_halves(), preferred_element_type=jnp.float32) * out_scale  1.51 us
  transfers between devices with their start and end apart: 9, of which 7 were waited for; matrix products, arithmetic and copies ran while one was open for 15% of the time, Pallas kernels for 0%

profile of v9, /device:TPU:12, one launch (start us, length us, event | category | flops | bytes accessed | tf_op | source)
XLA Modules:
  0.0 53.1 jit_solution(10062547235710275797)
XLA Ops:
  0.0 0.0 copy-start
  0.0 0.8 %eq.91 = s32[256]{0:T(256)S(1)} reshape(s32[1,1,8,32]{3,2,1,0:T(8,128)} %param.16) | data formatting | bytes 2048 | tf_op jit(solution)/shard_map/eq | solution.py:127
  0.8 0.7 %iota_compare_fusion.1 = pred[8,32]{1,0:T(8,128)(4,1)S(1)} fusion(s32[8]{0:T(128)} %bitcast.89), kind=kLoop, calls=%fused_computation.147 | loop fusion | flops 256 | bytes 288 | tf_op jit(solution)/shard_map/lt | solution.py:125
  1.6 0.1 lt.109
  1.6 0.7 %convert.18 = bf16[1,128]{1,0:T(2,128)(2,1)S(1)} convert(s32[1,128]{1,0:T(1,128)} %param.15) | non-fusion elementwise | flops 128 | bytes 768 | tf_op jit(solution)/shard_map/convert.4
  2.3 0.7 %convert.17 = bf16[1,128]{1,0:T(2,128)(2,1)S(1)} convert(s32[1,128]{1,0:T(1,128)} %param.14) | non-fusion elementwise | flops 128 | bytes 768 | tf_op jit(solution)/shard_map/convert.3
  3.0 0.1 pad.20.clone
  3.0 0.0 copy-done
  3.0 0.5 convolution_convert_fusion
  3.5 0.3 convolution_convert_fusion.1
  3.8 0.1 pad_maximum_fusion
  3.9 0.7 %dynamic-slice_bitcast_fusion = (bf16[32,2176]{1,0:T(8,128)(2,1)S(1)}, bf16[32,2176]{1,0:T(8,128)(2,1)S(1)}, bf16[32,2176]{1,0:T(8,128)(2,1)S(1)}, bf16[32,2176]...) fusion(bf16[8,32,2176]{2,1,0:T(8,128)(2,1)S(1)} %bitcast.68, ...), kind=kLoop, calls=%fused_computation.52 | loop fusion | bytes 2228256 | tf_op jit(solution)/shard_map/jit(dynamic_index_in_dim)/squeeze | solution.py:105
  4.7 1.5 %collective-permute-start = (bf16[32,2176]{1,0:T(8,128)(2,1)S(1)}, bf16[32,2176]{1,0:T(8,128)(2,1)S(1)}, u32[]{:S(2)}, u32[]{:S(2)}) collective-permute-start(bf16[32,2176]{1,0:T(8,128)(2,1)S(1)} %get-tuple-element.67), channel_id=1, source_target_pairs={{0,4},{4,8},{8,12},{12,16},{16,20},{20,24},{24,28},{28,0},{1,5},{5... | collective-permute-start | bytes 417800 | tf_op jit(solution)/shard_map/ppermute | solution.py:106
  6.2 1.6 %collective-permute-start.1 = (bf16[32,2176]{1,0:T(8,128)(2,1)S(1)}, bf16[32,2176]{1,0:T(8,128)(2,1)S(1)}, u32[]{:S(2)}, u32[]{:S(2)}) collective-permute-start(bf16[32,2176]{1,0:T(8,128)(2,1)S(1)} %get-tuple-element.66), channel_id=1, source_target_pairs={{0,8},{4,12},{8,16},{12,20},{16,24},{20,28},{24,0},{28,4},{1,9},{5... | collective-permute-start | bytes 417800 | tf_op jit(solution)/shard_map/ppermute | solution.py:106
  7.8 1.2 %collective-permute-start.2 = (bf16[32,2176]{1,0:T(8,128)(2,1)S(1)}, bf16[32,2176]{1,0:T(8,128)(2,1)S(1)}, u32[]{:S(2)}, u32[]{:S(2)}) collective-permute-start(bf16[32,2176]{1,0:T(8,128)(2,1)S(1)} %get-tuple-element.65), channel_id=1, source_target_pairs={{0,12},{4,16},{8,20},{12,24},{16,28},{20,0},{24,4},{28,8},{1,13},{... | collective-permute-start | bytes 417800 | tf_op jit(solution)/shard_map/ppermute | solution.py:106
  9.0 1.7 %collective-permute-start.3 = (bf16[32,2176]{1,0:T(8,128)(2,1)S(1)}, bf16[32,2176]{1,0:T(8,128)(2,1)S(1)}, u32[]{:S(2)}, u32[]{:S(2)}) collective-permute-start(bf16[32,2176]{1,0:T(8,128)(2,1)S(1)} %get-tuple-element.64), channel_id=1, source_target_pairs={{0,16},{4,20},{8,24},{12,28},{16,0},{20,4},{24,8},{28,12},{1,17},{... | collective-permute-start | bytes 417800 | tf_op jit(solution)/shard_map/ppermute | solution.py:106
  10.7 1.3 %collective-permute-start.4 = (bf16[32,2176]{1,0:T(8,128)(2,1)S(1)}, bf16[32,2176]{1,0:T(8,128)(2,1)S(1)}, u32[]{:S(2)}, u32[]{:S(2)}) collective-permute-start(bf16[32,2176]{1,0:T(8,128)(2,1)S(1)} %get-tuple-element.63), channel_id=1, source_target_pairs={{0,20},{4,24},{8,28},{12,0},{16,4},{20,8},{24,12},{28,16},{1,21},{... | collective-permute-start | bytes 417800 | tf_op jit(solution)/shard_map/ppermute | solution.py:106
  12.0 0.1 scatter.15
  12.1 0.1 scatter.16
  12.2 0.1 scatter.19
  12.3 0.1 iota_add_fusion
  12.3 0.1 add.403
  12.5 0.0 collective-permute-done
  12.5 1.2 %collective-permute-start.5 = (bf16[32,2176]{1,0:T(8,128)(2,1)S(1)}, bf16[32,2176]{1,0:T(8,128)(2,1)S(1)}, u32[]{:S(2)}, u32[]{:S(2)}) collective-permute-start(bf16[32,2176]{1,0:T(8,128)(2,1)S(1)} %get-tuple-element.62), channel_id=1, source_target_pairs={{0,24},{4,28},{8,0},{12,4},{16,8},{20,12},{24,16},{28,20},{1,25},{... | collective-permute-start | bytes 417800 | tf_op jit(solution)/shard_map/ppermute | solution.py:106
  13.7 0.7 %bitcast_dynamic-update-slice_fusion.6 = bf16[8,32,2176]{2,1,0:T(8,128)(2,1)} fusion(bf16[8,32,2176]{2,1,0:T(8,128)(2,1)} %get-tuple-element.68, bf16[32,2176]{1,0:T(8,128)(2,1)S(1)} %collective-permute-done), kind=kLoop, calls=%fused_computation.51 | loop fusion | bytes 278528
  14.4 10.8 %collective-permute-done.1 = bf16[32,2176]{1,0:T(8,128)(2,1)S(1)} collective-permute-done((bf16[32,2176]{1,0:T(8,128)(2,1)S(1)}, bf16[32,2176]{1,0:T(8,128)(2,1)S(1)}, u32[]{:S(2)}, u32[]{:S(2)}) %collective-permute-start.1) | collective-permute-done | bytes 139296 | tf_op jit(solution)/shard_map/ppermute | solution.py:106
  25.2 0.0 collective-permute-start.6
  25.2 0.7 %bitcast_dynamic-update-slice_fusion.5 = bf16[8,32,2176]{2,1,0:T(8,128)(2,1)} fusion(bf16[8,32,2176]{2,1,0:T(8,128)(2,1)} %bitcast_dynamic-update-slice_fusion.6, bf16[32,2176]{1,0:T(8,128)(2,1)S(1)} %collective-permute-done.1), kind=kLoop, calls=%fused_computation.50 | loop fusion | bytes 278528
  25.9 2.3 %collective-permute-done.2 = bf16[32,2176]{1,0:T(8,128)(2,1)S(1)} collective-permute-done((bf16[32,2176]{1,0:T(8,128)(2,1)S(1)}, bf16[32,2176]{1,0:T(8,128)(2,1)S(1)}, u32[]{:S(2)}, u32[]{:S(2)}) %collective-permute-start.2) | collective-permute-done | bytes 139296 | tf_op jit(solution)/shard_map/ppermute | solution.py:106
  28.2 0.7 %bitcast_dynamic-update-slice_fusion.4 = bf16[8,32,2176]{2,1,0:T(8,128)(2,1)} fusion(bf16[8,32,2176]{2,1,0:T(8,128)(2,1)} %bitcast_dynamic-update-slice_fusion.5, bf16[32,2176]{1,0:T(8,128)(2,1)S(1)} %collective-permute-done.2), kind=kLoop, calls=%fused_computation.49 | loop fusion | bytes 278528
  28.9 1.2 %collective-permute-done.3 = bf16[32,2176]{1,0:T(8,128)(2,1)S(1)} collective-permute-done((bf16[32,2176]{1,0:T(8,128)(2,1)S(1)}, bf16[32,2176]{1,0:T(8,128)(2,1)S(1)}, u32[]{:S(2)}, u32[]{:S(2)}) %collective-permute-start.3) | collective-permute-done | bytes 139296 | tf_op jit(solution)/shard_map/ppermute | solution.py:106
  30.0 0.7 %bitcast_dynamic-update-slice_fusion.3 = bf16[8,32,2176]{2,1,0:T(8,128)(2,1)} fusion(bf16[8,32,2176]{2,1,0:T(8,128)(2,1)} %bitcast_dynamic-update-slice_fusion.4, bf16[32,2176]{1,0:T(8,128)(2,1)S(1)} %collective-permute-done.3), kind=kLoop, calls=%fused_computation.48 | loop fusion | bytes 278528
  30.7 0.0 collective-permute-done.4
  30.7 0.7 %bitcast_dynamic-update-slice_fusion.2 = bf16[8,32,2176]{2,1,0:T(8,128)(2,1)} fusion(bf16[8,32,2176]{2,1,0:T(8,128)(2,1)} %bitcast_dynamic-update-slice_fusion.3, bf16[32,2176]{1,0:T(8,128)(2,1)S(1)} %collective-permute-done.4), kind=kLoop, calls=%fused_computation.47 | loop fusion | bytes 278528
  31.4 0.5 collective-permute-done.5
  31.8 0.7 %bitcast_dynamic-update-slice_fusion.1 = bf16[8,32,2176]{2,1,0:T(8,128)(2,1)} fusion(bf16[8,32,2176]{2,1,0:T(8,128)(2,1)} %bitcast_dynamic-update-slice_fusion.2, bf16[32,2176]{1,0:T(8,128)(2,1)S(1)} %collective-permute-done.5), kind=kLoop, calls=%fused_computation.46 | loop fusion | bytes 278528
  32.5 0.6 %collective-permute-done.6 = bf16[32,2176]{1,0:T(8,128)(2,1)S(1)} collective-permute-done((bf16[32,2176]{1,0:T(8,128)(2,1)S(1)}, bf16[32,2176]{1,0:T(8,128)(2,1)S(1)}, u32[]{:S(2)}, u32[]{:S(2)}) %collective-permute-start.6) | collective-permute-done | bytes 139296 | tf_op jit(solution)/shard_map/ppermute | solution.py:106
  33.1 0.7 %bitcast_dynamic-update-slice_fusion = bf16[8,32,2176]{2,1,0:T(8,128)(2,1)} fusion(bf16[8,32,2176]{2,1,0:T(8,128)(2,1)} %bitcast_dynamic-update-slice_fusion.1, bf16[32,2176]{1,0:T(8,128)(2,1)S(1)} %collective-permute-done.6), kind=kLoop, calls=%fused_computation.45 | loop fusion | bytes 278528 | tf_op jit(solution)/shard_map/stack | solution.py:107
  33.7 1.2 %fusion.74 = (f32[256]{0:T(256)S(1)}, f32[256]{0:T(256)S(1)}) fusion(bf16[256,2176]{1,0:T(8,128)(2,1)} %bitcast.69), kind=kLoop, calls=%fused_computation.118 | loop fusion | flops 6656 | bytes 2560 | tf_op jit(solution)/shard_map/div | solution.py:19
  34.9 1.0 %fusion.73 = (s32[256]{0:T(256)S(1)}, s32[256]{0:T(256)S(1)}) fusion(bf16[256,2176]{1,0:T(8,128)(2,1)} %bitcast.70), kind=kLoop, calls=%fused_computation.117 | loop fusion | flops 768 | bytes 2560 | tf_op jit(solution)/shard_map/jit(floor_divide)/div | solution.py:26
  35.9 1.0 %fusion.81 = pred[256]{0:T(512)(128)(4,1)S(1)} fusion(bf16[256,2176]{1,0:T(8,128)(2,1)} %bitcast.71), kind=kLoop, calls=%fused_computation.123 | loop fusion | flops 768 | bytes 768 | tf_op jit(solution)/shard_map/jit(floor_divide)/ne | solution.py:26
  36.9 0.1 fusion.99
  37.0 2.1 %fusion.9 = f32[256,2048]{1,0:T(8,128)S(1)} fusion(bf16[256,2176]{1,0:T(8,128)(2,1)} %bitcast.72, f32[256]{0:T(256)S(1)} %bitcast.87, s32[256]{0:T(256)S(1)} %get-tuple-element.108, f32[256]{0:T(256)S(1)} %bitcast.86, s32[256]{0:T(256)S(1)} %get-tuple-element.104, f32[256]{0:T(256)S(1)} %bitcast.85, s32[256]{0:T(256)S(1)} %get-tuple-element.105, ...), kind=kOutput, calls=%fused_computation.15 | convolution fusion | flops 271581184 | bytes 3180544 | tf_op jit(solution)/shard_map/dot_general | solution.py:149
  39.1 0.1 slice.168
  39.2 0.1 collective-permute-start.7
  39.3 0.1 multiply_subtract_fusion.1
  39.4 0.5 fusion.85
  39.9 0.6 %fusion.88 = (f32[1024,32]{0,1:T(8,128)S(1)}, f32[1024,32]{0,1:T(8,128)S(1)}) fusion(s32[32]{0:T(128)S(1)} %iota_multiply_fusion), kind=kLoop, calls=%fused_computation.130 | loop fusion | flops 458752 | bytes 262272 | tf_op jit(solution)/shard_map/cos | solution.py:51
  40.5 1.2 %multiply_subtract_fusion = (f32[1024,32,32]{0,2,1:T(8,128)S(1)}, f32[1024,32,32]{0,2,1:T(8,128)S(1)}) fusion(f32[1024,32]{0,1:T(8,128)S(1)} %get-tuple-element.121, f32[1024,32]{0,1:T(8,128)S(1)} %get-tuple-element.112, f32[1024,32]{0,1:T(8,128)S(1)} %get-tuple-element.122, f32[1024,32]{0,1:T(8,128)S(1)} %get-tuple-element.111), kind=kLoop, calls=%fused_computation.9 | loop fusion | flops 6291456 | bytes 8912896 | tf_op jit(solution)/shard_map/sub | solution.py:53
  41.7 0.2 collective-permute-done.7
  41.9 0.1 slice_add_fusion
  42.1 1.6 %collective-permute-start.8 = (bf16[64,2048]{1,0:T(8,128)(2,1)S(1)}, bf16[64,2048]{1,0:T(8,128)(2,1)S(1)}, u32[]{:S(2)}, u32[]{:S(2)}) collective-permute-start(bf16[64,2048]{1,0:T(8,128)(2,1)S(1)} %slice.188), channel_id=1, source_target_pairs={{0,2},{1,3},{2,0},{3,1},{4,6},{5,7},{6,4},{7,5},{8,10},{9,11},{10,... | collective-permute-start | bytes 786440 | tf_op jit(solution)/shard_map/ppermute | solution.py:93
  43.7 1.3 %fusion.5 = (bf16[1024,1024]{0,1:T(8,128)(2,1)S(1)}, bf16[1024,1024]{0,1:T(8,128)(2,1)S(1)}) fusion(f32[1024,32,32]{0,2,1:T(8,128)S(1)} %get-tuple-element.71, f32[1024]{0:T(1024)S(1)} %multiply_subtract_fusion.1, f32[1024,32,32]{0,2,1:T(8,128)S(1)} %get-tuple-element.72), kind=kLoop, calls=%fused_computation.7 | loop fusion | flops 4194304 | bytes 12587008 | tf_op jit(solution)/shard_map/convert
  44.9 5.7 %collective-permute-done.8 = bf16[64,2048]{1,0:T(8,128)(2,1)S(1)} collective-permute-done((bf16[64,2048]{1,0:T(8,128)(2,1)S(1)}, bf16[64,2048]{1,0:T(8,128)(2,1)S(1)}, u32[]{:S(2)}, u32[]{:S(2)}) %collective-permute-start.8) | collective-permute-done | bytes 262176 | tf_op jit(solution)/shard_map/ppermute | solution.py:93
  50.7 1.5 %fusion.6 = f32[128,1024]{1,0:T(8,128)S(1)} fusion(bf16[1024,1024]{0,1:T(8,128)(2,1)S(1)} %get-tuple-element.92, bf16[1024,1024]{0,1:T(8,128)(2,1)S(1)} %get-tuple-element.91, bf16[64,1024]{1,0:T(8,128)(2,1)S(1)} %get-tuple-element.74, bf16[64,1024]{1,0:T(8,128)(2,1)S(1)} %get-tuple-element.73, bf16[64,2048]{1,0:T(8,128)(2,1)S(1)} %fusion.11), kind=kOutput, calls=%fused_computation.11 | convolution fusion | flops 546963456 | bytes 5242880 | tf_op jit(solution)/shard_map/dot_general | solution.py:160
  52.3 0.8 %pad_maximum_fusion.1 = f32[64,2048]{1,0:T(8,128)} fusion(f32[64,1024]{1,0:T(8,128)S(1)} %get-tuple-element.70, f32[64,1024]{1,0:T(8,128)S(1)} %get-tuple-element.69), kind=kLoop, calls=%fused_computation.25 | loop fusion | flops 131072 | bytes 1048576 | tf_op jit(solution)/shard_map/concatenate | solution.py:162
  (13 shorter events, 0.2 us)
Async XLA Ops:
  0.0 3.0 %copy-start = (bf16[1,128,2048]{2,1,0:T(8,128)(2,1)S(1)}, bf16[1,128,2048]{2,1,0:T(8,128)(2,1)}, u32[]{:S(2)}) copy-start(bf16[1,128,2048]{2,1,0:T(8,128)(2,1)} %param.13) | copy-start | bytes 1572868
  4.7 7.8 %collective-permute-start = (bf16[32,2176]{1,0:T(8,128)(2,1)S(1)}, bf16[32,2176]{1,0:T(8,128)(2,1)S(1)}, u32[]{:S(2)}, u32[]{:S(2)}) collective-permute-start(bf16[32,2176]{1,0:T(8,128)(2,1)S(1)} %get-tuple-element.67), channel_id=1, source_target_pairs={{0,4},{4,8},{8,12},{12,16},{16,20},{20,24},{24,28},{28,0},{1,5},{5... | collective-permute-start | bytes 417800 | tf_op jit(solution)/shard_map/ppermute | solution.py:106
  6.2 19.0 %collective-permute-start.1 = (bf16[32,2176]{1,0:T(8,128)(2,1)S(1)}, bf16[32,2176]{1,0:T(8,128)(2,1)S(1)}, u32[]{:S(2)}, u32[]{:S(2)}) collective-permute-start(bf16[32,2176]{1,0:T(8,128)(2,1)S(1)} %get-tuple-element.66), channel_id=1, source_target_pairs={{0,8},{4,12},{8,16},{12,20},{16,24},{20,28},{24,0},{28,4},{1,9},{5... | collective-permute-start | bytes 417800 | tf_op jit(solution)/shard_map/ppermute | solution.py:106
  7.8 20.4 %collective-permute-start.2 = (bf16[32,2176]{1,0:T(8,128)(2,1)S(1)}, bf16[32,2176]{1,0:T(8,128)(2,1)S(1)}, u32[]{:S(2)}, u32[]{:S(2)}) collective-permute-start(bf16[32,2176]{1,0:T(8,128)(2,1)S(1)} %get-tuple-element.65), channel_id=1, source_target_pairs={{0,12},{4,16},{8,20},{12,24},{16,28},{20,0},{24,4},{28,8},{1,13},{... | collective-permute-start | bytes 417800 | tf_op jit(solution)/shard_map/ppermute | solution.py:106
  9.0 21.1 %collective-permute-start.3 = (bf16[32,2176]{1,0:T(8,128)(2,1)S(1)}, bf16[32,2176]{1,0:T(8,128)(2,1)S(1)}, u32[]{:S(2)}, u32[]{:S(2)}) collective-permute-start(bf16[32,2176]{1,0:T(8,128)(2,1)S(1)} %get-tuple-element.64), channel_id=1, source_target_pairs={{0,16},{4,20},{8,24},{12,28},{16,0},{20,4},{24,8},{28,12},{1,17},{... | collective-permute-start | bytes 417800 | tf_op jit(solution)/shard_map/ppermute | solution.py:106
  10.7 20.0 %collective-permute-start.4 = (bf16[32,2176]{1,0:T(8,128)(2,1)S(1)}, bf16[32,2176]{1,0:T(8,128)(2,1)S(1)}, u32[]{:S(2)}, u32[]{:S(2)}) collective-permute-start(bf16[32,2176]{1,0:T(8,128)(2,1)S(1)} %get-tuple-element.63), channel_id=1, source_target_pairs={{0,20},{4,24},{8,28},{12,0},{16,4},{20,8},{24,12},{28,16},{1,21},{... | collective-permute-start | bytes 417800 | tf_op jit(solution)/shard_map/ppermute | solution.py:106
  12.5 19.4 %collective-permute-start.5 = (bf16[32,2176]{1,0:T(8,128)(2,1)S(1)}, bf16[32,2176]{1,0:T(8,128)(2,1)S(1)}, u32[]{:S(2)}, u32[]{:S(2)}) collective-permute-start(bf16[32,2176]{1,0:T(8,128)(2,1)S(1)} %get-tuple-element.62), channel_id=1, source_target_pairs={{0,24},{4,28},{8,0},{12,4},{16,8},{20,12},{24,16},{28,20},{1,25},{... | collective-permute-start | bytes 417800 | tf_op jit(solution)/shard_map/ppermute | solution.py:106
  25.2 7.9 %collective-permute-start.6 = (bf16[32,2176]{1,0:T(8,128)(2,1)S(1)}, bf16[32,2176]{1,0:T(8,128)(2,1)S(1)}, u32[]{:S(2)}, u32[]{:S(2)}) collective-permute-start(bf16[32,2176]{1,0:T(8,128)(2,1)S(1)} %get-tuple-element.61), channel_id=1, source_target_pairs={{0,28},{4,0},{8,4},{12,8},{16,12},{20,16},{24,20},{28,24},{1,29},{... | collective-permute-start | bytes 417800 | tf_op jit(solution)/shard_map/ppermute | solution.py:106
  39.2 2.7 %collective-permute-start.7 = (f32[128,2048]{1,0:T(8,128)S(1)}, f32[128,2048]{1,0:T(8,128)S(1)}, u32[]{:S(2)}, u32[]{:S(2)}) collective-permute-start(f32[128,2048]{1,0:T(8,128)S(1)} %slice.168), channel_id=1, source_target_pairs={{0,1},{1,0},{2,3},{3,2},{4,5},{5,4},{6,7},{7,6},{8,9},{9,8},{10,11... | collective-permute-start | bytes 3145736 | tf_op jit(solution)/shard_map/ppermute | solution.py:93
  42.1 8.6 %collective-permute-start.8 = (bf16[64,2048]{1,0:T(8,128)(2,1)S(1)}, bf16[64,2048]{1,0:T(8,128)(2,1)S(1)}, u32[]{:S(2)}, u32[]{:S(2)}) collective-permute-start(bf16[64,2048]{1,0:T(8,128)(2,1)S(1)} %slice.188), channel_id=1, source_target_pairs={{0,2},{1,3},{2,0},{3,1},{4,6},{5,7},{6,4},{7,5},{8,10},{9,11},{10,... | collective-permute-start | bytes 786440 | tf_op jit(solution)/shard_map/ppermute | solution.py:93

commit v10 on v5

--- a/solution.py
+++ b/solution.py
@@ -111,9 +111,19 @@
     cell_share = TS * TS // time_groups
     vis_rows = visibility[0]
     row_count, row_width = vis_rows.shape
-    slot_table = slot_rows[0, 0]
-    live_count = counts[0, 0]
-    tile_count, slot_depth = slot_table.shape
+    tile_count, slot_depth = slot_rows.shape[2:]
+    slot_size = tile_count * slot_depth
+    (ints,) = lax.optimization_barrier(
+        (
+            jnp.concatenate(
+                [slot_rows.reshape(-1), counts.reshape(-1), anchor.reshape(-1), offset.reshape(-1)]
+            ),
+        )
+    )
+    slot_table = ints[:slot_size].reshape(tile_count, slot_depth)
+    live_count = ints[slot_size:slot_size + tile_count]
+    anchor_row = ints[slot_size + tile_count:slot_size + tile_count + row_count]
+    offset_row = ints[slot_size + tile_count + row_count:]
     if uv_size <= 16:
         uv_index = lax.axis_index("uv")
         slot_table = lax.dynamic_slice_in_dim(
@@ -129,7 +139,8 @@
     ).astype(jnp.bfloat16)
     picked = jnp.dot(pick, vis_rows, preferred_element_type=jnp.float32).astype(jnp.bfloat16)
     meta_rows = jnp.concatenate(
-        [anchor, offset, jnp.zeros((META - 2, row_count), jnp.int32)], axis=0
+        [anchor_row[None, :], offset_row[None, :], jnp.zeros((META - 2, row_count), jnp.int32)],
+        axis=0,
     ).astype(jnp.bfloat16)
     meta = lax.dot_general(
         pick, meta_rows, (((1,), (1,)), ((), ())), preferred_element_type=jnp.float32

time: 48.2 us -> 47.1 us (0.977)
  other arithmetic: 8.05 us -> 6.01 us
  local copies, waits for them, and re-layouts: 1.28 us -> 2.26 us
    another operation x3 -> x2, other arithmetic: 2.59 us -> 1.28 us
    reshape x0 -> x2, local copies, waits for them, and re-layouts: none -> 0.9 us  [the longest x1 0.82 us: per_device(): slot_rows.reshape(-1)]
    concatenate x0 -> x1, other arithmetic: none -> 0.76 us  [per_device(): jnp.concatenate([slot_rows.reshape(-1), counts.reshape(-1), anchor.reshap...]
    concatenate x1, other arithmetic: 0.77 us -> 0.01 us  [per_device(): jnp.concatenate([slot_table, slot_table], axis=0)]
    concatenate x1, other arithmetic: 0.8 us -> 0.07 us  [per_device(): jnp.concatenate([live_count, live_count], axis=0)]
where the time goes in v10:
time: 47.1 us; the launch traced here: 46.9 us
  waiting for transfers between devices  25.1 us (53%)
  starting transfers between devices  10.2 us (22%)
  other arithmetic  6.01 us (13%)
  matrix products  3.12 us (7%)
  local copies, waits for them, and re-layouts  2.26 us (5%)
    ppermute x7, waiting for transfers between devices, uv_exchange(): pieces.append(lax.ppermute(outgoing[shift], 'uv', perm))  19.1 us
    ppermute x7, starting transfers between devices, uv_exchange(): pieces.append(lax.ppermute(outgoing[shift], 'uv', perm))  8.61 us
    ppermute x2, waiting for transfers between devices, halving_reduce(): received = lax.ppermute(outgoing, 'tm', perm)  5.94 us
    ppermute x2, starting transfers between devices, halving_reduce(): received = lax.ppermute(outgoing, 'tm', perm)  1.64 us
    dot_general x1, matrix products, per_device(): jnp.dot(lhs, delay_halves(), preferred_element_type=jnp.float32) * out_scale  1.51 us
    another operation x2, other arithmetic  1.28 us
    sub x1, other arithmetic, delay_halves(): c_hi[:, :, None] * c_lo[:, None, :] - s_hi[:, :, None] * s_lo[:, None, :]  1.22 us
  transfers between devices with their start and end apart: 9, of which 7 were waited for; matrix products, arithmetic and copies ran while one was open for 9% of the time, Pallas kernels for 0%

profile of v10, /device:TPU:12, one launch (start us, length us, event | category | flops | bytes accessed | tf_op | source)
XLA Modules:
  0.0 46.9 jit_solution(2009340364029936701)
XLA Ops:
  0.0 0.0 copy-start
  0.0 0.8 %reshape.431 = s32[256]{0:T(256)S(1)} reshape(s32[1,1,8,32]{3,2,1,0:T(8,128)} %param.16) | data formatting | bytes 2048 | tf_op jit(solution)/shard_map/reshape | solution.py:119
  0.8 0.8 %pad_add_fusion = s32[520]{0:T(1024)S(1)} fusion(s32[128]{0:T(128)} %bitcast.87, s32[128]{0:T(128)} %bitcast.88, s32[8]{0:T(128)} %bitcast.89, s32[256]{0:T(256)S(1)} %reshape.431), kind=kLoop, calls=%fused_computation.135 | loop fusion | flops 1560 | bytes 4160 | tf_op jit(solution)/shard_map/concatenate | solution.py:118
  1.6 0.1 reshape.435
  1.7 0.1 eq.83
  1.8 0.1 pad_add_fusion.1
  1.9 0.1 dynamic_slice.7
  1.9 0.1 iota_compare_fusion.1
  2.0 0.1 lt.56
  2.1 0.1 slice_bitcast_fusion.1
  2.2 0.1 pad.20.clone
  2.3 0.0 copy-done
  2.3 0.5 %convolution_convert_fusion = bf16[256,2048]{1,0:T(8,128)(2,1)S(1)} fusion(bf16[1,128,2048]{2,1,0:T(8,128)(2,1)S(1)} %copy-done, s32[256]{0:T(256)S(1)} %eq.83, pred[256]{0:T(512)(128)(4,1)S(1)} %lt.56), kind=kOutput, calls=%fused_computation.17 | convolution fusion | flops 134807552 | bytes 1574144 | tf_op jit(solution)/shard_map/dot_general | solution.py:140
  2.8 0.3 convolution_convert_fusion.1
  3.0 0.1 pad_maximum_fusion.1
  3.1 1.6 %collective-permute-start = (bf16[32,2176]{1,0:T(8,128)(2,1)S(1)}, bf16[32,2176]{1,0:T(8,128)(2,1)S(1)}, u32[]{:S(2)}, u32[]{:S(2)}) collective-permute-start(bf16[32,2176]{1,0:T(8,128)(2,1)S(1)} %get-tuple-element.62), channel_id=1, source_target_pairs={{0,4},{4,8},{8,12},{12,16},{16,20},{20,24},{24,28},{28,0},{1,5},{5... | collective-permute-start | bytes 417800 | tf_op jit(solution)/shard_map/ppermute | solution.py:104
  4.7 1.6 %collective-permute-start.1 = (bf16[32,2176]{1,0:T(8,128)(2,1)S(1)}, bf16[32,2176]{1,0:T(8,128)(2,1)S(1)}, u32[]{:S(2)}, u32[]{:S(2)}) collective-permute-start(bf16[32,2176]{1,0:T(8,128)(2,1)S(1)} %get-tuple-element.63), channel_id=1, source_target_pairs={{0,8},{4,12},{8,16},{12,20},{16,24},{20,28},{24,0},{28,4},{1,9},{5... | collective-permute-start | bytes 417800 | tf_op jit(solution)/shard_map/ppermute | solution.py:104
  6.3 1.2 %collective-permute-start.2 = (bf16[32,2176]{1,0:T(8,128)(2,1)S(1)}, bf16[32,2176]{1,0:T(8,128)(2,1)S(1)}, u32[]{:S(2)}, u32[]{:S(2)}) collective-permute-start(bf16[32,2176]{1,0:T(8,128)(2,1)S(1)} %get-tuple-element.64), channel_id=1, source_target_pairs={{0,12},{4,16},{8,20},{12,24},{16,28},{20,0},{24,4},{28,8},{1,13},{... | collective-permute-start | bytes 417800 | tf_op jit(solution)/shard_map/ppermute | solution.py:104
  7.4 1.7 %collective-permute-start.3 = (bf16[32,2176]{1,0:T(8,128)(2,1)S(1)}, bf16[32,2176]{1,0:T(8,128)(2,1)S(1)}, u32[]{:S(2)}, u32[]{:S(2)}) collective-permute-start(bf16[32,2176]{1,0:T(8,128)(2,1)S(1)} %get-tuple-element.65), channel_id=1, source_target_pairs={{0,16},{4,20},{8,24},{12,28},{16,0},{20,4},{24,8},{28,12},{1,17},{... | collective-permute-start | bytes 417800 | tf_op jit(solution)/shard_map/ppermute | solution.py:104
  9.1 1.3 %collective-permute-start.4 = (bf16[32,2176]{1,0:T(8,128)(2,1)S(1)}, bf16[32,2176]{1,0:T(8,128)(2,1)S(1)}, u32[]{:S(2)}, u32[]{:S(2)}) collective-permute-start(bf16[32,2176]{1,0:T(8,128)(2,1)S(1)} %get-tuple-element.66), channel_id=1, source_target_pairs={{0,20},{4,24},{8,28},{12,0},{16,4},{20,8},{24,12},{28,16},{1,21},{... | collective-permute-start | bytes 417800 | tf_op jit(solution)/shard_map/ppermute | solution.py:104
  10.4 0.1 scatter.15
  10.6 0.1 scatter.16
  10.7 0.1 scatter.19
  10.8 0.1 iota_add_fusion
  10.8 0.1 add.339
  11.0 0.0 collective-permute-done
  11.0 1.3 %collective-permute-start.5 = (bf16[32,2176]{1,0:T(8,128)(2,1)S(1)}, bf16[32,2176]{1,0:T(8,128)(2,1)S(1)}, u32[]{:S(2)}, u32[]{:S(2)}) collective-permute-start(bf16[32,2176]{1,0:T(8,128)(2,1)S(1)} %get-tuple-element.67), channel_id=1, source_target_pairs={{0,24},{4,28},{8,0},{12,4},{16,8},{20,12},{24,16},{28,20},{1,25},{... | collective-permute-start | bytes 417800 | tf_op jit(solution)/shard_map/ppermute | solution.py:104
  12.3 11.4 %collective-permute-done.1 = bf16[32,2176]{1,0:T(8,128)(2,1)S(1)} collective-permute-done((bf16[32,2176]{1,0:T(8,128)(2,1)S(1)}, bf16[32,2176]{1,0:T(8,128)(2,1)S(1)}, u32[]{:S(2)}, u32[]{:S(2)}) %collective-permute-start.1) | collective-permute-done | bytes 139296 | tf_op jit(solution)/shard_map/ppermute | solution.py:104
  23.7 0.0 collective-permute-start.6
  23.7 3.0 %collective-permute-done.2 = bf16[32,2176]{1,0:T(8,128)(2,1)S(1)} collective-permute-done((bf16[32,2176]{1,0:T(8,128)(2,1)S(1)}, bf16[32,2176]{1,0:T(8,128)(2,1)S(1)}, u32[]{:S(2)}, u32[]{:S(2)}) %collective-permute-start.2) | collective-permute-done | bytes 139296 | tf_op jit(solution)/shard_map/ppermute | solution.py:104
  26.7 1.8 %collective-permute-done.3 = bf16[32,2176]{1,0:T(8,128)(2,1)S(1)} collective-permute-done((bf16[32,2176]{1,0:T(8,128)(2,1)S(1)}, bf16[32,2176]{1,0:T(8,128)(2,1)S(1)}, u32[]{:S(2)}, u32[]{:S(2)}) %collective-permute-start.3) | collective-permute-done | bytes 139296 | tf_op jit(solution)/shard_map/ppermute | solution.py:104
  28.5 0.0 collective-permute-done.4
  28.6 1.8 %collective-permute-done.5 = bf16[32,2176]{1,0:T(8,128)(2,1)S(1)} collective-permute-done((bf16[32,2176]{1,0:T(8,128)(2,1)S(1)}, bf16[32,2176]{1,0:T(8,128)(2,1)S(1)}, u32[]{:S(2)}, u32[]{:S(2)}) %collective-permute-start.5) | collective-permute-done | bytes 139296 | tf_op jit(solution)/shard_map/ppermute | solution.py:104
  30.3 1.2 %collective-permute-done.6 = bf16[32,2176]{1,0:T(8,128)(2,1)S(1)} collective-permute-done((bf16[32,2176]{1,0:T(8,128)(2,1)S(1)}, bf16[32,2176]{1,0:T(8,128)(2,1)S(1)}, u32[]{:S(2)}, u32[]{:S(2)}) %collective-permute-start.6) | collective-permute-done | bytes 139296 | tf_op jit(solution)/shard_map/ppermute | solution.py:104
  31.6 0.1 fusion.99
  31.6 0.1 copy.11
  31.8 0.1 copy.12
  31.9 0.1 fusion.89
  32.1 0.9 %fusion.9 = f32[256,2048]{1,0:T(8,128)S(1)} fusion(bf16[256,2176]{1,0:T(8,128)(2,1)S(1)} %bitcast.66, f32[256]{0:T(256)S(1)} %bitcast.85, s32[256]{0:T(256)S(1)} %get-tuple-element.111, f32[256]{0:T(256)S(1)} %bitcast.84, s32[256]{0:T(256)S(1)} %get-tuple-element.107, f32[256]{0:T(256)S(1)} %bitcast.83, s32[256]{0:T(256)S(1)} %get-tuple-element.108, ...), kind=kOutput, calls=%fused_computation.21 | convolution fusion | flops 271581184 | bytes 3180544 | tf_op jit(solution)/shard_map/dot_general | solution.py:160
  32.9 0.1 slice.243
  33.0 0.1 collective-permute-start.7
  33.1 0.1 multiply_subtract_fusion.1
  33.2 0.5 %fusion.75 = (f32[1024,32]{0,1:T(8,128)S(1)}, f32[1024,32]{0,1:T(8,128)S(1)}) fusion(), kind=kLoop, calls=%fused_computation.113 | loop fusion | flops 458752 | bytes 262144 | tf_op jit(solution)/shard_map/sin | solution.py:52
  33.7 0.6 %fusion.78 = (f32[1024,32]{0,1:T(8,128)S(1)}, f32[1024,32]{0,1:T(8,128)S(1)}) fusion(s32[32]{0:T(128)S(1)} %iota_multiply_fusion), kind=kLoop, calls=%fused_computation.116 | loop fusion | flops 458752 | bytes 262272 | tf_op jit(solution)/shard_map/cos | solution.py:51
  34.3 1.2 %multiply_subtract_fusion = (f32[1024,32,32]{0,2,1:T(8,128)S(1)}, f32[1024,32,32]{0,2,1:T(8,128)S(1)}) fusion(f32[1024,32]{0,1:T(8,128)S(1)} %get-tuple-element.124, f32[1024,32]{0,1:T(8,128)S(1)} %get-tuple-element.115, f32[1024,32]{0,1:T(8,128)S(1)} %get-tuple-element.125, f32[1024,32]{0,1:T(8,128)S(1)} %get-tuple-element.114), kind=kLoop, calls=%fused_computation.9 | loop fusion | flops 6291456 | bytes 8912896 | tf_op jit(solution)/shard_map/sub | solution.py:53
  35.5 0.2 collective-permute-done.7
  35.7 0.1 slice_add_fusion
  35.9 1.6 %collective-permute-start.8 = (bf16[64,2048]{1,0:T(8,128)(2,1)S(1)}, bf16[64,2048]{1,0:T(8,128)(2,1)S(1)}, u32[]{:S(2)}, u32[]{:S(2)}) collective-permute-start(bf16[64,2048]{1,0:T(8,128)(2,1)S(1)} %slice.306), channel_id=1, source_target_pairs={{0,2},{1,3},{2,0},{3,1},{4,6},{5,7},{6,4},{7,5},{8,10},{9,11},{10,... | collective-permute-start | bytes 786440 | tf_op jit(solution)/shard_map/ppermute | solution.py:93
  37.5 1.3 %fusion.5 = (bf16[1024,1024]{0,1:T(8,128)(2,1)S(1)}, bf16[1024,1024]{0,1:T(8,128)(2,1)S(1)}) fusion(f32[1024,32,32]{0,2,1:T(8,128)S(1)} %get-tuple-element.70, f32[1024]{0:T(1024)S(1)} %multiply_subtract_fusion.1, f32[1024,32,32]{0,2,1:T(8,128)S(1)} %get-tuple-element.71), kind=kLoop, calls=%fused_computation.7 | loop fusion | flops 4194304 | bytes 12587008 | tf_op jit(solution)/shard_map/convert
  38.7 5.7 %collective-permute-done.8 = bf16[64,2048]{1,0:T(8,128)(2,1)S(1)} collective-permute-done((bf16[64,2048]{1,0:T(8,128)(2,1)S(1)}, bf16[64,2048]{1,0:T(8,128)(2,1)S(1)}, u32[]{:S(2)}, u32[]{:S(2)}) %collective-permute-start.8) | collective-permute-done | bytes 262176 | tf_op jit(solution)/shard_map/ppermute | solution.py:93
  44.5 1.5 %fusion.6 = f32[128,1024]{1,0:T(8,128)S(1)} fusion(bf16[1024,1024]{0,1:T(8,128)(2,1)S(1)} %get-tuple-element.91, bf16[1024,1024]{0,1:T(8,128)(2,1)S(1)} %get-tuple-element.90, bf16[64,1024]{1,0:T(8,128)(2,1)S(1)} %get-tuple-element.73, bf16[64,1024]{1,0:T(8,128)(2,1)S(1)} %get-tuple-element.72, bf16[64,2048]{1,0:T(8,128)(2,1)S(1)} %fusion.11), kind=kOutput, calls=%fused_computation.18 | convolution fusion | flops 546963456 | bytes 5242880 | tf_op jit(solution)/shard_map/dot_general | solution.py:171
  46.1 0.8 %pad_maximum_fusion = f32[64,2048]{1,0:T(8,128)} fusion(f32[64,1024]{1,0:T(8,128)S(1)} %get-tuple-element.69, f32[64,1024]{1,0:T(8,128)S(1)} %get-tuple-element.68), kind=kLoop, calls=%fused_computation.31 | loop fusion | flops 131072 | bytes 1048576 | tf_op jit(solution)/shard_map/concatenate | solution.py:173
  (29 shorter events, 0.5 us)
Async XLA Ops:
  0.0 2.3 %copy-start = (bf16[1,128,2048]{2,1,0:T(8,128)(2,1)S(1)}, bf16[1,128,2048]{2,1,0:T(8,128)(2,1)}, u32[]{:S(2)}) copy-start(bf16[1,128,2048]{2,1,0:T(8,128)(2,1)} %param.13) | copy-start | bytes 1572868
  3.1 7.9 %collective-permute-start = (bf16[32,2176]{1,0:T(8,128)(2,1)S(1)}, bf16[32,2176]{1,0:T(8,128)(2,1)S(1)}, u32[]{:S(2)}, u32[]{:S(2)}) collective-permute-start(bf16[32,2176]{1,0:T(8,128)(2,1)S(1)} %get-tuple-element.62), channel_id=1, source_target_pairs={{0,4},{4,8},{8,12},{12,16},{16,20},{20,24},{24,28},{28,0},{1,5},{5... | collective-permute-start | bytes 417800 | tf_op jit(solution)/shard_map/ppermute | solution.py:104
  4.7 19.0 %collective-permute-start.1 = (bf16[32,2176]{1,0:T(8,128)(2,1)S(1)}, bf16[32,2176]{1,0:T(8,128)(2,1)S(1)}, u32[]{:S(2)}, u32[]{:S(2)}) collective-permute-start(bf16[32,2176]{1,0:T(8,128)(2,1)S(1)} %get-tuple-element.63), channel_id=1, source_target_pairs={{0,8},{4,12},{8,16},{12,20},{16,24},{20,28},{24,0},{28,4},{1,9},{5... | collective-permute-start | bytes 417800 | tf_op jit(solution)/shard_map/ppermute | solution.py:104
  6.3 20.4 %collective-permute-start.2 = (bf16[32,2176]{1,0:T(8,128)(2,1)S(1)}, bf16[32,2176]{1,0:T(8,128)(2,1)S(1)}, u32[]{:S(2)}, u32[]{:S(2)}) collective-permute-start(bf16[32,2176]{1,0:T(8,128)(2,1)S(1)} %get-tuple-element.64), channel_id=1, source_target_pairs={{0,12},{4,16},{8,20},{12,24},{16,28},{20,0},{24,4},{28,8},{1,13},{... | collective-permute-start | bytes 417800 | tf_op jit(solution)/shard_map/ppermute | solution.py:104
  7.4 21.1 %collective-permute-start.3 = (bf16[32,2176]{1,0:T(8,128)(2,1)S(1)}, bf16[32,2176]{1,0:T(8,128)(2,1)S(1)}, u32[]{:S(2)}, u32[]{:S(2)}) collective-permute-start(bf16[32,2176]{1,0:T(8,128)(2,1)S(1)} %get-tuple-element.65), channel_id=1, source_target_pairs={{0,16},{4,20},{8,24},{12,28},{16,0},{20,4},{24,8},{28,12},{1,17},{... | collective-permute-start | bytes 417800 | tf_op jit(solution)/shard_map/ppermute | solution.py:104
  9.1 19.4 %collective-permute-start.4 = (bf16[32,2176]{1,0:T(8,128)(2,1)S(1)}, bf16[32,2176]{1,0:T(8,128)(2,1)S(1)}, u32[]{:S(2)}, u32[]{:S(2)}) collective-permute-start(bf16[32,2176]{1,0:T(8,128)(2,1)S(1)} %get-tuple-element.66), channel_id=1, source_target_pairs={{0,20},{4,24},{8,28},{12,0},{16,4},{20,8},{24,12},{28,16},{1,21},{... | collective-permute-start | bytes 417800 | tf_op jit(solution)/shard_map/ppermute | solution.py:104
  11.0 19.3 %collective-permute-start.5 = (bf16[32,2176]{1,0:T(8,128)(2,1)S(1)}, bf16[32,2176]{1,0:T(8,128)(2,1)S(1)}, u32[]{:S(2)}, u32[]{:S(2)}) collective-permute-start(bf16[32,2176]{1,0:T(8,128)(2,1)S(1)} %get-tuple-element.67), channel_id=1, source_target_pairs={{0,24},{4,28},{8,0},{12,4},{16,8},{20,12},{24,16},{28,20},{1,25},{... | collective-permute-start | bytes 417800 | tf_op jit(solution)/shard_map/ppermute | solution.py:104
  23.7 7.8 %collective-permute-start.6 = (bf16[32,2176]{1,0:T(8,128)(2,1)S(1)}, bf16[32,2176]{1,0:T(8,128)(2,1)S(1)}, u32[]{:S(2)}, u32[]{:S(2)}) collective-permute-start(bf16[32,2176]{1,0:T(8,128)(2,1)S(1)} %get-tuple-element.61), channel_id=1, source_target_pairs={{0,28},{4,0},{8,4},{12,8},{16,12},{20,16},{24,20},{28,24},{1,29},{... | collective-permute-start | bytes 417800 | tf_op jit(solution)/shard_map/ppermute | solution.py:104
  33.0 2.7 %collective-permute-start.7 = (f32[128,2048]{1,0:T(8,128)S(1)}, f32[128,2048]{1,0:T(8,128)S(1)}, u32[]{:S(2)}, u32[]{:S(2)}) collective-permute-start(f32[128,2048]{1,0:T(8,128)S(1)} %slice.243), channel_id=1, source_target_pairs={{0,1},{1,0},{2,3},{3,2},{4,5},{5,4},{6,7},{7,6},{8,9},{9,8},{10,11... | collective-permute-start | bytes 3145736 | tf_op jit(solution)/shard_map/ppermute | solution.py:93
  35.9 8.6 %collective-permute-start.8 = (bf16[64,2048]{1,0:T(8,128)(2,1)S(1)}, bf16[64,2048]{1,0:T(8,128)(2,1)S(1)}, u32[]{:S(2)}, u32[]{:S(2)}) collective-permute-start(bf16[64,2048]{1,0:T(8,128)(2,1)S(1)} %slice.306), channel_id=1, source_target_pairs={{0,2},{1,3},{2,0},{3,1},{4,6},{5,7},{6,4},{7,5},{8,10},{9,11},{10,... | collective-permute-start | bytes 786440 | tf_op jit(solution)/shard_map/ppermute | solution.py:93

commit v11 on v10

--- a/solution.py
+++ b/solution.py
@@ -41,8 +41,7 @@
     return (along_y * along_x).astype(jnp.bfloat16)
 
 
-def delay_halves():
-    freq = jnp.arange(NCH, dtype=jnp.int32)
+def delay_halves(freq):
     hi = jnp.arange(NCH // SPLIT, dtype=jnp.int32)
     lo = jnp.arange(SPLIT, dtype=jnp.int32)
     scale = 2.0 * math.pi / NCH
@@ -81,9 +80,11 @@
     return cells.reshape(-1)
 
 
-def halving_reduce(partial, time_groups):
+def halving_reduce(partial, time_groups, gated=None):
     level_bits = int(math.log2(time_groups))
     for level in range(level_bits):
+        if level == 1 and gated is not None:
+            partial, gated = lax.optimization_barrier((partial, gated))
         half = partial.shape[0] // 2
         bit = 1 << level
         perm = [(i, i ^ bit) for i in range(time_groups)]
@@ -92,7 +93,7 @@
             outgoing = outgoing.astype(jnp.bfloat16)
         received = lax.ppermute(outgoing, "tm", perm)
         partial = partial[half:] + received.astype(jnp.float32)
-    return partial
+    return partial, gated
 
 
 def uv_exchange(outgoing, uv_size):
@@ -158,8 +159,11 @@
         cells = jnp.arange(TS * TS, dtype=jnp.int32)
     weights = tap_matrix(cells, arr_anchor, arr_offset)
     partial = jnp.dot(weights, arrived[:, :row_width], preferred_element_type=jnp.float32)
-    if pow2:
-        summed = halving_reduce(partial, time_groups)
+    freq = jnp.arange(NCH, dtype=jnp.int32)
+    if pow2 and time_groups > 2:
+        summed, freq = halving_reduce(partial, time_groups, freq)
+    elif pow2:
+        summed, _ = halving_reduce(partial, time_groups)
     else:
         summed = lax.psum_scatter(partial, "tm", scatter_dimension=0, tiled=True)
     grid = summed.astype(jnp.bfloat16)
@@ -168,7 +172,7 @@
         [grid, jnp.concatenate([grid_im, -grid_re], axis=1)], axis=0
     )
     out_scale = 4.0 / math.sqrt(NCH * time_groups * ROWS_DEV)
-    both = jnp.dot(lhs, delay_halves(), preferred_element_type=jnp.float32) * out_scale
+    both = jnp.dot(lhs, delay_halves(freq), preferred_element_type=jnp.float32) * out_scale
     cells_out = grid.shape[0]
     return jnp.concatenate([both[:cells_out], both[cells_out:]], axis=1)
 

time: 47.1 us -> 50 us (1.062)
  starting transfers between devices: 10.2 us -> 14.7 us
  waiting for transfers between devices: 25.1 us -> 23.5 us
    ppermute x7, starting transfers between devices: 8.61 us -> 13.1 us  [uv_exchange(): pieces.append(lax.ppermute(outgoing[shift], 'uv', perm))]
    ppermute x7, waiting for transfers between devices: 19.1 us -> 17.6 us  [uv_exchange(): pieces.append(lax.ppermute(outgoing[shift], 'uv', perm))]
    sin x1 -> x0, other arithmetic: 0.53 us -> none  [delay_halves(): c_lo, s_lo = (jnp.cos(ang_lo), jnp.sin(ang_lo))]
  transfers between devices with their start and end apart: 9 -> 9, of which waited for: 7 -> 7; matrix products, arithmetic and copies ran while one was open for 9% -> 8% of each run, Pallas kernels for 0% -> 0%
where the time goes in v11:
time: 50 us; the launch traced here: 49.8 us
  waiting for transfers between devices  23.5 us (47%)
  starting transfers between devices  14.7 us (29%)
  other arithmetic  5.97 us (12%)
  matrix products  3.12 us (6%)
  local copies, waits for them, and re-layouts  2.27 us (5%)
    ppermute x7, waiting for transfers between devices, uv_exchange(): pieces.append(lax.ppermute(outgoing[shift], 'uv', perm))  17.6 us
    ppermute x7, starting transfers between devices, uv_exchange(): pieces.append(lax.ppermute(outgoing[shift], 'uv', perm))  13.1 us
    ppermute x2, waiting for transfers between devices, halving_reduce(): received = lax.ppermute(outgoing, 'tm', perm)  5.92 us
    ppermute x2, starting transfers between devices, halving_reduce(): received = lax.ppermute(outgoing, 'tm', perm)  1.64 us
    dot_general x1, matrix products, per_device(): jnp.dot(lhs, delay_halves(freq), preferred_element_type=jnp.float32)  1.51 us
    another operation x2, other arithmetic  1.28 us
    sub x1, other arithmetic, delay_halves(): c_hi[:, :, None] * c_lo[:, None, :] - s_hi[:, :, None] * s_lo[:, None, :]  1.22 us
    cos x1, other arithmetic, delay_halves(): c_hi, s_hi = (jnp.cos(ang_hi), jnp.sin(ang_hi))  1.05 us
  transfers between devices with their start and end apart: 9, of which 7 were waited for; matrix products, arithmetic and copies ran while one was open for 8% of the time, Pallas kernels for 0%

profile of v11, /device:TPU:12, one launch (start us, length us, event | category | flops | bytes accessed | tf_op | source)
XLA Modules:
  0.0 49.8 jit_solution(5895217003826115770)
XLA Ops:
  0.0 0.0 copy-start
  0.0 0.8 %reshape.442 = s32[256]{0:T(256)S(1)} reshape(s32[1,1,8,32]{3,2,1,0:T(8,128)} %param.16) | data formatting | bytes 2048 | tf_op jit(solution)/shard_map/reshape | solution.py:120
  0.8 0.8 %pad_add_fusion = s32[520]{0:T(1024)S(1)} fusion(s32[128]{0:T(128)} %bitcast.87, s32[128]{0:T(128)} %bitcast.88, s32[8]{0:T(128)} %bitcast.89, s32[256]{0:T(256)S(1)} %reshape.442), kind=kLoop, calls=%fused_computation.133 | loop fusion | flops 1560 | bytes 4160 | tf_op jit(solution)/shard_map/concatenate | solution.py:119
  1.6 0.1 pad_add_fusion.1
  1.7 0.1 dynamic_slice.7
  1.8 0.1 iota_compare_fusion.1
  1.8 0.1 lt.52
  1.9 0.1 slice_bitcast_fusion.1
  2.0 0.1 reshape.446
  2.1 0.1 eq.83
  2.2 0.1 pad.20.clone
  2.3 0.0 copy-done
  2.3 0.5 convolution_convert_fusion
  2.8 0.3 convolution_convert_fusion.1
  3.0 0.1 pad_maximum_fusion.1
  3.1 0.6 %collective-permute-start.6 = (bf16[32,2176]{1,0:T(8,128)(2,1)S(1)}, bf16[32,2176]{1,0:T(8,128)(2,1)S(1)}, u32[]{:S(2)}, u32[]{:S(2)}) collective-permute-start(bf16[32,2176]{1,0:T(8,128)(2,1)S(1)} %get-tuple-element.65), channel_id=1, source_target_pairs={{0,28},{4,0},{8,4},{12,8},{16,12},{20,16},{24,20},{28,24},{1,29},{... | collective-permute-start | bytes 417800 | tf_op jit(solution)/shard_map/ppermute | solution.py:105
  3.7 2.4 %collective-permute-start = (bf16[32,2176]{1,0:T(8,128)(2,1)S(1)}, bf16[32,2176]{1,0:T(8,128)(2,1)S(1)}, u32[]{:S(2)}, u32[]{:S(2)}) collective-permute-start(bf16[32,2176]{1,0:T(8,128)(2,1)S(1)} %get-tuple-element.66), channel_id=1, source_target_pairs={{0,4},{4,8},{8,12},{12,16},{16,20},{20,24},{24,28},{28,0},{1,5},{5... | collective-permute-start | bytes 417800 | tf_op jit(solution)/shard_map/ppermute | solution.py:105
  6.1 1.6 %collective-permute-start.1 = (bf16[32,2176]{1,0:T(8,128)(2,1)S(1)}, bf16[32,2176]{1,0:T(8,128)(2,1)S(1)}, u32[]{:S(2)}, u32[]{:S(2)}) collective-permute-start(bf16[32,2176]{1,0:T(8,128)(2,1)S(1)} %get-tuple-element.67), channel_id=1, source_target_pairs={{0,8},{4,12},{8,16},{12,20},{16,24},{20,28},{24,0},{28,4},{1,9},{5... | collective-permute-start | bytes 417800 | tf_op jit(solution)/shard_map/ppermute | solution.py:105
  7.7 2.8 %collective-permute-start.2 = (bf16[32,2176]{1,0:T(8,128)(2,1)S(1)}, bf16[32,2176]{1,0:T(8,128)(2,1)S(1)}, u32[]{:S(2)}, u32[]{:S(2)}) collective-permute-start(bf16[32,2176]{1,0:T(8,128)(2,1)S(1)} %get-tuple-element.68), channel_id=1, source_target_pairs={{0,12},{4,16},{8,20},{12,24},{16,28},{20,0},{24,4},{28,8},{1,13},{... | collective-permute-start | bytes 417800 | tf_op jit(solution)/shard_map/ppermute | solution.py:105
  10.5 0.0 collective-permute-start.3
  10.5 0.1 scatter.15
  10.6 0.1 scatter.16
  10.7 0.1 scatter.19
  10.8 0.1 iota_add_fusion
  10.9 0.1 add.329
  11.0 0.7 %collective-permute-done = bf16[32,2176]{1,0:T(8,128)(2,1)S(1)} collective-permute-done((bf16[32,2176]{1,0:T(8,128)(2,1)S(1)}, bf16[32,2176]{1,0:T(8,128)(2,1)S(1)}, u32[]{:S(2)}, u32[]{:S(2)}) %collective-permute-start) | collective-permute-done | bytes 139296 | tf_op jit(solution)/shard_map/ppermute | solution.py:105
  11.8 5.7 %collective-permute-start.4 = (bf16[32,2176]{1,0:T(8,128)(2,1)S(1)}, bf16[32,2176]{1,0:T(8,128)(2,1)S(1)}, u32[]{:S(2)}, u32[]{:S(2)}) collective-permute-start(bf16[32,2176]{1,0:T(8,128)(2,1)S(1)} %get-tuple-element.70), channel_id=1, source_target_pairs={{0,20},{4,24},{8,28},{12,0},{16,4},{20,8},{24,12},{28,16},{1,21},{... | collective-permute-start | bytes 417800 | tf_op jit(solution)/shard_map/ppermute | solution.py:105
  17.5 7.6 %collective-permute-done.1 = bf16[32,2176]{1,0:T(8,128)(2,1)S(1)} collective-permute-done((bf16[32,2176]{1,0:T(8,128)(2,1)S(1)}, bf16[32,2176]{1,0:T(8,128)(2,1)S(1)}, u32[]{:S(2)}, u32[]{:S(2)}) %collective-permute-start.1) | collective-permute-done | bytes 139296 | tf_op jit(solution)/shard_map/ppermute | solution.py:105
  25.1 0.0 collective-permute-start.5
  25.1 3.0 %collective-permute-done.2 = bf16[32,2176]{1,0:T(8,128)(2,1)S(1)} collective-permute-done((bf16[32,2176]{1,0:T(8,128)(2,1)S(1)}, bf16[32,2176]{1,0:T(8,128)(2,1)S(1)}, u32[]{:S(2)}, u32[]{:S(2)}) %collective-permute-start.2) | collective-permute-done | bytes 139296 | tf_op jit(solution)/shard_map/ppermute | solution.py:105
  28.1 1.5 %collective-permute-done.3 = bf16[32,2176]{1,0:T(8,128)(2,1)S(1)} collective-permute-done((bf16[32,2176]{1,0:T(8,128)(2,1)S(1)}, bf16[32,2176]{1,0:T(8,128)(2,1)S(1)}, u32[]{:S(2)}, u32[]{:S(2)}) %collective-permute-start.3) | collective-permute-done | bytes 139296 | tf_op jit(solution)/shard_map/ppermute | solution.py:105
  29.7 0.0 collective-permute-done.4
  29.7 4.7 %collective-permute-done.5 = bf16[32,2176]{1,0:T(8,128)(2,1)S(1)} collective-permute-done((bf16[32,2176]{1,0:T(8,128)(2,1)S(1)}, bf16[32,2176]{1,0:T(8,128)(2,1)S(1)}, u32[]{:S(2)}, u32[]{:S(2)}) %collective-permute-start.5) | collective-permute-done | bytes 139296 | tf_op jit(solution)/shard_map/ppermute | solution.py:105
  34.5 0.0 collective-permute-done.6
  34.5 0.1 fusion.95
  34.6 0.1 copy.11
  34.8 0.1 copy.12
  34.9 0.1 fusion.85
  35.0 0.8 %fusion.9 = f32[256,2048]{1,0:T(8,128)S(1)} fusion(bf16[256,2176]{1,0:T(8,128)(2,1)S(1)} %bitcast.66, f32[256]{0:T(256)S(1)} %bitcast.85, s32[256]{0:T(256)S(1)} %get-tuple-element.119, f32[256]{0:T(256)S(1)} %bitcast.84, s32[256]{0:T(256)S(1)} %get-tuple-element.115, f32[256]{0:T(256)S(1)} %bitcast.83, s32[256]{0:T(256)S(1)} %get-tuple-element.116, ...), kind=kOutput, calls=%fused_computation.21 | convolution fusion | flops 271581184 | bytes 3180544 | tf_op jit(solution)/shard_map/dot_general | solution.py:161
  35.9 0.1 slice.243
  36.0 0.1 collective-permute-start.7
  36.1 2.6 %collective-permute-done.7 = f32[128,2048]{1,0:T(8,128)S(1)} collective-permute-done((f32[128,2048]{1,0:T(8,128)S(1)}, f32[128,2048]{1,0:T(8,128)S(1)}, u32[]{:S(2)}, u32[]{:S(2)}) %collective-permute-start.7) | collective-permute-done | bytes 1048608 | tf_op jit(solution)/shard_map/ppermute | solution.py:94
  38.7 0.1 slice_add_fusion
  38.9 0.1 multiply_subtract_fusion.1
  39.0 1.6 %collective-permute-start.8 = (bf16[64,2048]{1,0:T(8,128)(2,1)S(1)}, bf16[64,2048]{1,0:T(8,128)(2,1)S(1)}, u32[]{:S(2)}, u32[]{:S(2)}) collective-permute-start(bf16[64,2048]{1,0:T(8,128)(2,1)S(1)} %slice.303), channel_id=1, source_target_pairs={{0,2},{1,3},{2,0},{3,1},{4,6},{5,7},{6,4},{7,5},{8,10},{9,11},{10,... | collective-permute-start | bytes 786440 | tf_op jit(solution)/shard_map/ppermute | solution.py:94
  40.5 1.1 %fusion.74 = (f32[1024,32]{0,1:T(8,128)S(1)}, f32[1024,32]{0,1:T(8,128)S(1)}, f32[1024,32]{0,1:T(8,128)S(1)}, f32[1024,32]{0,1:T(8,128)S(1)}) fusion(s32[32]{0:T(128)S(1)} %iota_multiply_fusion, s32[1024]{0:T(1024)S(1)} %iota.38), kind=kLoop, calls=%fused_computation.114 | loop fusion | flops 917504 | bytes 528512 | tf_op jit(solution)/shard_map/cos | solution.py:50
  41.6 1.2 %multiply_subtract_fusion = (f32[1024,32,32]{0,2,1:T(8,128)S(1)}, f32[1024,32,32]{0,2,1:T(8,128)S(1)}) fusion(f32[1024,32]{0,1:T(8,128)S(1)} %get-tuple-element.98, f32[1024,32]{0,1:T(8,128)S(1)} %get-tuple-element.95, f32[1024,32]{0,1:T(8,128)S(1)} %get-tuple-element.99, f32[1024,32]{0,1:T(8,128)S(1)} %get-tuple-element.94), kind=kLoop, calls=%fused_computation.9 | loop fusion | flops 6291456 | bytes 8912896 | tf_op jit(solution)/shard_map/sub | solution.py:52
  42.8 1.3 %fusion.5 = (bf16[1024,1024]{0,1:T(8,128)(2,1)S(1)}, bf16[1024,1024]{0,1:T(8,128)(2,1)S(1)}) fusion(f32[1024,32,32]{0,2,1:T(8,128)S(1)} %get-tuple-element.74, f32[1024]{0:T(1024)S(1)} %multiply_subtract_fusion.1, f32[1024,32,32]{0,2,1:T(8,128)S(1)} %get-tuple-element.75), kind=kLoop, calls=%fused_computation.7 | loop fusion | flops 4194304 | bytes 12587008 | tf_op jit(solution)/shard_map/convert
  44.1 3.3 %collective-permute-done.8 = bf16[64,2048]{1,0:T(8,128)(2,1)S(1)} collective-permute-done((bf16[64,2048]{1,0:T(8,128)(2,1)S(1)}, bf16[64,2048]{1,0:T(8,128)(2,1)S(1)}, u32[]{:S(2)}, u32[]{:S(2)}) %collective-permute-start.8) | collective-permute-done | bytes 262176 | tf_op jit(solution)/shard_map/ppermute | solution.py:94
  47.5 1.5 %fusion.6 = f32[128,1024]{1,0:T(8,128)S(1)} fusion(bf16[1024,1024]{0,1:T(8,128)(2,1)S(1)} %get-tuple-element.97, bf16[1024,1024]{0,1:T(8,128)(2,1)S(1)} %get-tuple-element.96, bf16[64,1024]{1,0:T(8,128)(2,1)S(1)} %get-tuple-element.77, bf16[64,1024]{1,0:T(8,128)(2,1)S(1)} %get-tuple-element.76, bf16[64,2048]{1,0:T(8,128)(2,1)S(1)} %add_convert_fusion), kind=kOutput, calls=%fused_computation.18 | convolution fusion | flops 546963456 | bytes 5242880 | tf_op jit(solution)/shard_map/dot_general | solution.py:175
  49.0 0.8 %pad_maximum_fusion = f32[64,2048]{1,0:T(8,128)} fusion(f32[64,1024]{1,0:T(8,128)S(1)} %get-tuple-element.73, f32[64,1024]{1,0:T(8,128)S(1)} %get-tuple-element.72), kind=kLoop, calls=%fused_computation.29 | loop fusion | flops 131072 | bytes 1048576 | tf_op jit(solution)/shard_map/concatenate | solution.py:177
  (30 shorter events, 0.5 us)
Async XLA Ops:
  0.0 2.3 %copy-start = (bf16[1,128,2048]{2,1,0:T(8,128)(2,1)S(1)}, bf16[1,128,2048]{2,1,0:T(8,128)(2,1)}, u32[]{:S(2)}) copy-start(bf16[1,128,2048]{2,1,0:T(8,128)(2,1)} %param.13) | copy-start | bytes 1572868
  3.1 31.4 %collective-permute-start.6 = (bf16[32,2176]{1,0:T(8,128)(2,1)S(1)}, bf16[32,2176]{1,0:T(8,128)(2,1)S(1)}, u32[]{:S(2)}, u32[]{:S(2)}) collective-permute-start(bf16[32,2176]{1,0:T(8,128)(2,1)S(1)} %get-tuple-element.65), channel_id=1, source_target_pairs={{0,28},{4,0},{8,4},{12,8},{16,12},{20,16},{24,20},{28,24},{1,29},{... | collective-permute-start | bytes 417800 | tf_op jit(solution)/shard_map/ppermute | solution.py:105
  3.7 8.1 %collective-permute-start = (bf16[32,2176]{1,0:T(8,128)(2,1)S(1)}, bf16[32,2176]{1,0:T(8,128)(2,1)S(1)}, u32[]{:S(2)}, u32[]{:S(2)}) collective-permute-start(bf16[32,2176]{1,0:T(8,128)(2,1)S(1)} %get-tuple-element.66), channel_id=1, source_target_pairs={{0,4},{4,8},{8,12},{12,16},{16,20},{20,24},{24,28},{28,0},{1,5},{5... | collective-permute-start | bytes 417800 | tf_op jit(solution)/shard_map/ppermute | solution.py:105
  6.1 19.0 %collective-permute-start.1 = (bf16[32,2176]{1,0:T(8,128)(2,1)S(1)}, bf16[32,2176]{1,0:T(8,128)(2,1)S(1)}, u32[]{:S(2)}, u32[]{:S(2)}) collective-permute-start(bf16[32,2176]{1,0:T(8,128)(2,1)S(1)} %get-tuple-element.67), channel_id=1, source_target_pairs={{0,8},{4,12},{8,16},{12,20},{16,24},{20,28},{24,0},{28,4},{1,9},{5... | collective-permute-start | bytes 417800 | tf_op jit(solution)/shard_map/ppermute | solution.py:105
  7.7 20.4 %collective-permute-start.2 = (bf16[32,2176]{1,0:T(8,128)(2,1)S(1)}, bf16[32,2176]{1,0:T(8,128)(2,1)S(1)}, u32[]{:S(2)}, u32[]{:S(2)}) collective-permute-start(bf16[32,2176]{1,0:T(8,128)(2,1)S(1)} %get-tuple-element.68), channel_id=1, source_target_pairs={{0,12},{4,16},{8,20},{12,24},{16,28},{20,0},{24,4},{28,8},{1,13},{... | collective-permute-start | bytes 417800 | tf_op jit(solution)/shard_map/ppermute | solution.py:105
  10.5 19.2 %collective-permute-start.3 = (bf16[32,2176]{1,0:T(8,128)(2,1)S(1)}, bf16[32,2176]{1,0:T(8,128)(2,1)S(1)}, u32[]{:S(2)}, u32[]{:S(2)}) collective-permute-start(bf16[32,2176]{1,0:T(8,128)(2,1)S(1)} %get-tuple-element.69), channel_id=1, source_target_pairs={{0,16},{4,20},{8,24},{12,28},{16,0},{20,4},{24,8},{28,12},{1,17},{... | collective-permute-start | bytes 417800 | tf_op jit(solution)/shard_map/ppermute | solution.py:105
  11.8 17.9 %collective-permute-start.4 = (bf16[32,2176]{1,0:T(8,128)(2,1)S(1)}, bf16[32,2176]{1,0:T(8,128)(2,1)S(1)}, u32[]{:S(2)}, u32[]{:S(2)}) collective-permute-start(bf16[32,2176]{1,0:T(8,128)(2,1)S(1)} %get-tuple-element.70), channel_id=1, source_target_pairs={{0,20},{4,24},{8,28},{12,0},{16,4},{20,8},{24,12},{28,16},{1,21},{... | collective-permute-start | bytes 417800 | tf_op jit(solution)/shard_map/ppermute | solution.py:105
  25.1 9.3 %collective-permute-start.5 = (bf16[32,2176]{1,0:T(8,128)(2,1)S(1)}, bf16[32,2176]{1,0:T(8,128)(2,1)S(1)}, u32[]{:S(2)}, u32[]{:S(2)}) collective-permute-start(bf16[32,2176]{1,0:T(8,128)(2,1)S(1)} %get-tuple-element.71), channel_id=1, source_target_pairs={{0,24},{4,28},{8,0},{12,4},{16,8},{20,12},{24,16},{28,20},{1,25},{... | collective-permute-start | bytes 417800 | tf_op jit(solution)/shard_map/ppermute | solution.py:105
  36.0 2.7 %collective-permute-start.7 = (f32[128,2048]{1,0:T(8,128)S(1)}, f32[128,2048]{1,0:T(8,128)S(1)}, u32[]{:S(2)}, u32[]{:S(2)}) collective-permute-start(f32[128,2048]{1,0:T(8,128)S(1)} %slice.243), channel_id=1, source_target_pairs={{0,1},{1,0},{2,3},{3,2},{4,5},{5,4},{6,7},{7,6},{8,9},{9,8},{10,11... | collective-permute-start | bytes 3145736 | tf_op jit(solution)/shard_map/ppermute | solution.py:94
  39.0 8.4 %collective-permute-start.8 = (bf16[64,2048]{1,0:T(8,128)(2,1)S(1)}, bf16[64,2048]{1,0:T(8,128)(2,1)S(1)}, u32[]{:S(2)}, u32[]{:S(2)}) collective-permute-start(bf16[64,2048]{1,0:T(8,128)(2,1)S(1)} %slice.303), channel_id=1, source_target_pairs={{0,2},{1,3},{2,0},{3,1},{4,6},{5,7},{6,4},{7,5},{8,10},{9,11},{10,... | collective-permute-start | bytes 786440 | tf_op jit(solution)/shard_map/ppermute | solution.py:94

commit v12 on v10

--- a/solution.py
+++ b/solution.py
@@ -113,17 +113,19 @@
     row_count, row_width = vis_rows.shape
     tile_count, slot_depth = slot_rows.shape[2:]
     slot_size = tile_count * slot_depth
+    lanes = max(row_count, slot_depth, tile_count)
+    pad = lambda x: jnp.pad(x, ((0, 0), (0, lanes - x.shape[1])))
     (ints,) = lax.optimization_barrier(
         (
             jnp.concatenate(
-                [slot_rows.reshape(-1), counts.reshape(-1), anchor.reshape(-1), offset.reshape(-1)]
+                [pad(slot_rows[0, 0]), pad(counts[0]), pad(anchor), pad(offset)], axis=0
             ),
         )
     )
-    slot_table = ints[:slot_size].reshape(tile_count, slot_depth)
-    live_count = ints[slot_size:slot_size + tile_count]
-    anchor_row = ints[slot_size + tile_count:slot_size + tile_count + row_count]
-    offset_row = ints[slot_size + tile_count + row_count:]
+    slot_table = ints[:tile_count, :slot_depth]
+    live_count = ints[tile_count, :tile_count]
+    anchor_row = ints[tile_count + 1, :row_count]
+    offset_row = ints[tile_count + 2, :row_count]
     if uv_size <= 16:
         uv_index = lax.axis_index("uv")
         slot_table = lax.dynamic_slice_in_dim(

time: 47.1 us -> 46 us (0.977)
  local copies, waits for them, and re-layouts: 2.26 us -> 1.21 us
    reshape x2 -> x0, local copies, waits for them, and re-layouts: 0.9 us -> none  [the longest x1 0.82 us: per_device(): slot_rows.reshape(-1)]
where the time goes in v12:
time: 46 us; the launch traced here: 45.9 us
  waiting for transfers between devices  25.1 us (55%)
  starting transfers between devices  10.3 us (22%)
  other arithmetic  6.02 us (13%)
  matrix products  3.1 us (7%)
  local copies, waits for them, and re-layouts  1.21 us (3%)
    ppermute x7, waiting for transfers between devices, uv_exchange(): pieces.append(lax.ppermute(outgoing[shift], 'uv', perm))  19.1 us
    ppermute x7, starting transfers between devices, uv_exchange(): pieces.append(lax.ppermute(outgoing[shift], 'uv', perm))  8.62 us
    ppermute x2, waiting for transfers between devices, halving_reduce(): received = lax.ppermute(outgoing, 'tm', perm)  5.93 us
    ppermute x2, starting transfers between devices, halving_reduce(): received = lax.ppermute(outgoing, 'tm', perm)  1.64 us
    dot_general x1, matrix products, per_device(): jnp.dot(lhs, delay_halves(), preferred_element_type=jnp.float32) * out_scale  1.51 us
    another operation x2, other arithmetic  1.28 us
    sub x1, other arithmetic, delay_halves(): c_hi[:, :, None] * c_lo[:, None, :] - s_hi[:, :, None] * s_lo[:, None, :]  1.22 us
  transfers between devices with their start and end apart: 9, of which 7 were waited for; matrix products, arithmetic and copies ran while one was open for 9% of the time, Pallas kernels for 0%

profile of v12, /device:TPU:12, one launch (start us, length us, event | category | flops | bytes accessed | tf_op | source)
XLA Modules:
  0.0 45.9 jit_solution(6903247656439143047)
XLA Ops:
  0.0 0.0 copy-start
  0.0 0.8 %fusion.89 = s32[11,128]{1,0:T(8,128)S(1)} fusion(s32[1,8]{1,0:T(1,128)} %bitcast.83, s32[8,32]{1,0:T(8,128)} %bitcast.62, s32[1,128]{1,0:T(1,128)} %param.15, s32[1,128]{1,0:T(1,128)} %param.14), kind=kLoop, calls=%fused_computation.130 | loop fusion | flops 4224 | bytes 7712 | tf_op jit(solution)/shard_map/concatenate | solution.py:120
  0.8 0.1 eq.83
  0.9 0.1 pad_add_fusion.1
  1.0 0.1 dynamic_slice.7
  1.1 0.1 iota_compare_fusion.1
  1.1 0.1 lt.56
  1.2 0.3 convolution_convert_fusion.1
  1.5 0.0 copy-done
  1.5 0.5 %convolution_convert_fusion = bf16[256,2048]{1,0:T(8,128)(2,1)S(1)} fusion(bf16[1,128,2048]{2,1,0:T(8,128)(2,1)S(1)} %copy-done, s32[256]{0:T(256)S(1)} %eq.83, pred[256]{0:T(512)(128)(4,1)S(1)} %lt.56), kind=kOutput, calls=%fused_computation.17 | convolution fusion | flops 134807552 | bytes 1574144 | tf_op jit(solution)/shard_map/dot_general | solution.py:142
  2.0 0.1 pad_maximum_fusion.1
  2.1 1.6 %collective-permute-start = (bf16[32,2176]{1,0:T(8,128)(2,1)S(1)}, bf16[32,2176]{1,0:T(8,128)(2,1)S(1)}, u32[]{:S(2)}, u32[]{:S(2)}) collective-permute-start(bf16[32,2176]{1,0:T(8,128)(2,1)S(1)} %get-tuple-element.62), channel_id=1, source_target_pairs={{0,4},{4,8},{8,12},{12,16},{16,20},{20,24},{24,28},{28,0},{1,5},{5... | collective-permute-start | bytes 417800 | tf_op jit(solution)/shard_map/ppermute | solution.py:104
  3.6 1.6 %collective-permute-start.1 = (bf16[32,2176]{1,0:T(8,128)(2,1)S(1)}, bf16[32,2176]{1,0:T(8,128)(2,1)S(1)}, u32[]{:S(2)}, u32[]{:S(2)}) collective-permute-start(bf16[32,2176]{1,0:T(8,128)(2,1)S(1)} %get-tuple-element.63), channel_id=1, source_target_pairs={{0,8},{4,12},{8,16},{12,20},{16,24},{20,28},{24,0},{28,4},{1,9},{5... | collective-permute-start | bytes 417800 | tf_op jit(solution)/shard_map/ppermute | solution.py:104
  5.2 1.2 %collective-permute-start.2 = (bf16[32,2176]{1,0:T(8,128)(2,1)S(1)}, bf16[32,2176]{1,0:T(8,128)(2,1)S(1)}, u32[]{:S(2)}, u32[]{:S(2)}) collective-permute-start(bf16[32,2176]{1,0:T(8,128)(2,1)S(1)} %get-tuple-element.64), channel_id=1, source_target_pairs={{0,12},{4,16},{8,20},{12,24},{16,28},{20,0},{24,4},{28,8},{1,13},{... | collective-permute-start | bytes 417800 | tf_op jit(solution)/shard_map/ppermute | solution.py:104
  6.4 1.7 %collective-permute-start.3 = (bf16[32,2176]{1,0:T(8,128)(2,1)S(1)}, bf16[32,2176]{1,0:T(8,128)(2,1)S(1)}, u32[]{:S(2)}, u32[]{:S(2)}) collective-permute-start(bf16[32,2176]{1,0:T(8,128)(2,1)S(1)} %get-tuple-element.65), channel_id=1, source_target_pairs={{0,16},{4,20},{8,24},{12,28},{16,0},{20,4},{24,8},{28,12},{1,17},{... | collective-permute-start | bytes 417800 | tf_op jit(solution)/shard_map/ppermute | solution.py:104
  8.1 1.3 %collective-permute-start.4 = (bf16[32,2176]{1,0:T(8,128)(2,1)S(1)}, bf16[32,2176]{1,0:T(8,128)(2,1)S(1)}, u32[]{:S(2)}, u32[]{:S(2)}) collective-permute-start(bf16[32,2176]{1,0:T(8,128)(2,1)S(1)} %get-tuple-element.66), channel_id=1, source_target_pairs={{0,20},{4,24},{8,28},{12,0},{16,4},{20,8},{24,12},{28,16},{1,21},{... | collective-permute-start | bytes 417800 | tf_op jit(solution)/shard_map/ppermute | solution.py:104
  9.4 0.1 scatter.15
  9.5 0.1 scatter.16
  9.6 0.1 scatter.19
  9.7 0.1 iota_add_fusion
  9.8 0.1 add.345
  9.9 0.0 collective-permute-done
  9.9 1.3 %collective-permute-start.5 = (bf16[32,2176]{1,0:T(8,128)(2,1)S(1)}, bf16[32,2176]{1,0:T(8,128)(2,1)S(1)}, u32[]{:S(2)}, u32[]{:S(2)}) collective-permute-start(bf16[32,2176]{1,0:T(8,128)(2,1)S(1)} %get-tuple-element.67), channel_id=1, source_target_pairs={{0,24},{4,28},{8,0},{12,4},{16,8},{20,12},{24,16},{28,20},{1,25},{... | collective-permute-start | bytes 417800 | tf_op jit(solution)/shard_map/ppermute | solution.py:104
  11.2 11.4 %collective-permute-done.1 = bf16[32,2176]{1,0:T(8,128)(2,1)S(1)} collective-permute-done((bf16[32,2176]{1,0:T(8,128)(2,1)S(1)}, bf16[32,2176]{1,0:T(8,128)(2,1)S(1)}, u32[]{:S(2)}, u32[]{:S(2)}) %collective-permute-start.1) | collective-permute-done | bytes 139296 | tf_op jit(solution)/shard_map/ppermute | solution.py:104
  22.6 0.0 collective-permute-start.6
  22.6 3.0 %collective-permute-done.2 = bf16[32,2176]{1,0:T(8,128)(2,1)S(1)} collective-permute-done((bf16[32,2176]{1,0:T(8,128)(2,1)S(1)}, bf16[32,2176]{1,0:T(8,128)(2,1)S(1)}, u32[]{:S(2)}, u32[]{:S(2)}) %collective-permute-start.2) | collective-permute-done | bytes 139296 | tf_op jit(solution)/shard_map/ppermute | solution.py:104
  25.6 1.8 %collective-permute-done.3 = bf16[32,2176]{1,0:T(8,128)(2,1)S(1)} collective-permute-done((bf16[32,2176]{1,0:T(8,128)(2,1)S(1)}, bf16[32,2176]{1,0:T(8,128)(2,1)S(1)}, u32[]{:S(2)}, u32[]{:S(2)}) %collective-permute-start.3) | collective-permute-done | bytes 139296 | tf_op jit(solution)/shard_map/ppermute | solution.py:104
  27.5 0.0 collective-permute-done.4
  27.5 1.8 %collective-permute-done.5 = bf16[32,2176]{1,0:T(8,128)(2,1)S(1)} collective-permute-done((bf16[32,2176]{1,0:T(8,128)(2,1)S(1)}, bf16[32,2176]{1,0:T(8,128)(2,1)S(1)}, u32[]{:S(2)}, u32[]{:S(2)}) %collective-permute-start.5) | collective-permute-done | bytes 139296 | tf_op jit(solution)/shard_map/ppermute | solution.py:104
  29.3 1.2 %collective-permute-done.6 = bf16[32,2176]{1,0:T(8,128)(2,1)S(1)} collective-permute-done((bf16[32,2176]{1,0:T(8,128)(2,1)S(1)}, bf16[32,2176]{1,0:T(8,128)(2,1)S(1)}, u32[]{:S(2)}, u32[]{:S(2)}) %collective-permute-start.6) | collective-permute-done | bytes 139296 | tf_op jit(solution)/shard_map/ppermute | solution.py:104
  30.5 0.1 fusion.97
  30.6 0.1 copy.11
  30.7 0.1 copy.12
  30.9 0.1 fusion.85
  31.0 0.8 %fusion.9 = f32[256,2048]{1,0:T(8,128)S(1)} fusion(bf16[256,2176]{1,0:T(8,128)(2,1)S(1)} %bitcast.61, f32[256]{0:T(256)S(1)} %bitcast.81, s32[256]{0:T(256)S(1)} %get-tuple-element.109, f32[256]{0:T(256)S(1)} %bitcast.80, s32[256]{0:T(256)S(1)} %get-tuple-element.105, f32[256]{0:T(256)S(1)} %bitcast.79, s32[256]{0:T(256)S(1)} %get-tuple-element.106, ...), kind=kOutput, calls=%fused_computation.21 | convolution fusion | flops 271581184 | bytes 3180544 | tf_op jit(solution)/shard_map/dot_general | solution.py:162
  31.9 0.1 slice.243
  32.0 0.1 collective-permute-start.7
  32.1 0.1 multiply_subtract_fusion.1
  32.1 0.5 %fusion.75 = (f32[1024,32]{0,1:T(8,128)S(1)}, f32[1024,32]{0,1:T(8,128)S(1)}) fusion(), kind=kLoop, calls=%fused_computation.113 | loop fusion | flops 458752 | bytes 262144 | tf_op jit(solution)/shard_map/sin | solution.py:52
  32.7 0.6 %fusion.78 = (f32[1024,32]{0,1:T(8,128)S(1)}, f32[1024,32]{0,1:T(8,128)S(1)}) fusion(s32[32]{0:T(128)S(1)} %iota_multiply_fusion), kind=kLoop, calls=%fused_computation.116 | loop fusion | flops 458752 | bytes 262272 | tf_op jit(solution)/shard_map/cos | solution.py:51
  33.2 1.2 %multiply_subtract_fusion = (f32[1024,32,32]{0,2,1:T(8,128)S(1)}, f32[1024,32,32]{0,2,1:T(8,128)S(1)}) fusion(f32[1024,32]{0,1:T(8,128)S(1)} %get-tuple-element.122, f32[1024,32]{0,1:T(8,128)S(1)} %get-tuple-element.113, f32[1024,32]{0,1:T(8,128)S(1)} %get-tuple-element.123, f32[1024,32]{0,1:T(8,128)S(1)} %get-tuple-element.112), kind=kLoop, calls=%fused_computation.9 | loop fusion | flops 6291456 | bytes 8912896 | tf_op jit(solution)/shard_map/sub | solution.py:53
  34.5 0.2 collective-permute-done.7
  34.7 0.1 slice_add_fusion
  34.9 1.6 %collective-permute-start.8 = (bf16[64,2048]{1,0:T(8,128)(2,1)S(1)}, bf16[64,2048]{1,0:T(8,128)(2,1)S(1)}, u32[]{:S(2)}, u32[]{:S(2)}) collective-permute-start(bf16[64,2048]{1,0:T(8,128)(2,1)S(1)} %slice.306), channel_id=1, source_target_pairs={{0,2},{1,3},{2,0},{3,1},{4,6},{5,7},{6,4},{7,5},{8,10},{9,11},{10,... | collective-permute-start | bytes 786440 | tf_op jit(solution)/shard_map/ppermute | solution.py:93
  36.4 1.3 %fusion.5 = (bf16[1024,1024]{0,1:T(8,128)(2,1)S(1)}, bf16[1024,1024]{0,1:T(8,128)(2,1)S(1)}) fusion(f32[1024,32,32]{0,2,1:T(8,128)S(1)} %get-tuple-element.70, f32[1024]{0:T(1024)S(1)} %multiply_subtract_fusion.1, f32[1024,32,32]{0,2,1:T(8,128)S(1)} %get-tuple-element.71), kind=kLoop, calls=%fused_computation.7 | loop fusion | flops 4194304 | bytes 12587008 | tf_op jit(solution)/shard_map/convert
  37.7 5.7 %collective-permute-done.8 = bf16[64,2048]{1,0:T(8,128)(2,1)S(1)} collective-permute-done((bf16[64,2048]{1,0:T(8,128)(2,1)S(1)}, bf16[64,2048]{1,0:T(8,128)(2,1)S(1)}, u32[]{:S(2)}, u32[]{:S(2)}) %collective-permute-start.8) | collective-permute-done | bytes 262176 | tf_op jit(solution)/shard_map/ppermute | solution.py:93
  43.5 1.5 %fusion.6 = f32[128,1024]{1,0:T(8,128)S(1)} fusion(bf16[1024,1024]{0,1:T(8,128)(2,1)S(1)} %get-tuple-element.91, bf16[1024,1024]{0,1:T(8,128)(2,1)S(1)} %get-tuple-element.90, bf16[64,1024]{1,0:T(8,128)(2,1)S(1)} %get-tuple-element.73, bf16[64,1024]{1,0:T(8,128)(2,1)S(1)} %get-tuple-element.72, bf16[64,2048]{1,0:T(8,128)(2,1)S(1)} %fusion.11), kind=kOutput, calls=%fused_computation.18 | convolution fusion | flops 546963456 | bytes 5242880 | tf_op jit(solution)/shard_map/dot_general | solution.py:173
  45.1 0.8 %pad_maximum_fusion = f32[64,2048]{1,0:T(8,128)} fusion(f32[64,1024]{1,0:T(8,128)S(1)} %get-tuple-element.69, f32[64,1024]{1,0:T(8,128)S(1)} %get-tuple-element.68), kind=kLoop, calls=%fused_computation.31 | loop fusion | flops 131072 | bytes 1048576 | tf_op jit(solution)/shard_map/concatenate | solution.py:175
  (28 shorter events, 0.5 us)
Async XLA Ops:
  0.0 1.5 %copy-start = (bf16[1,128,2048]{2,1,0:T(8,128)(2,1)S(1)}, bf16[1,128,2048]{2,1,0:T(8,128)(2,1)}, u32[]{:S(2)}) copy-start(bf16[1,128,2048]{2,1,0:T(8,128)(2,1)} %param.13) | copy-start | bytes 1572868
  2.1 7.9 %collective-permute-start = (bf16[32,2176]{1,0:T(8,128)(2,1)S(1)}, bf16[32,2176]{1,0:T(8,128)(2,1)S(1)}, u32[]{:S(2)}, u32[]{:S(2)}) collective-permute-start(bf16[32,2176]{1,0:T(8,128)(2,1)S(1)} %get-tuple-element.62), channel_id=1, source_target_pairs={{0,4},{4,8},{8,12},{12,16},{16,20},{20,24},{24,28},{28,0},{1,5},{5... | collective-permute-start | bytes 417800 | tf_op jit(solution)/shard_map/ppermute | solution.py:104
  3.6 19.0 %collective-permute-start.1 = (bf16[32,2176]{1,0:T(8,128)(2,1)S(1)}, bf16[32,2176]{1,0:T(8,128)(2,1)S(1)}, u32[]{:S(2)}, u32[]{:S(2)}) collective-permute-start(bf16[32,2176]{1,0:T(8,128)(2,1)S(1)} %get-tuple-element.63), channel_id=1, source_target_pairs={{0,8},{4,12},{8,16},{12,20},{16,24},{20,28},{24,0},{28,4},{1,9},{5... | collective-permute-start | bytes 417800 | tf_op jit(solution)/shard_map/ppermute | solution.py:104
  5.2 20.4 %collective-permute-start.2 = (bf16[32,2176]{1,0:T(8,128)(2,1)S(1)}, bf16[32,2176]{1,0:T(8,128)(2,1)S(1)}, u32[]{:S(2)}, u32[]{:S(2)}) collective-permute-start(bf16[32,2176]{1,0:T(8,128)(2,1)S(1)} %get-tuple-element.64), channel_id=1, source_target_pairs={{0,12},{4,16},{8,20},{12,24},{16,28},{20,0},{24,4},{28,8},{1,13},{... | collective-permute-start | bytes 417800 | tf_op jit(solution)/shard_map/ppermute | solution.py:104
  6.4 21.1 %collective-permute-start.3 = (bf16[32,2176]{1,0:T(8,128)(2,1)S(1)}, bf16[32,2176]{1,0:T(8,128)(2,1)S(1)}, u32[]{:S(2)}, u32[]{:S(2)}) collective-permute-start(bf16[32,2176]{1,0:T(8,128)(2,1)S(1)} %get-tuple-element.65), channel_id=1, source_target_pairs={{0,16},{4,20},{8,24},{12,28},{16,0},{20,4},{24,8},{28,12},{1,17},{... | collective-permute-start | bytes 417800 | tf_op jit(solution)/shard_map/ppermute | solution.py:104
  8.1 19.4 %collective-permute-start.4 = (bf16[32,2176]{1,0:T(8,128)(2,1)S(1)}, bf16[32,2176]{1,0:T(8,128)(2,1)S(1)}, u32[]{:S(2)}, u32[]{:S(2)}) collective-permute-start(bf16[32,2176]{1,0:T(8,128)(2,1)S(1)} %get-tuple-element.66), channel_id=1, source_target_pairs={{0,20},{4,24},{8,28},{12,0},{16,4},{20,8},{24,12},{28,16},{1,21},{... | collective-permute-start | bytes 417800 | tf_op jit(solution)/shard_map/ppermute | solution.py:104
  9.9 19.3 %collective-permute-start.5 = (bf16[32,2176]{1,0:T(8,128)(2,1)S(1)}, bf16[32,2176]{1,0:T(8,128)(2,1)S(1)}, u32[]{:S(2)}, u32[]{:S(2)}) collective-permute-start(bf16[32,2176]{1,0:T(8,128)(2,1)S(1)} %get-tuple-element.67), channel_id=1, source_target_pairs={{0,24},{4,28},{8,0},{12,4},{16,8},{20,12},{24,16},{28,20},{1,25},{... | collective-permute-start | bytes 417800 | tf_op jit(solution)/shard_map/ppermute | solution.py:104
  22.6 7.9 %collective-permute-start.6 = (bf16[32,2176]{1,0:T(8,128)(2,1)S(1)}, bf16[32,2176]{1,0:T(8,128)(2,1)S(1)}, u32[]{:S(2)}, u32[]{:S(2)}) collective-permute-start(bf16[32,2176]{1,0:T(8,128)(2,1)S(1)} %get-tuple-element.61), channel_id=1, source_target_pairs={{0,28},{4,0},{8,4},{12,8},{16,12},{20,16},{24,20},{28,24},{1,29},{... | collective-permute-start | bytes 417800 | tf_op jit(solution)/shard_map/ppermute | solution.py:104
  32.0 2.7 %collective-permute-start.7 = (f32[128,2048]{1,0:T(8,128)S(1)}, f32[128,2048]{1,0:T(8,128)S(1)}, u32[]{:S(2)}, u32[]{:S(2)}) collective-permute-start(f32[128,2048]{1,0:T(8,128)S(1)} %slice.243), channel_id=1, source_target_pairs={{0,1},{1,0},{2,3},{3,2},{4,5},{5,4},{6,7},{7,6},{8,9},{9,8},{10,11... | collective-permute-start | bytes 3145736 | tf_op jit(solution)/shard_map/ppermute | solution.py:93
  34.9 8.6 %collective-permute-start.8 = (bf16[64,2048]{1,0:T(8,128)(2,1)S(1)}, bf16[64,2048]{1,0:T(8,128)(2,1)S(1)}, u32[]{:S(2)}, u32[]{:S(2)}) collective-permute-start(bf16[64,2048]{1,0:T(8,128)(2,1)S(1)} %slice.306), channel_id=1, source_target_pairs={{0,2},{1,3},{2,0},{3,1},{4,6},{5,7},{6,4},{7,5},{8,10},{9,11},{10,... | collective-permute-start | bytes 786440 | tf_op jit(solution)/shard_map/ppermute | solution.py:93

commit v13 on v12

--- a/solution.py
+++ b/solution.py
@@ -96,13 +96,24 @@
 
 
 def uv_exchange(outgoing, uv_size):
-    if uv_size > 16:
+    if uv_size > 16 or uv_size & (uv_size - 1):
         return lax.all_to_all(outgoing, "uv", split_axis=0, concat_axis=0, tiled=True)
     pieces = [outgoing[0]]
-    for shift in range(1, uv_size):
-        perm = [(i, (i + shift) % uv_size) for i in range(uv_size)]
-        pieces.append(lax.ppermute(outgoing[shift], "uv", perm))
+    for mask in range(1, uv_size):
+        perm = [(i, i ^ mask) for i in range(uv_size)]
+        pieces.append(lax.ppermute(outgoing[mask], "uv", perm))
     return jnp.stack(pieces)
+
+
+def xor_rows(table, index):
+    rows = table.shape[0]
+    bit = 1
+    while bit < rows:
+        split = table.reshape((rows // (2 * bit), 2, bit) + table.shape[1:])
+        flipped = split[:, ::-1]
+        table = jnp.where((index & bit) > 0, flipped, split).reshape(table.shape)
+        bit *= 2
+    return table
 
 
 def per_device(visibility, anchor, offset, slot_rows, counts):
@@ -126,14 +137,10 @@
     live_count = ints[tile_count, :tile_count]
     anchor_row = ints[tile_count + 1, :row_count]
     offset_row = ints[tile_count + 2, :row_count]
-    if uv_size <= 16:
+    if uv_size <= 16 and uv_size & (uv_size - 1) == 0:
         uv_index = lax.axis_index("uv")
-        slot_table = lax.dynamic_slice_in_dim(
-            jnp.concatenate([slot_table, slot_table], axis=0), uv_index, tile_count, 0
-        )
-        live_count = lax.dynamic_slice_in_dim(
-            jnp.concatenate([live_count, live_count], axis=0), uv_index, tile_count, 0
-        )
+        slot_table = xor_rows(slot_table, uv_index)
+        live_count = xor_rows(live_count, uv_index)
     is_live = (jnp.arange(slot_depth, dtype=jnp.int32)[None, :] < live_count[:, None]).reshape(-1)
     flat_index = slot_table.reshape(-1)
     pick = (

time: 46 us -> 49.2 us (1.070)
  the two profiles are of different devices: /device:TPU:12 before, /device:TPU:16 now
where the time goes in v13:
time: 49.2 us; the launch traced here: 49.1 us
  waiting for transfers between devices  28.3 us (58%)
  starting transfers between devices  9.58 us (19%)
  other arithmetic  5.97 us (12%)
  matrix products  3.11 us (6%)
  local copies, waits for them, and re-layouts  1.85 us (4%)
    ppermute x7, waiting for transfers between devices, uv_exchange(): pieces.append(lax.ppermute(outgoing[mask], 'uv', perm))  22.4 us
    ppermute x7, starting transfers between devices, uv_exchange(): pieces.append(lax.ppermute(outgoing[mask], 'uv', perm))  7.95 us
    ppermute x2, waiting for transfers between devices, halving_reduce(): received = lax.ppermute(outgoing, 'tm', perm)  5.94 us
    ppermute x2, starting transfers between devices, halving_reduce(): received = lax.ppermute(outgoing, 'tm', perm)  1.63 us
    dot_general x1, matrix products, per_device(): jnp.dot(lhs, delay_halves(), preferred_element_type=jnp.float32) * out_scale  1.51 us
    another operation x2, other arithmetic  1.28 us
    sub x1, other arithmetic, delay_halves(): c_hi[:, :, None] * c_lo[:, None, :] - s_hi[:, :, None] * s_lo[:, None, :]  1.22 us
  transfers between devices with their start and end apart: 9, of which 8 were waited for; matrix products, arithmetic and copies ran while one was open for 9% of the time, Pallas kernels for 0%

profile of v13, /device:TPU:16, one launch (start us, length us, event | category | flops | bytes accessed | tf_op | source)
XLA Modules:
  0.0 49.1 jit_solution(4673174673946891408)
XLA Ops:
  0.0 0.0 copy-start
  0.0 0.8 %fusion.89 = s32[11,128]{1,0:T(8,128)S(1)} fusion(s32[1,8]{1,0:T(1,128)} %bitcast.94, s32[8,32]{1,0:T(8,128)} %bitcast.73, s32[1,128]{1,0:T(1,128)} %param.15, s32[1,128]{1,0:T(1,128)} %param.14), kind=kLoop, calls=%fused_computation.130 | loop fusion | flops 4224 | bytes 7712 | tf_op jit(solution)/shard_map/concatenate | solution.py:131
  0.9 0.1 eq.83
  1.0 0.1 reshape_squeeze.3
  1.0 0.1 rev.21
  1.1 0.1 copy.15
  1.3 0.1 rev.22
  1.4 0.1 copy.10
  1.5 0.1 reshape_reshape.15
  1.6 0.1 lt.51
  1.7 0.1 iota_compare_fusion.1
  1.7 0.1 lt.54
  1.8 0.3 convolution_convert_fusion.1
  2.1 0.0 copy-done
  2.1 0.5 %convolution_convert_fusion = bf16[256,2048]{1,0:T(8,128)(2,1)S(1)} fusion(bf16[1,128,2048]{2,1,0:T(8,128)(2,1)S(1)} %copy-done, s32[256]{0:T(256)S(1)} %eq.83, pred[256]{0:T(512)(128)(4,1)S(1)} %lt.54), kind=kOutput, calls=%fused_computation.17 | convolution fusion | flops 134807552 | bytes 1574144 | tf_op jit(solution)/shard_map/dot_general | solution.py:149
  2.6 0.1 pad_maximum_fusion.1
  2.7 1.6 %collective-permute-start = (bf16[32,2176]{1,0:T(8,128)(2,1)S(1)}, bf16[32,2176]{1,0:T(8,128)(2,1)S(1)}, u32[]{:S(2)}, u32[]{:S(2)}) collective-permute-start(bf16[32,2176]{1,0:T(8,128)(2,1)S(1)} %get-tuple-element.62), channel_id=1, source_target_pairs={{0,4},{4,0},{8,12},{12,8},{16,20},{20,16},{24,28},{28,24},{1,5},{5... | collective-permute-start | bytes 417800 | tf_op jit(solution)/shard_map/ppermute | solution.py:104
  4.3 1.6 %collective-permute-start.1 = (bf16[32,2176]{1,0:T(8,128)(2,1)S(1)}, bf16[32,2176]{1,0:T(8,128)(2,1)S(1)}, u32[]{:S(2)}, u32[]{:S(2)}) collective-permute-start(bf16[32,2176]{1,0:T(8,128)(2,1)S(1)} %get-tuple-element.63), channel_id=1, source_target_pairs={{0,8},{4,12},{8,0},{12,4},{16,24},{20,28},{24,16},{28,20},{1,9},{5... | collective-permute-start | bytes 417800 | tf_op jit(solution)/shard_map/ppermute | solution.py:104
  5.8 0.4 collective-permute-start.2
  6.2 0.0 collective-permute-start.3
  6.2 3.9 %collective-permute-start.4 = (bf16[32,2176]{1,0:T(8,128)(2,1)S(1)}, bf16[32,2176]{1,0:T(8,128)(2,1)S(1)}, u32[]{:S(2)}, u32[]{:S(2)}) collective-permute-start(bf16[32,2176]{1,0:T(8,128)(2,1)S(1)} %get-tuple-element.66), channel_id=1, source_target_pairs={{0,20},{4,16},{8,28},{12,24},{16,4},{20,0},{24,12},{28,8},{1,21},{... | collective-permute-start | bytes 417800 | tf_op jit(solution)/shard_map/ppermute | solution.py:104
  10.1 0.1 scatter.15
  10.3 0.1 scatter.16
  10.4 0.1 scatter.19
  10.5 0.1 iota_add_fusion
  10.5 0.1 add.341
  10.7 0.0 collective-permute-done
  10.7 0.5 %collective-permute-start.5 = (bf16[32,2176]{1,0:T(8,128)(2,1)S(1)}, bf16[32,2176]{1,0:T(8,128)(2,1)S(1)}, u32[]{:S(2)}, u32[]{:S(2)}) collective-permute-start(bf16[32,2176]{1,0:T(8,128)(2,1)S(1)} %get-tuple-element.67), channel_id=1, source_target_pairs={{0,24},{4,28},{8,16},{12,20},{16,8},{20,12},{24,0},{28,4},{1,25},{... | collective-permute-start | bytes 417800 | tf_op jit(solution)/shard_map/ppermute | solution.py:104
  11.2 2.1 %collective-permute-done.1 = bf16[32,2176]{1,0:T(8,128)(2,1)S(1)} collective-permute-done((bf16[32,2176]{1,0:T(8,128)(2,1)S(1)}, bf16[32,2176]{1,0:T(8,128)(2,1)S(1)}, u32[]{:S(2)}, u32[]{:S(2)}) %collective-permute-start.1) | collective-permute-done | bytes 139296 | tf_op jit(solution)/shard_map/ppermute | solution.py:104
  13.3 0.0 collective-permute-start.6
  13.3 1.6 %collective-permute-done.2 = bf16[32,2176]{1,0:T(8,128)(2,1)S(1)} collective-permute-done((bf16[32,2176]{1,0:T(8,128)(2,1)S(1)}, bf16[32,2176]{1,0:T(8,128)(2,1)S(1)}, u32[]{:S(2)}, u32[]{:S(2)}) %collective-permute-start.2) | collective-permute-done | bytes 139296 | tf_op jit(solution)/shard_map/ppermute | solution.py:104
  15.0 1.8 %collective-permute-done.3 = bf16[32,2176]{1,0:T(8,128)(2,1)S(1)} collective-permute-done((bf16[32,2176]{1,0:T(8,128)(2,1)S(1)}, bf16[32,2176]{1,0:T(8,128)(2,1)S(1)}, u32[]{:S(2)}, u32[]{:S(2)}) %collective-permute-start.3) | collective-permute-done | bytes 139296 | tf_op jit(solution)/shard_map/ppermute | solution.py:104
  16.8 8.7 %collective-permute-done.4 = bf16[32,2176]{1,0:T(8,128)(2,1)S(1)} collective-permute-done((bf16[32,2176]{1,0:T(8,128)(2,1)S(1)}, bf16[32,2176]{1,0:T(8,128)(2,1)S(1)}, u32[]{:S(2)}, u32[]{:S(2)}) %collective-permute-start.4) | collective-permute-done | bytes 139296 | tf_op jit(solution)/shard_map/ppermute | solution.py:104
  25.5 5.7 %collective-permute-done.5 = bf16[32,2176]{1,0:T(8,128)(2,1)S(1)} collective-permute-done((bf16[32,2176]{1,0:T(8,128)(2,1)S(1)}, bf16[32,2176]{1,0:T(8,128)(2,1)S(1)}, u32[]{:S(2)}, u32[]{:S(2)}) %collective-permute-start.5) | collective-permute-done | bytes 139296 | tf_op jit(solution)/shard_map/ppermute | solution.py:104
  31.3 2.4 %collective-permute-done.6 = bf16[32,2176]{1,0:T(8,128)(2,1)S(1)} collective-permute-done((bf16[32,2176]{1,0:T(8,128)(2,1)S(1)}, bf16[32,2176]{1,0:T(8,128)(2,1)S(1)}, u32[]{:S(2)}, u32[]{:S(2)}) %collective-permute-start.6) | collective-permute-done | bytes 139296 | tf_op jit(solution)/shard_map/ppermute | solution.py:104
  33.7 0.1 fusion.96
  33.8 0.1 copy.16
  33.9 0.1 copy.17
  34.1 0.1 fusion.85
  34.2 0.9 %fusion.9 = f32[256,2048]{1,0:T(8,128)S(1)} fusion(bf16[256,2176]{1,0:T(8,128)(2,1)S(1)} %bitcast.66, f32[256]{0:T(256)S(1)} %bitcast.92, s32[256]{0:T(256)S(1)} %get-tuple-element.109, f32[256]{0:T(256)S(1)} %bitcast.91, s32[256]{0:T(256)S(1)} %get-tuple-element.105, f32[256]{0:T(256)S(1)} %bitcast.90, s32[256]{0:T(256)S(1)} %get-tuple-element.106, ...), kind=kOutput, calls=%fused_computation.21 | convolution fusion | flops 271581184 | bytes 3180544 | tf_op jit(solution)/shard_map/dot_general | solution.py:169
  35.1 0.1 slice.243
  35.2 0.1 collective-permute-start.7
  35.3 0.1 multiply_subtract_fusion.1
  35.3 0.5 %fusion.75 = (f32[1024,32]{0,1:T(8,128)S(1)}, f32[1024,32]{0,1:T(8,128)S(1)}) fusion(), kind=kLoop, calls=%fused_computation.113 | loop fusion | flops 458752 | bytes 262144 | tf_op jit(solution)/shard_map/sin | solution.py:52
  35.8 0.6 %fusion.78 = (f32[1024,32]{0,1:T(8,128)S(1)}, f32[1024,32]{0,1:T(8,128)S(1)}) fusion(s32[32]{0:T(128)S(1)} %iota_multiply_fusion), kind=kLoop, calls=%fused_computation.116 | loop fusion | flops 458752 | bytes 262272 | tf_op jit(solution)/shard_map/cos | solution.py:51
  36.4 1.2 %multiply_subtract_fusion = (f32[1024,32,32]{0,2,1:T(8,128)S(1)}, f32[1024,32,32]{0,2,1:T(8,128)S(1)}) fusion(f32[1024,32]{0,1:T(8,128)S(1)} %get-tuple-element.122, f32[1024,32]{0,1:T(8,128)S(1)} %get-tuple-element.113, f32[1024,32]{0,1:T(8,128)S(1)} %get-tuple-element.123, f32[1024,32]{0,1:T(8,128)S(1)} %get-tuple-element.112), kind=kLoop, calls=%fused_computation.9 | loop fusion | flops 6291456 | bytes 8912896 | tf_op jit(solution)/shard_map/sub | solution.py:53
  37.7 0.2 collective-permute-done.7
  37.9 0.1 slice_add_fusion
  38.0 1.6 %collective-permute-start.8 = (bf16[64,2048]{1,0:T(8,128)(2,1)S(1)}, bf16[64,2048]{1,0:T(8,128)(2,1)S(1)}, u32[]{:S(2)}, u32[]{:S(2)}) collective-permute-start(bf16[64,2048]{1,0:T(8,128)(2,1)S(1)} %slice.306), channel_id=1, source_target_pairs={{0,2},{1,3},{2,0},{3,1},{4,6},{5,7},{6,4},{7,5},{8,10},{9,11},{10,... | collective-permute-start | bytes 786440 | tf_op jit(solution)/shard_map/ppermute | solution.py:93
  39.6 1.3 %fusion.5 = (bf16[1024,1024]{0,1:T(8,128)(2,1)S(1)}, bf16[1024,1024]{0,1:T(8,128)(2,1)S(1)}) fusion(f32[1024,32,32]{0,2,1:T(8,128)S(1)} %get-tuple-element.70, f32[1024]{0:T(1024)S(1)} %multiply_subtract_fusion.1, f32[1024,32,32]{0,2,1:T(8,128)S(1)} %get-tuple-element.71), kind=kLoop, calls=%fused_computation.7 | loop fusion | flops 4194304 | bytes 12587008 | tf_op jit(solution)/shard_map/convert
  40.9 5.7 %collective-permute-done.8 = bf16[64,2048]{1,0:T(8,128)(2,1)S(1)} collective-permute-done((bf16[64,2048]{1,0:T(8,128)(2,1)S(1)}, bf16[64,2048]{1,0:T(8,128)(2,1)S(1)}, u32[]{:S(2)}, u32[]{:S(2)}) %collective-permute-start.8) | collective-permute-done | bytes 262176 | tf_op jit(solution)/shard_map/ppermute | solution.py:93
  46.7 1.5 %fusion.6 = f32[128,1024]{1,0:T(8,128)S(1)} fusion(bf16[1024,1024]{0,1:T(8,128)(2,1)S(1)} %get-tuple-element.91, bf16[1024,1024]{0,1:T(8,128)(2,1)S(1)} %get-tuple-element.90, bf16[64,1024]{1,0:T(8,128)(2,1)S(1)} %get-tuple-element.73, bf16[64,1024]{1,0:T(8,128)(2,1)S(1)} %get-tuple-element.72, bf16[64,2048]{1,0:T(8,128)(2,1)S(1)} %fusion.11), kind=kOutput, calls=%fused_computation.18 | convolution fusion | flops 546963456 | bytes 5242880 | tf_op jit(solution)/shard_map/dot_general | solution.py:180
  48.2 0.8 %pad_maximum_fusion = f32[64,2048]{1,0:T(8,128)} fusion(f32[64,1024]{1,0:T(8,128)S(1)} %get-tuple-element.69, f32[64,1024]{1,0:T(8,128)S(1)} %get-tuple-element.68), kind=kLoop, calls=%fused_computation.31 | loop fusion | flops 131072 | bytes 1048576 | tf_op jit(solution)/shard_map/concatenate | solution.py:182
  (35 shorter events, 0.6 us)
Async XLA Ops:
  0.0 2.1 %copy-start = (bf16[1,128,2048]{2,1,0:T(8,128)(2,1)S(1)}, bf16[1,128,2048]{2,1,0:T(8,128)(2,1)}, u32[]{:S(2)}) copy-start(bf16[1,128,2048]{2,1,0:T(8,128)(2,1)} %param.13) | copy-start | bytes 1572868
  2.7 8.0 %collective-permute-start = (bf16[32,2176]{1,0:T(8,128)(2,1)S(1)}, bf16[32,2176]{1,0:T(8,128)(2,1)S(1)}, u32[]{:S(2)}, u32[]{:S(2)}) collective-permute-start(bf16[32,2176]{1,0:T(8,128)(2,1)S(1)} %get-tuple-element.62), channel_id=1, source_target_pairs={{0,4},{4,0},{8,12},{12,8},{16,20},{20,16},{24,28},{28,24},{1,5},{5... | collective-permute-start | bytes 417800 | tf_op jit(solution)/shard_map/ppermute | solution.py:104
  4.3 9.0 %collective-permute-start.1 = (bf16[32,2176]{1,0:T(8,128)(2,1)S(1)}, bf16[32,2176]{1,0:T(8,128)(2,1)S(1)}, u32[]{:S(2)}, u32[]{:S(2)}) collective-permute-start(bf16[32,2176]{1,0:T(8,128)(2,1)S(1)} %get-tuple-element.63), channel_id=1, source_target_pairs={{0,8},{4,12},{8,0},{12,4},{16,24},{20,28},{24,16},{28,20},{1,9},{5... | collective-permute-start | bytes 417800 | tf_op jit(solution)/shard_map/ppermute | solution.py:104
  5.8 9.1 %collective-permute-start.2 = (bf16[32,2176]{1,0:T(8,128)(2,1)S(1)}, bf16[32,2176]{1,0:T(8,128)(2,1)S(1)}, u32[]{:S(2)}, u32[]{:S(2)}) collective-permute-start(bf16[32,2176]{1,0:T(8,128)(2,1)S(1)} %get-tuple-element.64), channel_id=1, source_target_pairs={{0,12},{4,8},{8,4},{12,0},{16,28},{20,24},{24,20},{28,16},{1,13},{... | collective-permute-start | bytes 417800 | tf_op jit(solution)/shard_map/ppermute | solution.py:104
  6.2 10.6 %collective-permute-start.3 = (bf16[32,2176]{1,0:T(8,128)(2,1)S(1)}, bf16[32,2176]{1,0:T(8,128)(2,1)S(1)}, u32[]{:S(2)}, u32[]{:S(2)}) collective-permute-start(bf16[32,2176]{1,0:T(8,128)(2,1)S(1)} %get-tuple-element.65), channel_id=1, source_target_pairs={{0,16},{4,20},{8,24},{12,28},{16,0},{20,4},{24,8},{28,12},{1,17},{... | collective-permute-start | bytes 417800 | tf_op jit(solution)/shard_map/ppermute | solution.py:104
  6.2 19.3 %collective-permute-start.4 = (bf16[32,2176]{1,0:T(8,128)(2,1)S(1)}, bf16[32,2176]{1,0:T(8,128)(2,1)S(1)}, u32[]{:S(2)}, u32[]{:S(2)}) collective-permute-start(bf16[32,2176]{1,0:T(8,128)(2,1)S(1)} %get-tuple-element.66), channel_id=1, source_target_pairs={{0,20},{4,16},{8,28},{12,24},{16,4},{20,0},{24,12},{28,8},{1,21},{... | collective-permute-start | bytes 417800 | tf_op jit(solution)/shard_map/ppermute | solution.py:104
  10.7 20.6 %collective-permute-start.5 = (bf16[32,2176]{1,0:T(8,128)(2,1)S(1)}, bf16[32,2176]{1,0:T(8,128)(2,1)S(1)}, u32[]{:S(2)}, u32[]{:S(2)}) collective-permute-start(bf16[32,2176]{1,0:T(8,128)(2,1)S(1)} %get-tuple-element.67), channel_id=1, source_target_pairs={{0,24},{4,28},{8,16},{12,20},{16,8},{20,12},{24,0},{28,4},{1,25},{... | collective-permute-start | bytes 417800 | tf_op jit(solution)/shard_map/ppermute | solution.py:104
  13.3 20.4 %collective-permute-start.6 = (bf16[32,2176]{1,0:T(8,128)(2,1)S(1)}, bf16[32,2176]{1,0:T(8,128)(2,1)S(1)}, u32[]{:S(2)}, u32[]{:S(2)}) collective-permute-start(bf16[32,2176]{1,0:T(8,128)(2,1)S(1)} %get-tuple-element.61), channel_id=1, source_target_pairs={{0,28},{4,24},{8,20},{12,16},{16,12},{20,8},{24,4},{28,0},{1,29},{... | collective-permute-start | bytes 417800 | tf_op jit(solution)/shard_map/ppermute | solution.py:104
  35.2 2.7 %collective-permute-start.7 = (f32[128,2048]{1,0:T(8,128)S(1)}, f32[128,2048]{1,0:T(8,128)S(1)}, u32[]{:S(2)}, u32[]{:S(2)}) collective-permute-start(f32[128,2048]{1,0:T(8,128)S(1)} %slice.243), channel_id=1, source_target_pairs={{0,1},{1,0},{2,3},{3,2},{4,5},{5,4},{6,7},{7,6},{8,9},{9,8},{10,11... | collective-permute-start | bytes 3145736 | tf_op jit(solution)/shard_map/ppermute | solution.py:93
  38.0 8.6 %collective-permute-start.8 = (bf16[64,2048]{1,0:T(8,128)(2,1)S(1)}, bf16[64,2048]{1,0:T(8,128)(2,1)S(1)}, u32[]{:S(2)}, u32[]{:S(2)}) collective-permute-start(bf16[64,2048]{1,0:T(8,128)(2,1)S(1)} %slice.306), channel_id=1, source_target_pairs={{0,2},{1,3},{2,0},{3,1},{4,6},{5,7},{6,4},{7,5},{8,10},{9,11},{10,... | collective-permute-start | bytes 786440 | tf_op jit(solution)/shard_map/ppermute | solution.py:93

commit v14 on v12

--- a/solution.py
+++ b/solution.py
@@ -61,7 +61,9 @@
     )
     tap_cos = (taper[:, None, None] * cosine).reshape(NCH, NCH)
     tap_sin = (taper[:, None, None] * sine).reshape(NCH, NCH)
-    return jnp.concatenate([tap_cos, tap_sin], axis=0).astype(jnp.bfloat16)
+    upper = jnp.concatenate([tap_cos, -tap_sin], axis=1)
+    lower = jnp.concatenate([tap_sin, tap_cos], axis=1)
+    return jnp.concatenate([upper, lower], axis=0).astype(jnp.bfloat16)
 
 
 def halving_order(tm_index, time_groups, cell_share):
@@ -165,14 +167,8 @@
     else:
         summed = lax.psum_scatter(partial, "tm", scatter_dimension=0, tiled=True)
     grid = summed.astype(jnp.bfloat16)
-    grid_re, grid_im = grid[:, :NCH], grid[:, NCH:]
-    lhs = jnp.concatenate(
-        [grid, jnp.concatenate([grid_im, -grid_re], axis=1)], axis=0
-    )
     out_scale = 4.0 / math.sqrt(NCH * time_groups * ROWS_DEV)
-    both = jnp.dot(lhs, delay_halves(), preferred_element_type=jnp.float32) * out_scale
-    cells_out = grid.shape[0]
-    return jnp.concatenate([both[:cells_out], both[cells_out:]], axis=1)
+    return jnp.dot(grid, delay_halves(), preferred_element_type=jnp.float32) * out_scale
 
 
 def solution(mesh):

time: 46 us -> 47.1 us (1.024)
  matrix products: 3.1 us -> 5.05 us
  other arithmetic: 6.02 us -> 5.44 us
    dot_general x1, matrix products: 1.51 us -> 3.46 us  [per_device(): jnp.dot(grid, delay_halves(), preferred_element_type=jnp.float32)]
    add x0 -> x1, other arithmetic: none -> 1.28 us  [delay_halves(): s_hi[:, :, None] * c_lo[:, None, :] + c_hi[:, :, None] * s_lo[:, None, :]]
    sub x1 -> x0, other arithmetic: 1.22 us -> none  [delay_halves(): c_hi[:, :, None] * c_lo[:, None, :] - s_hi[:, :, None] * s_lo[:, None, :]]
    concatenate x1 -> x0, other arithmetic: 0.83 us -> none  [per_device(): return jnp.concatenate([both[:cells_out], both[cells_out:]], axis=1)]
  transfers between devices with their start and end apart: 9 -> 9, of which waited for: 7 -> 7; matrix products, arithmetic and copies ran while one was open for 9% -> 10% of each run, Pallas kernels for 0% -> 0%
where the time goes in v14:
time: 47.1 us; the launch traced here: 47 us
  waiting for transfers between devices  24.8 us (53%)
  starting transfers between devices  10.3 us (22%)
  other arithmetic  5.44 us (12%)
  matrix products  5.05 us (11%)
  local copies, waits for them, and re-layouts  1.17 us (2%)
    ppermute x7, waiting for transfers between devices, uv_exchange(): pieces.append(lax.ppermute(outgoing[shift], 'uv', perm))  19.1 us
    ppermute x7, starting transfers between devices, uv_exchange(): pieces.append(lax.ppermute(outgoing[shift], 'uv', perm))  8.62 us
    ppermute x2, waiting for transfers between devices, halving_reduce(): received = lax.ppermute(outgoing, 'tm', perm)  5.69 us
    dot_general x1, matrix products, per_device(): jnp.dot(grid, delay_halves(), preferred_element_type=jnp.float32)  3.46 us
    ppermute x2, starting transfers between devices, halving_reduce(): received = lax.ppermute(outgoing, 'tm', perm)  1.64 us
    another operation x2, other arithmetic  1.53 us
    add x1, other arithmetic, delay_halves(): s_hi[:, :, None] * c_lo[:, None, :] + c_hi[:, :, None] * s_lo[:, None, :]  1.28 us
  transfers between devices with their start and end apart: 9, of which 7 were waited for; matrix products, arithmetic and copies ran while one was open for 10% of the time, Pallas kernels for 0%

profile of v14, /device:TPU:12, one launch (start us, length us, event | category | flops | bytes accessed | tf_op | source)
XLA Modules:
  0.0 47.0 jit_solution(2134269395620211468)
XLA Ops:
  0.0 0.0 copy-start
  0.0 0.8 %fusion.89 = s32[11,128]{1,0:T(8,128)S(1)} fusion(s32[1,8]{1,0:T(1,128)} %bitcast.85, s32[8,32]{1,0:T(8,128)} %bitcast.64, s32[1,128]{1,0:T(1,128)} %param.15, s32[1,128]{1,0:T(1,128)} %param.14), kind=kLoop, calls=%fused_computation.128 | loop fusion | flops 4224 | bytes 7712 | tf_op jit(solution)/shard_map/concatenate | solution.py:122
  0.8 0.1 eq.83
  0.9 0.1 pad_add_fusion.1
  1.0 0.1 dynamic_slice.7
  1.1 0.1 iota_compare_fusion.1
  1.1 0.1 lt.64
  1.2 0.3 convolution_convert_fusion.1
  1.5 0.0 copy-done
  1.5 0.5 %convolution_convert_fusion = bf16[256,2048]{1,0:T(8,128)(2,1)S(1)} fusion(bf16[1,128,2048]{2,1,0:T(8,128)(2,1)S(1)} %copy-done, s32[256]{0:T(256)S(1)} %eq.83, pred[256]{0:T(512)(128)(4,1)S(1)} %lt.64), kind=kOutput, calls=%fused_computation.22 | convolution fusion | flops 134807552 | bytes 1574144 | tf_op jit(solution)/shard_map/dot_general | solution.py:144
  2.0 0.1 pad_maximum_fusion
  2.1 1.6 %collective-permute-start = (bf16[32,2176]{1,0:T(8,128)(2,1)S(1)}, bf16[32,2176]{1,0:T(8,128)(2,1)S(1)}, u32[]{:S(2)}, u32[]{:S(2)}) collective-permute-start(bf16[32,2176]{1,0:T(8,128)(2,1)S(1)} %get-tuple-element.64), channel_id=1, source_target_pairs={{0,4},{4,8},{8,12},{12,16},{16,20},{20,24},{24,28},{28,0},{1,5},{5... | collective-permute-start | bytes 417800 | tf_op jit(solution)/shard_map/ppermute | solution.py:106
  3.6 1.6 %collective-permute-start.1 = (bf16[32,2176]{1,0:T(8,128)(2,1)S(1)}, bf16[32,2176]{1,0:T(8,128)(2,1)S(1)}, u32[]{:S(2)}, u32[]{:S(2)}) collective-permute-start(bf16[32,2176]{1,0:T(8,128)(2,1)S(1)} %get-tuple-element.65), channel_id=1, source_target_pairs={{0,8},{4,12},{8,16},{12,20},{16,24},{20,28},{24,0},{28,4},{1,9},{5... | collective-permute-start | bytes 417800 | tf_op jit(solution)/shard_map/ppermute | solution.py:106
  5.2 1.2 %collective-permute-start.2 = (bf16[32,2176]{1,0:T(8,128)(2,1)S(1)}, bf16[32,2176]{1,0:T(8,128)(2,1)S(1)}, u32[]{:S(2)}, u32[]{:S(2)}) collective-permute-start(bf16[32,2176]{1,0:T(8,128)(2,1)S(1)} %get-tuple-element.66), channel_id=1, source_target_pairs={{0,12},{4,16},{8,20},{12,24},{16,28},{20,0},{24,4},{28,8},{1,13},{... | collective-permute-start | bytes 417800 | tf_op jit(solution)/shard_map/ppermute | solution.py:106
  6.4 1.7 %collective-permute-start.3 = (bf16[32,2176]{1,0:T(8,128)(2,1)S(1)}, bf16[32,2176]{1,0:T(8,128)(2,1)S(1)}, u32[]{:S(2)}, u32[]{:S(2)}) collective-permute-start(bf16[32,2176]{1,0:T(8,128)(2,1)S(1)} %get-tuple-element.67), channel_id=1, source_target_pairs={{0,16},{4,20},{8,24},{12,28},{16,0},{20,4},{24,8},{28,12},{1,17},{... | collective-permute-start | bytes 417800 | tf_op jit(solution)/shard_map/ppermute | solution.py:106
  8.1 1.3 %collective-permute-start.4 = (bf16[32,2176]{1,0:T(8,128)(2,1)S(1)}, bf16[32,2176]{1,0:T(8,128)(2,1)S(1)}, u32[]{:S(2)}, u32[]{:S(2)}) collective-permute-start(bf16[32,2176]{1,0:T(8,128)(2,1)S(1)} %get-tuple-element.68), channel_id=1, source_target_pairs={{0,20},{4,24},{8,28},{12,0},{16,4},{20,8},{24,12},{28,16},{1,21},{... | collective-permute-start | bytes 417800 | tf_op jit(solution)/shard_map/ppermute | solution.py:106
  9.4 0.1 scatter.15
  9.5 0.1 scatter.16
  9.6 0.1 scatter.19
  9.7 0.1 iota_add_fusion
  9.8 0.1 add.361
  9.9 0.0 collective-permute-done
  9.9 1.3 %collective-permute-start.5 = (bf16[32,2176]{1,0:T(8,128)(2,1)S(1)}, bf16[32,2176]{1,0:T(8,128)(2,1)S(1)}, u32[]{:S(2)}, u32[]{:S(2)}) collective-permute-start(bf16[32,2176]{1,0:T(8,128)(2,1)S(1)} %get-tuple-element.69), channel_id=1, source_target_pairs={{0,24},{4,28},{8,0},{12,4},{16,8},{20,12},{24,16},{28,20},{1,25},{... | collective-permute-start | bytes 417800 | tf_op jit(solution)/shard_map/ppermute | solution.py:106
  11.2 11.4 %collective-permute-done.1 = bf16[32,2176]{1,0:T(8,128)(2,1)S(1)} collective-permute-done((bf16[32,2176]{1,0:T(8,128)(2,1)S(1)}, bf16[32,2176]{1,0:T(8,128)(2,1)S(1)}, u32[]{:S(2)}, u32[]{:S(2)}) %collective-permute-start.1) | collective-permute-done | bytes 139296 | tf_op jit(solution)/shard_map/ppermute | solution.py:106
  22.6 0.0 collective-permute-start.6
  22.6 3.0 %collective-permute-done.2 = bf16[32,2176]{1,0:T(8,128)(2,1)S(1)} collective-permute-done((bf16[32,2176]{1,0:T(8,128)(2,1)S(1)}, bf16[32,2176]{1,0:T(8,128)(2,1)S(1)}, u32[]{:S(2)}, u32[]{:S(2)}) %collective-permute-start.2) | collective-permute-done | bytes 139296 | tf_op jit(solution)/shard_map/ppermute | solution.py:106
  25.6 1.8 %collective-permute-done.3 = bf16[32,2176]{1,0:T(8,128)(2,1)S(1)} collective-permute-done((bf16[32,2176]{1,0:T(8,128)(2,1)S(1)}, bf16[32,2176]{1,0:T(8,128)(2,1)S(1)}, u32[]{:S(2)}, u32[]{:S(2)}) %collective-permute-start.3) | collective-permute-done | bytes 139296 | tf_op jit(solution)/shard_map/ppermute | solution.py:106
  27.5 0.0 collective-permute-done.4
  27.5 1.8 %collective-permute-done.5 = bf16[32,2176]{1,0:T(8,128)(2,1)S(1)} collective-permute-done((bf16[32,2176]{1,0:T(8,128)(2,1)S(1)}, bf16[32,2176]{1,0:T(8,128)(2,1)S(1)}, u32[]{:S(2)}, u32[]{:S(2)}) %collective-permute-start.5) | collective-permute-done | bytes 139296 | tf_op jit(solution)/shard_map/ppermute | solution.py:106
  29.3 1.2 %collective-permute-done.6 = bf16[32,2176]{1,0:T(8,128)(2,1)S(1)} collective-permute-done((bf16[32,2176]{1,0:T(8,128)(2,1)S(1)}, bf16[32,2176]{1,0:T(8,128)(2,1)S(1)}, u32[]{:S(2)}, u32[]{:S(2)}) %collective-permute-start.6) | collective-permute-done | bytes 139296 | tf_op jit(solution)/shard_map/ppermute | solution.py:106
  30.5 0.1 fusion.97
  30.6 0.1 copy.11
  30.7 0.1 copy.12
  30.9 0.1 fusion.85
  31.0 0.8 %fusion.13 = f32[256,2048]{1,0:T(8,128)S(1)} fusion(bf16[256,2176]{1,0:T(8,128)(2,1)S(1)} %bitcast.63, f32[256]{0:T(256)S(1)} %bitcast.83, s32[256]{0:T(256)S(1)} %get-tuple-element.106, f32[256]{0:T(256)S(1)} %bitcast.82, s32[256]{0:T(256)S(1)} %get-tuple-element.102, f32[256]{0:T(256)S(1)} %bitcast.81, s32[256]{0:T(256)S(1)} %get-tuple-element.103, ...), kind=kOutput, calls=%fused_computation.26 | convolution fusion | flops 271581184 | bytes 3180544 | tf_op jit(solution)/shard_map/dot_general | solution.py:164
  31.9 0.1 slice.227
  32.0 0.1 collective-permute-start.7
  32.1 0.1 multiply_subtract_fusion.1
  32.1 0.5 %fusion.75 = (f32[1024,32]{0,1:T(8,128)S(1)}, f32[1024,32]{0,1:T(8,128)S(1)}) fusion(), kind=kLoop, calls=%fused_computation.111 | loop fusion | flops 458752 | bytes 262144 | tf_op jit(solution)/shard_map/sin | solution.py:52
  32.7 0.6 %fusion.78 = (f32[1024,32]{0,1:T(8,128)S(1)}, f32[1024,32]{0,1:T(8,128)S(1)}) fusion(s32[32]{0:T(128)S(1)} %iota_multiply_fusion), kind=kLoop, calls=%fused_computation.114 | loop fusion | flops 458752 | bytes 262272 | tf_op jit(solution)/shard_map/cos | solution.py:51
  33.2 1.3 %multiply_add_fusion = (f32[1024,32,32]{0,2,1:T(8,128)S(1)}, f32[1024,32,32]{0,2,1:T(8,128)S(1)}) fusion(f32[1024,32]{0,1:T(8,128)S(1)} %get-tuple-element.119, f32[1024,32]{0,1:T(8,128)S(1)} %get-tuple-element.110, f32[1024,32]{0,1:T(8,128)S(1)} %get-tuple-element.120, f32[1024,32]{0,1:T(8,128)S(1)} %get-tuple-element.109), kind=kLoop, calls=%fused_computation.12 | loop fusion | flops 6291456 | bytes 8912896 | tf_op jit(solution)/shard_map/add | solution.py:54
  34.5 0.2 collective-permute-done.7
  34.7 0.1 slice_add_fusion
  34.9 1.6 %collective-permute-start.8 = (bf16[64,2048]{1,0:T(8,128)(2,1)S(1)}, bf16[64,2048]{1,0:T(8,128)(2,1)S(1)}, u32[]{:S(2)}, u32[]{:S(2)}) collective-permute-start(bf16[64,2048]{1,0:T(8,128)(2,1)S(1)} %slice.286), channel_id=1, source_target_pairs={{0,2},{1,3},{2,0},{3,1},{4,6},{5,7},{6,4},{7,5},{8,10},{9,11},{10,... | collective-permute-start | bytes 786440 | tf_op jit(solution)/shard_map/ppermute | solution.py:95
  36.4 1.5 %negate_convert_fusion = (bf16[1024,1024]{0,1:T(8,128)(2,1)S(1)}, bf16[1024,1024]{0,1:T(8,128)(2,1)S(1)}, bf16[1024,1024]{0,1:T(8,128)(2,1)S(1)}) fusion(f32[1024,32,32]{0,2,1:T(8,128)S(1)} %get-tuple-element.70, f32[1024]{0:T(1024)S(1)} %multiply_subtract_fusion.1, f32[1024,32,32]{0,2,1:T(8,128)S(1)} %get-tuple-element.71), kind=kLoop, calls=%fused_computation.11 | loop fusion | flops 6291456 | bytes 14684160 | tf_op jit(solution)/shard_map/convert.5
  38.0 5.5 %collective-permute-done.8 = bf16[64,2048]{1,0:T(8,128)(2,1)S(1)} collective-permute-done((bf16[64,2048]{1,0:T(8,128)(2,1)S(1)}, bf16[64,2048]{1,0:T(8,128)(2,1)S(1)}, u32[]{:S(2)}, u32[]{:S(2)}) %collective-permute-start.8) | collective-permute-done | bytes 262176 | tf_op jit(solution)/shard_map/ppermute | solution.py:95
  43.5 3.5 %fusion.10 = f32[64,2048]{1,0:T(8,128)} fusion(bf16[1024,1024]{0,1:T(8,128)(2,1)S(1)} %get-tuple-element.88, bf16[1024,1024]{0,1:T(8,128)(2,1)S(1)} %get-tuple-element.60, bf16[1024,1024]{0,1:T(8,128)(2,1)S(1)} %get-tuple-element.59, f32[128,2048]{1,0:T(8,128)S(1)} %slice_add_fusion, bf16[64,2048]{1,0:T(8,128)(2,1)S(1)} %collective-permute-done.8), kind=kOutput, calls=%fused_computation.23 | convolution fusion | flops 570949632 | bytes 7602176 | tf_op jit(solution)/shard_map/dot_general | solution.py:171
  (25 shorter events, 0.3 us)
Async XLA Ops:
  0.0 1.5 %copy-start = (bf16[1,128,2048]{2,1,0:T(8,128)(2,1)S(1)}, bf16[1,128,2048]{2,1,0:T(8,128)(2,1)}, u32[]{:S(2)}) copy-start(bf16[1,128,2048]{2,1,0:T(8,128)(2,1)} %param.13) | copy-start | bytes 1572868
  2.1 7.9 %collective-permute-start = (bf16[32,2176]{1,0:T(8,128)(2,1)S(1)}, bf16[32,2176]{1,0:T(8,128)(2,1)S(1)}, u32[]{:S(2)}, u32[]{:S(2)}) collective-permute-start(bf16[32,2176]{1,0:T(8,128)(2,1)S(1)} %get-tuple-element.64), channel_id=1, source_target_pairs={{0,4},{4,8},{8,12},{12,16},{16,20},{20,24},{24,28},{28,0},{1,5},{5... | collective-permute-start | bytes 417800 | tf_op jit(solution)/shard_map/ppermute | solution.py:106
  3.6 19.0 %collective-permute-start.1 = (bf16[32,2176]{1,0:T(8,128)(2,1)S(1)}, bf16[32,2176]{1,0:T(8,128)(2,1)S(1)}, u32[]{:S(2)}, u32[]{:S(2)}) collective-permute-start(bf16[32,2176]{1,0:T(8,128)(2,1)S(1)} %get-tuple-element.65), channel_id=1, source_target_pairs={{0,8},{4,12},{8,16},{12,20},{16,24},{20,28},{24,0},{28,4},{1,9},{5... | collective-permute-start | bytes 417800 | tf_op jit(solution)/shard_map/ppermute | solution.py:106
  5.2 20.4 %collective-permute-start.2 = (bf16[32,2176]{1,0:T(8,128)(2,1)S(1)}, bf16[32,2176]{1,0:T(8,128)(2,1)S(1)}, u32[]{:S(2)}, u32[]{:S(2)}) collective-permute-start(bf16[32,2176]{1,0:T(8,128)(2,1)S(1)} %get-tuple-element.66), channel_id=1, source_target_pairs={{0,12},{4,16},{8,20},{12,24},{16,28},{20,0},{24,4},{28,8},{1,13},{... | collective-permute-start | bytes 417800 | tf_op jit(solution)/shard_map/ppermute | solution.py:106
  6.4 21.1 %collective-permute-start.3 = (bf16[32,2176]{1,0:T(8,128)(2,1)S(1)}, bf16[32,2176]{1,0:T(8,128)(2,1)S(1)}, u32[]{:S(2)}, u32[]{:S(2)}) collective-permute-start(bf16[32,2176]{1,0:T(8,128)(2,1)S(1)} %get-tuple-element.67), channel_id=1, source_target_pairs={{0,16},{4,20},{8,24},{12,28},{16,0},{20,4},{24,8},{28,12},{1,17},{... | collective-permute-start | bytes 417800 | tf_op jit(solution)/shard_map/ppermute | solution.py:106
  8.1 19.4 %collective-permute-start.4 = (bf16[32,2176]{1,0:T(8,128)(2,1)S(1)}, bf16[32,2176]{1,0:T(8,128)(2,1)S(1)}, u32[]{:S(2)}, u32[]{:S(2)}) collective-permute-start(bf16[32,2176]{1,0:T(8,128)(2,1)S(1)} %get-tuple-element.68), channel_id=1, source_target_pairs={{0,20},{4,24},{8,28},{12,0},{16,4},{20,8},{24,12},{28,16},{1,21},{... | collective-permute-start | bytes 417800 | tf_op jit(solution)/shard_map/ppermute | solution.py:106
  9.9 19.3 %collective-permute-start.5 = (bf16[32,2176]{1,0:T(8,128)(2,1)S(1)}, bf16[32,2176]{1,0:T(8,128)(2,1)S(1)}, u32[]{:S(2)}, u32[]{:S(2)}) collective-permute-start(bf16[32,2176]{1,0:T(8,128)(2,1)S(1)} %get-tuple-element.69), channel_id=1, source_target_pairs={{0,24},{4,28},{8,0},{12,4},{16,8},{20,12},{24,16},{28,20},{1,25},{... | collective-permute-start | bytes 417800 | tf_op jit(solution)/shard_map/ppermute | solution.py:106
  22.6 7.9 %collective-permute-start.6 = (bf16[32,2176]{1,0:T(8,128)(2,1)S(1)}, bf16[32,2176]{1,0:T(8,128)(2,1)S(1)}, u32[]{:S(2)}, u32[]{:S(2)}) collective-permute-start(bf16[32,2176]{1,0:T(8,128)(2,1)S(1)} %get-tuple-element.63), channel_id=1, source_target_pairs={{0,28},{4,0},{8,4},{12,8},{16,12},{20,16},{24,20},{28,24},{1,29},{... | collective-permute-start | bytes 417800 | tf_op jit(solution)/shard_map/ppermute | solution.py:106
  32.0 2.7 %collective-permute-start.7 = (f32[128,2048]{1,0:T(8,128)S(1)}, f32[128,2048]{1,0:T(8,128)S(1)}, u32[]{:S(2)}, u32[]{:S(2)}) collective-permute-start(f32[128,2048]{1,0:T(8,128)S(1)} %slice.227), channel_id=1, source_target_pairs={{0,1},{1,0},{2,3},{3,2},{4,5},{5,4},{6,7},{7,6},{8,9},{9,8},{10,11... | collective-permute-start | bytes 3145736 | tf_op jit(solution)/shard_map/ppermute | solution.py:95
  34.9 8.6 %collective-permute-start.8 = (bf16[64,2048]{1,0:T(8,128)(2,1)S(1)}, bf16[64,2048]{1,0:T(8,128)(2,1)S(1)}, u32[]{:S(2)}, u32[]{:S(2)}) collective-permute-start(bf16[64,2048]{1,0:T(8,128)(2,1)S(1)} %slice.286), channel_id=1, source_target_pairs={{0,2},{1,3},{2,0},{3,1},{4,6},{5,7},{6,4},{7,5},{8,10},{9,11},{10,... | collective-permute-start | bytes 786440 | tf_op jit(solution)/shard_map/ppermute | solution.py:95

commit v15 on v11

--- a/solution.py
+++ b/solution.py
@@ -88,9 +88,7 @@
         half = partial.shape[0] // 2
         bit = 1 << level
         perm = [(i, i ^ bit) for i in range(time_groups)]
-        outgoing = partial[:half]
-        if level > 0:
-            outgoing = outgoing.astype(jnp.bfloat16)
+        outgoing = partial[:half].astype(jnp.bfloat16)
         received = lax.ppermute(outgoing, "tm", perm)
         partial = partial[half:] + received.astype(jnp.float32)
     return partial, gated
@@ -114,17 +112,19 @@
     row_count, row_width = vis_rows.shape
     tile_count, slot_depth = slot_rows.shape[2:]
     slot_size = tile_count * slot_depth
+    lanes = max(row_count, slot_depth, tile_count)
+    pad = lambda x: jnp.pad(x, ((0, 0), (0, lanes - x.shape[1])))
     (ints,) = lax.optimization_barrier(
         (
             jnp.concatenate(
-                [slot_rows.reshape(-1), counts.reshape(-1), anchor.reshape(-1), offset.reshape(-1)]
+                [pad(slot_rows[0, 0]), pad(counts[0]), pad(anchor), pad(offset)], axis=0
             ),
         )
     )
-    slot_table = ints[:slot_size].reshape(tile_count, slot_depth)
-    live_count = ints[slot_size:slot_size + tile_count]
-    anchor_row = ints[slot_size + tile_count:slot_size + tile_count + row_count]
-    offset_row = ints[slot_size + tile_count + row_count:]
+    slot_table = ints[:tile_count, :slot_depth]
+    live_count = ints[tile_count, :tile_count]
+    anchor_row = ints[tile_count + 1, :row_count]
+    offset_row = ints[tile_count + 2, :row_count]
     if uv_size <= 16:
         uv_index = lax.axis_index("uv")
         slot_table = lax.dynamic_slice_in_dim(

time: 50 us -> 48.1 us (0.962)
  local copies, waits for them, and re-layouts: 2.27 us -> 1.18 us
  waiting for transfers between devices: 23.5 us -> 22.8 us
    reshape x2 -> x0, local copies, waits for them, and re-layouts: 0.9 us -> none  [the longest x1 0.82 us: per_device(): slot_rows.reshape(-1)]
    ppermute x2, waiting for transfers between devices: 5.92 us -> 5.17 us  [halving_reduce(): received = lax.ppermute(outgoing, 'tm', perm)]
  transfers between devices with their start and end apart: 9 -> 9, of which waited for: 7 -> 7; matrix products, arithmetic and copies ran while one was open for 8% -> 9% of each run, Pallas kernels for 0% -> 0%
where the time goes in v15:
time: 48.1 us; the launch traced here: 48 us
  waiting for transfers between devices  22.8 us (47%)
  starting transfers between devices  14.7 us (31%)
  other arithmetic  5.96 us (12%)
  matrix products  3.1 us (6%)
  local copies, waits for them, and re-layouts  1.18 us (2%)
    ppermute x7, waiting for transfers between devices, uv_exchange(): pieces.append(lax.ppermute(outgoing[shift], 'uv', perm))  17.6 us
    ppermute x7, starting transfers between devices, uv_exchange(): pieces.append(lax.ppermute(outgoing[shift], 'uv', perm))  13.1 us
    ppermute x2, waiting for transfers between devices, halving_reduce(): received = lax.ppermute(outgoing, 'tm', perm)  5.17 us
    ppermute x2, starting transfers between devices, halving_reduce(): received = lax.ppermute(outgoing, 'tm', perm)  1.64 us
    dot_general x1, matrix products, per_device(): jnp.dot(lhs, delay_halves(freq), preferred_element_type=jnp.float32)  1.51 us
    another operation x2, other arithmetic  1.29 us
    sub x1, other arithmetic, delay_halves(): c_hi[:, :, None] * c_lo[:, None, :] - s_hi[:, :, None] * s_lo[:, None, :]  1.22 us
    cos x1, other arithmetic, delay_halves(): c_hi, s_hi = (jnp.cos(ang_hi), jnp.sin(ang_hi))  1.05 us
  transfers between devices with their start and end apart: 9, of which 7 were waited for; matrix products, arithmetic and copies ran while one was open for 9% of the time, Pallas kernels for 0%

profile of v15, /device:TPU:12, one launch (start us, length us, event | category | flops | bytes accessed | tf_op | source)
XLA Modules:
  0.0 48.0 jit_solution(8669732781685764194)
XLA Ops:
  0.0 0.0 copy-start
  0.0 0.8 %fusion.85 = s32[11,128]{1,0:T(8,128)S(1)} fusion(s32[1,8]{1,0:T(1,128)} %bitcast.83, s32[8,32]{1,0:T(8,128)} %bitcast.62, s32[1,128]{1,0:T(1,128)} %param.15, s32[1,128]{1,0:T(1,128)} %param.14), kind=kLoop, calls=%fused_computation.129 | loop fusion | flops 4224 | bytes 7712 | tf_op jit(solution)/shard_map/concatenate | solution.py:119
  0.8 0.1 eq.83
  0.9 0.1 pad_add_fusion.1
  1.0 0.1 dynamic_slice.7
  1.1 0.1 iota_compare_fusion.1
  1.1 0.1 lt.52
  1.2 0.3 convolution_convert_fusion.1
  1.5 0.0 copy-done
  1.5 0.5 %convolution_convert_fusion = bf16[256,2048]{1,0:T(8,128)(2,1)S(1)} fusion(bf16[1,128,2048]{2,1,0:T(8,128)(2,1)S(1)} %copy-done, s32[256]{0:T(256)S(1)} %eq.83, pred[256]{0:T(512)(128)(4,1)S(1)} %lt.52), kind=kOutput, calls=%fused_computation.17 | convolution fusion | flops 134807552 | bytes 1574144 | tf_op jit(solution)/shard_map/dot_general | solution.py:141
  2.0 0.1 pad_maximum_fusion.1
  2.1 0.6 %collective-permute-start.6 = (bf16[32,2176]{1,0:T(8,128)(2,1)S(1)}, bf16[32,2176]{1,0:T(8,128)(2,1)S(1)}, u32[]{:S(2)}, u32[]{:S(2)}) collective-permute-start(bf16[32,2176]{1,0:T(8,128)(2,1)S(1)} %get-tuple-element.65), channel_id=1, source_target_pairs={{0,28},{4,0},{8,4},{12,8},{16,12},{20,16},{24,20},{28,24},{1,29},{... | collective-permute-start | bytes 417800 | tf_op jit(solution)/shard_map/ppermute | solution.py:103
  2.6 2.4 %collective-permute-start = (bf16[32,2176]{1,0:T(8,128)(2,1)S(1)}, bf16[32,2176]{1,0:T(8,128)(2,1)S(1)}, u32[]{:S(2)}, u32[]{:S(2)}) collective-permute-start(bf16[32,2176]{1,0:T(8,128)(2,1)S(1)} %get-tuple-element.66), channel_id=1, source_target_pairs={{0,4},{4,8},{8,12},{12,16},{16,20},{20,24},{24,28},{28,0},{1,5},{5... | collective-permute-start | bytes 417800 | tf_op jit(solution)/shard_map/ppermute | solution.py:103
  5.0 1.6 %collective-permute-start.1 = (bf16[32,2176]{1,0:T(8,128)(2,1)S(1)}, bf16[32,2176]{1,0:T(8,128)(2,1)S(1)}, u32[]{:S(2)}, u32[]{:S(2)}) collective-permute-start(bf16[32,2176]{1,0:T(8,128)(2,1)S(1)} %get-tuple-element.67), channel_id=1, source_target_pairs={{0,8},{4,12},{8,16},{12,20},{16,24},{20,28},{24,0},{28,4},{1,9},{5... | collective-permute-start | bytes 417800 | tf_op jit(solution)/shard_map/ppermute | solution.py:103
  6.6 2.8 %collective-permute-start.2 = (bf16[32,2176]{1,0:T(8,128)(2,1)S(1)}, bf16[32,2176]{1,0:T(8,128)(2,1)S(1)}, u32[]{:S(2)}, u32[]{:S(2)}) collective-permute-start(bf16[32,2176]{1,0:T(8,128)(2,1)S(1)} %get-tuple-element.68), channel_id=1, source_target_pairs={{0,12},{4,16},{8,20},{12,24},{16,28},{20,0},{24,4},{28,8},{1,13},{... | collective-permute-start | bytes 417800 | tf_op jit(solution)/shard_map/ppermute | solution.py:103
  9.4 0.0 collective-permute-start.3
  9.5 0.1 scatter.15
  9.6 0.1 scatter.16
  9.7 0.1 scatter.19
  9.8 0.1 iota_add_fusion
  9.9 0.1 add.335
  10.0 0.8 %collective-permute-done = bf16[32,2176]{1,0:T(8,128)(2,1)S(1)} collective-permute-done((bf16[32,2176]{1,0:T(8,128)(2,1)S(1)}, bf16[32,2176]{1,0:T(8,128)(2,1)S(1)}, u32[]{:S(2)}, u32[]{:S(2)}) %collective-permute-start) | collective-permute-done | bytes 139296 | tf_op jit(solution)/shard_map/ppermute | solution.py:103
  10.7 5.7 %collective-permute-start.4 = (bf16[32,2176]{1,0:T(8,128)(2,1)S(1)}, bf16[32,2176]{1,0:T(8,128)(2,1)S(1)}, u32[]{:S(2)}, u32[]{:S(2)}) collective-permute-start(bf16[32,2176]{1,0:T(8,128)(2,1)S(1)} %get-tuple-element.70), channel_id=1, source_target_pairs={{0,20},{4,24},{8,28},{12,0},{16,4},{20,8},{24,12},{28,16},{1,21},{... | collective-permute-start | bytes 417800 | tf_op jit(solution)/shard_map/ppermute | solution.py:103
  16.5 7.6 %collective-permute-done.1 = bf16[32,2176]{1,0:T(8,128)(2,1)S(1)} collective-permute-done((bf16[32,2176]{1,0:T(8,128)(2,1)S(1)}, bf16[32,2176]{1,0:T(8,128)(2,1)S(1)}, u32[]{:S(2)}, u32[]{:S(2)}) %collective-permute-start.1) | collective-permute-done | bytes 139296 | tf_op jit(solution)/shard_map/ppermute | solution.py:103
  24.1 0.0 collective-permute-start.5
  24.1 3.0 %collective-permute-done.2 = bf16[32,2176]{1,0:T(8,128)(2,1)S(1)} collective-permute-done((bf16[32,2176]{1,0:T(8,128)(2,1)S(1)}, bf16[32,2176]{1,0:T(8,128)(2,1)S(1)}, u32[]{:S(2)}, u32[]{:S(2)}) %collective-permute-start.2) | collective-permute-done | bytes 139296 | tf_op jit(solution)/shard_map/ppermute | solution.py:103
  27.1 1.5 %collective-permute-done.3 = bf16[32,2176]{1,0:T(8,128)(2,1)S(1)} collective-permute-done((bf16[32,2176]{1,0:T(8,128)(2,1)S(1)}, bf16[32,2176]{1,0:T(8,128)(2,1)S(1)}, u32[]{:S(2)}, u32[]{:S(2)}) %collective-permute-start.3) | collective-permute-done | bytes 139296 | tf_op jit(solution)/shard_map/ppermute | solution.py:103
  28.6 0.0 collective-permute-done.4
  28.7 4.7 %collective-permute-done.5 = bf16[32,2176]{1,0:T(8,128)(2,1)S(1)} collective-permute-done((bf16[32,2176]{1,0:T(8,128)(2,1)S(1)}, bf16[32,2176]{1,0:T(8,128)(2,1)S(1)}, u32[]{:S(2)}, u32[]{:S(2)}) %collective-permute-start.5) | collective-permute-done | bytes 139296 | tf_op jit(solution)/shard_map/ppermute | solution.py:103
  33.4 0.0 collective-permute-done.6
  33.5 0.1 fusion.93
  33.6 0.1 copy.11
  33.7 0.1 copy.12
  33.9 0.1 fusion.81
  34.0 0.8 %fusion.9 = f32[256,2048]{1,0:T(8,128)S(1)} fusion(bf16[256,2176]{1,0:T(8,128)(2,1)S(1)} %bitcast.61, f32[256]{0:T(256)S(1)} %bitcast.81, s32[256]{0:T(256)S(1)} %get-tuple-element.117, f32[256]{0:T(256)S(1)} %bitcast.80, s32[256]{0:T(256)S(1)} %get-tuple-element.113, f32[256]{0:T(256)S(1)} %bitcast.79, s32[256]{0:T(256)S(1)} %get-tuple-element.114, ...), kind=kOutput, calls=%fused_computation.22 | convolution fusion | flops 271581184 | bytes 3180544 | tf_op jit(solution)/shard_map/dot_general | solution.py:161
  34.8 0.1 slice.305
  34.9 0.1 collective-permute-start.7
  35.0 1.9 %collective-permute-done.7 = bf16[128,2048]{1,0:T(8,128)(2,1)S(1)} collective-permute-done((bf16[128,2048]{1,0:T(8,128)(2,1)S(1)}, bf16[128,2048]{1,0:T(8,128)(2,1)S(1)}, u32[]{:S(2)}, u32[]{:S(2)}) %collective-permute-start.7) | collective-permute-done | bytes 524320 | tf_op jit(solution)/shard_map/ppermute | solution.py:92
  36.9 0.1 slice_add_fusion
  37.0 0.1 multiply_subtract_fusion.1
  37.1 1.6 %collective-permute-start.8 = (bf16[64,2048]{1,0:T(8,128)(2,1)S(1)}, bf16[64,2048]{1,0:T(8,128)(2,1)S(1)}, u32[]{:S(2)}, u32[]{:S(2)}) collective-permute-start(bf16[64,2048]{1,0:T(8,128)(2,1)S(1)} %slice.306), channel_id=1, source_target_pairs={{0,2},{1,3},{2,0},{3,1},{4,6},{5,7},{6,4},{7,5},{8,10},{9,11},{10,... | collective-permute-start | bytes 786440 | tf_op jit(solution)/shard_map/ppermute | solution.py:92
  38.7 1.1 %fusion.74 = (f32[1024,32]{0,1:T(8,128)S(1)}, f32[1024,32]{0,1:T(8,128)S(1)}, f32[1024,32]{0,1:T(8,128)S(1)}, f32[1024,32]{0,1:T(8,128)S(1)}) fusion(s32[32]{0:T(128)S(1)} %iota_multiply_fusion, s32[1024]{0:T(1024)S(1)} %iota.38), kind=kLoop, calls=%fused_computation.115 | loop fusion | flops 917504 | bytes 528512 | tf_op jit(solution)/shard_map/cos | solution.py:50
  39.7 1.2 %multiply_subtract_fusion = (f32[1024,32,32]{0,2,1:T(8,128)S(1)}, f32[1024,32,32]{0,2,1:T(8,128)S(1)}) fusion(f32[1024,32]{0,1:T(8,128)S(1)} %get-tuple-element.98, f32[1024,32]{0,1:T(8,128)S(1)} %get-tuple-element.95, f32[1024,32]{0,1:T(8,128)S(1)} %get-tuple-element.99, f32[1024,32]{0,1:T(8,128)S(1)} %get-tuple-element.94), kind=kLoop, calls=%fused_computation.9 | loop fusion | flops 6291456 | bytes 8912896 | tf_op jit(solution)/shard_map/sub | solution.py:52
  41.0 1.3 %fusion.5 = (bf16[1024,1024]{0,1:T(8,128)(2,1)S(1)}, bf16[1024,1024]{0,1:T(8,128)(2,1)S(1)}) fusion(f32[1024,32,32]{0,2,1:T(8,128)S(1)} %get-tuple-element.74, f32[1024]{0:T(1024)S(1)} %multiply_subtract_fusion.1, f32[1024,32,32]{0,2,1:T(8,128)S(1)} %get-tuple-element.75), kind=kLoop, calls=%fused_computation.7 | loop fusion | flops 4194304 | bytes 12587008 | tf_op jit(solution)/shard_map/convert
  42.2 3.3 %collective-permute-done.8 = bf16[64,2048]{1,0:T(8,128)(2,1)S(1)} collective-permute-done((bf16[64,2048]{1,0:T(8,128)(2,1)S(1)}, bf16[64,2048]{1,0:T(8,128)(2,1)S(1)}, u32[]{:S(2)}, u32[]{:S(2)}) %collective-permute-start.8) | collective-permute-done | bytes 262176 | tf_op jit(solution)/shard_map/ppermute | solution.py:92
  45.6 1.5 %fusion.6 = f32[128,1024]{1,0:T(8,128)S(1)} fusion(bf16[1024,1024]{0,1:T(8,128)(2,1)S(1)} %get-tuple-element.97, bf16[1024,1024]{0,1:T(8,128)(2,1)S(1)} %get-tuple-element.96, bf16[64,1024]{1,0:T(8,128)(2,1)S(1)} %get-tuple-element.77, bf16[64,1024]{1,0:T(8,128)(2,1)S(1)} %get-tuple-element.76, bf16[64,2048]{1,0:T(8,128)(2,1)S(1)} %add_convert_fusion), kind=kOutput, calls=%fused_computation.18 | convolution fusion | flops 546963456 | bytes 5242880 | tf_op jit(solution)/shard_map/dot_general | solution.py:175
  47.2 0.8 %pad_maximum_fusion = f32[64,2048]{1,0:T(8,128)} fusion(f32[64,1024]{1,0:T(8,128)S(1)} %get-tuple-element.73, f32[64,1024]{1,0:T(8,128)S(1)} %get-tuple-element.72), kind=kLoop, calls=%fused_computation.30 | loop fusion | flops 131072 | bytes 1048576 | tf_op jit(solution)/shard_map/concatenate | solution.py:177
  (29 shorter events, 0.5 us)
Async XLA Ops:
  0.0 1.5 %copy-start = (bf16[1,128,2048]{2,1,0:T(8,128)(2,1)S(1)}, bf16[1,128,2048]{2,1,0:T(8,128)(2,1)}, u32[]{:S(2)}) copy-start(bf16[1,128,2048]{2,1,0:T(8,128)(2,1)} %param.13) | copy-start | bytes 1572868
  2.1 31.4 %collective-permute-start.6 = (bf16[32,2176]{1,0:T(8,128)(2,1)S(1)}, bf16[32,2176]{1,0:T(8,128)(2,1)S(1)}, u32[]{:S(2)}, u32[]{:S(2)}) collective-permute-start(bf16[32,2176]{1,0:T(8,128)(2,1)S(1)} %get-tuple-element.65), channel_id=1, source_target_pairs={{0,28},{4,0},{8,4},{12,8},{16,12},{20,16},{24,20},{28,24},{1,29},{... | collective-permute-start | bytes 417800 | tf_op jit(solution)/shard_map/ppermute | solution.py:103
  2.6 8.1 %collective-permute-start = (bf16[32,2176]{1,0:T(8,128)(2,1)S(1)}, bf16[32,2176]{1,0:T(8,128)(2,1)S(1)}, u32[]{:S(2)}, u32[]{:S(2)}) collective-permute-start(bf16[32,2176]{1,0:T(8,128)(2,1)S(1)} %get-tuple-element.66), channel_id=1, source_target_pairs={{0,4},{4,8},{8,12},{12,16},{16,20},{20,24},{24,28},{28,0},{1,5},{5... | collective-permute-start | bytes 417800 | tf_op jit(solution)/shard_map/ppermute | solution.py:103
  5.0 19.0 %collective-permute-start.1 = (bf16[32,2176]{1,0:T(8,128)(2,1)S(1)}, bf16[32,2176]{1,0:T(8,128)(2,1)S(1)}, u32[]{:S(2)}, u32[]{:S(2)}) collective-permute-start(bf16[32,2176]{1,0:T(8,128)(2,1)S(1)} %get-tuple-element.67), channel_id=1, source_target_pairs={{0,8},{4,12},{8,16},{12,20},{16,24},{20,28},{24,0},{28,4},{1,9},{5... | collective-permute-start | bytes 417800 | tf_op jit(solution)/shard_map/ppermute | solution.py:103
  6.6 20.5 %collective-permute-start.2 = (bf16[32,2176]{1,0:T(8,128)(2,1)S(1)}, bf16[32,2176]{1,0:T(8,128)(2,1)S(1)}, u32[]{:S(2)}, u32[]{:S(2)}) collective-permute-start(bf16[32,2176]{1,0:T(8,128)(2,1)S(1)} %get-tuple-element.68), channel_id=1, source_target_pairs={{0,12},{4,16},{8,20},{12,24},{16,28},{20,0},{24,4},{28,8},{1,13},{... | collective-permute-start | bytes 417800 | tf_op jit(solution)/shard_map/ppermute | solution.py:103
  9.4 19.2 %collective-permute-start.3 = (bf16[32,2176]{1,0:T(8,128)(2,1)S(1)}, bf16[32,2176]{1,0:T(8,128)(2,1)S(1)}, u32[]{:S(2)}, u32[]{:S(2)}) collective-permute-start(bf16[32,2176]{1,0:T(8,128)(2,1)S(1)} %get-tuple-element.69), channel_id=1, source_target_pairs={{0,16},{4,20},{8,24},{12,28},{16,0},{20,4},{24,8},{28,12},{1,17},{... | collective-permute-start | bytes 417800 | tf_op jit(solution)/shard_map/ppermute | solution.py:103
  10.7 17.9 %collective-permute-start.4 = (bf16[32,2176]{1,0:T(8,128)(2,1)S(1)}, bf16[32,2176]{1,0:T(8,128)(2,1)S(1)}, u32[]{:S(2)}, u32[]{:S(2)}) collective-permute-start(bf16[32,2176]{1,0:T(8,128)(2,1)S(1)} %get-tuple-element.70), channel_id=1, source_target_pairs={{0,20},{4,24},{8,28},{12,0},{16,4},{20,8},{24,12},{28,16},{1,21},{... | collective-permute-start | bytes 417800 | tf_op jit(solution)/shard_map/ppermute | solution.py:103
  24.1 9.3 %collective-permute-start.5 = (bf16[32,2176]{1,0:T(8,128)(2,1)S(1)}, bf16[32,2176]{1,0:T(8,128)(2,1)S(1)}, u32[]{:S(2)}, u32[]{:S(2)}) collective-permute-start(bf16[32,2176]{1,0:T(8,128)(2,1)S(1)} %get-tuple-element.71), channel_id=1, source_target_pairs={{0,24},{4,28},{8,0},{12,4},{16,8},{20,12},{24,16},{28,20},{1,25},{... | collective-permute-start | bytes 417800 | tf_op jit(solution)/shard_map/ppermute | solution.py:103
  34.9 2.0 %collective-permute-start.7 = (bf16[128,2048]{1,0:T(8,128)(2,1)S(1)}, bf16[128,2048]{1,0:T(8,128)(2,1)S(1)}, u32[]{:S(2)}, u32[]{:S(2)}) collective-permute-start(bf16[128,2048]{1,0:T(8,128)(2,1)S(1)} %slice.305), channel_id=1, source_target_pairs={{0,1},{1,0},{2,3},{3,2},{4,5},{5,4},{6,7},{7,6},{8,9},{9,8},{10,11... | collective-permute-start | bytes 1572872 | tf_op jit(solution)/shard_map/ppermute | solution.py:92
  37.1 8.4 %collective-permute-start.8 = (bf16[64,2048]{1,0:T(8,128)(2,1)S(1)}, bf16[64,2048]{1,0:T(8,128)(2,1)S(1)}, u32[]{:S(2)}, u32[]{:S(2)}) collective-permute-start(bf16[64,2048]{1,0:T(8,128)(2,1)S(1)} %slice.306), channel_id=1, source_target_pairs={{0,2},{1,3},{2,0},{3,1},{4,6},{5,7},{6,4},{7,5},{8,10},{9,11},{10,... | collective-permute-start | bytes 786440 | tf_op jit(solution)/shard_map/ppermute | solution.py:92

commit v16 on v14

--- a/solution.py
+++ b/solution.py
@@ -3,6 +3,7 @@
 import jax
 import jax.numpy as jnp
 from jax import lax
+from jax.experimental import pallas as pl
 from jax.sharding import PartitionSpec as P
 
 NCH = 1024
@@ -61,9 +62,30 @@
     )
     tap_cos = (taper[:, None, None] * cosine).reshape(NCH, NCH)
     tap_sin = (taper[:, None, None] * sine).reshape(NCH, NCH)
-    upper = jnp.concatenate([tap_cos, -tap_sin], axis=1)
-    lower = jnp.concatenate([tap_sin, tap_cos], axis=1)
-    return jnp.concatenate([upper, lower], axis=0).astype(jnp.bfloat16)
+    return jnp.concatenate([tap_cos, tap_sin], axis=0).astype(jnp.bfloat16)
+
+
+def final_transform(grid, halves, scale):
+    cells = grid.shape[0]
+    half = halves.shape[1]
+
+    def kernel(g_ref, h_ref, o_ref):
+        grid_re = g_ref[:, :half]
+        grid_im = g_ref[:, half:]
+        tap_cos = h_ref[:half, :]
+        tap_sin = h_ref[half:, :]
+        real = jnp.dot(grid_re, tap_cos, preferred_element_type=jnp.float32) + jnp.dot(
+            grid_im, tap_sin, preferred_element_type=jnp.float32
+        )
+        imag = jnp.dot(grid_im, tap_cos, preferred_element_type=jnp.float32) - jnp.dot(
+            grid_re, tap_sin, preferred_element_type=jnp.float32
+        )
+        o_ref[:, :half] = real * scale
+        o_ref[:, half:] = imag * scale
+
+    return pl.pallas_call(
+        kernel, out_shape=jax.ShapeDtypeStruct((cells, 2 * half), jnp.float32)
+    )(grid, halves)
 
 
 def halving_order(tm_index, time_groups, cell_share):
@@ -168,7 +190,7 @@
         summed = lax.psum_scatter(partial, "tm", scatter_dimension=0, tiled=True)
     grid = summed.astype(jnp.bfloat16)
     out_scale = 4.0 / math.sqrt(NCH * time_groups * ROWS_DEV)
-    return jnp.dot(grid, delay_halves(), preferred_element_type=jnp.float32) * out_scale
+    return final_transform(grid, delay_halves(), out_scale)
 
 
 def solution(mesh):

time: 47.1 us -> 74.7 us (1.59)
  local copies, waits for them, and re-layouts: 1.17 us -> 18.4 us
  other arithmetic: 5.44 us -> 16.1 us
  waiting for transfers between devices: 24.8 us -> 18.4 us
  Pallas kernels: 0 us -> 4.64 us
  starting transfers between devices: 10.3 us -> 13.7 us
  matrix products: 5.05 us -> 2.86 us
    ppermute x7, waiting for transfers between devices: 19.1 us -> 13.6 us  [uv_exchange(): pieces.append(lax.ppermute(outgoing[shift], 'uv', perm))]
    sub x0 -> x1, local copies, waits for them, and re-layouts: none -> 5.41 us  [delay_halves(): c_hi[:, :, None] * c_lo[:, None, :] - s_hi[:, :, None] * s_lo[:, None, :]]
    add x0 -> x1, local copies, waits for them, and re-layouts: none -> 5.37 us  [delay_halves(): s_hi[:, :, None] * c_lo[:, None, :] + c_hi[:, :, None] * s_lo[:, None, :]]
    pallas_call x0 -> x1, Pallas kernels: none -> 4.64 us  [final_transform(): pl.pallas_call(kernel, out_shape=jax.ShapeDtypeStruct((cells, 2 * half),...]
    sub x0 -> x1, other arithmetic: none -> 4.48 us  [delay_halves(): c_hi[:, :, None] * c_lo[:, None, :] - s_hi[:, :, None] * s_lo[:, None, :]]
    unnamed x10, local copies, waits for them, and re-layouts: 0.28 us -> 4.18 us
    ppermute x7, starting transfers between devices: 8.62 us -> 12.1 us  [uv_exchange(): pieces.append(lax.ppermute(outgoing[shift], 'uv', perm))]
    dot_general x1 -> x0, matrix products: 3.46 us -> none  [per_device(): jnp.dot(grid, delay_halves(), preferred_element_type=jnp.float32)]
  transfers between devices with their start and end apart: 9 -> 9, of which waited for: 7 -> 5; matrix products, arithmetic and copies ran while one was open for 10% -> 38% of each run, Pallas kernels for 0% -> 0%
where the time goes in v16:
time: 74.7 us; the launch traced here: 74.3 us
  local copies, waits for them, and re-layouts  18.4 us (25%)
  waiting for transfers between devices  18.4 us (25%)
  other arithmetic  16.1 us (22%)
  starting transfers between devices  13.7 us (18%)
  Pallas kernels  4.64 us (6%)
  matrix products  2.86 us (4%)
    ppermute x7, waiting for transfers between devices, uv_exchange(): pieces.append(lax.ppermute(outgoing[shift], 'uv', perm))  13.6 us
    ppermute x7, starting transfers between devices, uv_exchange(): pieces.append(lax.ppermute(outgoing[shift], 'uv', perm))  12.1 us
    sub x1, local copies, waits for them, and re-layouts, delay_halves(): c_hi[:, :, None] * c_lo[:, None, :] - s_hi[:, :, None] * s_lo[:, None, :]  5.41 us
    add x1, local copies, waits for them, and re-layouts, delay_halves(): s_hi[:, :, None] * c_lo[:, None, :] + c_hi[:, :, None] * s_lo[:, None, :]  5.37 us
    ppermute x2, waiting for transfers between devices, halving_reduce(): received = lax.ppermute(outgoing, 'tm', perm)  4.81 us
    pallas_call x1, Pallas kernels, final_transform(): pl.pallas_call(kernel, out_shape=jax.ShapeDtypeStruct((cells, 2 * half),...  4.64 us
    sub x1, other arithmetic, delay_halves(): c_hi[:, :, None] * c_lo[:, None, :] - s_hi[:, :, None] * s_lo[:, None, :]  4.48 us
    unnamed x10, local copies, waits for them, and re-layouts  4.18 us
  transfers between devices with their start and end apart: 9, of which 5 were waited for; matrix products, arithmetic and copies ran while one was open for 38% of the time, Pallas kernels for 0%

profile of v16, /device:TPU:12, one launch (start us, length us, event | category | flops | bytes accessed | tf_op | source)
XLA Modules:
  0.0 74.3 jit_solution(1991968771599480417)
XLA Ops:
  0.0 0.0 copy-start
  0.0 0.8 %fusion.75 = s32[11,128]{1,0:T(8,128)S(1)} fusion(s32[1,8]{1,0:T(1,128)} %bitcast.79, s32[8,32]{1,0:T(8,128)} %bitcast.58, s32[1,128]{1,0:T(1,128)} %param.15, s32[1,128]{1,0:T(1,128)} %param.14), kind=kLoop, calls=%fused_computation.117 | loop fusion | flops 4224 | bytes 7712 | tf_op jit(solution)/shard_map/concatenate | solution.py:144
  0.8 0.1 eq.83
  0.9 0.1 pad_add_fusion.1
  1.0 0.1 dynamic_slice.7
  1.1 0.1 iota_compare_fusion.1
  1.1 0.1 lt.56
  1.2 0.3 convolution_convert_fusion.1
  1.5 0.0 copy-done
  1.5 0.5 convolution_convert_fusion
  2.0 0.1 pad_maximum_fusion.1
  2.1 0.6 collective-permute-start.6
  2.6 2.4 %collective-permute-start = (bf16[32,2176]{1,0:T(8,128)(2,1)S(1)}, bf16[32,2176]{1,0:T(8,128)(2,1)S(1)}, u32[]{:S(2)}, u32[]{:S(2)}) collective-permute-start(bf16[32,2176]{1,0:T(8,128)(2,1)S(1)} %get-tuple-element.62), channel_id=1, source_target_pairs={{0,4},{4,8},{8,12},{12,16},{16,20},{20,24},{24,28},{28,0},{1,5},{5... | collective-permute-start | bytes 417800 | tf_op jit(solution)/shard_map/ppermute | solution.py:128
  5.0 1.6 %collective-permute-start.1 = (bf16[32,2176]{1,0:T(8,128)(2,1)S(1)}, bf16[32,2176]{1,0:T(8,128)(2,1)S(1)}, u32[]{:S(2)}, u32[]{:S(2)}) collective-permute-start(bf16[32,2176]{1,0:T(8,128)(2,1)S(1)} %get-tuple-element.63), channel_id=1, source_target_pairs={{0,8},{4,12},{8,16},{12,20},{16,24},{20,28},{24,0},{28,4},{1,9},{5... | collective-permute-start | bytes 417800 | tf_op jit(solution)/shard_map/ppermute | solution.py:128
  6.6 2.8 %collective-permute-start.2 = (bf16[32,2176]{1,0:T(8,128)(2,1)S(1)}, bf16[32,2176]{1,0:T(8,128)(2,1)S(1)}, u32[]{:S(2)}, u32[]{:S(2)}) collective-permute-start(bf16[32,2176]{1,0:T(8,128)(2,1)S(1)} %get-tuple-element.64), channel_id=1, source_target_pairs={{0,12},{4,16},{8,20},{12,24},{16,28},{20,0},{24,4},{28,8},{1,13},{... | collective-permute-start | bytes 417800 | tf_op jit(solution)/shard_map/ppermute | solution.py:128
  9.4 0.0 collective-permute-start.3
  9.4 0.7 bitcast_dynamic-update-slice_fusion.7
  10.1 0.1 scatter.15
  10.2 0.1 scatter.16
  10.3 0.1 scatter.19
  10.4 0.1 iota_add_fusion
  10.5 0.1 add.345
  10.6 0.6 fusion.64
  11.2 0.5 fusion.61
  11.7 0.0 collective-permute-done
  11.7 4.7 %collective-permute-start.4 = (bf16[32,2176]{1,0:T(8,128)(2,1)S(1)}, bf16[32,2176]{1,0:T(8,128)(2,1)S(1)}, u32[]{:S(2)}, u32[]{:S(2)}) collective-permute-start(bf16[32,2176]{1,0:T(8,128)(2,1)S(1)} %get-tuple-element.66), channel_id=1, source_target_pairs={{0,20},{4,24},{8,28},{12,0},{16,4},{20,8},{24,12},{28,16},{1,21},{... | collective-permute-start | bytes 417800 | tf_op jit(solution)/shard_map/ppermute | solution.py:128
  16.5 0.7 bitcast_dynamic-update-slice_fusion.6
  17.1 6.9 %collective-permute-done.1 = bf16[32,2176]{1,0:T(8,128)(2,1)S(1)} collective-permute-done((bf16[32,2176]{1,0:T(8,128)(2,1)S(1)}, bf16[32,2176]{1,0:T(8,128)(2,1)S(1)}, u32[]{:S(2)}, u32[]{:S(2)}) %collective-permute-start.1) | collective-permute-done | bytes 139296 | tf_op jit(solution)/shard_map/ppermute | solution.py:128
  24.1 0.0 collective-permute-start.5
  24.1 0.7 bitcast_dynamic-update-slice_fusion.5
  24.7 2.3 %collective-permute-done.2 = bf16[32,2176]{1,0:T(8,128)(2,1)S(1)} collective-permute-done((bf16[32,2176]{1,0:T(8,128)(2,1)S(1)}, bf16[32,2176]{1,0:T(8,128)(2,1)S(1)}, u32[]{:S(2)}, u32[]{:S(2)}) %collective-permute-start.2) | collective-permute-done | bytes 139296 | tf_op jit(solution)/shard_map/ppermute | solution.py:128
  27.1 0.7 bitcast_dynamic-update-slice_fusion.4
  27.7 0.9 %collective-permute-done.3 = bf16[32,2176]{1,0:T(8,128)(2,1)S(1)} collective-permute-done((bf16[32,2176]{1,0:T(8,128)(2,1)S(1)}, bf16[32,2176]{1,0:T(8,128)(2,1)S(1)}, u32[]{:S(2)}, u32[]{:S(2)}) %collective-permute-start.3) | collective-permute-done | bytes 139296 | tf_op jit(solution)/shard_map/ppermute | solution.py:128
  28.6 0.7 bitcast_dynamic-update-slice_fusion.3
  29.3 0.0 collective-permute-done.4
  29.3 0.7 bitcast_dynamic-update-slice_fusion.2
  30.0 3.5 %collective-permute-done.5 = bf16[32,2176]{1,0:T(8,128)(2,1)S(1)} collective-permute-done((bf16[32,2176]{1,0:T(8,128)(2,1)S(1)}, bf16[32,2176]{1,0:T(8,128)(2,1)S(1)}, u32[]{:S(2)}, u32[]{:S(2)}) %collective-permute-start.5) | collective-permute-done | bytes 139296 | tf_op jit(solution)/shard_map/ppermute | solution.py:128
  33.4 0.7 bitcast_dynamic-update-slice_fusion.1
  34.1 0.0 collective-permute-done.6
  34.1 0.7 bitcast_dynamic-update-slice_fusion
  34.8 1.0 %fusion.82 = (bf16[256,1]{1,0:T(8,128)(2,1)S(1)}, bf16[256,1]{1,0:T(8,128)(2,1)S(1)}) fusion(bf16[256,2176]{1,0:T(8,128)(2,1)} %bitcast.56), kind=kLoop, calls=%fused_computation.169 | loop fusion | bytes 2048 | tf_op jit(solution)/shard_map/slice | solution.py:177
  35.8 0.1 copy.13
  35.9 0.1 copy.14
  36.1 0.1 fusion.71
  36.2 2.1 %fusion = f32[256,2048]{1,0:T(8,128)S(1)} fusion(bf16[256,2176]{1,0:T(8,128)(2,1)} %bitcast.57, f32[256]{0:T(256)S(1)} %bitcast.77, s32[256]{0:T(256)S(1)} %get-tuple-element.105, f32[256]{0:T(256)S(1)} %bitcast.76, s32[256]{0:T(256)S(1)} %get-tuple-element.101, f32[256]{0:T(256)S(1)} %bitcast.75, s32[256]{0:T(256)S(1)} %get-tuple-element.102, ...), kind=kOutput, calls=%fused_computation.15 | convolution fusion | flops 271581184 | bytes 3180544 | tf_op jit(solution)/shard_map/dot_general | solution.py:186
  38.3 1.1 %slice.227 = f32[128,2048]{1,0:T(8,128)} slice(f32[256,2048]{1,0:T(8,128)S(1)} %fusion), slice={[0:128], [0:2048]} | slice | bytes 2097152 | tf_op jit(solution)/shard_map/slice | solution.py:114
  39.4 0.0 collective-permute-start.7
  39.4 4.5 %multiply_subtract_fusion = (f32[1024,32,32]{0,2,1:T(8,128)}, f32[1024,32,32]{0,2,1:T(8,128)}) fusion(f32[1024,32]{0,1:T(8,128)S(1)} %get-tuple-element.124, f32[1024,32]{0,1:T(8,128)S(1)} %get-tuple-element.107, f32[1024,32]{0,1:T(8,128)S(1)} %get-tuple-element.125, f32[1024,32]{0,1:T(8,128)S(1)} %get-tuple-element.106), kind=kLoop, calls=%fused_computation.4 | loop fusion | flops 6291456 | bytes 8912896 | tf_op jit(solution)/shard_map/sub | solution.py:54
  43.9 5.4 %copy.10 = f32[1024,1024]{1,0:T(8,128)} copy(f32[1024,1024]{0,1:T(8,128)} %bitcast.55) | data formatting | bytes 8388608 | tf_op jit(solution)/shard_map/sub | solution.py:54
  49.3 5.4 %copy.11 = f32[1024,1024]{1,0:T(8,128)} copy(f32[1024,1024]{0,1:T(8,128)} %bitcast.54) | data formatting | bytes 8388608 | tf_op jit(solution)/shard_map/add | solution.py:55
  54.7 0.1 multiply_subtract_fusion.1
  54.8 4.0 %multiply_convert_fusion.1 = (bf16[1024,1024]{1,0:T(8,128)(2,1)S(1)}, bf16[1024,1024]{1,0:T(8,128)(2,1)S(1)}) fusion(f32[1024,1024]{1,0:T(8,128)} %copy.10, f32[1024]{0:T(1024)S(1)} %multiply_subtract_fusion.1, f32[1024,1024]{1,0:T(8,128)} %copy.11), kind=kLoop, calls=%fused_computation.3 | loop fusion | flops 4194304 | bytes 12587008 | tf_op jit(solution)/shard_map/convert
  58.8 0.0 collective-permute-done.7
  58.8 1.3 %slice_add_fusion = f32[128,2048]{1,0:T(8,128)S(1)} fusion(f32[128,2048]{1,0:T(8,128)} %collective-permute-done.7, f32[256,2048]{1,0:T(8,128)S(1)} %fusion), kind=kLoop, calls=%fused_computation.14 | loop fusion | flops 262144 | bytes 3145728 | tf_op jit(solution)/shard_map/add | solution.py:118
  60.1 1.6 %collective-permute-start.8 = (bf16[64,2048]{1,0:T(8,128)(2,1)S(1)}, bf16[64,2048]{1,0:T(8,128)(2,1)S(1)}, u32[]{:S(2)}, u32[]{:S(2)}) collective-permute-start(bf16[64,2048]{1,0:T(8,128)(2,1)S(1)} %slice.285), channel_id=1, source_target_pairs={{0,2},{1,3},{2,0},{3,1},{4,6},{5,7},{6,4},{7,5},{8,10},{9,11},{10,... | collective-permute-start | bytes 786440 | tf_op jit(solution)/shard_map/ppermute | solution.py:117
  61.7 2.4 %pad_maximum_fusion.h_ref = bf16[2048,1024]{1,0:T(8,128)(2,1)} fusion(bf16[1024,1024]{1,0:T(8,128)(2,1)S(1)} %get-tuple-element.87, bf16[1024,1024]{1,0:T(8,128)(2,1)S(1)} %get-tuple-element.86), kind=kLoop, calls=%fused_computation | loop fusion | flops 8388608 | bytes 8388608 | tf_op jit(solution)/shard_map/concatenate | solution.py:65
  64.1 4.8 %collective-permute-done.8 = bf16[64,2048]{1,0:T(8,128)(2,1)S(1)} collective-permute-done((bf16[64,2048]{1,0:T(8,128)(2,1)S(1)}, bf16[64,2048]{1,0:T(8,128)(2,1)S(1)}, u32[]{:S(2)}, u32[]{:S(2)}) %collective-permute-start.8) | collective-permute-done | bytes 262176 | tf_op jit(solution)/shard_map/ppermute | solution.py:117
  68.9 0.8 %fusion.2.g_ref = bf16[64,2048]{1,0:T(8,128)(2,1)} fusion(f32[128,2048]{1,0:T(8,128)S(1)} %slice_add_fusion, bf16[64,2048]{1,0:T(8,128)(2,1)S(1)} %collective-permute-done.8), kind=kLoop, calls=%fused_computation.19 | loop fusion | flops 393216 | bytes 1048576 | tf_op jit(solution)/shard_map/convert_element_type | solution.py:191
  69.7 4.6 %shard_map.55 = f32[64,2048]{1,0:T(8,128)} custom-call(bf16[64,2048]{1,0:T(8,128)(2,1)} %fusion.2.g_ref, bf16[2048,1024]{1,0:T(8,128)(2,1)} %pad_maximum_fusion.h_ref), custom_call_target="tpu_custom_call" | custom-call | tf_op jit(solution)/shard_map/pallas_call | solution.py:86
  (17 shorter events, 0.2 us)
Async XLA Ops:
  0.0 1.5 %copy-start = (bf16[1,128,2048]{2,1,0:T(8,128)(2,1)S(1)}, bf16[1,128,2048]{2,1,0:T(8,128)(2,1)}, u32[]{:S(2)}) copy-start(bf16[1,128,2048]{2,1,0:T(8,128)(2,1)} %param.13) | copy-start | bytes 1572868
  2.1 32.0 %collective-permute-start.6 = (bf16[32,2176]{1,0:T(8,128)(2,1)S(1)}, bf16[32,2176]{1,0:T(8,128)(2,1)S(1)}, u32[]{:S(2)}, u32[]{:S(2)}) collective-permute-start(bf16[32,2176]{1,0:T(8,128)(2,1)S(1)} %get-tuple-element.61), channel_id=1, source_target_pairs={{0,28},{4,0},{8,4},{12,8},{16,12},{20,16},{24,20},{28,24},{1,29},{... | collective-permute-start | bytes 417800 | tf_op jit(solution)/shard_map/ppermute | solution.py:128
  2.6 9.1 %collective-permute-start = (bf16[32,2176]{1,0:T(8,128)(2,1)S(1)}, bf16[32,2176]{1,0:T(8,128)(2,1)S(1)}, u32[]{:S(2)}, u32[]{:S(2)}) collective-permute-start(bf16[32,2176]{1,0:T(8,128)(2,1)S(1)} %get-tuple-element.62), channel_id=1, source_target_pairs={{0,4},{4,8},{8,12},{12,16},{16,20},{20,24},{24,28},{28,0},{1,5},{5... | collective-permute-start | bytes 417800 | tf_op jit(solution)/shard_map/ppermute | solution.py:128
  5.0 19.0 %collective-permute-start.1 = (bf16[32,2176]{1,0:T(8,128)(2,1)S(1)}, bf16[32,2176]{1,0:T(8,128)(2,1)S(1)}, u32[]{:S(2)}, u32[]{:S(2)}) collective-permute-start(bf16[32,2176]{1,0:T(8,128)(2,1)S(1)} %get-tuple-element.63), channel_id=1, source_target_pairs={{0,8},{4,12},{8,16},{12,20},{16,24},{20,28},{24,0},{28,4},{1,9},{5... | collective-permute-start | bytes 417800 | tf_op jit(solution)/shard_map/ppermute | solution.py:128
  6.6 20.5 %collective-permute-start.2 = (bf16[32,2176]{1,0:T(8,128)(2,1)S(1)}, bf16[32,2176]{1,0:T(8,128)(2,1)S(1)}, u32[]{:S(2)}, u32[]{:S(2)}) collective-permute-start(bf16[32,2176]{1,0:T(8,128)(2,1)S(1)} %get-tuple-element.64), channel_id=1, source_target_pairs={{0,12},{4,16},{8,20},{12,24},{16,28},{20,0},{24,4},{28,8},{1,13},{... | collective-permute-start | bytes 417800 | tf_op jit(solution)/shard_map/ppermute | solution.py:128
  9.4 19.2 %collective-permute-start.3 = (bf16[32,2176]{1,0:T(8,128)(2,1)S(1)}, bf16[32,2176]{1,0:T(8,128)(2,1)S(1)}, u32[]{:S(2)}, u32[]{:S(2)}) collective-permute-start(bf16[32,2176]{1,0:T(8,128)(2,1)S(1)} %get-tuple-element.65), channel_id=1, source_target_pairs={{0,16},{4,20},{8,24},{12,28},{16,0},{20,4},{24,8},{28,12},{1,17},{... | collective-permute-start | bytes 417800 | tf_op jit(solution)/shard_map/ppermute | solution.py:128
  11.7 17.6 %collective-permute-start.4 = (bf16[32,2176]{1,0:T(8,128)(2,1)S(1)}, bf16[32,2176]{1,0:T(8,128)(2,1)S(1)}, u32[]{:S(2)}, u32[]{:S(2)}) collective-permute-start(bf16[32,2176]{1,0:T(8,128)(2,1)S(1)} %get-tuple-element.66), channel_id=1, source_target_pairs={{0,20},{4,24},{8,28},{12,0},{16,4},{20,8},{24,12},{28,16},{1,21},{... | collective-permute-start | bytes 417800 | tf_op jit(solution)/shard_map/ppermute | solution.py:128
  24.1 9.3 %collective-permute-start.5 = (bf16[32,2176]{1,0:T(8,128)(2,1)S(1)}, bf16[32,2176]{1,0:T(8,128)(2,1)S(1)}, u32[]{:S(2)}, u32[]{:S(2)}) collective-permute-start(bf16[32,2176]{1,0:T(8,128)(2,1)S(1)} %get-tuple-element.67), channel_id=1, source_target_pairs={{0,24},{4,28},{8,0},{12,4},{16,8},{20,12},{24,16},{28,20},{1,25},{... | collective-permute-start | bytes 417800 | tf_op jit(solution)/shard_map/ppermute | solution.py:128
  39.4 19.3 %collective-permute-start.7 = (f32[128,2048]{1,0:T(8,128)}, f32[128,2048]{1,0:T(8,128)}, u32[]{:S(2)}, u32[]{:S(2)}) collective-permute-start(f32[128,2048]{1,0:T(8,128)} %slice.227), channel_id=1, source_target_pairs={{0,1},{1,0},{2,3},{3,2},{4,5},{5,4},{6,7},{7,6},{8,9},{9,8},{10,11... | collective-permute-start | bytes 3145736 | tf_op jit(solution)/shard_map/ppermute | solution.py:117
  60.1 8.8 %collective-permute-start.8 = (bf16[64,2048]{1,0:T(8,128)(2,1)S(1)}, bf16[64,2048]{1,0:T(8,128)(2,1)S(1)}, u32[]{:S(2)}, u32[]{:S(2)}) collective-permute-start(bf16[64,2048]{1,0:T(8,128)(2,1)S(1)} %slice.285), channel_id=1, source_target_pairs={{0,2},{1,3},{2,0},{3,1},{4,6},{5,7},{6,4},{7,5},{8,10},{9,11},{10,... | collective-permute-start | bytes 786440 | tf_op jit(solution)/shard_map/ppermute | solution.py:117

commit v17 on v12

--- a/solution.py
+++ b/solution.py
@@ -134,32 +134,56 @@
         live_count = lax.dynamic_slice_in_dim(
             jnp.concatenate([live_count, live_count], axis=0), uv_index, tile_count, 0
         )
-    is_live = (jnp.arange(slot_depth, dtype=jnp.int32)[None, :] < live_count[:, None]).reshape(-1)
-    flat_index = slot_table.reshape(-1)
-    pick = (
-        (flat_index[:, None] == jnp.arange(row_count, dtype=jnp.int32)[None, :]) & is_live[:, None]
-    ).astype(jnp.bfloat16)
-    picked = jnp.dot(pick, vis_rows, preferred_element_type=jnp.float32).astype(jnp.bfloat16)
+    is_live = jnp.arange(slot_depth, dtype=jnp.int32)[None, :] < live_count[:, None]
+    pair_index = slot_table.reshape(-1, 2)
+    pair_live = is_live.reshape(-1, 2)
+    rows_iota = jnp.arange(row_count, dtype=jnp.int32)[None, :]
+    picks = [
+        ((pair_index[:, h:h + 1] == rows_iota) & pair_live[:, h:h + 1]).astype(jnp.bfloat16)
+        for h in range(2)
+    ]
+    picked = [
+        jnp.dot(pick, vis_rows, preferred_element_type=jnp.float32).astype(jnp.bfloat16)
+        for pick in picks
+    ]
+    zero_rows = jnp.zeros((2, row_count), jnp.int32)
     meta_rows = jnp.concatenate(
-        [anchor_row[None, :], offset_row[None, :], jnp.zeros((META - 2, row_count), jnp.int32)],
-        axis=0,
+        [
+            jnp.concatenate(
+                [anchor_row[None, :], offset_row[None, :], zero_rows,
+                 jnp.zeros((META - 4, row_count), jnp.int32)], axis=0
+            ),
+            jnp.concatenate(
+                [zero_rows, anchor_row[None, :], offset_row[None, :],
+                 jnp.zeros((META - 4, row_count), jnp.int32)], axis=0
+            ),
+        ],
+        axis=1,
     ).astype(jnp.bfloat16)
     meta = lax.dot_general(
-        pick, meta_rows, (((1,), (1,)), ((), ())), preferred_element_type=jnp.float32
+        jnp.concatenate(picks, axis=1), meta_rows, (((1,), (1,)), ((), ())),
+        preferred_element_type=jnp.float32,
     ).astype(jnp.bfloat16)
-    outgoing = jnp.concatenate([picked, meta], axis=1).reshape(tile_count, slot_depth, row_width + META)
+    pair_depth = slot_depth // 2
+    width = 2 * row_width + META
+    outgoing = jnp.concatenate(picked + [meta], axis=1).reshape(tile_count, pair_depth, width)
     arrived = uv_exchange(outgoing, uv_size)
-    arrived = arrived.reshape(-1, row_width + META)
-    arr_anchor = arrived[:, row_width].astype(jnp.int32)
-    arr_offset = arrived[:, row_width + 1].astype(jnp.int32)
+    arrived = arrived.reshape(-1, width)
     tm_index = lax.axis_index("tm")
     pow2 = time_groups & (time_groups - 1) == 0
     if pow2:
         cells = halving_order(tm_index, time_groups, cell_share)
     else:
         cells = jnp.arange(TS * TS, dtype=jnp.int32)
-    weights = tap_matrix(cells, arr_anchor, arr_offset)
-    partial = jnp.dot(weights, arrived[:, :row_width], preferred_element_type=jnp.float32)
+    partial = None
+    for h in range(2):
+        arr_anchor = arrived[:, 2 * row_width + 2 * h].astype(jnp.int32)
+        arr_offset = arrived[:, 2 * row_width + 2 * h + 1].astype(jnp.int32)
+        weights = tap_matrix(cells, arr_anchor, arr_offset)
+        part = jnp.dot(
+            weights, arrived[:, h * row_width:(h + 1) * row_width], preferred_element_type=jnp.float32
+        )
+        partial = part if partial is None else partial + part
     if pow2:
         summed = halving_reduce(partial, time_groups)
     else:

time: 46 us -> 46.7 us (1.015)
  waiting for transfers between devices: 25.1 us -> 24.4 us
  local copies, waits for them, and re-layouts: 1.21 us -> 1.8 us
  matrix products: 3.1 us -> 3.63 us
    ppermute x7, waiting for transfers between devices: 19.1 us -> 18.4 us  [uv_exchange(): pieces.append(lax.ppermute(outgoing[shift], 'uv', perm))]
    dot_general x2 -> x3, matrix products: 1.1 us -> 1.44 us  [the longest x2 1.26 us: per_device(): jnp.dot(weights, arrived[:, h * row_width:(h + 1) * row_width], preferred...]
where the time goes in v17:
time: 46.7 us; the launch traced here: 46.6 us
  waiting for transfers between devices  24.4 us (52%)
  starting transfers between devices  10.2 us (22%)
  other arithmetic  6.16 us (13%)
  matrix products  3.63 us (8%)
  local copies, waits for them, and re-layouts  1.8 us (4%)
    ppermute x7, waiting for transfers between devices, uv_exchange(): pieces.append(lax.ppermute(outgoing[shift], 'uv', perm))  18.4 us
    ppermute x7, starting transfers between devices, uv_exchange(): pieces.append(lax.ppermute(outgoing[shift], 'uv', perm))  8.61 us
    ppermute x2, waiting for transfers between devices, halving_reduce(): received = lax.ppermute(outgoing, 'tm', perm)  5.94 us
    ppermute x2, starting transfers between devices, halving_reduce(): received = lax.ppermute(outgoing, 'tm', perm)  1.64 us
    dot_general x1, matrix products, per_device(): jnp.dot(lhs, delay_halves(), preferred_element_type=jnp.float32) * out_scale  1.51 us
    another operation x2, other arithmetic  1.28 us
    dot_general x2, matrix products, per_device(): jnp.dot(weights, arrived[:, h * row_width:(h + 1) * row_width], preferred...  1.26 us
    sub x1, other arithmetic, delay_halves(): c_hi[:, :, None] * c_lo[:, None, :] - s_hi[:, :, None] * s_lo[:, None, :]  1.22 us
  transfers between devices with their start and end apart: 9, of which 7 were waited for; matrix products, arithmetic and copies ran while one was open for 9% of the time, Pallas kernels for 0%

profile of v17, /device:TPU:12, one launch (start us, length us, event | category | flops | bytes accessed | tf_op | source)
XLA Modules:
  0.0 46.6 jit_solution(387540582177372073)
XLA Ops:
  0.0 0.0 copy-start
  0.0 0.8 %fusion.124 = s32[11,128]{1,0:T(8,128)S(1)} fusion(s32[1,8]{1,0:T(1,128)} %bitcast.152, s32[8,32]{1,0:T(8,128)} %bitcast.151, s32[1,128]{1,0:T(1,128)} %param.15, s32[1,128]{1,0:T(1,128)} %param.14), kind=kLoop, calls=%fused_computation.157 | loop fusion | flops 4224 | bytes 7712 | tf_op jit(solution)/shard_map/concatenate | solution.py:120
  0.8 0.1 reshape.522
  0.9 0.2 slice_reduce_fusion.1
  1.1 0.1 lt.75
  1.2 0.1 pad_add_fusion.1
  1.3 0.1 dynamic_slice.7
  1.3 0.1 lt.76
  1.4 0.1 lt.77
  1.5 0.1 fusion.118
  1.6 0.0 copy-done
  1.6 0.3 convolution_convert_fusion
  2.0 0.1 fusion.117
  2.1 0.3 convolution_convert_fusion.1
  2.5 0.2 convolution_convert_fusion.2
  2.7 0.1 pad_maximum_fusion
  2.7 0.1 fusion.154
  2.8 1.6 %collective-permute-start = (bf16[16,4224]{1,0:T(8,128)(2,1)S(1)}, bf16[16,4224]{1,0:T(8,128)(2,1)S(1)}, u32[]{:S(2)}, u32[]{:S(2)}) collective-permute-start(bf16[16,4224]{1,0:T(8,128)(2,1)S(1)} %get-tuple-element.73), channel_id=1, source_target_pairs={{0,4},{4,8},{8,12},{12,16},{16,20},{20,24},{24,28},{28,0},{1,5},{5... | collective-permute-start | bytes 405512 | tf_op jit(solution)/shard_map/ppermute | solution.py:104
  4.4 1.6 %collective-permute-start.1 = (bf16[16,4224]{1,0:T(8,128)(2,1)S(1)}, bf16[16,4224]{1,0:T(8,128)(2,1)S(1)}, u32[]{:S(2)}, u32[]{:S(2)}) collective-permute-start(bf16[16,4224]{1,0:T(8,128)(2,1)S(1)} %get-tuple-element.72), channel_id=1, source_target_pairs={{0,8},{4,12},{8,16},{12,20},{16,24},{20,28},{24,0},{28,4},{1,9},{5... | collective-permute-start | bytes 405512 | tf_op jit(solution)/shard_map/ppermute | solution.py:104
  6.0 1.2 %collective-permute-start.2 = (bf16[16,4224]{1,0:T(8,128)(2,1)S(1)}, bf16[16,4224]{1,0:T(8,128)(2,1)S(1)}, u32[]{:S(2)}, u32[]{:S(2)}) collective-permute-start(bf16[16,4224]{1,0:T(8,128)(2,1)S(1)} %get-tuple-element.71), channel_id=1, source_target_pairs={{0,12},{4,16},{8,20},{12,24},{16,28},{20,0},{24,4},{28,8},{1,13},{... | collective-permute-start | bytes 405512 | tf_op jit(solution)/shard_map/ppermute | solution.py:104
  7.1 1.7 %collective-permute-start.3 = (bf16[16,4224]{1,0:T(8,128)(2,1)S(1)}, bf16[16,4224]{1,0:T(8,128)(2,1)S(1)}, u32[]{:S(2)}, u32[]{:S(2)}) collective-permute-start(bf16[16,4224]{1,0:T(8,128)(2,1)S(1)} %get-tuple-element.70), channel_id=1, source_target_pairs={{0,16},{4,20},{8,24},{12,28},{16,0},{20,4},{24,8},{28,12},{1,17},{... | collective-permute-start | bytes 405512 | tf_op jit(solution)/shard_map/ppermute | solution.py:104
  8.8 1.3 %collective-permute-start.4 = (bf16[16,4224]{1,0:T(8,128)(2,1)S(1)}, bf16[16,4224]{1,0:T(8,128)(2,1)S(1)}, u32[]{:S(2)}, u32[]{:S(2)}) collective-permute-start(bf16[16,4224]{1,0:T(8,128)(2,1)S(1)} %get-tuple-element.69), channel_id=1, source_target_pairs={{0,20},{4,24},{8,28},{12,0},{16,4},{20,8},{24,12},{28,16},{1,21},{... | collective-permute-start | bytes 405512 | tf_op jit(solution)/shard_map/ppermute | solution.py:104
  10.2 0.1 scatter.15
  10.3 0.1 scatter.16
  10.4 0.1 scatter.19
  10.5 0.1 iota_add_fusion
  10.6 0.1 add.575
  10.7 0.0 collective-permute-done
  10.7 1.3 %collective-permute-start.5 = (bf16[16,4224]{1,0:T(8,128)(2,1)S(1)}, bf16[16,4224]{1,0:T(8,128)(2,1)S(1)}, u32[]{:S(2)}, u32[]{:S(2)}) collective-permute-start(bf16[16,4224]{1,0:T(8,128)(2,1)S(1)} %get-tuple-element.68), channel_id=1, source_target_pairs={{0,24},{4,28},{8,0},{12,4},{16,8},{20,12},{24,16},{28,20},{1,25},{... | collective-permute-start | bytes 405512 | tf_op jit(solution)/shard_map/ppermute | solution.py:104
  12.0 10.9 %collective-permute-done.1 = bf16[16,4224]{1,0:T(8,128)(2,1)S(1)} collective-permute-done((bf16[16,4224]{1,0:T(8,128)(2,1)S(1)}, bf16[16,4224]{1,0:T(8,128)(2,1)S(1)}, u32[]{:S(2)}, u32[]{:S(2)}) %collective-permute-start.1) | collective-permute-done | bytes 135200 | tf_op jit(solution)/shard_map/ppermute | solution.py:104
  22.9 0.0 collective-permute-start.6
  22.9 2.9 %collective-permute-done.2 = bf16[16,4224]{1,0:T(8,128)(2,1)S(1)} collective-permute-done((bf16[16,4224]{1,0:T(8,128)(2,1)S(1)}, bf16[16,4224]{1,0:T(8,128)(2,1)S(1)}, u32[]{:S(2)}, u32[]{:S(2)}) %collective-permute-start.2) | collective-permute-done | bytes 135200 | tf_op jit(solution)/shard_map/ppermute | solution.py:104
  25.8 1.7 %collective-permute-done.3 = bf16[16,4224]{1,0:T(8,128)(2,1)S(1)} collective-permute-done((bf16[16,4224]{1,0:T(8,128)(2,1)S(1)}, bf16[16,4224]{1,0:T(8,128)(2,1)S(1)}, u32[]{:S(2)}, u32[]{:S(2)}) %collective-permute-start.3) | collective-permute-done | bytes 135200 | tf_op jit(solution)/shard_map/ppermute | solution.py:104
  27.5 0.0 collective-permute-done.4
  27.6 1.8 %collective-permute-done.5 = bf16[16,4224]{1,0:T(8,128)(2,1)S(1)} collective-permute-done((bf16[16,4224]{1,0:T(8,128)(2,1)S(1)}, bf16[16,4224]{1,0:T(8,128)(2,1)S(1)}, u32[]{:S(2)}, u32[]{:S(2)}) %collective-permute-start.5) | collective-permute-done | bytes 135200 | tf_op jit(solution)/shard_map/ppermute | solution.py:104
  29.3 1.2 %collective-permute-done.6 = bf16[16,4224]{1,0:T(8,128)(2,1)S(1)} collective-permute-done((bf16[16,4224]{1,0:T(8,128)(2,1)S(1)}, bf16[16,4224]{1,0:T(8,128)(2,1)S(1)}, u32[]{:S(2)}, u32[]{:S(2)}) %collective-permute-start.6) | collective-permute-done | bytes 135200 | tf_op jit(solution)/shard_map/ppermute | solution.py:104
  30.6 0.1 fusion.153
  30.7 0.1 copy.25
  30.7 0.1 copy.23
  30.9 0.1 fusion.126
  31.0 0.1 copy.24
  31.0 0.1 copy.22
  31.3 0.6 %fusion.10 = f32[256,2048]{1,0:T(8,128)S(1)} fusion(bf16[128,4224]{1,0:T(8,128)(2,1)S(1)} %bitcast.149, f32[128]{0:T(128)S(1)} %get-tuple-element.105, s32[128]{0:T(128)S(1)} %get-tuple-element.151, f32[128]{0:T(128)S(1)} %get-tuple-element.106, s32[128]{0:T(128)S(1)} %get-tuple-element.147, f32[128]{0:T(128)S(1)} %get-tuple-element.107, ...), kind=kOutput, calls=%fused_computation.20 | convolution fusion | flops 135790592 | bytes 2639872 | tf_op jit(solution)/shard_map/dot_general | solution.py:183
  31.9 0.6 %convolution_add_fusion = f32[256,2048]{1,0:T(8,128)S(1)} fusion(f32[256,2048]{1,0:T(8,128)S(1)} %fusion.10, bf16[128,4224]{1,0:T(8,128)(2,1)S(1)} %bitcast.150, f32[128]{0:T(128)S(1)} %get-tuple-element.89, s32[128]{0:T(128)S(1)} %get-tuple-element.135, f32[128]{0:T(128)S(1)} %get-tuple-element.90, s32[128]{0:T(128)S(1)} %get-tuple-element.131, ...), kind=kOutput, calls=%fused_computation.10 | convolution fusion | flops 136314880 | bytes 4737024 | tf_op jit(solution)/shard_map/dot_general | solution.py:183
  32.6 0.1 slice.318
  32.7 0.1 collective-permute-start.7
  32.7 0.1 multiply_subtract_fusion.1
  32.8 0.5 %fusion.47 = (f32[1024,32]{0,1:T(8,128)S(1)}, f32[1024,32]{0,1:T(8,128)S(1)}) fusion(), kind=kLoop, calls=%fused_computation.77 | loop fusion | flops 458752 | bytes 262144 | tf_op jit(solution)/shard_map/sin | solution.py:52
  33.3 0.6 %fusion.50 = (f32[1024,32]{0,1:T(8,128)S(1)}, f32[1024,32]{0,1:T(8,128)S(1)}) fusion(s32[32]{0:T(128)S(1)} %iota_multiply_fusion), kind=kLoop, calls=%fused_computation.80 | loop fusion | flops 458752 | bytes 262272 | tf_op jit(solution)/shard_map/cos | solution.py:51
  33.9 1.2 %multiply_subtract_fusion = (f32[1024,32,32]{0,2,1:T(8,128)S(1)}, f32[1024,32,32]{0,2,1:T(8,128)S(1)}) fusion(f32[1024,32]{0,1:T(8,128)S(1)} %get-tuple-element.162, f32[1024,32]{0,1:T(8,128)S(1)} %get-tuple-element.155, f32[1024,32]{0,1:T(8,128)S(1)} %get-tuple-element.163, f32[1024,32]{0,1:T(8,128)S(1)} %get-tuple-element.154), kind=kLoop, calls=%fused_computation.9 | loop fusion | flops 6291456 | bytes 8912896 | tf_op jit(solution)/shard_map/sub | solution.py:53
  35.2 0.2 collective-permute-done.7
  35.4 0.1 slice_add_fusion
  35.5 1.6 %collective-permute-start.8 = (bf16[64,2048]{1,0:T(8,128)(2,1)S(1)}, bf16[64,2048]{1,0:T(8,128)(2,1)S(1)}, u32[]{:S(2)}, u32[]{:S(2)}) collective-permute-start(bf16[64,2048]{1,0:T(8,128)(2,1)S(1)} %slice.376), channel_id=1, source_target_pairs={{0,2},{1,3},{2,0},{3,1},{4,6},{5,7},{6,4},{7,5},{8,10},{9,11},{10,... | collective-permute-start | bytes 786440 | tf_op jit(solution)/shard_map/ppermute | solution.py:93
  37.1 1.3 %fusion.5 = (bf16[1024,1024]{0,1:T(8,128)(2,1)S(1)}, bf16[1024,1024]{0,1:T(8,128)(2,1)S(1)}) fusion(f32[1024,32,32]{0,2,1:T(8,128)S(1)} %get-tuple-element.76, f32[1024]{0:T(1024)S(1)} %multiply_subtract_fusion.1, f32[1024,32,32]{0,2,1:T(8,128)S(1)} %get-tuple-element.77), kind=kLoop, calls=%fused_computation.7 | loop fusion | flops 4194304 | bytes 12587008 | tf_op jit(solution)/shard_map/convert.1
  38.4 5.7 %collective-permute-done.8 = bf16[64,2048]{1,0:T(8,128)(2,1)S(1)} collective-permute-done((bf16[64,2048]{1,0:T(8,128)(2,1)S(1)}, bf16[64,2048]{1,0:T(8,128)(2,1)S(1)}, u32[]{:S(2)}, u32[]{:S(2)}) %collective-permute-start.8) | collective-permute-done | bytes 262176 | tf_op jit(solution)/shard_map/ppermute | solution.py:93
  44.2 1.5 %fusion.6 = f32[128,1024]{1,0:T(8,128)S(1)} fusion(bf16[1024,1024]{0,1:T(8,128)(2,1)S(1)} %get-tuple-element.113, bf16[1024,1024]{0,1:T(8,128)(2,1)S(1)} %get-tuple-element.112, bf16[64,1024]{1,0:T(8,128)(2,1)S(1)} %get-tuple-element.79, bf16[64,1024]{1,0:T(8,128)(2,1)S(1)} %get-tuple-element.78, bf16[64,2048]{1,0:T(8,128)(2,1)S(1)} %fusion.9), kind=kOutput, calls=%fused_computation.13 | convolution fusion | flops 546963456 | bytes 5242880 | tf_op jit(solution)/shard_map/dot_general | solution.py:197
  45.7 0.8 %pad_maximum_fusion.1 = f32[64,2048]{1,0:T(8,128)} fusion(f32[64,1024]{1,0:T(8,128)S(1)} %get-tuple-element.75, f32[64,1024]{1,0:T(8,128)S(1)} %get-tuple-element.74), kind=kLoop, calls=%fused_computation.28 | loop fusion | flops 131072 | bytes 1048576 | tf_op jit(solution)/shard_map/concatenate | solution.py:199
  (37 shorter events, 0.5 us)
Async XLA Ops:
  0.0 1.6 %copy-start = (bf16[1,128,2048]{2,1,0:T(8,128)(2,1)S(1)}, bf16[1,128,2048]{2,1,0:T(8,128)(2,1)}, u32[]{:S(2)}) copy-start(bf16[1,128,2048]{2,1,0:T(8,128)(2,1)} %param.13) | copy-start | bytes 1572868
  2.8 7.9 %collective-permute-start = (bf16[16,4224]{1,0:T(8,128)(2,1)S(1)}, bf16[16,4224]{1,0:T(8,128)(2,1)S(1)}, u32[]{:S(2)}, u32[]{:S(2)}) collective-permute-start(bf16[16,4224]{1,0:T(8,128)(2,1)S(1)} %get-tuple-element.73), channel_id=1, source_target_pairs={{0,4},{4,8},{8,12},{12,16},{16,20},{20,24},{24,28},{28,0},{1,5},{5... | collective-permute-start | bytes 405512 | tf_op jit(solution)/shard_map/ppermute | solution.py:104
  4.4 18.5 %collective-permute-start.1 = (bf16[16,4224]{1,0:T(8,128)(2,1)S(1)}, bf16[16,4224]{1,0:T(8,128)(2,1)S(1)}, u32[]{:S(2)}, u32[]{:S(2)}) collective-permute-start(bf16[16,4224]{1,0:T(8,128)(2,1)S(1)} %get-tuple-element.72), channel_id=1, source_target_pairs={{0,8},{4,12},{8,16},{12,20},{16,24},{20,28},{24,0},{28,4},{1,9},{5... | collective-permute-start | bytes 405512 | tf_op jit(solution)/shard_map/ppermute | solution.py:104
  6.0 19.8 %collective-permute-start.2 = (bf16[16,4224]{1,0:T(8,128)(2,1)S(1)}, bf16[16,4224]{1,0:T(8,128)(2,1)S(1)}, u32[]{:S(2)}, u32[]{:S(2)}) collective-permute-start(bf16[16,4224]{1,0:T(8,128)(2,1)S(1)} %get-tuple-element.71), channel_id=1, source_target_pairs={{0,12},{4,16},{8,20},{12,24},{16,28},{20,0},{24,4},{28,8},{1,13},{... | collective-permute-start | bytes 405512 | tf_op jit(solution)/shard_map/ppermute | solution.py:104
  7.1 20.4 %collective-permute-start.3 = (bf16[16,4224]{1,0:T(8,128)(2,1)S(1)}, bf16[16,4224]{1,0:T(8,128)(2,1)S(1)}, u32[]{:S(2)}, u32[]{:S(2)}) collective-permute-start(bf16[16,4224]{1,0:T(8,128)(2,1)S(1)} %get-tuple-element.70), channel_id=1, source_target_pairs={{0,16},{4,20},{8,24},{12,28},{16,0},{20,4},{24,8},{28,12},{1,17},{... | collective-permute-start | bytes 405512 | tf_op jit(solution)/shard_map/ppermute | solution.py:104
  8.8 18.7 %collective-permute-start.4 = (bf16[16,4224]{1,0:T(8,128)(2,1)S(1)}, bf16[16,4224]{1,0:T(8,128)(2,1)S(1)}, u32[]{:S(2)}, u32[]{:S(2)}) collective-permute-start(bf16[16,4224]{1,0:T(8,128)(2,1)S(1)} %get-tuple-element.69), channel_id=1, source_target_pairs={{0,20},{4,24},{8,28},{12,0},{16,4},{20,8},{24,12},{28,16},{1,21},{... | collective-permute-start | bytes 405512 | tf_op jit(solution)/shard_map/ppermute | solution.py:104
  10.7 18.6 %collective-permute-start.5 = (bf16[16,4224]{1,0:T(8,128)(2,1)S(1)}, bf16[16,4224]{1,0:T(8,128)(2,1)S(1)}, u32[]{:S(2)}, u32[]{:S(2)}) collective-permute-start(bf16[16,4224]{1,0:T(8,128)(2,1)S(1)} %get-tuple-element.68), channel_id=1, source_target_pairs={{0,24},{4,28},{8,0},{12,4},{16,8},{20,12},{24,16},{28,20},{1,25},{... | collective-permute-start | bytes 405512 | tf_op jit(solution)/shard_map/ppermute | solution.py:104
  22.9 7.7 %collective-permute-start.6 = (bf16[16,4224]{1,0:T(8,128)(2,1)S(1)}, bf16[16,4224]{1,0:T(8,128)(2,1)S(1)}, u32[]{:S(2)}, u32[]{:S(2)}) collective-permute-start(bf16[16,4224]{1,0:T(8,128)(2,1)S(1)} %get-tuple-element.67), channel_id=1, source_target_pairs={{0,28},{4,0},{8,4},{12,8},{16,12},{20,16},{24,20},{28,24},{1,29},{... | collective-permute-start | bytes 405512 | tf_op jit(solution)/shard_map/ppermute | solution.py:104
  32.7 2.7 %collective-permute-start.7 = (f32[128,2048]{1,0:T(8,128)S(1)}, f32[128,2048]{1,0:T(8,128)S(1)}, u32[]{:S(2)}, u32[]{:S(2)}) collective-permute-start(f32[128,2048]{1,0:T(8,128)S(1)} %slice.318), channel_id=1, source_target_pairs={{0,1},{1,0},{2,3},{3,2},{4,5},{5,4},{6,7},{7,6},{8,9},{9,8},{10,11... | collective-permute-start | bytes 3145736 | tf_op jit(solution)/shard_map/ppermute | solution.py:93
  35.5 8.6 %collective-permute-start.8 = (bf16[64,2048]{1,0:T(8,128)(2,1)S(1)}, bf16[64,2048]{1,0:T(8,128)(2,1)S(1)}, u32[]{:S(2)}, u32[]{:S(2)}) collective-permute-start(bf16[64,2048]{1,0:T(8,128)(2,1)S(1)} %slice.376), channel_id=1, source_target_pairs={{0,2},{1,3},{2,0},{3,1},{4,6},{5,7},{6,4},{7,5},{8,10},{9,11},{10,... | collective-permute-start | bytes 786440 | tf_op jit(solution)/shard_map/ppermute | solution.py:93

commit v18 on v12

--- a/solution.py
+++ b/solution.py
@@ -95,14 +95,38 @@
     return partial
 
 
-def uv_exchange(outgoing, uv_size):
+def uv_exchange(outgoing, uv_size, tm_size):
     if uv_size > 16:
         return lax.all_to_all(outgoing, "uv", split_axis=0, concat_axis=0, tiled=True)
-    pieces = [outgoing[0]]
-    for shift in range(1, uv_size):
-        perm = [(i, (i + shift) % uv_size) for i in range(uv_size)]
-        pieces.append(lax.ppermute(outgoing[shift], "uv", perm))
-    return jnp.stack(pieces)
+    if tm_size % 2:
+        pieces = [outgoing[0]]
+        for shift in range(1, uv_size):
+            perm = [(i, (i + shift) % uv_size) for i in range(uv_size)]
+            pieces.append(lax.ppermute(outgoing[shift], "uv", perm))
+        return jnp.stack(pieces)
+    shifts = list(range(1, uv_size))
+    count = (len(shifts) + 1) // 2
+    sets = [shifts[:count], shifts[count:] + [None] * (2 * count - len(shifts))]
+    zero = jnp.zeros(outgoing.shape[1:], outgoing.dtype)
+    stacks = [jnp.stack([outgoing[k] if k else zero for k in group]) for group in sets]
+    side = lax.axis_index("tm") % 2
+    mine = jnp.where(side == 0, stacks[0], stacks[1])
+    theirs = jnp.where(side == 0, stacks[1], stacks[0])
+    pair_perm = [(i, i ^ 1) for i in range(tm_size)]
+    partner = lax.ppermute(theirs, "tm", pair_perm)
+    kept, passed = [], []
+    for j in range(count):
+        perm = []
+        for u in range(uv_size):
+            for t in range(tm_size):
+                shift = sets[t % 2][j]
+                if shift:
+                    perm.append((u * tm_size + t, ((u + shift) % uv_size) * tm_size + t))
+        got = lax.ppermute(jnp.stack([mine[j], partner[j]]), ("uv", "tm"), perm)
+        kept.append(got[0])
+        passed.append(got[1])
+    forwarded = lax.ppermute(jnp.stack(passed), "tm", pair_perm)
+    return jnp.concatenate([outgoing[:1], jnp.stack(kept), forwarded], axis=0)
 
 
 def per_device(visibility, anchor, offset, slot_rows, counts):
@@ -148,7 +172,7 @@
         pick, meta_rows, (((1,), (1,)), ((), ())), preferred_element_type=jnp.float32
     ).astype(jnp.bfloat16)
     outgoing = jnp.concatenate([picked, meta], axis=1).reshape(tile_count, slot_depth, row_width + META)
-    arrived = uv_exchange(outgoing, uv_size)
+    arrived = uv_exchange(outgoing, uv_size, time_groups)
     arrived = arrived.reshape(-1, row_width + META)
     arr_anchor = arrived[:, row_width].astype(jnp.int32)
     arr_offset = arrived[:, row_width + 1].astype(jnp.int32)

time: 46 us -> 54.8 us (1.19)
  the two profiles are of different devices: /device:TPU:12 before, /device:TPU:0 now
where the time goes in v18:
time: 54.8 us; the launch traced here: 54.6 us
  waiting for transfers between devices  31.1 us (57%)
  starting transfers between devices  11.7 us (21%)
  other arithmetic  6.52 us (12%)
  matrix products  3.5 us (6%)
  local copies, waits for them, and re-layouts  1.52 us (3%)
    ppermute x4, waiting for transfers between devices, uv_exchange(): got = lax.ppermute(jnp.stack([mine[j], partner[j]]), ('uv', 'tm'), perm)  22.3 us
    ppermute x4, starting transfers between devices, uv_exchange(): got = lax.ppermute(jnp.stack([mine[j], partner[j]]), ('uv', 'tm'), perm)  9.39 us
    ppermute x2, waiting for transfers between devices, halving_reduce(): received = lax.ppermute(outgoing, 'tm', perm)  5.82 us
    ppermute x1, waiting for transfers between devices, uv_exchange(): forwarded = lax.ppermute(jnp.stack(passed), 'tm', pair_perm)  1.77 us
    ppermute x2, starting transfers between devices, halving_reduce(): received = lax.ppermute(outgoing, 'tm', perm)  1.76 us
    dot_general x1, matrix products, per_device(): jnp.dot(lhs, delay_halves(), preferred_element_type=jnp.float32) * out_scale  1.52 us
    another operation x2, other arithmetic  1.28 us
    dot_general x1, matrix products, per_device(): jnp.dot(weights, arrived[:, :row_width], preferred_element_type=jnp.float32)  1.24 us
  transfers between devices with their start and end apart: 8, of which 7 were waited for; matrix products, arithmetic and copies ran while one was open for 8% of the time, Pallas kernels for 0%

profile of v18, /device:TPU:0, one launch (start us, length us, event | category | flops | bytes accessed | tf_op | source)
XLA Modules:
  0.0 54.6 jit_solution(12473621490372752018)
XLA Ops:
  0.0 0.0 copy-start
  0.0 0.8 %fusion.96 = s32[11,128]{1,0:T(8,128)S(1)} fusion(s32[1,8]{1,0:T(1,128)} %bitcast.44, s32[8,32]{1,0:T(8,128)} %bitcast.43, s32[1,128]{1,0:T(1,128)} %param.15, s32[1,128]{1,0:T(1,128)} %param.14), kind=kLoop, calls=%fused_computation.144 | loop fusion | flops 4224 | bytes 7712 | tf_op jit(solution)/shard_map/concatenate | solution.py:144
  0.8 0.1 eq.88
  0.9 0.1 pad_add_fusion.1
  1.0 0.1 dynamic_slice.7
  1.1 0.1 iota_compare_fusion.1
  1.1 0.1 lt.64
  1.2 0.3 convolution_convert_fusion.1
  1.5 0.0 copy-done
  1.5 0.5 convolution_convert_fusion
  2.0 0.1 fusion.61
  2.1 0.1 pad.43.clone
  2.1 0.2 broadcast_select_fusion.1
  2.4 0.5 collective-permute-start
  2.9 0.1 scatter.15
  3.1 0.1 scatter.16
  3.2 0.1 scatter.19
  3.3 0.1 fusion.106
  3.3 1.2 %collective-permute-done = bf16[4,32,2176]{2,1,0:T(8,128)(2,1)S(1)} collective-permute-done((bf16[4,32,2176]{2,1,0:T(8,128)(2,1)S(1)}, bf16[4,32,2176]{2,1,0:T(8,128)(2,1)S(1)}, u32[]{:S(2)}, u32[]{:S(2)}) %collective-permute-start) | collective-permute-done | bytes 557088 | tf_op jit(solution)/shard_map/ppermute | solution.py:116
  4.6 5.9 %collective-permute-start.4 = (bf16[2,32,2176]{2,1,0:T(8,128)(2,1)S(1)}, bf16[2,32,2176]{2,1,0:T(8,128)(2,1)S(1)}, u32[]{:S(2)}, u32[]{:S(2)}) collective-permute-start(bf16[2,32,2176]{2,1,0:T(8,128)(2,1)S(1)} %pad_maximum_fusion.6), channel_id=1, source_target_pairs={{0,16},{2,18},{4,20},{6,22},{8,24},{10,26},{12,28},{14,30},{16,0},... | collective-permute-start | bytes 835592 | tf_op jit(solution)/shard_map/ppermute | solution.py:125
  10.5 2.6 %collective-permute-start.3 = (bf16[2,32,2176]{2,1,0:T(8,128)(2,1)S(1)}, bf16[2,32,2176]{2,1,0:T(8,128)(2,1)S(1)}, u32[]{:S(2)}, u32[]{:S(2)}) collective-permute-start(bf16[2,32,2176]{2,1,0:T(8,128)(2,1)S(1)} %pad_maximum_fusion.5), channel_id=1, source_target_pairs={{0,12},{1,29},{2,14},{3,31},{4,16},{5,1},{6,18},{7,3},{8,20},{9,5}... | collective-permute-start | bytes 835592 | tf_op jit(solution)/shard_map/ppermute | solution.py:125
  13.1 0.1 collective-permute-start.1
  13.2 0.9 %collective-permute-start.2 = (bf16[2,32,2176]{2,1,0:T(8,128)(2,1)S(1)}, bf16[2,32,2176]{2,1,0:T(8,128)(2,1)S(1)}, u32[]{:S(2)}, u32[]{:S(2)}) collective-permute-start(bf16[2,32,2176]{2,1,0:T(8,128)(2,1)S(1)} %pad_maximum_fusion.4), channel_id=1, source_target_pairs={{0,8},{1,25},{2,10},{3,27},{4,12},{5,29},{6,14},{7,31},{8,16},{9,1... | collective-permute-start | bytes 835592 | tf_op jit(solution)/shard_map/ppermute | solution.py:125
  14.1 14.4 %collective-permute-done.1 = bf16[2,32,2176]{2,1,0:T(8,128)(2,1)S(1)} collective-permute-done((bf16[2,32,2176]{2,1,0:T(8,128)(2,1)S(1)}, bf16[2,32,2176]{2,1,0:T(8,128)(2,1)S(1)}, u32[]{:S(2)}, u32[]{:S(2)}) %collective-permute-start.1) | collective-permute-done | bytes 278560 | tf_op jit(solution)/shard_map/ppermute | solution.py:125
  28.6 1.8 %collective-permute-done.2 = bf16[2,32,2176]{2,1,0:T(8,128)(2,1)S(1)} collective-permute-done((bf16[2,32,2176]{2,1,0:T(8,128)(2,1)S(1)}, bf16[2,32,2176]{2,1,0:T(8,128)(2,1)S(1)}, u32[]{:S(2)}, u32[]{:S(2)}) %collective-permute-start.2) | collective-permute-done | bytes 278560 | tf_op jit(solution)/shard_map/ppermute | solution.py:125
  30.4 6.1 %collective-permute-done.3 = bf16[2,32,2176]{2,1,0:T(8,128)(2,1)S(1)} collective-permute-done((bf16[2,32,2176]{2,1,0:T(8,128)(2,1)S(1)}, bf16[2,32,2176]{2,1,0:T(8,128)(2,1)S(1)}, u32[]{:S(2)}, u32[]{:S(2)}) %collective-permute-start.3) | collective-permute-done | bytes 278560 | tf_op jit(solution)/shard_map/ppermute | solution.py:125
  36.5 0.0 collective-permute-done.4
  36.5 0.1 pad_maximum_fusion.1
  36.6 0.1 collective-permute-start.5
  36.7 0.1 iota_add_fusion
  36.8 0.1 add.351
  36.9 1.8 %collective-permute-done.5 = bf16[4,32,2176]{2,1,0:T(8,128)(2,1)S(1)} collective-permute-done((bf16[4,32,2176]{2,1,0:T(8,128)(2,1)S(1)}, bf16[4,32,2176]{2,1,0:T(8,128)(2,1)S(1)}, u32[]{:S(2)}, u32[]{:S(2)}) %collective-permute-start.5) | collective-permute-done | bytes 557088 | tf_op jit(solution)/shard_map/ppermute | solution.py:128
  38.7 0.1 constant_dynamic-update-slice_fusion
  38.7 0.1 fusion.105
  38.8 0.1 copy.11
  39.0 0.1 copy.12
  39.1 0.1 multiply_reduce_fusion
  39.2 0.1 fusion.92
  39.3 0.1 slice_reduce_fusion.7
  39.3 1.2 %fusion.9 = f32[256,2048]{1,0:T(8,128)S(1)} fusion(bf16[288,2176]{1,0:T(8,128)(2,1)S(1)} %bitcast.42, f32[288]{0:T(512)S(1)} %get-tuple-element.62, s32[288]{0:T(512)S(1)} %get-tuple-element.122, f32[288]{0:T(512)S(1)} %get-tuple-element.63, s32[288]{0:T(512)S(1)} %get-tuple-element.121, f32[288]{0:T(512)S(1)} %get-tuple-element.64, ...), kind=kOutput, calls=%fused_computation.19 | convolution fusion | flops 305528832 | bytes 3344384 | tf_op jit(solution)/shard_map/dot_general | solution.py:186
  40.6 0.1 slice.344
  40.7 0.2 collective-permute-start.6
  40.9 0.1 multiply_subtract_fusion.1
  41.0 0.5 fusion.82
  41.5 0.6 %fusion.85 = (f32[1024,32]{0,1:T(8,128)S(1)}, f32[1024,32]{0,1:T(8,128)S(1)}) fusion(s32[32]{0:T(128)S(1)} %iota_multiply_fusion), kind=kLoop, calls=%fused_computation.129 | loop fusion | flops 458752 | bytes 262272 | tf_op jit(solution)/shard_map/cos | solution.py:51
  42.1 1.2 %multiply_subtract_fusion = (f32[1024,32,32]{0,2,1:T(8,128)S(1)}, f32[1024,32,32]{0,2,1:T(8,128)S(1)}) fusion(f32[1024,32]{0,1:T(8,128)S(1)} %get-tuple-element.130, f32[1024,32]{0,1:T(8,128)S(1)} %get-tuple-element.129, f32[1024,32]{0,1:T(8,128)S(1)} %get-tuple-element.131, f32[1024,32]{0,1:T(8,128)S(1)} %get-tuple-element.128), kind=kLoop, calls=%fused_computation.9 | loop fusion | flops 6291456 | bytes 8912896 | tf_op jit(solution)/shard_map/sub | solution.py:53
  43.3 0.1 collective-permute-done.6
  43.4 0.1 slice_add_fusion
  43.6 1.6 %collective-permute-start.7 = (bf16[64,2048]{1,0:T(8,128)(2,1)S(1)}, bf16[64,2048]{1,0:T(8,128)(2,1)S(1)}, u32[]{:S(2)}, u32[]{:S(2)}) collective-permute-start(bf16[64,2048]{1,0:T(8,128)(2,1)S(1)} %slice.451), channel_id=1, source_target_pairs={{0,2},{1,3},{2,0},{3,1},{4,6},{5,7},{6,4},{7,5},{8,10},{9,11},{10,... | collective-permute-start | bytes 786440 | tf_op jit(solution)/shard_map/ppermute | solution.py:93
  45.1 1.3 %fusion.5 = (bf16[1024,1024]{0,1:T(8,128)(2,1)S(1)}, bf16[1024,1024]{0,1:T(8,128)(2,1)S(1)}) fusion(f32[1024,32,32]{0,2,1:T(8,128)S(1)} %get-tuple-element.96, f32[1024]{0:T(1024)S(1)} %multiply_subtract_fusion.1, f32[1024,32,32]{0,2,1:T(8,128)S(1)} %get-tuple-element.97), kind=kLoop, calls=%fused_computation.7 | loop fusion | flops 4194304 | bytes 12587008 | tf_op jit(solution)/shard_map/convert
  46.4 5.7 %collective-permute-done.7 = bf16[64,2048]{1,0:T(8,128)(2,1)S(1)} collective-permute-done((bf16[64,2048]{1,0:T(8,128)(2,1)S(1)}, bf16[64,2048]{1,0:T(8,128)(2,1)S(1)}, u32[]{:S(2)}, u32[]{:S(2)}) %collective-permute-start.7) | collective-permute-done | bytes 262176 | tf_op jit(solution)/shard_map/ppermute | solution.py:93
  52.2 1.5 %fusion.6 = f32[128,1024]{1,0:T(8,128)S(1)} fusion(bf16[1024,1024]{0,1:T(8,128)(2,1)S(1)} %get-tuple-element.109, bf16[1024,1024]{0,1:T(8,128)(2,1)S(1)} %get-tuple-element.108, bf16[64,1024]{1,0:T(8,128)(2,1)S(1)} %get-tuple-element.107, bf16[64,1024]{1,0:T(8,128)(2,1)S(1)} %get-tuple-element.106, bf16[64,2048]{1,0:T(8,128)(2,1)S(1)} %fusion.11), kind=kOutput, calls=%fused_computation.18 | convolution fusion | flops 546963456 | bytes 5242880 | tf_op jit(solution)/shard_map/dot_general | solution.py:197
  53.8 0.8 %pad_maximum_fusion.2 = f32[64,2048]{1,0:T(8,128)} fusion(f32[64,1024]{1,0:T(8,128)S(1)} %get-tuple-element.95, f32[64,1024]{1,0:T(8,128)S(1)} %get-tuple-element.94), kind=kLoop, calls=%fused_computation.36 | loop fusion | flops 131072 | bytes 1048576 | tf_op jit(solution)/shard_map/concatenate | solution.py:199
  (27 shorter events, 0.6 us)
Async XLA Ops:
  0.0 1.5 %copy-start = (bf16[1,128,2048]{2,1,0:T(8,128)(2,1)S(1)}, bf16[1,128,2048]{2,1,0:T(8,128)(2,1)}, u32[]{:S(2)}) copy-start(bf16[1,128,2048]{2,1,0:T(8,128)(2,1)} %param.13) | copy-start | bytes 1572868
  2.4 2.1 %collective-permute-start = (bf16[4,32,2176]{2,1,0:T(8,128)(2,1)S(1)}, bf16[4,32,2176]{2,1,0:T(8,128)(2,1)S(1)}, u32[]{:S(2)}, u32[]{:S(2)}) collective-permute-start(bf16[4,32,2176]{2,1,0:T(8,128)(2,1)S(1)} %get-tuple-element.85), channel_id=1, source_target_pairs={{0,1},{1,0},{2,3},{3,2},{4,5},{5,4},{6,7},{7,6},{8,9},{9,8},{10,11... | collective-permute-start | bytes 1671176 | tf_op jit(solution)/shard_map/ppermute | solution.py:116
  4.6 31.9 %collective-permute-start.4 = (bf16[2,32,2176]{2,1,0:T(8,128)(2,1)S(1)}, bf16[2,32,2176]{2,1,0:T(8,128)(2,1)S(1)}, u32[]{:S(2)}, u32[]{:S(2)}) collective-permute-start(bf16[2,32,2176]{2,1,0:T(8,128)(2,1)S(1)} %pad_maximum_fusion.6), channel_id=1, source_target_pairs={{0,16},{2,18},{4,20},{6,22},{8,24},{10,26},{12,28},{14,30},{16,0},... | collective-permute-start | bytes 835592 | tf_op jit(solution)/shard_map/ppermute | solution.py:125
  10.5 26.0 %collective-permute-start.3 = (bf16[2,32,2176]{2,1,0:T(8,128)(2,1)S(1)}, bf16[2,32,2176]{2,1,0:T(8,128)(2,1)S(1)}, u32[]{:S(2)}, u32[]{:S(2)}) collective-permute-start(bf16[2,32,2176]{2,1,0:T(8,128)(2,1)S(1)} %pad_maximum_fusion.5), channel_id=1, source_target_pairs={{0,12},{1,29},{2,14},{3,31},{4,16},{5,1},{6,18},{7,3},{8,20},{9,5}... | collective-permute-start | bytes 835592 | tf_op jit(solution)/shard_map/ppermute | solution.py:125
  13.1 15.4 %collective-permute-start.1 = (bf16[2,32,2176]{2,1,0:T(8,128)(2,1)S(1)}, bf16[2,32,2176]{2,1,0:T(8,128)(2,1)S(1)}, u32[]{:S(2)}, u32[]{:S(2)}) collective-permute-start(bf16[2,32,2176]{2,1,0:T(8,128)(2,1)S(1)} %pad_maximum_fusion.3), channel_id=1, source_target_pairs={{0,4},{1,21},{2,6},{3,23},{4,8},{5,25},{6,10},{7,27},{8,12},{9,29}... | collective-permute-start | bytes 835592 | tf_op jit(solution)/shard_map/ppermute | solution.py:125
  13.2 17.1 %collective-permute-start.2 = (bf16[2,32,2176]{2,1,0:T(8,128)(2,1)S(1)}, bf16[2,32,2176]{2,1,0:T(8,128)(2,1)S(1)}, u32[]{:S(2)}, u32[]{:S(2)}) collective-permute-start(bf16[2,32,2176]{2,1,0:T(8,128)(2,1)S(1)} %pad_maximum_fusion.4), channel_id=1, source_target_pairs={{0,8},{1,25},{2,10},{3,27},{4,12},{5,29},{6,14},{7,31},{8,16},{9,1... | collective-permute-start | bytes 835592 | tf_op jit(solution)/shard_map/ppermute | solution.py:125
  36.6 2.0 %collective-permute-start.5 = (bf16[4,32,2176]{2,1,0:T(8,128)(2,1)S(1)}, bf16[4,32,2176]{2,1,0:T(8,128)(2,1)S(1)}, u32[]{:S(2)}, u32[]{:S(2)}) collective-permute-start(bf16[4,32,2176]{2,1,0:T(8,128)(2,1)S(1)} %pad_maximum_fusion.1), channel_id=1, source_target_pairs={{0,1},{1,0},{2,3},{3,2},{4,5},{5,4},{6,7},{7,6},{8,9},{9,8},{10,11... | collective-permute-start | bytes 1671176 | tf_op jit(solution)/shard_map/ppermute | solution.py:128
  40.7 2.7 %collective-permute-start.6 = (f32[128,2048]{1,0:T(8,128)S(1)}, f32[128,2048]{1,0:T(8,128)S(1)}, u32[]{:S(2)}, u32[]{:S(2)}) collective-permute-start(f32[128,2048]{1,0:T(8,128)S(1)} %slice.344), channel_id=1, source_target_pairs={{0,1},{1,0},{2,3},{3,2},{4,5},{5,4},{6,7},{7,6},{8,9},{9,8},{10,11... | collective-permute-start | bytes 3145736 | tf_op jit(solution)/shard_map/ppermute | solution.py:93
  43.6 8.6 %collective-permute-start.7 = (bf16[64,2048]{1,0:T(8,128)(2,1)S(1)}, bf16[64,2048]{1,0:T(8,128)(2,1)S(1)}, u32[]{:S(2)}, u32[]{:S(2)}) collective-permute-start(bf16[64,2048]{1,0:T(8,128)(2,1)S(1)} %slice.451), channel_id=1, source_target_pairs={{0,2},{1,3},{2,0},{3,1},{4,6},{5,7},{6,4},{7,5},{8,10},{9,11},{10,... | collective-permute-start | bytes 786440 | tf_op jit(solution)/shard_map/ppermute | solution.py:93

commit v19 on v12

--- a/solution.py
+++ b/solution.py
@@ -99,7 +99,10 @@
     if uv_size > 16:
         return lax.all_to_all(outgoing, "uv", split_axis=0, concat_axis=0, tiled=True)
     pieces = [outgoing[0]]
-    for shift in range(1, uv_size):
+    half = uv_size // 2
+    order = [half] + [k for k in range(2, uv_size, 2) if k != half]
+    order += [k for k in range(1, uv_size, 2)]
+    for shift in order:
         perm = [(i, (i + shift) % uv_size) for i in range(uv_size)]
         pieces.append(lax.ppermute(outgoing[shift], "uv", perm))
     return jnp.stack(pieces)

time: 46 us -> 46.4 us (level)
  the two profiles are of different devices: /device:TPU:12 before, /device:TPU:0 now
where the time goes in v19:
time: 46.4 us; the launch traced here: 46.3 us
  waiting for transfers between devices  21.1 us (45%)
  starting transfers between devices  14.5 us (31%)
  other arithmetic  6.02 us (13%)
  matrix products  3.11 us (7%)
  local copies, waits for them, and re-layouts  1.21 us (3%)
    ppermute x7, waiting for transfers between devices, uv_exchange(): pieces.append(lax.ppermute(outgoing[shift], 'uv', perm))  15.4 us
    ppermute x7, starting transfers between devices, uv_exchange(): pieces.append(lax.ppermute(outgoing[shift], 'uv', perm))  11.8 us
    ppermute x2, waiting for transfers between devices, halving_reduce(): received = lax.ppermute(outgoing, 'tm', perm)  5.69 us
    ppermute x2, starting transfers between devices, halving_reduce(): received = lax.ppermute(outgoing, 'tm', perm)  2.75 us
    dot_general x1, matrix products, per_device(): jnp.dot(lhs, delay_halves(), preferred_element_type=jnp.float32) * out_scale  1.52 us
    another operation x2, other arithmetic  1.28 us
    sub x1, other arithmetic, delay_halves(): c_hi[:, :, None] * c_lo[:, None, :] - s_hi[:, :, None] * s_lo[:, None, :]  1.22 us
  transfers between devices with their start and end apart: 9, of which 6 were waited for; matrix products, arithmetic and copies ran while one was open for 9% of the time, Pallas kernels for 0%

profile of v19, /device:TPU:0, one launch (start us, length us, event | category | flops | bytes accessed | tf_op | source)
XLA Modules:
  0.0 46.3 jit_solution(13149448239948424175)
XLA Ops:
  0.0 0.0 copy-start
  0.0 0.8 %fusion.89 = s32[11,128]{1,0:T(8,128)S(1)} fusion(s32[1,8]{1,0:T(1,128)} %bitcast.83, s32[8,32]{1,0:T(8,128)} %bitcast.62, s32[1,128]{1,0:T(1,128)} %param.15, s32[1,128]{1,0:T(1,128)} %param.14), kind=kLoop, calls=%fused_computation.130 | loop fusion | flops 4224 | bytes 7712 | tf_op jit(solution)/shard_map/concatenate | solution.py:123
  0.8 0.1 eq.83
  0.9 0.1 pad_add_fusion.1
  1.0 0.1 dynamic_slice.7
  1.1 0.1 iota_compare_fusion.1
  1.1 0.1 lt.56
  1.2 0.3 convolution_convert_fusion.1
  1.5 0.0 copy-done
  1.5 0.5 %convolution_convert_fusion = bf16[256,2048]{1,0:T(8,128)(2,1)S(1)} fusion(bf16[1,128,2048]{2,1,0:T(8,128)(2,1)S(1)} %copy-done, s32[256]{0:T(256)S(1)} %eq.83, pred[256]{0:T(512)(128)(4,1)S(1)} %lt.56), kind=kOutput, calls=%fused_computation.17 | convolution fusion | flops 134807552 | bytes 1574144 | tf_op jit(solution)/shard_map/dot_general | solution.py:145
  2.0 0.1 pad_maximum_fusion.1
  2.1 4.1 %collective-permute-start = (bf16[32,2176]{1,0:T(8,128)(2,1)S(1)}, bf16[32,2176]{1,0:T(8,128)(2,1)S(1)}, u32[]{:S(2)}, u32[]{:S(2)}) collective-permute-start(bf16[32,2176]{1,0:T(8,128)(2,1)S(1)} %get-tuple-element.62), channel_id=1, source_target_pairs={{0,16},{4,20},{8,24},{12,28},{16,0},{20,4},{24,8},{28,12},{1,17},{... | collective-permute-start | bytes 417800 | tf_op jit(solution)/shard_map/ppermute | solution.py:107
  6.2 1.6 %collective-permute-start.1 = (bf16[32,2176]{1,0:T(8,128)(2,1)S(1)}, bf16[32,2176]{1,0:T(8,128)(2,1)S(1)}, u32[]{:S(2)}, u32[]{:S(2)}) collective-permute-start(bf16[32,2176]{1,0:T(8,128)(2,1)S(1)} %get-tuple-element.63), channel_id=1, source_target_pairs={{0,8},{4,12},{8,16},{12,20},{16,24},{20,28},{24,0},{28,4},{1,9},{5... | collective-permute-start | bytes 417800 | tf_op jit(solution)/shard_map/ppermute | solution.py:107
  7.7 2.2 %collective-permute-start.2 = (bf16[32,2176]{1,0:T(8,128)(2,1)S(1)}, bf16[32,2176]{1,0:T(8,128)(2,1)S(1)}, u32[]{:S(2)}, u32[]{:S(2)}) collective-permute-start(bf16[32,2176]{1,0:T(8,128)(2,1)S(1)} %get-tuple-element.64), channel_id=1, source_target_pairs={{0,24},{4,28},{8,0},{12,4},{16,8},{20,12},{24,16},{28,20},{1,25},{... | collective-permute-start | bytes 417800 | tf_op jit(solution)/shard_map/ppermute | solution.py:107
  10.0 1.5 %collective-permute-start.3 = (bf16[32,2176]{1,0:T(8,128)(2,1)S(1)}, bf16[32,2176]{1,0:T(8,128)(2,1)S(1)}, u32[]{:S(2)}, u32[]{:S(2)}) collective-permute-start(bf16[32,2176]{1,0:T(8,128)(2,1)S(1)} %get-tuple-element.65), channel_id=1, source_target_pairs={{0,4},{4,8},{8,12},{12,16},{16,20},{20,24},{24,28},{28,0},{1,5},{5... | collective-permute-start | bytes 417800 | tf_op jit(solution)/shard_map/ppermute | solution.py:107
  11.5 0.0 collective-permute-start.4
  11.5 0.1 scatter.15
  11.7 0.1 scatter.16
  11.8 0.1 scatter.19
  11.9 0.1 iota_add_fusion
  11.9 0.1 add.345
  12.1 5.2 %collective-permute-done = bf16[32,2176]{1,0:T(8,128)(2,1)S(1)} collective-permute-done((bf16[32,2176]{1,0:T(8,128)(2,1)S(1)}, bf16[32,2176]{1,0:T(8,128)(2,1)S(1)}, u32[]{:S(2)}, u32[]{:S(2)}) %collective-permute-start) | collective-permute-done | bytes 139296 | tf_op jit(solution)/shard_map/ppermute | solution.py:107
  17.3 0.7 %collective-permute-start.5 = (bf16[32,2176]{1,0:T(8,128)(2,1)S(1)}, bf16[32,2176]{1,0:T(8,128)(2,1)S(1)}, u32[]{:S(2)}, u32[]{:S(2)}) collective-permute-start(bf16[32,2176]{1,0:T(8,128)(2,1)S(1)} %get-tuple-element.67), channel_id=1, source_target_pairs={{0,20},{4,24},{8,28},{12,0},{16,4},{20,8},{24,12},{28,16},{1,21},{... | collective-permute-start | bytes 417800 | tf_op jit(solution)/shard_map/ppermute | solution.py:107
  18.0 0.0 collective-permute-done.1
  18.0 1.6 %collective-permute-start.6 = (bf16[32,2176]{1,0:T(8,128)(2,1)S(1)}, bf16[32,2176]{1,0:T(8,128)(2,1)S(1)}, u32[]{:S(2)}, u32[]{:S(2)}) collective-permute-start(bf16[32,2176]{1,0:T(8,128)(2,1)S(1)} %get-tuple-element.61), channel_id=1, source_target_pairs={{0,28},{4,0},{8,4},{12,8},{16,12},{20,16},{24,20},{28,24},{1,29},{... | collective-permute-start | bytes 417800 | tf_op jit(solution)/shard_map/ppermute | solution.py:107
  19.7 0.3 collective-permute-done.2
  20.0 1.8 %collective-permute-done.3 = bf16[32,2176]{1,0:T(8,128)(2,1)S(1)} collective-permute-done((bf16[32,2176]{1,0:T(8,128)(2,1)S(1)}, bf16[32,2176]{1,0:T(8,128)(2,1)S(1)}, u32[]{:S(2)}, u32[]{:S(2)}) %collective-permute-start.3) | collective-permute-done | bytes 139296 | tf_op jit(solution)/shard_map/ppermute | solution.py:107
  21.8 8.1 %collective-permute-done.4 = bf16[32,2176]{1,0:T(8,128)(2,1)S(1)} collective-permute-done((bf16[32,2176]{1,0:T(8,128)(2,1)S(1)}, bf16[32,2176]{1,0:T(8,128)(2,1)S(1)}, u32[]{:S(2)}, u32[]{:S(2)}) %collective-permute-start.4) | collective-permute-done | bytes 139296 | tf_op jit(solution)/shard_map/ppermute | solution.py:107
  29.9 0.0 collective-permute-done.5
  30.0 0.0 collective-permute-done.6
  30.0 0.1 fusion.97
  30.1 0.1 copy.11
  30.2 0.1 copy.12
  30.4 0.1 fusion.85
  30.5 0.8 %fusion.9 = f32[256,2048]{1,0:T(8,128)S(1)} fusion(bf16[256,2176]{1,0:T(8,128)(2,1)S(1)} %bitcast.61, f32[256]{0:T(256)S(1)} %bitcast.81, s32[256]{0:T(256)S(1)} %get-tuple-element.109, f32[256]{0:T(256)S(1)} %bitcast.80, s32[256]{0:T(256)S(1)} %get-tuple-element.105, f32[256]{0:T(256)S(1)} %bitcast.79, s32[256]{0:T(256)S(1)} %get-tuple-element.106, ...), kind=kOutput, calls=%fused_computation.21 | convolution fusion | flops 271581184 | bytes 3180544 | tf_op jit(solution)/shard_map/dot_general | solution.py:165
  31.4 0.1 slice.243
  31.5 0.1 collective-permute-start.7
  31.6 0.1 multiply_subtract_fusion.1
  31.6 0.5 %fusion.75 = (f32[1024,32]{0,1:T(8,128)S(1)}, f32[1024,32]{0,1:T(8,128)S(1)}) fusion(), kind=kLoop, calls=%fused_computation.113 | loop fusion | flops 458752 | bytes 262144 | tf_op jit(solution)/shard_map/sin | solution.py:52
  32.1 0.6 %fusion.78 = (f32[1024,32]{0,1:T(8,128)S(1)}, f32[1024,32]{0,1:T(8,128)S(1)}) fusion(s32[32]{0:T(128)S(1)} %iota_multiply_fusion), kind=kLoop, calls=%fused_computation.116 | loop fusion | flops 458752 | bytes 262272 | tf_op jit(solution)/shard_map/cos | solution.py:51
  32.7 1.2 %multiply_subtract_fusion = (f32[1024,32,32]{0,2,1:T(8,128)S(1)}, f32[1024,32,32]{0,2,1:T(8,128)S(1)}) fusion(f32[1024,32]{0,1:T(8,128)S(1)} %get-tuple-element.122, f32[1024,32]{0,1:T(8,128)S(1)} %get-tuple-element.113, f32[1024,32]{0,1:T(8,128)S(1)} %get-tuple-element.123, f32[1024,32]{0,1:T(8,128)S(1)} %get-tuple-element.112), kind=kLoop, calls=%fused_computation.9 | loop fusion | flops 6291456 | bytes 8912896 | tf_op jit(solution)/shard_map/sub | solution.py:53
  34.0 0.2 collective-permute-done.7
  34.2 0.1 slice_add_fusion
  34.3 2.7 %collective-permute-start.8 = (bf16[64,2048]{1,0:T(8,128)(2,1)S(1)}, bf16[64,2048]{1,0:T(8,128)(2,1)S(1)}, u32[]{:S(2)}, u32[]{:S(2)}) collective-permute-start(bf16[64,2048]{1,0:T(8,128)(2,1)S(1)} %slice.306), channel_id=1, source_target_pairs={{0,2},{1,3},{2,0},{3,1},{4,6},{5,7},{6,4},{7,5},{8,10},{9,11},{10,... | collective-permute-start | bytes 786440 | tf_op jit(solution)/shard_map/ppermute | solution.py:93
  37.0 1.3 %fusion.5 = (bf16[1024,1024]{0,1:T(8,128)(2,1)S(1)}, bf16[1024,1024]{0,1:T(8,128)(2,1)S(1)}) fusion(f32[1024,32,32]{0,2,1:T(8,128)S(1)} %get-tuple-element.70, f32[1024]{0:T(1024)S(1)} %multiply_subtract_fusion.1, f32[1024,32,32]{0,2,1:T(8,128)S(1)} %get-tuple-element.71), kind=kLoop, calls=%fused_computation.7 | loop fusion | flops 4194304 | bytes 12587008 | tf_op jit(solution)/shard_map/convert
  38.3 5.5 %collective-permute-done.8 = bf16[64,2048]{1,0:T(8,128)(2,1)S(1)} collective-permute-done((bf16[64,2048]{1,0:T(8,128)(2,1)S(1)}, bf16[64,2048]{1,0:T(8,128)(2,1)S(1)}, u32[]{:S(2)}, u32[]{:S(2)}) %collective-permute-start.8) | collective-permute-done | bytes 262176 | tf_op jit(solution)/shard_map/ppermute | solution.py:93
  43.9 1.5 %fusion.6 = f32[128,1024]{1,0:T(8,128)S(1)} fusion(bf16[1024,1024]{0,1:T(8,128)(2,1)S(1)} %get-tuple-element.91, bf16[1024,1024]{0,1:T(8,128)(2,1)S(1)} %get-tuple-element.90, bf16[64,1024]{1,0:T(8,128)(2,1)S(1)} %get-tuple-element.73, bf16[64,1024]{1,0:T(8,128)(2,1)S(1)} %get-tuple-element.72, bf16[64,2048]{1,0:T(8,128)(2,1)S(1)} %fusion.11), kind=kOutput, calls=%fused_computation.18 | convolution fusion | flops 546963456 | bytes 5242880 | tf_op jit(solution)/shard_map/dot_general | solution.py:176
  45.4 0.8 %pad_maximum_fusion = f32[64,2048]{1,0:T(8,128)} fusion(f32[64,1024]{1,0:T(8,128)S(1)} %get-tuple-element.69, f32[64,1024]{1,0:T(8,128)S(1)} %get-tuple-element.68), kind=kLoop, calls=%fused_computation.31 | loop fusion | flops 131072 | bytes 1048576 | tf_op jit(solution)/shard_map/concatenate | solution.py:178
  (28 shorter events, 0.5 us)
Async XLA Ops:
  0.0 1.5 %copy-start = (bf16[1,128,2048]{2,1,0:T(8,128)(2,1)S(1)}, bf16[1,128,2048]{2,1,0:T(8,128)(2,1)}, u32[]{:S(2)}) copy-start(bf16[1,128,2048]{2,1,0:T(8,128)(2,1)} %param.13) | copy-start | bytes 1572868
  2.1 15.2 %collective-permute-start = (bf16[32,2176]{1,0:T(8,128)(2,1)S(1)}, bf16[32,2176]{1,0:T(8,128)(2,1)S(1)}, u32[]{:S(2)}, u32[]{:S(2)}) collective-permute-start(bf16[32,2176]{1,0:T(8,128)(2,1)S(1)} %get-tuple-element.62), channel_id=1, source_target_pairs={{0,16},{4,20},{8,24},{12,28},{16,0},{20,4},{24,8},{28,12},{1,17},{... | collective-permute-start | bytes 417800 | tf_op jit(solution)/shard_map/ppermute | solution.py:107
  6.2 11.8 %collective-permute-start.1 = (bf16[32,2176]{1,0:T(8,128)(2,1)S(1)}, bf16[32,2176]{1,0:T(8,128)(2,1)S(1)}, u32[]{:S(2)}, u32[]{:S(2)}) collective-permute-start(bf16[32,2176]{1,0:T(8,128)(2,1)S(1)} %get-tuple-element.63), channel_id=1, source_target_pairs={{0,8},{4,12},{8,16},{12,20},{16,24},{20,28},{24,0},{28,4},{1,9},{5... | collective-permute-start | bytes 417800 | tf_op jit(solution)/shard_map/ppermute | solution.py:107
  7.7 12.2 %collective-permute-start.2 = (bf16[32,2176]{1,0:T(8,128)(2,1)S(1)}, bf16[32,2176]{1,0:T(8,128)(2,1)S(1)}, u32[]{:S(2)}, u32[]{:S(2)}) collective-permute-start(bf16[32,2176]{1,0:T(8,128)(2,1)S(1)} %get-tuple-element.64), channel_id=1, source_target_pairs={{0,24},{4,28},{8,0},{12,4},{16,8},{20,12},{24,16},{28,20},{1,25},{... | collective-permute-start | bytes 417800 | tf_op jit(solution)/shard_map/ppermute | solution.py:107
  10.0 11.8 %collective-permute-start.3 = (bf16[32,2176]{1,0:T(8,128)(2,1)S(1)}, bf16[32,2176]{1,0:T(8,128)(2,1)S(1)}, u32[]{:S(2)}, u32[]{:S(2)}) collective-permute-start(bf16[32,2176]{1,0:T(8,128)(2,1)S(1)} %get-tuple-element.65), channel_id=1, source_target_pairs={{0,4},{4,8},{8,12},{12,16},{16,20},{20,24},{24,28},{28,0},{1,5},{5... | collective-permute-start | bytes 417800 | tf_op jit(solution)/shard_map/ppermute | solution.py:107
  11.5 18.4 %collective-permute-start.4 = (bf16[32,2176]{1,0:T(8,128)(2,1)S(1)}, bf16[32,2176]{1,0:T(8,128)(2,1)S(1)}, u32[]{:S(2)}, u32[]{:S(2)}) collective-permute-start(bf16[32,2176]{1,0:T(8,128)(2,1)S(1)} %get-tuple-element.66), channel_id=1, source_target_pairs={{0,12},{4,16},{8,20},{12,24},{16,28},{20,0},{24,4},{28,8},{1,13},{... | collective-permute-start | bytes 417800 | tf_op jit(solution)/shard_map/ppermute | solution.py:107
  17.3 12.7 %collective-permute-start.5 = (bf16[32,2176]{1,0:T(8,128)(2,1)S(1)}, bf16[32,2176]{1,0:T(8,128)(2,1)S(1)}, u32[]{:S(2)}, u32[]{:S(2)}) collective-permute-start(bf16[32,2176]{1,0:T(8,128)(2,1)S(1)} %get-tuple-element.67), channel_id=1, source_target_pairs={{0,20},{4,24},{8,28},{12,0},{16,4},{20,8},{24,12},{28,16},{1,21},{... | collective-permute-start | bytes 417800 | tf_op jit(solution)/shard_map/ppermute | solution.py:107
  18.0 12.0 %collective-permute-start.6 = (bf16[32,2176]{1,0:T(8,128)(2,1)S(1)}, bf16[32,2176]{1,0:T(8,128)(2,1)S(1)}, u32[]{:S(2)}, u32[]{:S(2)}) collective-permute-start(bf16[32,2176]{1,0:T(8,128)(2,1)S(1)} %get-tuple-element.61), channel_id=1, source_target_pairs={{0,28},{4,0},{8,4},{12,8},{16,12},{20,16},{24,20},{28,24},{1,29},{... | collective-permute-start | bytes 417800 | tf_op jit(solution)/shard_map/ppermute | solution.py:107
  31.5 2.7 %collective-permute-start.7 = (f32[128,2048]{1,0:T(8,128)S(1)}, f32[128,2048]{1,0:T(8,128)S(1)}, u32[]{:S(2)}, u32[]{:S(2)}) collective-permute-start(f32[128,2048]{1,0:T(8,128)S(1)} %slice.243), channel_id=1, source_target_pairs={{0,1},{1,0},{2,3},{3,2},{4,5},{5,4},{6,7},{7,6},{8,9},{9,8},{10,11... | collective-permute-start | bytes 3145736 | tf_op jit(solution)/shard_map/ppermute | solution.py:93
  34.3 9.4 %collective-permute-start.8 = (bf16[64,2048]{1,0:T(8,128)(2,1)S(1)}, bf16[64,2048]{1,0:T(8,128)(2,1)S(1)}, u32[]{:S(2)}, u32[]{:S(2)}) collective-permute-start(bf16[64,2048]{1,0:T(8,128)(2,1)S(1)} %slice.306), channel_id=1, source_target_pairs={{0,2},{1,3},{2,0},{3,1},{4,6},{5,7},{6,4},{7,5},{8,10},{9,11},{10,... | collective-permute-start | bytes 786440 | tf_op jit(solution)/shard_map/ppermute | solution.py:93

commit v20 on v12

--- a/solution.py
+++ b/solution.py
@@ -83,6 +83,15 @@
 
 def halving_reduce(partial, time_groups):
     level_bits = int(math.log2(time_groups))
+    if level_bits == 2:
+        share = partial.shape[0] // 4
+        near = [(i, i ^ 1) for i in range(time_groups)]
+        far = [(i, i ^ 2) for i in range(time_groups)]
+        first = lax.ppermute(partial[:share], "tm", near)
+        second = lax.ppermute(partial[share:2 * share], "tm", near)
+        forward = partial[2 * share:3 * share] + first
+        received = lax.ppermute(forward.astype(jnp.bfloat16), "tm", far)
+        return (partial[3 * share:] + second) + received.astype(jnp.float32)
     for level in range(level_bits):
         half = partial.shape[0] // 2
         bit = 1 << level

time: 46 us -> 48.7 us (1.059)
  local copies, waits for them, and re-layouts: 1.21 us -> 6.55 us
  waiting for transfers between devices: 25.1 us -> 19.9 us
  matrix products: 3.1 us -> 4.38 us
  other arithmetic: 6.02 us -> 6.72 us
    ppermute x7, waiting for transfers between devices: 19.1 us -> 13.5 us  [uv_exchange(): pieces.append(lax.ppermute(outgoing[shift], 'uv', perm))]
    unnamed x10, local copies, waits for them, and re-layouts: 0.28 us -> 4.13 us
    dot_general x1, matrix products: 0.85 us -> 2.13 us  [per_device(): jnp.dot(weights, arrived[:, :row_width], preferred_element_type=jnp.float32)]
    slice x1, local copies, waits for them, and re-layouts: 0.09 us -> 1 us  [per_device(): arr_anchor = arrived[:, row_width].astype(jnp.int32)]
    another operation x1, local copies, waits for them, and re-layouts: 0.02 us -> 0.68 us  [uv_exchange(): return jnp.stack(pieces)]
    unnamed x1, other arithmetic: 0.01 us -> 0.65 us
    ppermute x2 -> x3, waiting for transfers between devices: 5.93 us -> 6.35 us  [the longest x1 5.8 us: halving_reduce(): received = lax.ppermute(forward.astype(jnp.bfloat16), 'tm', far)]
    ppermute x2 -> x3, starting transfers between devices: 1.64 us -> 1.77 us  [the longest x1 1.5 us: halving_reduce(): received = lax.ppermute(forward.astype(jnp.bfloat16), 'tm', far)]
  transfers between devices with their start and end apart: 9 -> 10, of which waited for: 7 -> 7; matrix products, arithmetic and copies ran while one was open for 9% -> 18% of each run, Pallas kernels for 0% -> 0%
where the time goes in v20:
time: 48.7 us; the launch traced here: 48.1 us
  waiting for transfers between devices  19.9 us (41%)
  starting transfers between devices  10.4 us (21%)
  other arithmetic  6.72 us (14%)
  local copies, waits for them, and re-layouts  6.55 us (13%)
  matrix products  4.38 us (9%)
    ppermute x7, waiting for transfers between devices, uv_exchange(): pieces.append(lax.ppermute(outgoing[shift], 'uv', perm))  13.5 us
    ppermute x7, starting transfers between devices, uv_exchange(): pieces.append(lax.ppermute(outgoing[shift], 'uv', perm))  8.62 us
    ppermute x1, waiting for transfers between devices, halving_reduce(): received = lax.ppermute(forward.astype(jnp.bfloat16), 'tm', far)  5.8 us
    unnamed x10, local copies, waits for them, and re-layouts  4.13 us
    dot_general x1, matrix products, per_device(): jnp.dot(weights, arrived[:, :row_width], preferred_element_type=jnp.float32)  2.13 us
    dot_general x1, matrix products, per_device(): jnp.dot(lhs, delay_halves(), preferred_element_type=jnp.float32) * out_scale  1.51 us
    ppermute x1, starting transfers between devices, halving_reduce(): received = lax.ppermute(forward.astype(jnp.bfloat16), 'tm', far)  1.5 us
    another operation x2, other arithmetic  1.28 us
  transfers between devices with their start and end apart: 10, of which 7 were waited for; matrix products, arithmetic and copies ran while one was open for 18% of the time, Pallas kernels for 0%

profile of v20, /device:TPU:12, one launch (start us, length us, event | category | flops | bytes accessed | tf_op | source)
XLA Modules:
  0.0 48.1 jit_solution(345237755072473718)
XLA Ops:
  0.0 0.0 copy-start
  0.0 0.8 %fusion.91 = s32[11,128]{1,0:T(8,128)S(1)} fusion(s32[1,8]{1,0:T(1,128)} %bitcast.83, s32[8,32]{1,0:T(8,128)} %bitcast.62, s32[1,128]{1,0:T(1,128)} %param.15, s32[1,128]{1,0:T(1,128)} %param.14), kind=kLoop, calls=%fused_computation.131 | loop fusion | flops 4224 | bytes 7712 | tf_op jit(solution)/shard_map/concatenate | solution.py:129
  0.8 0.1 eq.83
  0.9 0.1 pad_add_fusion.1
  1.0 0.1 dynamic_slice.7
  1.1 0.1 iota_compare_fusion.1
  1.1 0.1 lt.56
  1.2 0.3 convolution_convert_fusion.1
  1.5 0.0 copy-done
  1.5 0.5 %convolution_convert_fusion = bf16[256,2048]{1,0:T(8,128)(2,1)S(1)} fusion(bf16[1,128,2048]{2,1,0:T(8,128)(2,1)S(1)} %copy-done, s32[256]{0:T(256)S(1)} %eq.83, pred[256]{0:T(512)(128)(4,1)S(1)} %lt.56), kind=kOutput, calls=%fused_computation.17 | convolution fusion | flops 134807552 | bytes 1574144 | tf_op jit(solution)/shard_map/dot_general | solution.py:151
  2.0 0.1 pad_maximum_fusion.1
  2.0 1.6 %collective-permute-start = (bf16[32,2176]{1,0:T(8,128)(2,1)S(1)}, bf16[32,2176]{1,0:T(8,128)(2,1)S(1)}, u32[]{:S(2)}, u32[]{:S(2)}) collective-permute-start(bf16[32,2176]{1,0:T(8,128)(2,1)S(1)} %get-tuple-element.64), channel_id=1, source_target_pairs={{0,4},{4,8},{8,12},{12,16},{16,20},{20,24},{24,28},{28,0},{1,5},{5... | collective-permute-start | bytes 417800 | tf_op jit(solution)/shard_map/ppermute | solution.py:113
  3.6 1.6 %collective-permute-start.1 = (bf16[32,2176]{1,0:T(8,128)(2,1)S(1)}, bf16[32,2176]{1,0:T(8,128)(2,1)S(1)}, u32[]{:S(2)}, u32[]{:S(2)}) collective-permute-start(bf16[32,2176]{1,0:T(8,128)(2,1)S(1)} %get-tuple-element.65), channel_id=1, source_target_pairs={{0,8},{4,12},{8,16},{12,20},{16,24},{20,28},{24,0},{28,4},{1,9},{5... | collective-permute-start | bytes 417800 | tf_op jit(solution)/shard_map/ppermute | solution.py:113
  5.2 1.2 %collective-permute-start.2 = (bf16[32,2176]{1,0:T(8,128)(2,1)S(1)}, bf16[32,2176]{1,0:T(8,128)(2,1)S(1)}, u32[]{:S(2)}, u32[]{:S(2)}) collective-permute-start(bf16[32,2176]{1,0:T(8,128)(2,1)S(1)} %get-tuple-element.66), channel_id=1, source_target_pairs={{0,12},{4,16},{8,20},{12,24},{16,28},{20,0},{24,4},{28,8},{1,13},{... | collective-permute-start | bytes 417800 | tf_op jit(solution)/shard_map/ppermute | solution.py:113
  6.4 1.7 %collective-permute-start.3 = (bf16[32,2176]{1,0:T(8,128)(2,1)S(1)}, bf16[32,2176]{1,0:T(8,128)(2,1)S(1)}, u32[]{:S(2)}, u32[]{:S(2)}) collective-permute-start(bf16[32,2176]{1,0:T(8,128)(2,1)S(1)} %get-tuple-element.67), channel_id=1, source_target_pairs={{0,16},{4,20},{8,24},{12,28},{16,0},{20,4},{24,8},{28,12},{1,17},{... | collective-permute-start | bytes 417800 | tf_op jit(solution)/shard_map/ppermute | solution.py:113
  8.1 1.3 %collective-permute-start.4 = (bf16[32,2176]{1,0:T(8,128)(2,1)S(1)}, bf16[32,2176]{1,0:T(8,128)(2,1)S(1)}, u32[]{:S(2)}, u32[]{:S(2)}) collective-permute-start(bf16[32,2176]{1,0:T(8,128)(2,1)S(1)} %get-tuple-element.68), channel_id=1, source_target_pairs={{0,20},{4,24},{8,28},{12,0},{16,4},{20,8},{24,12},{28,16},{1,21},{... | collective-permute-start | bytes 417800 | tf_op jit(solution)/shard_map/ppermute | solution.py:113
  9.4 0.7 %bitcast_dynamic-update-slice_fusion.7 = bf16[8,32,2176]{2,1,0:T(8,128)(2,1)} fusion(bf16[256,128]{1,0:T(8,128)(2,1)S(1)} %convolution_convert_fusion.1, bf16[256,2048]{1,0:T(8,128)(2,1)S(1)} %convolution_convert_fusion), kind=kLoop, calls=%fused_computation.63 | loop fusion | flops 278527 | bytes 1253376
  10.0 0.6 %fusion.80 = (f32[1024,32]{0,1:T(8,128)S(1)}, f32[1024,32]{0,1:T(8,128)S(1)}) fusion(s32[32]{0:T(128)S(1)} %iota_multiply_fusion), kind=kLoop, calls=%fused_computation.117 | loop fusion | flops 458752 | bytes 262272 | tf_op jit(solution)/shard_map/cos | solution.py:51
  10.6 0.1 scatter.15
  10.7 0.1 scatter.16
  10.8 0.1 scatter.19
  11.0 0.1 iota_add_fusion
  11.0 0.1 add.348
  11.2 0.5 %fusion.77 = (f32[1024,32]{0,1:T(8,128)S(1)}, f32[1024,32]{0,1:T(8,128)S(1)}) fusion(), kind=kLoop, calls=%fused_computation.114 | loop fusion | flops 458752 | bytes 262144 | tf_op jit(solution)/shard_map/sin | solution.py:52
  11.7 0.0 collective-permute-done
  11.7 1.3 %collective-permute-start.5 = (bf16[32,2176]{1,0:T(8,128)(2,1)S(1)}, bf16[32,2176]{1,0:T(8,128)(2,1)S(1)}, u32[]{:S(2)}, u32[]{:S(2)}) collective-permute-start(bf16[32,2176]{1,0:T(8,128)(2,1)S(1)} %get-tuple-element.69), channel_id=1, source_target_pairs={{0,24},{4,28},{8,0},{12,4},{16,8},{20,12},{24,16},{28,20},{1,25},{... | collective-permute-start | bytes 417800 | tf_op jit(solution)/shard_map/ppermute | solution.py:113
  13.0 0.7 %bitcast_dynamic-update-slice_fusion.6 = bf16[8,32,2176]{2,1,0:T(8,128)(2,1)} fusion(bf16[8,32,2176]{2,1,0:T(8,128)(2,1)} %bitcast_dynamic-update-slice_fusion.7, bf16[32,2176]{1,0:T(8,128)(2,1)S(1)} %collective-permute-done), kind=kLoop, calls=%fused_computation.62 | loop fusion | bytes 278528
  13.7 9.0 %collective-permute-done.1 = bf16[32,2176]{1,0:T(8,128)(2,1)S(1)} collective-permute-done((bf16[32,2176]{1,0:T(8,128)(2,1)S(1)}, bf16[32,2176]{1,0:T(8,128)(2,1)S(1)}, u32[]{:S(2)}, u32[]{:S(2)}) %collective-permute-start.1) | collective-permute-done | bytes 139296 | tf_op jit(solution)/shard_map/ppermute | solution.py:113
  22.6 0.0 collective-permute-start.6
  22.6 0.7 %bitcast_dynamic-update-slice_fusion.5 = bf16[8,32,2176]{2,1,0:T(8,128)(2,1)} fusion(bf16[8,32,2176]{2,1,0:T(8,128)(2,1)} %bitcast_dynamic-update-slice_fusion.6, bf16[32,2176]{1,0:T(8,128)(2,1)S(1)} %collective-permute-done.1), kind=kLoop, calls=%fused_computation.61 | loop fusion | bytes 278528
  23.3 2.3 %collective-permute-done.2 = bf16[32,2176]{1,0:T(8,128)(2,1)S(1)} collective-permute-done((bf16[32,2176]{1,0:T(8,128)(2,1)S(1)}, bf16[32,2176]{1,0:T(8,128)(2,1)S(1)}, u32[]{:S(2)}, u32[]{:S(2)}) %collective-permute-start.2) | collective-permute-done | bytes 139296 | tf_op jit(solution)/shard_map/ppermute | solution.py:113
  25.6 0.7 %bitcast_dynamic-update-slice_fusion.4 = bf16[8,32,2176]{2,1,0:T(8,128)(2,1)} fusion(bf16[8,32,2176]{2,1,0:T(8,128)(2,1)} %bitcast_dynamic-update-slice_fusion.5, bf16[32,2176]{1,0:T(8,128)(2,1)S(1)} %collective-permute-done.2), kind=kLoop, calls=%fused_computation.60 | loop fusion | bytes 278528
  26.3 1.2 %collective-permute-done.3 = bf16[32,2176]{1,0:T(8,128)(2,1)S(1)} collective-permute-done((bf16[32,2176]{1,0:T(8,128)(2,1)S(1)}, bf16[32,2176]{1,0:T(8,128)(2,1)S(1)}, u32[]{:S(2)}, u32[]{:S(2)}) %collective-permute-start.3) | collective-permute-done | bytes 139296 | tf_op jit(solution)/shard_map/ppermute | solution.py:113
  27.4 0.7 %bitcast_dynamic-update-slice_fusion.3 = bf16[8,32,2176]{2,1,0:T(8,128)(2,1)} fusion(bf16[8,32,2176]{2,1,0:T(8,128)(2,1)} %bitcast_dynamic-update-slice_fusion.4, bf16[32,2176]{1,0:T(8,128)(2,1)S(1)} %collective-permute-done.3), kind=kLoop, calls=%fused_computation.59 | loop fusion | bytes 278528
  28.1 0.0 collective-permute-done.4
  28.1 0.7 %bitcast_dynamic-update-slice_fusion.2 = bf16[8,32,2176]{2,1,0:T(8,128)(2,1)} fusion(bf16[8,32,2176]{2,1,0:T(8,128)(2,1)} %bitcast_dynamic-update-slice_fusion.3, bf16[32,2176]{1,0:T(8,128)(2,1)S(1)} %collective-permute-done.4), kind=kLoop, calls=%fused_computation.58 | loop fusion | bytes 278528
  28.8 0.5 collective-permute-done.5
  29.3 0.7 %bitcast_dynamic-update-slice_fusion.1 = bf16[8,32,2176]{2,1,0:T(8,128)(2,1)} fusion(bf16[8,32,2176]{2,1,0:T(8,128)(2,1)} %bitcast_dynamic-update-slice_fusion.2, bf16[32,2176]{1,0:T(8,128)(2,1)S(1)} %collective-permute-done.5), kind=kLoop, calls=%fused_computation.57 | loop fusion | bytes 278528
  29.9 0.6 %collective-permute-done.6 = bf16[32,2176]{1,0:T(8,128)(2,1)S(1)} collective-permute-done((bf16[32,2176]{1,0:T(8,128)(2,1)S(1)}, bf16[32,2176]{1,0:T(8,128)(2,1)S(1)}, u32[]{:S(2)}, u32[]{:S(2)}) %collective-permute-start.6) | collective-permute-done | bytes 139296 | tf_op jit(solution)/shard_map/ppermute | solution.py:113
  30.5 0.7 %bitcast_dynamic-update-slice_fusion = bf16[8,32,2176]{2,1,0:T(8,128)(2,1)} fusion(bf16[8,32,2176]{2,1,0:T(8,128)(2,1)} %bitcast_dynamic-update-slice_fusion.1, bf16[32,2176]{1,0:T(8,128)(2,1)S(1)} %collective-permute-done.6), kind=kLoop, calls=%fused_computation.56 | loop fusion | bytes 278528 | tf_op jit(solution)/shard_map/stack | solution.py:114
  31.2 1.0 %fusion.99 = (bf16[256,1]{1,0:T(8,128)(2,1)S(1)}, bf16[256,1]{1,0:T(8,128)(2,1)S(1)}) fusion(bf16[256,2176]{1,0:T(8,128)(2,1)} %bitcast.60), kind=kLoop, calls=%fused_computation.184 | loop fusion | bytes 2048 | tf_op jit(solution)/shard_map/slice | solution.py:162
  32.2 0.1 copy.11
  32.3 0.1 copy.12
  32.5 0.1 fusion.87
  32.6 2.1 %fusion.9 = f32[256,2048]{1,0:T(8,128)S(1)} fusion(bf16[256,2176]{1,0:T(8,128)(2,1)} %bitcast.61, f32[256]{0:T(256)S(1)} %bitcast.81, s32[256]{0:T(256)S(1)} %get-tuple-element.111, f32[256]{0:T(256)S(1)} %bitcast.80, s32[256]{0:T(256)S(1)} %get-tuple-element.107, f32[256]{0:T(256)S(1)} %bitcast.79, s32[256]{0:T(256)S(1)} %get-tuple-element.108, ...), kind=kOutput, calls=%fused_computation.20 | convolution fusion | flops 271581184 | bytes 3180544 | tf_op jit(solution)/shard_map/dot_general | solution.py:171
  34.8 0.1 collective-permute-start.8
  34.9 0.1 multiply_subtract_fusion.1
  34.9 1.3 %multiply_subtract_fusion = (f32[1024,32,32]{0,2,1:T(8,128)S(1)}, f32[1024,32,32]{0,2,1:T(8,128)S(1)}) fusion(f32[1024,32]{0,1:T(8,128)S(1)} %get-tuple-element.130, f32[1024,32]{0,1:T(8,128)S(1)} %get-tuple-element.115, f32[1024,32]{0,1:T(8,128)S(1)} %get-tuple-element.131, f32[1024,32]{0,1:T(8,128)S(1)} %get-tuple-element.114), kind=kLoop, calls=%fused_computation.9 | loop fusion | flops 6291456 | bytes 8912896 | tf_op jit(solution)/shard_map/sub | solution.py:53
  36.2 0.5 %collective-permute-done.8 = f32[64,2048]{1,0:T(8,128)S(1)} collective-permute-done((f32[64,2048]{1,0:T(8,128)S(1)}, f32[64,2048]{1,0:T(8,128)S(1)}, u32[]{:S(2)}, u32[]{:S(2)}) %collective-permute-start.8) | collective-permute-done | bytes 524320 | tf_op jit(solution)/shard_map/ppermute | solution.py:90
  36.7 0.1 fusion.11
  36.9 0.2 collective-permute-start.7
  37.1 1.5 %collective-permute-start.9 = (bf16[64,2048]{1,0:T(8,128)(2,1)S(1)}, bf16[64,2048]{1,0:T(8,128)(2,1)S(1)}, u32[]{:S(2)}, u32[]{:S(2)}) collective-permute-start(bf16[64,2048]{1,0:T(8,128)(2,1)S(1)} %get-tuple-element.59), channel_id=1, source_target_pairs={{0,2},{1,3},{2,0},{3,1},{4,6},{5,7},{6,4},{7,5},{8,10},{9,11},{10,... | collective-permute-start | bytes 786440 | tf_op jit(solution)/shard_map/ppermute | solution.py:93
  38.6 1.3 %fusion.5 = (bf16[1024,1024]{0,1:T(8,128)(2,1)S(1)}, bf16[1024,1024]{0,1:T(8,128)(2,1)S(1)}) fusion(f32[1024,32,32]{0,2,1:T(8,128)S(1)} %get-tuple-element.72, f32[1024]{0:T(1024)S(1)} %multiply_subtract_fusion.1, f32[1024,32,32]{0,2,1:T(8,128)S(1)} %get-tuple-element.73), kind=kLoop, calls=%fused_computation.7 | loop fusion | flops 4194304 | bytes 12587008 | tf_op jit(solution)/shard_map/convert
  39.8 5.8 %collective-permute-done.9 = bf16[64,2048]{1,0:T(8,128)(2,1)S(1)} collective-permute-done((bf16[64,2048]{1,0:T(8,128)(2,1)S(1)}, bf16[64,2048]{1,0:T(8,128)(2,1)S(1)}, u32[]{:S(2)}, u32[]{:S(2)}) %collective-permute-start.9) | collective-permute-done | bytes 262176 | tf_op jit(solution)/shard_map/ppermute | solution.py:93
  45.6 0.0 collective-permute-done.7
  45.6 0.1 fusion.13
  45.7 1.5 %fusion.6 = f32[128,1024]{1,0:T(8,128)S(1)} fusion(bf16[1024,1024]{0,1:T(8,128)(2,1)S(1)} %get-tuple-element.93, bf16[1024,1024]{0,1:T(8,128)(2,1)S(1)} %get-tuple-element.92, bf16[64,1024]{1,0:T(8,128)(2,1)S(1)} %get-tuple-element.75, bf16[64,1024]{1,0:T(8,128)(2,1)S(1)} %get-tuple-element.74, bf16[64,2048]{1,0:T(8,128)(2,1)S(1)} %fusion.13), kind=kOutput, calls=%fused_computation.18 | convolution fusion | flops 546963456 | bytes 5242880 | tf_op jit(solution)/shard_map/dot_general | solution.py:182
  47.3 0.8 %pad_maximum_fusion = f32[64,2048]{1,0:T(8,128)} fusion(f32[64,1024]{1,0:T(8,128)S(1)} %get-tuple-element.71, f32[64,1024]{1,0:T(8,128)S(1)} %get-tuple-element.70), kind=kLoop, calls=%fused_computation.32 | loop fusion | flops 131072 | bytes 1048576 | tf_op jit(solution)/shard_map/concatenate | solution.py:184
  (19 shorter events, 0.3 us)
Async XLA Ops:
  0.0 1.5 %copy-start = (bf16[1,128,2048]{2,1,0:T(8,128)(2,1)S(1)}, bf16[1,128,2048]{2,1,0:T(8,128)(2,1)}, u32[]{:S(2)}) copy-start(bf16[1,128,2048]{2,1,0:T(8,128)(2,1)} %param.13) | copy-start | bytes 1572868
  2.0 9.6 %collective-permute-start = (bf16[32,2176]{1,0:T(8,128)(2,1)S(1)}, bf16[32,2176]{1,0:T(8,128)(2,1)S(1)}, u32[]{:S(2)}, u32[]{:S(2)}) collective-permute-start(bf16[32,2176]{1,0:T(8,128)(2,1)S(1)} %get-tuple-element.64), channel_id=1, source_target_pairs={{0,4},{4,8},{8,12},{12,16},{16,20},{20,24},{24,28},{28,0},{1,5},{5... | collective-permute-start | bytes 417800 | tf_op jit(solution)/shard_map/ppermute | solution.py:113
  3.6 19.0 %collective-permute-start.1 = (bf16[32,2176]{1,0:T(8,128)(2,1)S(1)}, bf16[32,2176]{1,0:T(8,128)(2,1)S(1)}, u32[]{:S(2)}, u32[]{:S(2)}) collective-permute-start(bf16[32,2176]{1,0:T(8,128)(2,1)S(1)} %get-tuple-element.65), channel_id=1, source_target_pairs={{0,8},{4,12},{8,16},{12,20},{16,24},{20,28},{24,0},{28,4},{1,9},{5... | collective-permute-start | bytes 417800 | tf_op jit(solution)/shard_map/ppermute | solution.py:113
  5.2 20.4 %collective-permute-start.2 = (bf16[32,2176]{1,0:T(8,128)(2,1)S(1)}, bf16[32,2176]{1,0:T(8,128)(2,1)S(1)}, u32[]{:S(2)}, u32[]{:S(2)}) collective-permute-start(bf16[32,2176]{1,0:T(8,128)(2,1)S(1)} %get-tuple-element.66), channel_id=1, source_target_pairs={{0,12},{4,16},{8,20},{12,24},{16,28},{20,0},{24,4},{28,8},{1,13},{... | collective-permute-start | bytes 417800 | tf_op jit(solution)/shard_map/ppermute | solution.py:113
  6.4 21.1 %collective-permute-start.3 = (bf16[32,2176]{1,0:T(8,128)(2,1)S(1)}, bf16[32,2176]{1,0:T(8,128)(2,1)S(1)}, u32[]{:S(2)}, u32[]{:S(2)}) collective-permute-start(bf16[32,2176]{1,0:T(8,128)(2,1)S(1)} %get-tuple-element.67), channel_id=1, source_target_pairs={{0,16},{4,20},{8,24},{12,28},{16,0},{20,4},{24,8},{28,12},{1,17},{... | collective-permute-start | bytes 417800 | tf_op jit(solution)/shard_map/ppermute | solution.py:113
  8.1 20.1 %collective-permute-start.4 = (bf16[32,2176]{1,0:T(8,128)(2,1)S(1)}, bf16[32,2176]{1,0:T(8,128)(2,1)S(1)}, u32[]{:S(2)}, u32[]{:S(2)}) collective-permute-start(bf16[32,2176]{1,0:T(8,128)(2,1)S(1)} %get-tuple-element.68), channel_id=1, source_target_pairs={{0,20},{4,24},{8,28},{12,0},{16,4},{20,8},{24,12},{28,16},{1,21},{... | collective-permute-start | bytes 417800 | tf_op jit(solution)/shard_map/ppermute | solution.py:113
  11.7 17.6 %collective-permute-start.5 = (bf16[32,2176]{1,0:T(8,128)(2,1)S(1)}, bf16[32,2176]{1,0:T(8,128)(2,1)S(1)}, u32[]{:S(2)}, u32[]{:S(2)}) collective-permute-start(bf16[32,2176]{1,0:T(8,128)(2,1)S(1)} %get-tuple-element.69), channel_id=1, source_target_pairs={{0,24},{4,28},{8,0},{12,4},{16,8},{20,12},{24,16},{28,20},{1,25},{... | collective-permute-start | bytes 417800 | tf_op jit(solution)/shard_map/ppermute | solution.py:113
  22.6 7.9 %collective-permute-start.6 = (bf16[32,2176]{1,0:T(8,128)(2,1)S(1)}, bf16[32,2176]{1,0:T(8,128)(2,1)S(1)}, u32[]{:S(2)}, u32[]{:S(2)}) collective-permute-start(bf16[32,2176]{1,0:T(8,128)(2,1)S(1)} %get-tuple-element.63), channel_id=1, source_target_pairs={{0,28},{4,0},{8,4},{12,8},{16,12},{20,16},{24,20},{28,24},{1,29},{... | collective-permute-start | bytes 417800 | tf_op jit(solution)/shard_map/ppermute | solution.py:113
  34.8 2.0 %collective-permute-start.8 = (f32[64,2048]{1,0:T(8,128)S(1)}, f32[64,2048]{1,0:T(8,128)S(1)}, u32[]{:S(2)}, u32[]{:S(2)}) collective-permute-start(f32[64,2048]{1,0:T(8,128)S(1)} %slice.244), channel_id=1, source_target_pairs={{0,1},{1,0},{2,3},{3,2},{4,5},{5,4},{6,7},{7,6},{8,9},{9,8},{10,11... | collective-permute-start | bytes 1572872 | tf_op jit(solution)/shard_map/ppermute | solution.py:90
  36.9 8.8 %collective-permute-start.7 = (f32[64,2048]{1,0:T(8,128)S(1)}, f32[64,2048]{1,0:T(8,128)S(1)}, u32[]{:S(2)}, u32[]{:S(2)}) collective-permute-start(f32[64,2048]{1,0:T(8,128)S(1)} %get-tuple-element.60), channel_id=1, source_target_pairs={{0,1},{1,0},{2,3},{3,2},{4,5},{5,4},{6,7},{7,6},{8,9},{9,8},{10,11... | collective-permute-start | bytes 1572872 | tf_op jit(solution)/shard_map/ppermute | solution.py:91
  37.1 8.6 %collective-permute-start.9 = (bf16[64,2048]{1,0:T(8,128)(2,1)S(1)}, bf16[64,2048]{1,0:T(8,128)(2,1)S(1)}, u32[]{:S(2)}, u32[]{:S(2)}) collective-permute-start(bf16[64,2048]{1,0:T(8,128)(2,1)S(1)} %get-tuple-element.59), channel_id=1, source_target_pairs={{0,2},{1,3},{2,0},{3,1},{4,6},{5,7},{6,4},{7,5},{8,10},{9,11},{10,... | collective-permute-start | bytes 786440 | tf_op jit(solution)/shard_map/ppermute | solution.py:93

commit v21 on v12

--- a/solution.py
+++ b/solution.py
@@ -50,8 +50,6 @@
     ang_lo = scale * ((freq[:, None] * lo[None, :]) % NCH).astype(jnp.float32)
     c_hi, s_hi = jnp.cos(ang_hi), jnp.sin(ang_hi)
     c_lo, s_lo = jnp.cos(ang_lo), jnp.sin(ang_lo)
-    cosine = c_hi[:, :, None] * c_lo[:, None, :] - s_hi[:, :, None] * s_lo[:, None, :]
-    sine = s_hi[:, :, None] * c_lo[:, None, :] + c_hi[:, :, None] * s_lo[:, None, :]
     window_arg = 2.0 * math.pi * freq.astype(jnp.float32) / (NCH - 1)
     taper = (
         0.35875
@@ -59,8 +57,9 @@
         + 0.14128 * jnp.cos(2.0 * window_arg)
         - 0.01168 * jnp.cos(3.0 * window_arg)
     )
-    tap_cos = (taper[:, None, None] * cosine).reshape(NCH, NCH)
-    tap_sin = (taper[:, None, None] * sine).reshape(NCH, NCH)
+    wc_hi, ws_hi = taper[:, None] * c_hi, taper[:, None] * s_hi
+    tap_cos = (wc_hi[:, :, None] * c_lo[:, None, :] - ws_hi[:, :, None] * s_lo[:, None, :]).reshape(NCH, NCH)
+    tap_sin = (ws_hi[:, :, None] * c_lo[:, None, :] + wc_hi[:, :, None] * s_lo[:, None, :]).reshape(NCH, NCH)
     return jnp.concatenate([tap_cos, tap_sin], axis=0).astype(jnp.bfloat16)
 
 
@@ -87,9 +86,7 @@
         half = partial.shape[0] // 2
         bit = 1 << level
         perm = [(i, i ^ bit) for i in range(time_groups)]
-        outgoing = partial[:half]
-        if level > 0:
-            outgoing = outgoing.astype(jnp.bfloat16)
+        outgoing = partial[:half].astype(jnp.bfloat16)
         received = lax.ppermute(outgoing, "tm", perm)
         partial = partial[half:] + received.astype(jnp.float32)
     return partial

time: 46 us -> 48.2 us (1.048)
  starting transfers between devices: 10.3 us -> 14.7 us
  waiting for transfers between devices: 25.1 us -> 23.4 us
  other arithmetic: 6.02 us -> 5.31 us
    ppermute x7, starting transfers between devices: 8.62 us -> 13.1 us  [uv_exchange(): pieces.append(lax.ppermute(outgoing[shift], 'uv', perm))]
    ppermute x7, waiting for transfers between devices: 19.1 us -> 17.6 us  [uv_exchange(): pieces.append(lax.ppermute(outgoing[shift], 'uv', perm))]
    sub x1 -> x0, other arithmetic: 1.22 us -> none  [delay_halves(): c_hi[:, :, None] * c_lo[:, None, :] - s_hi[:, :, None] * s_lo[:, None, :]]
    mul x0 -> x1, other arithmetic: none -> 1.03 us  [delay_halves(): wc_hi, ws_hi = (taper[:, None] * c_hi, taper[:, None] * s_hi)]
    sin x1 -> x0, other arithmetic: 0.53 us -> none  [delay_halves(): c_lo, s_lo = (jnp.cos(ang_lo), jnp.sin(ang_lo))]
  transfers between devices with their start and end apart: 9 -> 9, of which waited for: 7 -> 7; matrix products, arithmetic and copies ran while one was open for 9% -> 7% of each run, Pallas kernels for 0% -> 0%
where the time goes in v21:
time: 48.2 us; the launch traced here: 48 us
  waiting for transfers between devices  23.4 us (49%)
  starting transfers between devices  14.7 us (30%)
  other arithmetic  5.31 us (11%)
  matrix products  3.1 us (6%)
  local copies, waits for them, and re-layouts  1.19 us (2%)
    ppermute x7, waiting for transfers between devices, uv_exchange(): pieces.append(lax.ppermute(outgoing[shift], 'uv', perm))  17.6 us
    ppermute x7, starting transfers between devices, uv_exchange(): pieces.append(lax.ppermute(outgoing[shift], 'uv', perm))  13.1 us
    ppermute x2, waiting for transfers between devices, halving_reduce(): received = lax.ppermute(outgoing, 'tm', perm)  5.83 us
    ppermute x2, starting transfers between devices, halving_reduce(): received = lax.ppermute(outgoing, 'tm', perm)  1.64 us
    dot_general x1, matrix products, per_device(): jnp.dot(lhs, delay_halves(), preferred_element_type=jnp.float32) * out_scale  1.51 us
    another operation x2, other arithmetic  1.39 us
    mul x1, other arithmetic, delay_halves(): wc_hi, ws_hi = (taper[:, None] * c_hi, taper[:, None] * s_hi)  1.03 us
  transfers between devices with their start and end apart: 9, of which 7 were waited for; matrix products, arithmetic and copies ran while one was open for 7% of the time, Pallas kernels for 0%

profile of v21, /device:TPU:12, one launch (start us, length us, event | category | flops | bytes accessed | tf_op | source)
XLA Modules:
  0.0 48.0 jit_solution(3056524952845351977)
XLA Ops:
  0.0 0.0 copy-start
  0.0 0.8 %fusion.85 = s32[11,128]{1,0:T(8,128)S(1)} fusion(s32[1,8]{1,0:T(1,128)} %bitcast.79, s32[8,32]{1,0:T(8,128)} %bitcast.58, s32[1,128]{1,0:T(1,128)} %param.15, s32[1,128]{1,0:T(1,128)} %param.14), kind=kLoop, calls=%fused_computation.127 | loop fusion | flops 4224 | bytes 7712 | tf_op jit(solution)/shard_map/concatenate | solution.py:117
  0.8 0.1 eq.83
  0.9 0.1 pad_add_fusion.1
  1.0 0.1 dynamic_slice.7
  1.1 0.1 iota_compare_fusion.1
  1.1 0.1 lt.56
  1.2 0.3 convolution_convert_fusion.1
  1.5 0.0 copy-done
  1.5 0.5 %convolution_convert_fusion = bf16[256,2048]{1,0:T(8,128)(2,1)S(1)} fusion(bf16[1,128,2048]{2,1,0:T(8,128)(2,1)S(1)} %copy-done, s32[256]{0:T(256)S(1)} %eq.83, pred[256]{0:T(512)(128)(4,1)S(1)} %lt.56), kind=kOutput, calls=%fused_computation.13 | convolution fusion | flops 134807552 | bytes 1574144 | tf_op jit(solution)/shard_map/dot_general | solution.py:139
  2.0 0.1 pad_maximum_fusion.1
  2.1 0.6 %collective-permute-start.6 = (bf16[32,2176]{1,0:T(8,128)(2,1)S(1)}, bf16[32,2176]{1,0:T(8,128)(2,1)S(1)}, u32[]{:S(2)}, u32[]{:S(2)}) collective-permute-start(bf16[32,2176]{1,0:T(8,128)(2,1)S(1)} %get-tuple-element.61), channel_id=1, source_target_pairs={{0,28},{4,0},{8,4},{12,8},{16,12},{20,16},{24,20},{28,24},{1,29},{... | collective-permute-start | bytes 417800 | tf_op jit(solution)/shard_map/ppermute | solution.py:101
  2.6 2.4 %collective-permute-start = (bf16[32,2176]{1,0:T(8,128)(2,1)S(1)}, bf16[32,2176]{1,0:T(8,128)(2,1)S(1)}, u32[]{:S(2)}, u32[]{:S(2)}) collective-permute-start(bf16[32,2176]{1,0:T(8,128)(2,1)S(1)} %get-tuple-element.62), channel_id=1, source_target_pairs={{0,4},{4,8},{8,12},{12,16},{16,20},{20,24},{24,28},{28,0},{1,5},{5... | collective-permute-start | bytes 417800 | tf_op jit(solution)/shard_map/ppermute | solution.py:101
  5.0 1.6 %collective-permute-start.1 = (bf16[32,2176]{1,0:T(8,128)(2,1)S(1)}, bf16[32,2176]{1,0:T(8,128)(2,1)S(1)}, u32[]{:S(2)}, u32[]{:S(2)}) collective-permute-start(bf16[32,2176]{1,0:T(8,128)(2,1)S(1)} %get-tuple-element.63), channel_id=1, source_target_pairs={{0,8},{4,12},{8,16},{12,20},{16,24},{20,28},{24,0},{28,4},{1,9},{5... | collective-permute-start | bytes 417800 | tf_op jit(solution)/shard_map/ppermute | solution.py:101
  6.6 2.8 %collective-permute-start.2 = (bf16[32,2176]{1,0:T(8,128)(2,1)S(1)}, bf16[32,2176]{1,0:T(8,128)(2,1)S(1)}, u32[]{:S(2)}, u32[]{:S(2)}) collective-permute-start(bf16[32,2176]{1,0:T(8,128)(2,1)S(1)} %get-tuple-element.64), channel_id=1, source_target_pairs={{0,12},{4,16},{8,20},{12,24},{16,28},{20,0},{24,4},{28,8},{1,13},{... | collective-permute-start | bytes 417800 | tf_op jit(solution)/shard_map/ppermute | solution.py:101
  9.4 0.0 collective-permute-start.3
  9.5 0.1 scatter.15
  9.6 0.1 scatter.16
  9.7 0.1 scatter.19
  9.8 0.1 iota_add_fusion
  9.9 0.1 add.345
  10.0 0.8 %collective-permute-done = bf16[32,2176]{1,0:T(8,128)(2,1)S(1)} collective-permute-done((bf16[32,2176]{1,0:T(8,128)(2,1)S(1)}, bf16[32,2176]{1,0:T(8,128)(2,1)S(1)}, u32[]{:S(2)}, u32[]{:S(2)}) %collective-permute-start) | collective-permute-done | bytes 139296 | tf_op jit(solution)/shard_map/ppermute | solution.py:101
  10.7 5.7 %collective-permute-start.4 = (bf16[32,2176]{1,0:T(8,128)(2,1)S(1)}, bf16[32,2176]{1,0:T(8,128)(2,1)S(1)}, u32[]{:S(2)}, u32[]{:S(2)}) collective-permute-start(bf16[32,2176]{1,0:T(8,128)(2,1)S(1)} %get-tuple-element.66), channel_id=1, source_target_pairs={{0,20},{4,24},{8,28},{12,0},{16,4},{20,8},{24,12},{28,16},{1,21},{... | collective-permute-start | bytes 417800 | tf_op jit(solution)/shard_map/ppermute | solution.py:101
  16.5 7.6 %collective-permute-done.1 = bf16[32,2176]{1,0:T(8,128)(2,1)S(1)} collective-permute-done((bf16[32,2176]{1,0:T(8,128)(2,1)S(1)}, bf16[32,2176]{1,0:T(8,128)(2,1)S(1)}, u32[]{:S(2)}, u32[]{:S(2)}) %collective-permute-start.1) | collective-permute-done | bytes 139296 | tf_op jit(solution)/shard_map/ppermute | solution.py:101
  24.1 0.0 collective-permute-start.5
  24.1 3.0 %collective-permute-done.2 = bf16[32,2176]{1,0:T(8,128)(2,1)S(1)} collective-permute-done((bf16[32,2176]{1,0:T(8,128)(2,1)S(1)}, bf16[32,2176]{1,0:T(8,128)(2,1)S(1)}, u32[]{:S(2)}, u32[]{:S(2)}) %collective-permute-start.2) | collective-permute-done | bytes 139296 | tf_op jit(solution)/shard_map/ppermute | solution.py:101
  27.1 1.5 %collective-permute-done.3 = bf16[32,2176]{1,0:T(8,128)(2,1)S(1)} collective-permute-done((bf16[32,2176]{1,0:T(8,128)(2,1)S(1)}, bf16[32,2176]{1,0:T(8,128)(2,1)S(1)}, u32[]{:S(2)}, u32[]{:S(2)}) %collective-permute-start.3) | collective-permute-done | bytes 139296 | tf_op jit(solution)/shard_map/ppermute | solution.py:101
  28.6 0.0 collective-permute-done.4
  28.7 4.7 %collective-permute-done.5 = bf16[32,2176]{1,0:T(8,128)(2,1)S(1)} collective-permute-done((bf16[32,2176]{1,0:T(8,128)(2,1)S(1)}, bf16[32,2176]{1,0:T(8,128)(2,1)S(1)}, u32[]{:S(2)}, u32[]{:S(2)}) %collective-permute-start.5) | collective-permute-done | bytes 139296 | tf_op jit(solution)/shard_map/ppermute | solution.py:101
  33.4 0.0 collective-permute-done.6
  33.5 0.1 fusion.93
  33.6 0.1 copy.11
  33.7 0.1 copy.12
  33.9 0.1 fusion.81
  34.0 0.8 %fusion.7 = f32[256,2048]{1,0:T(8,128)S(1)} fusion(bf16[256,2176]{1,0:T(8,128)(2,1)S(1)} %bitcast.57, f32[256]{0:T(256)S(1)} %bitcast.77, s32[256]{0:T(256)S(1)} %get-tuple-element.109, f32[256]{0:T(256)S(1)} %bitcast.76, s32[256]{0:T(256)S(1)} %get-tuple-element.105, f32[256]{0:T(256)S(1)} %bitcast.75, s32[256]{0:T(256)S(1)} %get-tuple-element.106, ...), kind=kOutput, calls=%fused_computation.18 | convolution fusion | flops 271581184 | bytes 3180544 | tf_op jit(solution)/shard_map/dot_general | solution.py:159
  34.8 0.1 slice.308
  34.9 0.1 collective-permute-start.7
  35.0 0.1 multiply_subtract_fusion
  35.1 0.5 %fusion.74 = f32[1024,32]{0,1:T(8,128)S(1)} fusion(), kind=kLoop, calls=%fused_computation.113 | loop fusion | flops 458752 | bytes 131072 | tf_op jit(solution)/shard_map/cos | solution.py:52
  35.6 1.0 %cosine_multiply_fusion = (f32[1024,32]{0,1:T(8,128)S(1)}, f32[1024,32]{0,1:T(8,128)S(1)}, f32[1024,32]{0,1:T(8,128)S(1)}) fusion(s32[32]{0:T(128)S(1)} %iota_multiply_fusion, f32[1024]{0:T(1024)S(1)} %multiply_subtract_fusion), kind=kLoop, calls=%fused_computation.70 | loop fusion | flops 983040 | bytes 397440 | tf_op jit(solution)/shard_map/mul | solution.py:60
  36.6 0.3 collective-permute-done.7
  36.9 0.1 slice_add_fusion
  37.0 1.6 %collective-permute-start.8 = (bf16[64,2048]{1,0:T(8,128)(2,1)S(1)}, bf16[64,2048]{1,0:T(8,128)(2,1)S(1)}, u32[]{:S(2)}, u32[]{:S(2)}) collective-permute-start(bf16[64,2048]{1,0:T(8,128)(2,1)S(1)} %slice.309), channel_id=1, source_target_pairs={{0,2},{1,3},{2,0},{3,1},{4,6},{5,7},{6,4},{7,5},{8,10},{9,11},{10,... | collective-permute-start | bytes 786440 | tf_op jit(solution)/shard_map/ppermute | solution.py:90
  38.6 1.4 %subtract_convert_fusion = (bf16[1024,32,32]{0,2,1:T(8,128)(2,1)S(1)}, bf16[1024,32,32]{0,2,1:T(8,128)(2,1)S(1)}) fusion(f32[1024,32]{0,1:T(8,128)S(1)} %get-tuple-element.120, f32[1024,32]{0,1:T(8,128)S(1)} %get-tuple-element.91, f32[1024,32]{0,1:T(8,128)S(1)} %fusion.74, f32[1024,32]{0,1:T(8,128)S(1)} %get-tuple-element.90), kind=kLoop, calls=%fused_computation.5 | loop fusion | flops 8388608 | bytes 4718592 | tf_op jit(solution)/shard_map/convert.3
  40.0 5.5 %collective-permute-done.8 = bf16[64,2048]{1,0:T(8,128)(2,1)S(1)} collective-permute-done((bf16[64,2048]{1,0:T(8,128)(2,1)S(1)}, bf16[64,2048]{1,0:T(8,128)(2,1)S(1)}, u32[]{:S(2)}, u32[]{:S(2)}) %collective-permute-start.8) | collective-permute-done | bytes 262176 | tf_op jit(solution)/shard_map/ppermute | solution.py:90
  45.6 1.5 %fusion.4 = f32[128,1024]{1,0:T(8,128)S(1)} fusion(bf16[1024,1024]{0,1:T(8,128)(2,1)S(1)} %bitcast.55, bf16[1024,1024]{0,1:T(8,128)(2,1)S(1)} %bitcast.54, bf16[64,1024]{1,0:T(8,128)(2,1)S(1)} %get-tuple-element.73, bf16[64,1024]{1,0:T(8,128)(2,1)S(1)} %get-tuple-element.72, bf16[64,2048]{1,0:T(8,128)(2,1)S(1)} %fusion.9), kind=kOutput, calls=%fused_computation.14 | convolution fusion | flops 546963456 | bytes 5242880 | tf_op jit(solution)/shard_map/dot_general | solution.py:170
  47.2 0.8 %pad_maximum_fusion = f32[64,2048]{1,0:T(8,128)} fusion(f32[64,1024]{1,0:T(8,128)S(1)} %get-tuple-element.69, f32[64,1024]{1,0:T(8,128)S(1)} %get-tuple-element.68), kind=kLoop, calls=%fused_computation.28 | loop fusion | flops 131072 | bytes 1048576 | tf_op jit(solution)/shard_map/concatenate | solution.py:172
  (28 shorter events, 0.5 us)
Async XLA Ops:
  0.0 1.5 %copy-start = (bf16[1,128,2048]{2,1,0:T(8,128)(2,1)S(1)}, bf16[1,128,2048]{2,1,0:T(8,128)(2,1)}, u32[]{:S(2)}) copy-start(bf16[1,128,2048]{2,1,0:T(8,128)(2,1)} %param.13) | copy-start | bytes 1572868
  2.1 31.4 %collective-permute-start.6 = (bf16[32,2176]{1,0:T(8,128)(2,1)S(1)}, bf16[32,2176]{1,0:T(8,128)(2,1)S(1)}, u32[]{:S(2)}, u32[]{:S(2)}) collective-permute-start(bf16[32,2176]{1,0:T(8,128)(2,1)S(1)} %get-tuple-element.61), channel_id=1, source_target_pairs={{0,28},{4,0},{8,4},{12,8},{16,12},{20,16},{24,20},{28,24},{1,29},{... | collective-permute-start | bytes 417800 | tf_op jit(solution)/shard_map/ppermute | solution.py:101
  2.6 8.1 %collective-permute-start = (bf16[32,2176]{1,0:T(8,128)(2,1)S(1)}, bf16[32,2176]{1,0:T(8,128)(2,1)S(1)}, u32[]{:S(2)}, u32[]{:S(2)}) collective-permute-start(bf16[32,2176]{1,0:T(8,128)(2,1)S(1)} %get-tuple-element.62), channel_id=1, source_target_pairs={{0,4},{4,8},{8,12},{12,16},{16,20},{20,24},{24,28},{28,0},{1,5},{5... | collective-permute-start | bytes 417800 | tf_op jit(solution)/shard_map/ppermute | solution.py:101
  5.0 19.0 %collective-permute-start.1 = (bf16[32,2176]{1,0:T(8,128)(2,1)S(1)}, bf16[32,2176]{1,0:T(8,128)(2,1)S(1)}, u32[]{:S(2)}, u32[]{:S(2)}) collective-permute-start(bf16[32,2176]{1,0:T(8,128)(2,1)S(1)} %get-tuple-element.63), channel_id=1, source_target_pairs={{0,8},{4,12},{8,16},{12,20},{16,24},{20,28},{24,0},{28,4},{1,9},{5... | collective-permute-start | bytes 417800 | tf_op jit(solution)/shard_map/ppermute | solution.py:101
  6.6 20.5 %collective-permute-start.2 = (bf16[32,2176]{1,0:T(8,128)(2,1)S(1)}, bf16[32,2176]{1,0:T(8,128)(2,1)S(1)}, u32[]{:S(2)}, u32[]{:S(2)}) collective-permute-start(bf16[32,2176]{1,0:T(8,128)(2,1)S(1)} %get-tuple-element.64), channel_id=1, source_target_pairs={{0,12},{4,16},{8,20},{12,24},{16,28},{20,0},{24,4},{28,8},{1,13},{... | collective-permute-start | bytes 417800 | tf_op jit(solution)/shard_map/ppermute | solution.py:101
  9.4 19.2 %collective-permute-start.3 = (bf16[32,2176]{1,0:T(8,128)(2,1)S(1)}, bf16[32,2176]{1,0:T(8,128)(2,1)S(1)}, u32[]{:S(2)}, u32[]{:S(2)}) collective-permute-start(bf16[32,2176]{1,0:T(8,128)(2,1)S(1)} %get-tuple-element.65), channel_id=1, source_target_pairs={{0,16},{4,20},{8,24},{12,28},{16,0},{20,4},{24,8},{28,12},{1,17},{... | collective-permute-start | bytes 417800 | tf_op jit(solution)/shard_map/ppermute | solution.py:101
  10.7 17.9 %collective-permute-start.4 = (bf16[32,2176]{1,0:T(8,128)(2,1)S(1)}, bf16[32,2176]{1,0:T(8,128)(2,1)S(1)}, u32[]{:S(2)}, u32[]{:S(2)}) collective-permute-start(bf16[32,2176]{1,0:T(8,128)(2,1)S(1)} %get-tuple-element.66), channel_id=1, source_target_pairs={{0,20},{4,24},{8,28},{12,0},{16,4},{20,8},{24,12},{28,16},{1,21},{... | collective-permute-start | bytes 417800 | tf_op jit(solution)/shard_map/ppermute | solution.py:101
  24.1 9.3 %collective-permute-start.5 = (bf16[32,2176]{1,0:T(8,128)(2,1)S(1)}, bf16[32,2176]{1,0:T(8,128)(2,1)S(1)}, u32[]{:S(2)}, u32[]{:S(2)}) collective-permute-start(bf16[32,2176]{1,0:T(8,128)(2,1)S(1)} %get-tuple-element.67), channel_id=1, source_target_pairs={{0,24},{4,28},{8,0},{12,4},{16,8},{20,12},{24,16},{28,20},{1,25},{... | collective-permute-start | bytes 417800 | tf_op jit(solution)/shard_map/ppermute | solution.py:101
  34.9 2.0 %collective-permute-start.7 = (bf16[128,2048]{1,0:T(8,128)(2,1)S(1)}, bf16[128,2048]{1,0:T(8,128)(2,1)S(1)}, u32[]{:S(2)}, u32[]{:S(2)}) collective-permute-start(bf16[128,2048]{1,0:T(8,128)(2,1)S(1)} %slice.308), channel_id=1, source_target_pairs={{0,1},{1,0},{2,3},{3,2},{4,5},{5,4},{6,7},{7,6},{8,9},{9,8},{10,11... | collective-permute-start | bytes 1572872 | tf_op jit(solution)/shard_map/ppermute | solution.py:90
  37.0 8.5 %collective-permute-start.8 = (bf16[64,2048]{1,0:T(8,128)(2,1)S(1)}, bf16[64,2048]{1,0:T(8,128)(2,1)S(1)}, u32[]{:S(2)}, u32[]{:S(2)}) collective-permute-start(bf16[64,2048]{1,0:T(8,128)(2,1)S(1)} %slice.309), channel_id=1, source_target_pairs={{0,2},{1,3},{2,0},{3,1},{4,6},{5,7},{6,4},{7,5},{8,10},{9,11},{10,... | collective-permute-start | bytes 786440 | tf_op jit(solution)/shard_map/ppermute | solution.py:90

commit v22 on v12

--- a/solution.py
+++ b/solution.py
@@ -87,9 +87,7 @@
         half = partial.shape[0] // 2
         bit = 1 << level
         perm = [(i, i ^ bit) for i in range(time_groups)]
-        outgoing = partial[:half]
-        if level > 0:
-            outgoing = outgoing.astype(jnp.bfloat16)
+        outgoing = partial[:half].astype(jnp.bfloat16)
         received = lax.ppermute(outgoing, "tm", perm)
         partial = partial[half:] + received.astype(jnp.float32)
     return partial

time: 46 us -> 48.3 us (1.050)
  waiting for transfers between devices: 25.1 us -> 19.6 us
  local copies, waits for them, and re-layouts: 1.21 us -> 6.65 us
  matrix products: 3.1 us -> 4.37 us
  other arithmetic: 6.02 us -> 6.71 us
    ppermute x7, waiting for transfers between devices: 19.1 us -> 13.5 us  [uv_exchange(): pieces.append(lax.ppermute(outgoing[shift], 'uv', perm))]
    unnamed x10, local copies, waits for them, and re-layouts: 0.28 us -> 4.18 us
    dot_general x1, matrix products: 0.85 us -> 2.12 us  [per_device(): jnp.dot(weights, arrived[:, :row_width], preferred_element_type=jnp.float32)]
    slice x1, local copies, waits for them, and re-layouts: 0.09 us -> 1 us  [per_device(): arr_anchor = arrived[:, row_width].astype(jnp.int32)]
    another operation x1, local copies, waits for them, and re-layouts: 0.02 us -> 0.68 us  [uv_exchange(): return jnp.stack(pieces)]
    unnamed x1, other arithmetic: 0.01 us -> 0.66 us
  transfers between devices with their start and end apart: 9 -> 9, of which waited for: 7 -> 7; matrix products, arithmetic and copies ran while one was open for 9% -> 19% of each run, Pallas kernels for 0% -> 0%
where the time goes in v22:
time: 48.3 us; the launch traced here: 47.8 us
  waiting for transfers between devices  19.6 us (41%)
  starting transfers between devices  10.3 us (21%)
  other arithmetic  6.71 us (14%)
  local copies, waits for them, and re-layouts  6.65 us (14%)
  matrix products  4.37 us (9%)
    ppermute x7, waiting for transfers between devices, uv_exchange(): pieces.append(lax.ppermute(outgoing[shift], 'uv', perm))  13.5 us
    ppermute x7, starting transfers between devices, uv_exchange(): pieces.append(lax.ppermute(outgoing[shift], 'uv', perm))  8.62 us
    ppermute x2, waiting for transfers between devices, halving_reduce(): received = lax.ppermute(outgoing, 'tm', perm)  6.12 us
    unnamed x10, local copies, waits for them, and re-layouts  4.18 us
    dot_general x1, matrix products, per_device(): jnp.dot(weights, arrived[:, :row_width], preferred_element_type=jnp.float32)  2.12 us
    ppermute x2, starting transfers between devices, halving_reduce(): received = lax.ppermute(outgoing, 'tm', perm)  1.64 us
    dot_general x1, matrix products, per_device(): jnp.dot(lhs, delay_halves(), preferred_element_type=jnp.float32) * out_scale  1.51 us
    another operation x2, other arithmetic  1.28 us
  transfers between devices with their start and end apart: 9, of which 7 were waited for; matrix products, arithmetic and copies ran while one was open for 19% of the time, Pallas kernels for 0%

profile of v22, /device:TPU:12, one launch (start us, length us, event | category | flops | bytes accessed | tf_op | source)
XLA Modules:
  0.0 47.8 jit_solution(17863289310925994024)
XLA Ops:
  0.0 0.0 copy-start
  0.0 0.8 %fusion.89 = s32[11,128]{1,0:T(8,128)S(1)} fusion(s32[1,8]{1,0:T(1,128)} %bitcast.83, s32[8,32]{1,0:T(8,128)} %bitcast.62, s32[1,128]{1,0:T(1,128)} %param.15, s32[1,128]{1,0:T(1,128)} %param.14), kind=kLoop, calls=%fused_computation.131 | loop fusion | flops 4224 | bytes 7712 | tf_op jit(solution)/shard_map/concatenate | solution.py:118
  0.8 0.1 eq.83
  0.9 0.1 pad_add_fusion.1
  1.0 0.1 dynamic_slice.7
  1.1 0.1 iota_compare_fusion.1
  1.1 0.1 lt.56
  1.2 0.3 convolution_convert_fusion.1
  1.5 0.0 copy-done
  1.5 0.5 %convolution_convert_fusion = bf16[256,2048]{1,0:T(8,128)(2,1)S(1)} fusion(bf16[1,128,2048]{2,1,0:T(8,128)(2,1)S(1)} %copy-done, s32[256]{0:T(256)S(1)} %eq.83, pred[256]{0:T(512)(128)(4,1)S(1)} %lt.56), kind=kOutput, calls=%fused_computation.17 | convolution fusion | flops 134807552 | bytes 1574144 | tf_op jit(solution)/shard_map/dot_general | solution.py:140
  2.0 0.1 pad_maximum_fusion.1
  2.0 1.6 %collective-permute-start = (bf16[32,2176]{1,0:T(8,128)(2,1)S(1)}, bf16[32,2176]{1,0:T(8,128)(2,1)S(1)}, u32[]{:S(2)}, u32[]{:S(2)}) collective-permute-start(bf16[32,2176]{1,0:T(8,128)(2,1)S(1)} %get-tuple-element.62), channel_id=1, source_target_pairs={{0,4},{4,8},{8,12},{12,16},{16,20},{20,24},{24,28},{28,0},{1,5},{5... | collective-permute-start | bytes 417800 | tf_op jit(solution)/shard_map/ppermute | solution.py:102
  3.6 1.6 %collective-permute-start.1 = (bf16[32,2176]{1,0:T(8,128)(2,1)S(1)}, bf16[32,2176]{1,0:T(8,128)(2,1)S(1)}, u32[]{:S(2)}, u32[]{:S(2)}) collective-permute-start(bf16[32,2176]{1,0:T(8,128)(2,1)S(1)} %get-tuple-element.63), channel_id=1, source_target_pairs={{0,8},{4,12},{8,16},{12,20},{16,24},{20,28},{24,0},{28,4},{1,9},{5... | collective-permute-start | bytes 417800 | tf_op jit(solution)/shard_map/ppermute | solution.py:102
  5.2 1.2 %collective-permute-start.2 = (bf16[32,2176]{1,0:T(8,128)(2,1)S(1)}, bf16[32,2176]{1,0:T(8,128)(2,1)S(1)}, u32[]{:S(2)}, u32[]{:S(2)}) collective-permute-start(bf16[32,2176]{1,0:T(8,128)(2,1)S(1)} %get-tuple-element.64), channel_id=1, source_target_pairs={{0,12},{4,16},{8,20},{12,24},{16,28},{20,0},{24,4},{28,8},{1,13},{... | collective-permute-start | bytes 417800 | tf_op jit(solution)/shard_map/ppermute | solution.py:102
  6.4 1.7 %collective-permute-start.3 = (bf16[32,2176]{1,0:T(8,128)(2,1)S(1)}, bf16[32,2176]{1,0:T(8,128)(2,1)S(1)}, u32[]{:S(2)}, u32[]{:S(2)}) collective-permute-start(bf16[32,2176]{1,0:T(8,128)(2,1)S(1)} %get-tuple-element.65), channel_id=1, source_target_pairs={{0,16},{4,20},{8,24},{12,28},{16,0},{20,4},{24,8},{28,12},{1,17},{... | collective-permute-start | bytes 417800 | tf_op jit(solution)/shard_map/ppermute | solution.py:102
  8.1 1.3 %collective-permute-start.4 = (bf16[32,2176]{1,0:T(8,128)(2,1)S(1)}, bf16[32,2176]{1,0:T(8,128)(2,1)S(1)}, u32[]{:S(2)}, u32[]{:S(2)}) collective-permute-start(bf16[32,2176]{1,0:T(8,128)(2,1)S(1)} %get-tuple-element.66), channel_id=1, source_target_pairs={{0,20},{4,24},{8,28},{12,0},{16,4},{20,8},{24,12},{28,16},{1,21},{... | collective-permute-start | bytes 417800 | tf_op jit(solution)/shard_map/ppermute | solution.py:102
  9.4 0.7 %bitcast_dynamic-update-slice_fusion.7 = bf16[8,32,2176]{2,1,0:T(8,128)(2,1)} fusion(bf16[256,128]{1,0:T(8,128)(2,1)S(1)} %convolution_convert_fusion.1, bf16[256,2048]{1,0:T(8,128)(2,1)S(1)} %convolution_convert_fusion), kind=kLoop, calls=%fused_computation.63 | loop fusion | flops 278527 | bytes 1253376
  10.0 0.6 %fusion.78 = (f32[1024,32]{0,1:T(8,128)S(1)}, f32[1024,32]{0,1:T(8,128)S(1)}) fusion(s32[32]{0:T(128)S(1)} %iota_multiply_fusion), kind=kLoop, calls=%fused_computation.117 | loop fusion | flops 458752 | bytes 262272 | tf_op jit(solution)/shard_map/cos | solution.py:51
  10.6 0.1 scatter.15
  10.8 0.1 scatter.16
  10.9 0.1 scatter.19
  11.0 0.1 iota_add_fusion
  11.0 0.1 add.345
  11.2 0.5 %fusion.75 = (f32[1024,32]{0,1:T(8,128)S(1)}, f32[1024,32]{0,1:T(8,128)S(1)}) fusion(), kind=kLoop, calls=%fused_computation.114 | loop fusion | flops 458752 | bytes 262144 | tf_op jit(solution)/shard_map/sin | solution.py:52
  11.7 0.0 collective-permute-done
  11.7 1.3 %collective-permute-start.5 = (bf16[32,2176]{1,0:T(8,128)(2,1)S(1)}, bf16[32,2176]{1,0:T(8,128)(2,1)S(1)}, u32[]{:S(2)}, u32[]{:S(2)}) collective-permute-start(bf16[32,2176]{1,0:T(8,128)(2,1)S(1)} %get-tuple-element.67), channel_id=1, source_target_pairs={{0,24},{4,28},{8,0},{12,4},{16,8},{20,12},{24,16},{28,20},{1,25},{... | collective-permute-start | bytes 417800 | tf_op jit(solution)/shard_map/ppermute | solution.py:102
  13.0 0.7 %bitcast_dynamic-update-slice_fusion.6 = bf16[8,32,2176]{2,1,0:T(8,128)(2,1)} fusion(bf16[8,32,2176]{2,1,0:T(8,128)(2,1)} %bitcast_dynamic-update-slice_fusion.7, bf16[32,2176]{1,0:T(8,128)(2,1)S(1)} %collective-permute-done), kind=kLoop, calls=%fused_computation.62 | loop fusion | bytes 278528
  13.7 9.0 %collective-permute-done.1 = bf16[32,2176]{1,0:T(8,128)(2,1)S(1)} collective-permute-done((bf16[32,2176]{1,0:T(8,128)(2,1)S(1)}, bf16[32,2176]{1,0:T(8,128)(2,1)S(1)}, u32[]{:S(2)}, u32[]{:S(2)}) %collective-permute-start.1) | collective-permute-done | bytes 139296 | tf_op jit(solution)/shard_map/ppermute | solution.py:102
  22.6 0.0 collective-permute-start.6
  22.6 0.7 %bitcast_dynamic-update-slice_fusion.5 = bf16[8,32,2176]{2,1,0:T(8,128)(2,1)} fusion(bf16[8,32,2176]{2,1,0:T(8,128)(2,1)} %bitcast_dynamic-update-slice_fusion.6, bf16[32,2176]{1,0:T(8,128)(2,1)S(1)} %collective-permute-done.1), kind=kLoop, calls=%fused_computation.61 | loop fusion | bytes 278528
  23.3 2.3 %collective-permute-done.2 = bf16[32,2176]{1,0:T(8,128)(2,1)S(1)} collective-permute-done((bf16[32,2176]{1,0:T(8,128)(2,1)S(1)}, bf16[32,2176]{1,0:T(8,128)(2,1)S(1)}, u32[]{:S(2)}, u32[]{:S(2)}) %collective-permute-start.2) | collective-permute-done | bytes 139296 | tf_op jit(solution)/shard_map/ppermute | solution.py:102
  25.6 0.7 %bitcast_dynamic-update-slice_fusion.4 = bf16[8,32,2176]{2,1,0:T(8,128)(2,1)} fusion(bf16[8,32,2176]{2,1,0:T(8,128)(2,1)} %bitcast_dynamic-update-slice_fusion.5, bf16[32,2176]{1,0:T(8,128)(2,1)S(1)} %collective-permute-done.2), kind=kLoop, calls=%fused_computation.60 | loop fusion | bytes 278528
  26.3 1.2 %collective-permute-done.3 = bf16[32,2176]{1,0:T(8,128)(2,1)S(1)} collective-permute-done((bf16[32,2176]{1,0:T(8,128)(2,1)S(1)}, bf16[32,2176]{1,0:T(8,128)(2,1)S(1)}, u32[]{:S(2)}, u32[]{:S(2)}) %collective-permute-start.3) | collective-permute-done | bytes 139296 | tf_op jit(solution)/shard_map/ppermute | solution.py:102
  27.4 0.7 %bitcast_dynamic-update-slice_fusion.3 = bf16[8,32,2176]{2,1,0:T(8,128)(2,1)} fusion(bf16[8,32,2176]{2,1,0:T(8,128)(2,1)} %bitcast_dynamic-update-slice_fusion.4, bf16[32,2176]{1,0:T(8,128)(2,1)S(1)} %collective-permute-done.3), kind=kLoop, calls=%fused_computation.59 | loop fusion | bytes 278528
  28.1 0.0 collective-permute-done.4
  28.1 0.7 %bitcast_dynamic-update-slice_fusion.2 = bf16[8,32,2176]{2,1,0:T(8,128)(2,1)} fusion(bf16[8,32,2176]{2,1,0:T(8,128)(2,1)} %bitcast_dynamic-update-slice_fusion.3, bf16[32,2176]{1,0:T(8,128)(2,1)S(1)} %collective-permute-done.4), kind=kLoop, calls=%fused_computation.58 | loop fusion | bytes 278528
  28.8 0.5 collective-permute-done.5
  29.3 0.7 %bitcast_dynamic-update-slice_fusion.1 = bf16[8,32,2176]{2,1,0:T(8,128)(2,1)} fusion(bf16[8,32,2176]{2,1,0:T(8,128)(2,1)} %bitcast_dynamic-update-slice_fusion.2, bf16[32,2176]{1,0:T(8,128)(2,1)S(1)} %collective-permute-done.5), kind=kLoop, calls=%fused_computation.57 | loop fusion | bytes 278528
  29.9 0.6 %collective-permute-done.6 = bf16[32,2176]{1,0:T(8,128)(2,1)S(1)} collective-permute-done((bf16[32,2176]{1,0:T(8,128)(2,1)S(1)}, bf16[32,2176]{1,0:T(8,128)(2,1)S(1)}, u32[]{:S(2)}, u32[]{:S(2)}) %collective-permute-start.6) | collective-permute-done | bytes 139296 | tf_op jit(solution)/shard_map/ppermute | solution.py:102
  30.5 0.7 %bitcast_dynamic-update-slice_fusion = bf16[8,32,2176]{2,1,0:T(8,128)(2,1)} fusion(bf16[8,32,2176]{2,1,0:T(8,128)(2,1)} %bitcast_dynamic-update-slice_fusion.1, bf16[32,2176]{1,0:T(8,128)(2,1)S(1)} %collective-permute-done.6), kind=kLoop, calls=%fused_computation.56 | loop fusion | bytes 278528 | tf_op jit(solution)/shard_map/stack | solution.py:103
  31.2 1.0 %fusion.97 = (bf16[256,1]{1,0:T(8,128)(2,1)S(1)}, bf16[256,1]{1,0:T(8,128)(2,1)S(1)}) fusion(bf16[256,2176]{1,0:T(8,128)(2,1)} %bitcast.60), kind=kLoop, calls=%fused_computation.184 | loop fusion | bytes 2048 | tf_op jit(solution)/shard_map/slice | solution.py:151
  32.2 0.1 copy.11
  32.3 0.1 copy.12
  32.5 0.1 fusion.85
  32.6 2.1 %fusion.9 = f32[256,2048]{1,0:T(8,128)S(1)} fusion(bf16[256,2176]{1,0:T(8,128)(2,1)} %bitcast.61, f32[256]{0:T(256)S(1)} %bitcast.81, s32[256]{0:T(256)S(1)} %get-tuple-element.109, f32[256]{0:T(256)S(1)} %bitcast.80, s32[256]{0:T(256)S(1)} %get-tuple-element.105, f32[256]{0:T(256)S(1)} %bitcast.79, s32[256]{0:T(256)S(1)} %get-tuple-element.106, ...), kind=kOutput, calls=%fused_computation.22 | convolution fusion | flops 271581184 | bytes 3180544 | tf_op jit(solution)/shard_map/dot_general | solution.py:160
  34.7 0.1 slice.308
  34.8 0.1 collective-permute-start.7
  34.9 0.1 multiply_subtract_fusion.1
  34.9 1.3 %multiply_subtract_fusion = (f32[1024,32,32]{0,2,1:T(8,128)S(1)}, f32[1024,32,32]{0,2,1:T(8,128)S(1)}) fusion(f32[1024,32]{0,1:T(8,128)S(1)} %get-tuple-element.122, f32[1024,32]{0,1:T(8,128)S(1)} %get-tuple-element.113, f32[1024,32]{0,1:T(8,128)S(1)} %get-tuple-element.123, f32[1024,32]{0,1:T(8,128)S(1)} %get-tuple-element.112), kind=kLoop, calls=%fused_computation.9 | loop fusion | flops 6291456 | bytes 8912896 | tf_op jit(solution)/shard_map/sub | solution.py:53
  36.2 0.5 %collective-permute-done.7 = bf16[128,2048]{1,0:T(8,128)(2,1)S(1)} collective-permute-done((bf16[128,2048]{1,0:T(8,128)(2,1)S(1)}, bf16[128,2048]{1,0:T(8,128)(2,1)S(1)}, u32[]{:S(2)}, u32[]{:S(2)}) %collective-permute-start.7) | collective-permute-done | bytes 524320 | tf_op jit(solution)/shard_map/ppermute | solution.py:91
  36.8 0.1 slice_add_fusion
  36.9 1.6 %collective-permute-start.8 = (bf16[64,2048]{1,0:T(8,128)(2,1)S(1)}, bf16[64,2048]{1,0:T(8,128)(2,1)S(1)}, u32[]{:S(2)}, u32[]{:S(2)}) collective-permute-start(bf16[64,2048]{1,0:T(8,128)(2,1)S(1)} %slice.309), channel_id=1, source_target_pairs={{0,2},{1,3},{2,0},{3,1},{4,6},{5,7},{6,4},{7,5},{8,10},{9,11},{10,... | collective-permute-start | bytes 786440 | tf_op jit(solution)/shard_map/ppermute | solution.py:91
  38.5 1.3 %fusion.5 = (bf16[1024,1024]{0,1:T(8,128)(2,1)S(1)}, bf16[1024,1024]{0,1:T(8,128)(2,1)S(1)}) fusion(f32[1024,32,32]{0,2,1:T(8,128)S(1)} %get-tuple-element.70, f32[1024]{0:T(1024)S(1)} %multiply_subtract_fusion.1, f32[1024,32,32]{0,2,1:T(8,128)S(1)} %get-tuple-element.71), kind=kLoop, calls=%fused_computation.7 | loop fusion | flops 4194304 | bytes 12587008 | tf_op jit(solution)/shard_map/convert
  39.8 5.6 %collective-permute-done.8 = bf16[64,2048]{1,0:T(8,128)(2,1)S(1)} collective-permute-done((bf16[64,2048]{1,0:T(8,128)(2,1)S(1)}, bf16[64,2048]{1,0:T(8,128)(2,1)S(1)}, u32[]{:S(2)}, u32[]{:S(2)}) %collective-permute-start.8) | collective-permute-done | bytes 262176 | tf_op jit(solution)/shard_map/ppermute | solution.py:91
  45.4 1.5 %fusion.6 = f32[128,1024]{1,0:T(8,128)S(1)} fusion(bf16[1024,1024]{0,1:T(8,128)(2,1)S(1)} %get-tuple-element.91, bf16[1024,1024]{0,1:T(8,128)(2,1)S(1)} %get-tuple-element.90, bf16[64,1024]{1,0:T(8,128)(2,1)S(1)} %get-tuple-element.73, bf16[64,1024]{1,0:T(8,128)(2,1)S(1)} %get-tuple-element.72, bf16[64,2048]{1,0:T(8,128)(2,1)S(1)} %fusion.11), kind=kOutput, calls=%fused_computation.18 | convolution fusion | flops 546963456 | bytes 5242880 | tf_op jit(solution)/shard_map/dot_general | solution.py:171
  47.0 0.8 %pad_maximum_fusion = f32[64,2048]{1,0:T(8,128)} fusion(f32[64,1024]{1,0:T(8,128)S(1)} %get-tuple-element.69, f32[64,1024]{1,0:T(8,128)S(1)} %get-tuple-element.68), kind=kLoop, calls=%fused_computation.32 | loop fusion | flops 131072 | bytes 1048576 | tf_op jit(solution)/shard_map/concatenate | solution.py:173
  (20 shorter events, 0.3 us)
Async XLA Ops:
  0.0 1.5 %copy-start = (bf16[1,128,2048]{2,1,0:T(8,128)(2,1)S(1)}, bf16[1,128,2048]{2,1,0:T(8,128)(2,1)}, u32[]{:S(2)}) copy-start(bf16[1,128,2048]{2,1,0:T(8,128)(2,1)} %param.13) | copy-start | bytes 1572868
  2.0 9.6 %collective-permute-start = (bf16[32,2176]{1,0:T(8,128)(2,1)S(1)}, bf16[32,2176]{1,0:T(8,128)(2,1)S(1)}, u32[]{:S(2)}, u32[]{:S(2)}) collective-permute-start(bf16[32,2176]{1,0:T(8,128)(2,1)S(1)} %get-tuple-element.62), channel_id=1, source_target_pairs={{0,4},{4,8},{8,12},{12,16},{16,20},{20,24},{24,28},{28,0},{1,5},{5... | collective-permute-start | bytes 417800 | tf_op jit(solution)/shard_map/ppermute | solution.py:102
  3.6 19.0 %collective-permute-start.1 = (bf16[32,2176]{1,0:T(8,128)(2,1)S(1)}, bf16[32,2176]{1,0:T(8,128)(2,1)S(1)}, u32[]{:S(2)}, u32[]{:S(2)}) collective-permute-start(bf16[32,2176]{1,0:T(8,128)(2,1)S(1)} %get-tuple-element.63), channel_id=1, source_target_pairs={{0,8},{4,12},{8,16},{12,20},{16,24},{20,28},{24,0},{28,4},{1,9},{5... | collective-permute-start | bytes 417800 | tf_op jit(solution)/shard_map/ppermute | solution.py:102
  5.2 20.4 %collective-permute-start.2 = (bf16[32,2176]{1,0:T(8,128)(2,1)S(1)}, bf16[32,2176]{1,0:T(8,128)(2,1)S(1)}, u32[]{:S(2)}, u32[]{:S(2)}) collective-permute-start(bf16[32,2176]{1,0:T(8,128)(2,1)S(1)} %get-tuple-element.64), channel_id=1, source_target_pairs={{0,12},{4,16},{8,20},{12,24},{16,28},{20,0},{24,4},{28,8},{1,13},{... | collective-permute-start | bytes 417800 | tf_op jit(solution)/shard_map/ppermute | solution.py:102
  6.4 21.1 %collective-permute-start.3 = (bf16[32,2176]{1,0:T(8,128)(2,1)S(1)}, bf16[32,2176]{1,0:T(8,128)(2,1)S(1)}, u32[]{:S(2)}, u32[]{:S(2)}) collective-permute-start(bf16[32,2176]{1,0:T(8,128)(2,1)S(1)} %get-tuple-element.65), channel_id=1, source_target_pairs={{0,16},{4,20},{8,24},{12,28},{16,0},{20,4},{24,8},{28,12},{1,17},{... | collective-permute-start | bytes 417800 | tf_op jit(solution)/shard_map/ppermute | solution.py:102
  8.1 20.0 %collective-permute-start.4 = (bf16[32,2176]{1,0:T(8,128)(2,1)S(1)}, bf16[32,2176]{1,0:T(8,128)(2,1)S(1)}, u32[]{:S(2)}, u32[]{:S(2)}) collective-permute-start(bf16[32,2176]{1,0:T(8,128)(2,1)S(1)} %get-tuple-element.66), channel_id=1, source_target_pairs={{0,20},{4,24},{8,28},{12,0},{16,4},{20,8},{24,12},{28,16},{1,21},{... | collective-permute-start | bytes 417800 | tf_op jit(solution)/shard_map/ppermute | solution.py:102
  11.7 17.6 %collective-permute-start.5 = (bf16[32,2176]{1,0:T(8,128)(2,1)S(1)}, bf16[32,2176]{1,0:T(8,128)(2,1)S(1)}, u32[]{:S(2)}, u32[]{:S(2)}) collective-permute-start(bf16[32,2176]{1,0:T(8,128)(2,1)S(1)} %get-tuple-element.67), channel_id=1, source_target_pairs={{0,24},{4,28},{8,0},{12,4},{16,8},{20,12},{24,16},{28,20},{1,25},{... | collective-permute-start | bytes 417800 | tf_op jit(solution)/shard_map/ppermute | solution.py:102
  22.6 7.9 %collective-permute-start.6 = (bf16[32,2176]{1,0:T(8,128)(2,1)S(1)}, bf16[32,2176]{1,0:T(8,128)(2,1)S(1)}, u32[]{:S(2)}, u32[]{:S(2)}) collective-permute-start(bf16[32,2176]{1,0:T(8,128)(2,1)S(1)} %get-tuple-element.61), channel_id=1, source_target_pairs={{0,28},{4,0},{8,4},{12,8},{16,12},{20,16},{24,20},{28,24},{1,29},{... | collective-permute-start | bytes 417800 | tf_op jit(solution)/shard_map/ppermute | solution.py:102
  34.8 2.0 %collective-permute-start.7 = (bf16[128,2048]{1,0:T(8,128)(2,1)S(1)}, bf16[128,2048]{1,0:T(8,128)(2,1)S(1)}, u32[]{:S(2)}, u32[]{:S(2)}) collective-permute-start(bf16[128,2048]{1,0:T(8,128)(2,1)S(1)} %slice.308), channel_id=1, source_target_pairs={{0,1},{1,0},{2,3},{3,2},{4,5},{5,4},{6,7},{7,6},{8,9},{9,8},{10,11... | collective-permute-start | bytes 1572872 | tf_op jit(solution)/shard_map/ppermute | solution.py:91
  36.9 8.4 %collective-permute-start.8 = (bf16[64,2048]{1,0:T(8,128)(2,1)S(1)}, bf16[64,2048]{1,0:T(8,128)(2,1)S(1)}, u32[]{:S(2)}, u32[]{:S(2)}) collective-permute-start(bf16[64,2048]{1,0:T(8,128)(2,1)S(1)} %slice.309), channel_id=1, source_target_pairs={{0,2},{1,3},{2,0},{3,1},{4,6},{5,7},{6,4},{7,5},{8,10},{9,11},{10,... | collective-permute-start | bytes 786440 | tf_op jit(solution)/shard_map/ppermute | solution.py:91
